TPU v7x, 32 devices: a whole 2x2x4 slice. The times are simulated.
32 devices in a mesh: groups: 2 (over x), seq: 8 (over z, y), rep: 2 (over core).
Axes of the slice: x: 2, y: 2, z: 4, core: 2. Of those that a mesh axis runs over, the one named last changes fastest.
Arguments:
- inputs: bfloat16 [4, 4096, 1536], P(('groups', 'rep'), 'seq'), parts along dimension 0, may hold values from -6 to 6
- lengths: int32 [4], P(('groups', 'rep')), parts along dimension 0, may hold values from 2049 to 4096, as said below
- conv_weight: bfloat16 [3, 48, 1536], replicated, may hold values from -0.5 to 0.5
- point_weight: bfloat16 [1536, 1536], replicated, may hold values from -0.15625 to 0.15625
- cotangent: bfloat16 [4, 4096, 1536], P(('groups', 'rep'), 'seq'), parts along dimension 0, may hold values from -6 to 6
Outputs:
- output: bfloat16 [4, 4096, 1536], P(('groups', 'rep'), 'seq'), parts along dimension 0
- grad_inputs: bfloat16 [4, 4096, 1536], P(('groups', 'rep'), 'seq'), parts along dimension 0
- grad_point: float32 [3072, 1536], P(('groups', 'seq', 'rep')), parts along dimension 0
- grad_conv: float32 [6, 48, 1536], P('groups'), parts along dimension 0
There are 2 independent parts, one for each index of `groups`. A program takes and returns all parts, laid end to end along the dimension named above; an argument that names none is the same for every part. Nothing has to cross between parts.
Inputs may be any that keep to these rules, and one draw needn't show every extreme that they name: `lengths`: one sample in each draw has all 4096 bins valid.
All inputs are finite; a program needn't handle non-finite values.
Results may differ from a plain program's by a relative error of at most 0.0031.
Values may be sent and summed in bfloat16 or wider, within the bound.
No kernel may reach another device: no remote copies, remote signals or barrier semaphores. Data moves between devices by JAX's collectives and lax.ppermute only.
A program may use at most 128 MiB of HBM per device.

v0:
```python
import math

import jax
import jax.numpy as jnp
from jax import lax
from jax.sharding import PartitionSpec as P

GROUP_CHANNELS = 48
DILATION_STEP = 64


def with_halo(cells, sides, width):
    for axis, dim in sides:
        count = lax.axis_size(axis)
        ends = count - 1
        head = lax.slice_in_dim(cells, 0, width, axis=dim)
        tail = lax.slice_in_dim(cells, cells.shape[dim] - width, cells.shape[dim], axis=dim)
        cells = jnp.concatenate(
            [
                lax.ppermute(tail, axis, [(i, (i + 1) % count) for i in range(ends)]),
                cells,
                lax.ppermute(head, axis, [((i + 1) % count, i) for i in range(ends)]),
            ],
            axis=dim,
        )
    return cells


def gelu_pair(pre):
    cdf = 0.5 * (1.0 + jax.scipy.special.erf(pre * 0.7071067811865476))
    dens = jnp.exp(-0.5 * pre * pre) * 0.3989422804014327
    return (pre * cdf, cdf + pre * dens)


def conv_taps(padded_input, weight, sequence_length):
    group_count = weight.shape[2] // GROUP_CHANNELS
    total = jnp.zeros(
        (padded_input.shape[0], sequence_length, group_count, GROUP_CHANNELS), jnp.float32
    )
    for kernel_offset in range(3):
        segment_window = padded_input[
            :, kernel_offset * DILATION_STEP : kernel_offset * DILATION_STEP + sequence_length
        ].reshape(padded_input.shape[0], sequence_length, group_count, GROUP_CHANNELS)
        wk = weight[kernel_offset].reshape(GROUP_CHANNELS, group_count, GROUP_CHANNELS)
        total = total + jnp.einsum(
            "slgi,igj->slgj", segment_window, wk, preferred_element_type=jnp.float32
        )
    return total.reshape(padded_input.shape[0], sequence_length, group_count * GROUP_CHANNELS)


def transpose_taps(padded_input, weight, sequence_length):
    group_count = weight.shape[2] // GROUP_CHANNELS
    total = jnp.zeros(
        (padded_input.shape[0], sequence_length, group_count, GROUP_CHANNELS), jnp.float32
    )
    for kernel_offset in range(3):
        segment_window = padded_input[
            :,
            (2 - kernel_offset) * DILATION_STEP : (2 - kernel_offset) * DILATION_STEP
            + sequence_length,
        ].reshape(padded_input.shape[0], sequence_length, group_count, GROUP_CHANNELS)
        wk = weight[kernel_offset].reshape(GROUP_CHANNELS, group_count, GROUP_CHANNELS)
        total = total + jnp.einsum(
            "slgj,igj->slgi", segment_window, wk, preferred_element_type=jnp.float32
        )
    return total.reshape(padded_input.shape[0], sequence_length, group_count * GROUP_CHANNELS)


def weight_taps(input_padded, output_gradient, sequence_length):
    group_count = output_gradient.shape[2] // GROUP_CHANNELS
    grouped = output_gradient.reshape(
        output_gradient.shape[0], sequence_length, group_count, GROUP_CHANNELS
    )
    taps = []
    for kernel_offset in range(3):
        segment_window = input_padded[
            :, kernel_offset * DILATION_STEP : kernel_offset * DILATION_STEP + sequence_length
        ].reshape(output_gradient.shape[0], sequence_length, group_count, GROUP_CHANNELS)
        taps.append(
            jnp.einsum(
                "slgi,slgj->igj", segment_window, grouped, preferred_element_type=jnp.float32
            ).reshape(GROUP_CHANNELS, group_count * GROUP_CHANNELS)
        )
    return jnp.stack(taps)


def on_device(inputs, lengths, conv_weight, point_weight, cotangent):
    local_bins = inputs.shape[1]
    chans = inputs.shape[2]
    seq_count = lax.axis_size("seq")
    rep_count = lax.axis_size("rep")
    seq_index = lax.axis_index("seq")
    positions = seq_index * local_bins + jnp.arange(local_bins, dtype=jnp.int32)
    mask = (positions[None, :] < lengths[:, None]).astype(jnp.float32)
    mask3 = mask[:, :, None]
    masked_input = (inputs.astype(jnp.float32) * mask3).astype(jnp.bfloat16)
    scale = 1.0 / math.sqrt(rep_count * seq_count * local_bins)
    padded_input = with_halo(masked_input, (("seq", 1),), DILATION_STEP)
    pre = conv_taps(padded_input, conv_weight, local_bins)
    act_val, slope = gelu_pair(pre)
    act = (act_val * mask3).astype(jnp.bfloat16)
    act_rows = act.reshape(local_bins, chans)
    cot_rows = cotangent.reshape(local_bins, chans)
    proj = jnp.dot(act_rows, point_weight, preferred_element_type=jnp.float32).reshape(inputs.shape)
    output = (inputs.astype(jnp.float32) + proj).astype(jnp.bfloat16)
    back = lax.dot_general(
        cot_rows, point_weight, (((1,), (1,)), ((), ())), preferred_element_type=jnp.float32
    )
    preactivation_gradient = (back.reshape(inputs.shape) * slope * mask3).astype(jnp.bfloat16)
    padded_gradient = with_halo(preactivation_gradient, (("seq", 1),), DILATION_STEP)
    spread = transpose_taps(padded_gradient, conv_weight, local_bins)
    conv_local = weight_taps(padded_input, preactivation_gradient, local_bins)
    grad_conv = lax.psum(conv_local, ("seq", "rep")) * scale
    grad_inputs = (cotangent.astype(jnp.float32) + mask3 * spread).astype(jnp.bfloat16)
    grad_point = lax.psum_scatter(
        lax.dot_general(
            act_rows, cot_rows, (((0,), (0,)), ((), ())), preferred_element_type=jnp.float32
        ),
        ("seq", "rep"),
        scatter_dimension=0,
        tiled=True,
    )
    grad_point = grad_point * scale
    return (output, grad_inputs, grad_point, grad_conv)


def solution(mesh):
    return jax.shard_map(
        on_device,
        mesh=mesh,
        in_specs=(
            P(("groups", "rep"), "seq", None),
            P(("groups", "rep")),
            P(),
            P(),
            P(("groups", "rep"), "seq", None),
        ),
        out_specs=(
            P(("groups", "rep"), "seq", None),
            P(("groups", "rep"), "seq", None),
            P(("groups", "seq", "rep"), None),
            P("groups", None, None),
        ),
        check_vma=False,
    )
```

profile of v0, /device:TPU:0, one launch (start us, length us, event | category | flops | bytes accessed | tf_op | source)
XLA Modules:
  0.0 282.3 jit_solution(17731582967760469702)
XLA Ops:
  11.7 6.2 %collective-permute-start = (bf16[1,64,1536]{2,1,0:T(8,128)(2,1)}, bf16[1,64,1536]{2,1,0:T(8,128)(2,1)}, u32[]{:S(2)}, u32[]{:S(2)}) collective-permute-start(bf16[1,64,1536]{2,1,0:T(8,128)(2,1)} %get-tuple-element.11), channel_id=1, source_target_pairs={{0,2},{2,4},{4,6},{6,8},{8,10},{10,12},{12,14},{1,3},{3,5},{5,7},{... | collective-permute-start | bytes 589832 | tf_op jit(solution)/shard_map/ppermute | solution.py:20
  21.5 1.8 copy.35
  25.2 3.2 %fusion.29 = f32[32,512,48]{1,2,0:T(8,128)} fusion(bf16[48,32,48]{0,2,1:T(8,128)(2,1)} %bitcast.90, bf16[512,32,48]{0,2,1:T(8,128)(2,1)S(1)} %bitcast.73), kind=kOutput, calls=%fused_computation.48 | convolution fusion | flops 75497472 | bytes 4866048 | tf_op jit(solution)/shard_map/slgi,igj->slgj/dot_general | solution.py:45
  28.4 2.9 %pad_maximum_fusion.2 = (bf16[1,512,1536]{2,1,0:T(8,128)(2,1)}, bf16[1,512,1536]{2,1,0:T(8,128)(2,1)}) fusion(bf16[1,64,1536]{2,1,0:T(8,128)(2,1)} %collective-permute-done.1, bf16[1,512,1536]{2,1,0:T(8,128)(2,1)S(1)} %fusion.1, bf16[1,64,1536]{2,1,0:T(8,128)(2,1)} %collective-permute-done), kind=kLoop, calls=%fused_computation.21 | loop fusion | flops 6291456 | bytes 5111808 | tf_op jit(solution)/shard_map/concatenate | solution.py:18
  31.3 2.6 copy.38
  35.7 2.0 fusion.28
  38.7 2.2 add_add_fusion.1
  40.9 3.7 %copy.41 = f32[512,1536]{1,0:T(8,128)} copy(f32[512,1536]{0,1:T(8,128)} %bitcast.79) | data formatting | bytes 6291456 | tf_op jit(solution)/shard_map/reshape | solution.py:48
  44.6 7.0 %fusion.7 = bf16[512,1536]{1,0:T(8,128)(2,1)} fusion(f32[512,1536]{1,0:T(8,128)} %copy.41, bf16[1536,1536]{1,0:T(8,128)(2,1)} %param.8, bf16[1,512,1536]{2,1,0:T(8,128)(2,1)S(1)} %copy-done.10, f32[512]{0:T(512)S(1)} %fusion.16), kind=kOutput, calls=%fused_computation.18 | convolution fusion | flops 2424569856 | bytes 11012096 | tf_op jit(solution)/shard_map/dot_general | solution.py:106
  53.3 3.0 %fusion.27 = f32[32,48,48]{2,1,0:T(8,128)} fusion(bf16[512,32,48]{0,2,1:T(8,128)(2,1)S(1)} %bitcast.69, bf16[512,32,48]{0,2,1:T(8,128)(2,1)} %bitcast.77), kind=kOutput, calls=%fused_computation.46 | convolution fusion | flops 75497472 | bytes 3440640 | tf_op jit(solution)/shard_map/slgi,slgj->igj/dot_general | solution.py:80
  59.1 2.1 copy.52
  62.4 2.0 pad_maximum_fusion.4
  64.5 8.6 %fusion.8 = f32[1536,1536]{1,0:T(8,128)} fusion(bf16[1,512,1536]{2,1,0:T(8,128)(2,1)} %param.9, f32[1,512,1,1,1,1,1536]{1,6,5,4,3,2,0:T(8,128)} %bitcast.80, f32[512]{0:T(512)S(1)} %fusion.16), kind=kOutput, calls=%fused_computation.23 | convolution fusion | flops 2420637696 | bytes 14157824 | tf_op jit(solution)/shard_map/dot_general | solution.py:116
  74.6 4.2 %collective-permute-start.3 = (bf16[1,64,1536]{2,1,0:T(8,128)(2,1)S(1)}, bf16[1,64,1536]{2,1,0:T(8,128)(2,1)S(1)}, u32[]{:S(2)}, u32[]{:S(2)}) collective-permute-start(bf16[1,64,1536]{2,1,0:T(8,128)(2,1)S(1)} %get-tuple-element.6), channel_id=1, source_target_pairs={{0,2},{2,4},{4,6},{6,8},{8,10},{10,12},{12,14},{1,3},{3,5},{5,7},{... | collective-permute-start | bytes 589832 | tf_op jit(solution)/shard_map/ppermute | solution.py:20
  80.4 7.6 %fusion.2 = bf16[1,512,1536]{2,1,0:T(8,128)(2,1)} fusion(bf16[1,512,1536]{2,1,0:T(8,128)(2,1)} %param.5, bf16[1536,1536]{1,0:T(8,128)(2,1)} %param.8, f32[512,1536]{1,0:T(8,128)} %copy.41, f32[512]{0:T(512)S(1)} %fusion.16), kind=kOutput, calls=%fused_computation.7 | convolution fusion | flops 2422996992 | bytes 11012096 | tf_op jit(solution)/shard_map/dot_general | solution.py:104
  88.0 2.3 fusion.24
  91.7 2.6 copy.49
  97.5 2.3 add_add_fusion
  99.8 2.4 copy.51
  102.1 3.0 %add_convert_fusion = bf16[1,512,1536]{2,1,0:T(8,128)(2,1)} fusion(f32[1,512,1536]{2,1,0:T(8,128)S(1)} %copy.51, bf16[1,512,1536]{2,1,0:T(8,128)(2,1)} %param.9, f32[512]{0:T(512)S(1)} %fusion.16), kind=kLoop, calls=%fused_computation.13 | loop fusion | flops 3145728 | bytes 6293504 | tf_op jit(solution)/shard_map/convert_element_type | solution.py:114
  105.1 53.9 %all-reduce.2.cloned.1.call-done = f32[3,48,1536]{2,1,0:T(8,128)} async-done(((f32[3,48,1536]{2,1,0:T(8,128)}), f32[3,48,1536]{2,1,0:T(8,128)}) %all-reduce.2.cloned.1.call-update) | async-done | bytes 884752 | tf_op jit(solution)/shard_map/psum | solution.py:113
  159.1 2.2 broadcast_multiply_fusion
  161.2 112.3 %reduce-scatter.2.cloned.1.call-done = f32[96,1536]{1,0:T(8,128)} async-done(((f32[1536,1536]{1,0:T(8,128)}), f32[96,1536]{1,0:T(8,128)}) %reduce-scatter.2.cloned.1.call-update) | async-done | bytes 589840 | tf_op jit(solution)/shard_map/reduce_scatter | solution.py:115
  273.5 1.9 broadcast_multiply_fusion.1
  (49 shorter events, 25.5 us)
Async XLA Ops:
  7.2 151.9 %all-reduce.2.cloned.1.call-start = ((), (), s32[]{:S(2)}) async-start(), calls=%async_computation.2 | async-start | bytes 1769472 | tf_op jit(solution)/shard_map/psum | solution.py:113
  10.4 18.0 %collective-permute-start.1 = (bf16[1,64,1536]{2,1,0:T(8,128)(2,1)}, bf16[1,64,1536]{2,1,0:T(8,128)(2,1)}, u32[]{:S(2)}, u32[]{:S(2)}) collective-permute-start(bf16[1,64,1536]{2,1,0:T(8,128)(2,1)} %get-tuple-element.10), channel_id=1, source_target_pairs={{2,0},{4,2},{6,4},{8,6},{10,8},{12,10},{14,12},{3,1},{5,3},{7,5},{... | collective-permute-start | bytes 589832 | tf_op jit(solution)/shard_map/ppermute | solution.py:22
  11.7 16.7 %collective-permute-start = (bf16[1,64,1536]{2,1,0:T(8,128)(2,1)}, bf16[1,64,1536]{2,1,0:T(8,128)(2,1)}, u32[]{:S(2)}, u32[]{:S(2)}) collective-permute-start(bf16[1,64,1536]{2,1,0:T(8,128)(2,1)} %get-tuple-element.11), channel_id=1, source_target_pairs={{0,2},{2,4},{4,6},{6,8},{8,10},{10,12},{12,14},{1,3},{3,5},{5,7},{... | collective-permute-start | bytes 589832 | tf_op jit(solution)/shard_map/ppermute | solution.py:20
  35.6 5.3 %copy-start = (bf16[1,512,1536]{1,2,0:T(8,128)(2,1)}, bf16[1,512,1536]{1,2,0:T(8,128)(2,1)S(1)}, u32[]{:S(2)}) copy-start(bf16[1,512,1536]{1,2,0:T(8,128)(2,1)S(1)} %copy.34) | copy-start | bytes 4718596
  35.6 2.1 copy-start.2
  35.6 3.0 %copy-start.4 = (f32[32,512,48]{1,2,0:T(8,128)S(1)}, f32[32,512,48]{1,2,0:T(8,128)}, u32[]{:S(2)}) copy-start(f32[32,512,48]{1,2,0:T(8,128)} %fusion.29) | copy-start | bytes 9437188
  40.9 3.7 %copy-start.10 = (bf16[1,512,1536]{2,1,0:T(8,128)(2,1)S(1)}, bf16[1,512,1536]{2,1,0:T(8,128)(2,1)}, u32[]{:S(2)}) copy-start(bf16[1,512,1536]{2,1,0:T(8,128)(2,1)} %param.9) | copy-start | bytes 4718596
  53.3 4.4 %copy-start.1 = (bf16[1,512,1536]{1,2,0:T(8,128)(2,1)S(1)}, bf16[1,512,1536]{1,2,0:T(8,128)(2,1)}, u32[]{:S(2)}) copy-start(bf16[1,512,1536]{1,2,0:T(8,128)(2,1)} %copy-done) | copy-start | bytes 4718596
  57.7 3.5 %copy-start.9 = (f32[32,48,48]{2,1,0:T(8,128)S(1)}, f32[32,48,48]{2,1,0:T(8,128)}, u32[]{:S(2)}) copy-start(f32[32,48,48]{2,1,0:T(8,128)} %fusion.26) | copy-start | bytes 884740
  57.7 4.5 %copy-start.8 = (f32[32,48,48]{2,1,0:T(8,128)S(1)}, f32[32,48,48]{2,1,0:T(8,128)}, u32[]{:S(2)}) copy-start(f32[32,48,48]{2,1,0:T(8,128)} %fusion.27) | copy-start | bytes 884740
  64.5 209.1 %reduce-scatter.2.cloned.1.call-start = ((), (), s32[]{:S(2)}) async-start(), calls=%async_computation.1 | async-start | bytes 10027008 | tf_op jit(solution)/shard_map/reduce_scatter | solution.py:115
  73.2 1.4 copy-start.5
  74.6 15.7 %collective-permute-start.3 = (bf16[1,64,1536]{2,1,0:T(8,128)(2,1)S(1)}, bf16[1,64,1536]{2,1,0:T(8,128)(2,1)S(1)}, u32[]{:S(2)}, u32[]{:S(2)}) collective-permute-start(bf16[1,64,1536]{2,1,0:T(8,128)(2,1)S(1)} %get-tuple-element.6), channel_id=1, source_target_pairs={{0,2},{2,4},{4,6},{6,8},{8,10},{10,12},{12,14},{1,3},{3,5},{5,7},{... | collective-permute-start | bytes 589832 | tf_op jit(solution)/shard_map/ppermute | solution.py:20
  78.8 9.2 %copy-start.7 = (bf16[1,48,1536]{1,2,0:T(8,128)(2,1)S(1)}, bf16[1,48,1536]{1,2,0:T(8,128)(2,1)}, u32[]{:S(2)}) copy-start(bf16[1,48,1536]{1,2,0:T(8,128)(2,1)} %copy.37) | copy-start | bytes 442372
  78.8 11.5 %collective-permute-start.2 = (bf16[1,64,1536]{2,1,0:T(8,128)(2,1)S(1)}, bf16[1,64,1536]{2,1,0:T(8,128)(2,1)S(1)}, u32[]{:S(2)}, u32[]{:S(2)}) collective-permute-start(bf16[1,64,1536]{2,1,0:T(8,128)(2,1)S(1)} %get-tuple-element.7), channel_id=1, source_target_pairs={{2,0},{4,2},{6,4},{8,6},{10,8},{12,10},{14,12},{3,1},{5,3},{7,5},{... | collective-permute-start | bytes 589832 | tf_op jit(solution)/shard_map/ppermute | solution.py:22
  95.0 2.0 copy-start.3
  95.0 2.5 copy-start.6
Sparse Core Ops, SparseCore 0:
  64.6 94.4 all-reduce.1
  163.2 110.3 reduce-scatter.1
where the time goes:
time: 283 us; the launch traced here: 282 us
  waiting for transfers between devices  166 us (59%)
  matrix products  42.8 us (15%)
  local copies, waits for them, and re-layouts  29.9 us (11%)
  other arithmetic  15.1 us (5%)
  between operations  14.9 us (5%)
  starting transfers between devices  13.3 us (5%)
    reduce_scatter x1, waiting for transfers between devices, on_device(): lax.psum_scatter(lax.dot_general(act_rows, cot_rows, (((0,), (0,)), ((),...  112 us
    psum x1, waiting for transfers between devices, on_device(): grad_conv = lax.psum(conv_local, ('seq', 'rep')) * scale  53.9 us
    ppermute x2, starting transfers between devices, with_halo(): lax.ppermute(tail, axis, [(i, (i + 1) % count) for i in range(ends)])  10.4 us
    dot_general x1, matrix products, on_device(): lax.dot_general(act_rows, cot_rows, (((0,), (0,)), ((), ())), preferred_e...  8.65 us
    dot_general x1, matrix products, on_device(): jnp.dot(act_rows, point_weight, preferred_element_type=jnp.float32)  7.61 us
    dot_general x3, matrix products, conv_taps(): jnp.einsum('slgi,igj->slgj', segment_window, wk, preferred_element_type=j...  7.38 us
    dot_general x1, matrix products, on_device(): lax.dot_general(cot_rows, point_weight, (((1,), (1,)), ((), ())), preferr...  6.98 us
    slice x4, local copies, waits for them, and re-layouts, conv_taps(): weight[kernel_offset].reshape(GROUP_CHANNELS, group_count, GROUP_CHANNELS)  6.61 us
  transfers between devices with their start and end apart: 6, of which 2 were waited for; matrix products, arithmetic and copies ran while one was open for 16% of the time, Pallas kernels for 0%

commit v1 on v0

--- a/solution.py
+++ b/solution.py
@@ -84,6 +84,47 @@
     return jnp.stack(taps)
 
 
+def swap(value, axis, distance):
+    count = lax.axis_size(axis)
+    return lax.ppermute(value, axis, [(i, i ^ distance) for i in range(count)])
+
+
+def tree_sum(value):
+    for axis in ("rep", "seq"):
+        count = lax.axis_size(axis)
+        if count & (count - 1):
+            value = lax.psum(value, axis)
+            continue
+        distance = 1
+        while distance < count:
+            value = value + swap(value, axis, distance)
+            distance *= 2
+    return value
+
+
+def point_gradient(act_rows, cot_rows, seq_count, rep_count):
+    chans = act_rows.shape[1]
+    block = chans // (seq_count * rep_count)
+    blocks = act_rows.reshape(act_rows.shape[0], seq_count, rep_count, block)
+    rep_index = lax.axis_index("rep")
+
+    def rows_of(owner):
+        cols = lax.dynamic_index_in_dim(blocks, owner, axis=2, keepdims=False)
+        cols = cols.reshape(act_rows.shape[0], seq_count * block)
+        return lax.dot_general(
+            cols, cot_rows, (((0,), (0,)), ((), ())), preferred_element_type=jnp.float32
+        )
+
+    if rep_count == 2:
+        mine = rows_of(rep_index) + swap(rows_of(1 - rep_index), "rep", 1)
+    else:
+        full = lax.dot_general(
+            act_rows, cot_rows, (((0,), (0,)), ((), ())), preferred_element_type=jnp.float32
+        ).reshape(seq_count, rep_count, block, chans)
+        mine = lax.psum_scatter(full, "rep", scatter_dimension=1, tiled=True)
+        mine = mine.reshape(seq_count * block, chans)
+    return lax.psum_scatter(mine, "seq", scatter_dimension=0, tiled=True)
+
 def on_device(inputs, lengths, conv_weight, point_weight, cotangent):
     local_bins = inputs.shape[1]
     chans = inputs.shape[2]
@@ -110,17 +151,9 @@
     padded_gradient = with_halo(preactivation_gradient, (("seq", 1),), DILATION_STEP)
     spread = transpose_taps(padded_gradient, conv_weight, local_bins)
     conv_local = weight_taps(padded_input, preactivation_gradient, local_bins)
-    grad_conv = lax.psum(conv_local, ("seq", "rep")) * scale
+    grad_conv = tree_sum(conv_local) * scale
     grad_inputs = (cotangent.astype(jnp.float32) + mask3 * spread).astype(jnp.bfloat16)
-    grad_point = lax.psum_scatter(
-        lax.dot_general(
-            act_rows, cot_rows, (((0,), (0,)), ((), ())), preferred_element_type=jnp.float32
-        ),
-        ("seq", "rep"),
-        scatter_dimension=0,
-        tiled=True,
-    )
-    grad_point = grad_point * scale
+    grad_point = point_gradient(act_rows, cot_rows, seq_count, rep_count) * scale
     return (output, grad_inputs, grad_point, grad_conv)
 
 

time: 283 us -> 207 us (0.73)
  waiting for transfers between devices: 166 us -> 88.6 us
  matrix products: 42.8 us -> 36.4 us
  starting transfers between devices: 13.3 us -> 17.6 us
    reduce_scatter x1, waiting for transfers between devices: 112 us -> 0.01 us  [point_gradient(): return lax.psum_scatter(mine, 'seq', scatter_dimension=0, tiled=True)]
    ppermute x0 -> x5, waiting for transfers between devices: none -> 88.5 us  [swap(): return lax.ppermute(value, axis, [(i, i ^ distance) for i in range(count)])]
    psum x1 -> x0, waiting for transfers between devices: 53.9 us -> none  [on_device(): grad_conv = lax.psum(conv_local, ('seq', 'rep')) * scale]
    ppermute x0 -> x5, starting transfers between devices: none -> 6.57 us  [swap(): return lax.ppermute(value, axis, [(i, i ^ distance) for i in range(count)])]
    add x0 -> x3, other arithmetic: none -> 3.78 us  [tree_sum(): value = value + swap(value, axis, distance)]
    dot_general x1 -> x2, matrix products: 8.65 us -> 4.9 us  [rows_of(): lax.dot_general(cols, cot_rows, (((0,), (0,)), ((), ())), preferred_eleme...]
  transfers between devices with their start and end apart: 6 -> 10, of which waited for: 2 -> 5; matrix products, arithmetic and copies ran while one was open for 16% -> 31% of each run, Pallas kernels for 0% -> 0%
where the time goes in v1:
time: 207 us; the launch traced here: 206 us
  waiting for transfers between devices  88.6 us (43%)
  matrix products  36.4 us (18%)
  local copies, waits for them, and re-layouts  30.8 us (15%)
  other arithmetic  17.8 us (9%)
  starting transfers between devices  17.6 us (9%)
  between operations  15 us (7%)
    ppermute x5, waiting for transfers between devices, swap(): return lax.ppermute(value, axis, [(i, i ^ distance) for i in range(count)])  88.5 us
    ppermute x2, starting transfers between devices, with_halo(): lax.ppermute(tail, axis, [(i, (i + 1) % count) for i in range(ends)])  8.13 us
    slice x4, local copies, waits for them, and re-layouts, conv_taps(): weight[kernel_offset].reshape(GROUP_CHANNELS, group_count, GROUP_CHANNELS)  7.33 us
    dot_general x3, matrix products, weight_taps(): jnp.einsum('slgi,slgj->igj', segment_window, grouped, preferred_element_t...  7.24 us
    dot_general x1, matrix products, on_device(): lax.dot_general(cot_rows, point_weight, (((1,), (1,)), ((), ())), preferr...  7.08 us
    ppermute x5, starting transfers between devices, swap(): return lax.ppermute(value, axis, [(i, i ^ distance) for i in range(count)])  6.57 us
    dot_general x1, matrix products, on_device(): jnp.dot(act_rows, point_weight, preferred_element_type=jnp.float32)  6.24 us
    dot_general x3, matrix products, conv_taps(): jnp.einsum('slgi,igj->slgj', segment_window, wk, preferred_element_type=j...  5.75 us
  transfers between devices with their start and end apart: 10, of which 5 were waited for; matrix products, arithmetic and copies ran while one was open for 31% of the time, Pallas kernels for 0%

profile of v1, /device:TPU:0, one launch (start us, length us, event | category | flops | bytes accessed | tf_op | source)
XLA Modules:
  0.0 206.2 jit_solution(7932541956366638251)
XLA Ops:
  11.7 6.2 %collective-permute-start = (bf16[1,64,1536]{2,1,0:T(8,128)(2,1)}, bf16[1,64,1536]{2,1,0:T(8,128)(2,1)}, u32[]{:S(2)}, u32[]{:S(2)}) collective-permute-start(bf16[1,64,1536]{2,1,0:T(8,128)(2,1)} %get-tuple-element.13), channel_id=1, source_target_pairs={{0,2},{2,4},{4,6},{6,8},{8,10},{10,12},{12,14},{1,3},{3,5},{5,7},{... | collective-permute-start | bytes 589832 | tf_op jit(solution)/shard_map/ppermute | solution.py:20
  18.6 2.4 %fusion.17 = (bf16[1,48,1536]{2,1,0:T(8,128)(2,1)}, bf16[1,48,1536]{2,1,0:T(8,128)(2,1)}, bf16[1,48,1536]{2,1,0:T(8,128)(2,1)}) fusion(bf16[3,48,1536]{2,1,0:T(8,128)(2,1)} %param.7), kind=kLoop, calls=%fused_computation.39 | loop fusion | bytes 884736 | tf_op jit(solution)/shard_map/slice | solution.py:44
  25.9 3.2 %fusion.24 = f32[32,512,48]{1,2,0:T(8,128)} fusion(bf16[48,32,48]{0,2,1:T(8,128)(2,1)} %bitcast.94, bf16[512,32,48]{0,2,1:T(8,128)(2,1)S(1)} %bitcast.78), kind=kOutput, calls=%fused_computation.46 | convolution fusion | flops 75497472 | bytes 4866048 | tf_op jit(solution)/shard_map/slgi,igj->slgj/dot_general | solution.py:45
  29.1 2.4 %pad_maximum_fusion.2 = (bf16[1,512,1536]{2,1,0:T(8,128)(2,1)}, bf16[1,512,1536]{2,1,0:T(8,128)(2,1)S(1)}) fusion(bf16[1,64,1536]{2,1,0:T(8,128)(2,1)} %collective-permute-done.1, bf16[1,512,1536]{2,1,0:T(8,128)(2,1)S(1)} %fusion.1, bf16[1,64,1536]{2,1,0:T(8,128)(2,1)} %collective-permute-done), kind=kLoop, calls=%fused_computation.22 | loop fusion | flops 6291456 | bytes 5111808 | tf_op jit(solution)/shard_map/concatenate | solution.py:18
  31.5 2.6 %copy.38 = bf16[1,512,1536]{1,2,0:T(8,128)(2,1)} copy(bf16[1,512,1536]{2,1,0:T(8,128)(2,1)} %get-tuple-element.10) | data formatting | bytes 3145728 | tf_op jit(solution)/shard_map/slice | solution.py:41
  41.3 7.9 %collective-permute-done.4 = f32[768,1536]{1,0:T(8,128)S(1)} collective-permute-done((f32[768,1536]{1,0:T(8,128)S(1)}, f32[768,1536]{1,0:T(8,128)S(1)}, u32[]{:S(2)}, u32[]{:S(2)}) %collective-permute-start.4) | collective-permute-done | bytes 4718624 | tf_op jit(solution)/shard_map/ppermute | solution.py:89
  49.2 3.5 %convolution_add_fusion = f32[768,1536]{1,0:T(8,128)} fusion(f32[768,1536]{1,0:T(8,128)S(1)} %collective-permute-done.4, bf16[512,768]{0,1:T(8,128)(2,1)S(1)} %bitcast.89, bf16[1,512,1536]{2,1,0:T(8,128)(2,1)S(1)} %copy-done), kind=kOutput, calls=%fused_computation.1 | convolution fusion | flops 1209139200 | bytes 11796480 | tf_op jit(solution)/shard_map/dot_general | solution.py:114
  52.8 2.4 %copy.41 = f32[512,1536]{1,0:T(8,128)} copy(f32[512,1536]{0,1:T(8,128)S(1)} %bitcast.77) | data formatting | bytes 6291456 | tf_op jit(solution)/shard_map/reshape | solution.py:48
  55.1 7.1 %fusion.7 = bf16[512,1536]{1,0:T(8,128)(2,1)S(1)} fusion(f32[512,1536]{1,0:T(8,128)} %copy.41, bf16[1536,1536]{1,0:T(8,128)(2,1)} %param.8, bf16[1,512,1536]{2,1,0:T(8,128)(2,1)} %param.9, f32[512]{0:T(512)S(1)} %fusion.13), kind=kOutput, calls=%fused_computation.19 | convolution fusion | flops 2424569856 | bytes 11012096 | tf_op jit(solution)/shard_map/dot_general | solution.py:147
  64.1 3.0 %fusion.20 = f32[32,48,48]{2,1,0:T(8,128)} fusion(bf16[512,32,48]{0,2,1:T(8,128)(2,1)S(1)} %bitcast.72, bf16[512,32,48]{0,2,1:T(8,128)(2,1)} %bitcast.81), kind=kOutput, calls=%fused_computation.42 | convolution fusion | flops 75497472 | bytes 3440640 | tf_op jit(solution)/shard_map/slgi,slgj->igj/dot_general | solution.py:80
  72.0 2.9 %fusion.22 = f32[32,48,48]{2,1,0:T(8,128)} fusion(bf16[512,32,48]{0,2,1:T(8,128)(2,1)S(1)} %bitcast.74, bf16[512,32,48]{0,2,1:T(8,128)(2,1)} %bitcast.82), kind=kOutput, calls=%fused_computation.44 | convolution fusion | flops 75497472 | bytes 3440640 | tf_op jit(solution)/shard_map/slgi,slgj->igj/dot_general | solution.py:80
  74.8 2.2 %copy.54 = f32[1,48,1536]{2,1,0:T(8,128)} copy(f32[1,48,1536]{1,2,0:T(8,128)} %bitcast.99) | data formatting | bytes 589824 | tf_op jit(solution)/shard_map/stack;reshape | solution.py:84
  78.6 2.3 %collective-permute-done.5 = f32[3,48,1536]{2,1,0:T(8,128)S(1)} collective-permute-done((f32[3,48,1536]{2,1,0:T(8,128)S(1)}, f32[3,48,1536]{2,1,0:T(8,128)S(1)}, u32[]{:S(2)}, u32[]{:S(2)}) %collective-permute-start.5) | collective-permute-done | bytes 884768 | tf_op jit(solution)/shard_map/ppermute | solution.py:89
  82.0 2.3 %collective-permute-start.6 = (f32[3,48,1536]{2,1,0:T(8,128)S(1)}, f32[3,48,1536]{2,1,0:T(8,128)S(1)}, u32[]{:S(2)}, u32[]{:S(2)}) collective-permute-start(f32[3,48,1536]{2,1,0:T(8,128)S(1)} %fusion.14), channel_id=1, source_target_pairs={{0,2},{2,0},{4,6},{6,4},{8,10},{10,8},{12,14},{14,12},{1,3},{3,1},... | collective-permute-start | bytes 2654216 | tf_op jit(solution)/shard_map/ppermute | solution.py:89
  87.9 6.2 %fusion.2 = bf16[1,512,1536]{2,1,0:T(8,128)(2,1)} fusion(bf16[1,512,1536]{2,1,0:T(8,128)(2,1)S(1)} %copy-done.18, bf16[1536,1536]{1,0:T(8,128)(2,1)} %param.8, f32[512,1536]{1,0:T(8,128)S(1)} %copy-done.17, f32[512]{0:T(512)S(1)} %fusion.13), kind=kOutput, calls=%fused_computation.8 | convolution fusion | flops 2422996992 | bytes 11012096 | tf_op jit(solution)/shard_map/dot_general | solution.py:145
  94.2 21.1 %collective-permute-done.6 = f32[3,48,1536]{2,1,0:T(8,128)S(1)} collective-permute-done((f32[3,48,1536]{2,1,0:T(8,128)S(1)}, f32[3,48,1536]{2,1,0:T(8,128)S(1)}, u32[]{:S(2)}, u32[]{:S(2)}) %collective-permute-start.6) | collective-permute-done | bytes 884768 | tf_op jit(solution)/shard_map/ppermute | solution.py:89
  116.4 2.7 %collective-permute-start.7 = (f32[3,48,1536]{2,1,0:T(8,128)}, f32[3,48,1536]{2,1,0:T(8,128)}, u32[]{:S(2)}, u32[]{:S(2)}) collective-permute-start(f32[3,48,1536]{2,1,0:T(8,128)} %fusion.47), channel_id=1, source_target_pairs={{0,4},{2,6},{4,0},{6,2},{8,12},{10,14},{12,8},{14,10},{1,5},{3,7},... | collective-permute-start | bytes 2654216 | tf_op jit(solution)/shard_map/ppermute | solution.py:89
  119.1 2.3 %fusion.19 = f32[32,512,48]{1,2,0:T(8,128)} fusion(bf16[512,32,48]{0,2,1:T(8,128)(2,1)S(1)} %bitcast.75, bf16[48,32,48]{0,2,1:T(8,128)(2,1)S(1)} %bitcast.95), kind=kOutput, calls=%fused_computation.41 | convolution fusion | flops 75497472 | bytes 4866048 | tf_op jit(solution)/shard_map/slgj,igj->slgi/dot_general | solution.py:63
  122.8 2.7 %copy.49 = bf16[1,512,1536]{1,2,0:T(8,128)(2,1)} copy(bf16[1,512,1536]{2,1,0:T(8,128)(2,1)} %get-tuple-element.6) | data formatting | bytes 3145728 | tf_op jit(solution)/shard_map/slice | solution.py:57
  126.9 14.1 %collective-permute-done.7 = f32[3,48,1536]{2,1,0:T(8,128)} collective-permute-done((f32[3,48,1536]{2,1,0:T(8,128)}, f32[3,48,1536]{2,1,0:T(8,128)}, u32[]{:S(2)}, u32[]{:S(2)}) %collective-permute-start.7) | collective-permute-done | bytes 884768 | tf_op jit(solution)/shard_map/ppermute | solution.py:89
  143.8 2.3 %add_add_fusion = f32[32,512,48]{1,2,0:T(8,128)} fusion(f32[32,512,48]{1,2,0:T(8,128)S(1)} %fusion.18, f32[32,512,48]{1,2,0:T(8,128)S(1)} %copy-done.6, bf16[512,32,48]{0,2,1:T(8,128)(2,1)S(1)} %bitcast.88, bf16[48,32,48]{0,2,1:T(8,128)(2,1)S(1)} %bitcast.91), kind=kOutput, calls=%fused_computation.15 | convolution fusion | flops 77070336 | bytes 11157504 | tf_op jit(solution)/shard_map/slgj,igj->slgi/dot_general | solution.py:63
  146.1 3.8 %copy.51 = f32[1,512,1536]{2,1,0:T(8,128)} copy(f32[1,512,1536]{1,2,0:T(8,128)} %bitcast.84) | data formatting | bytes 6291456 | tf_op jit(solution)/shard_map/reshape | solution.py:66
  149.9 3.5 %add_convert_fusion = bf16[1,512,1536]{2,1,0:T(8,128)(2,1)} fusion(f32[1,512,1536]{2,1,0:T(8,128)} %copy.51, bf16[1,512,1536]{2,1,0:T(8,128)(2,1)S(1)} %copy-done.1, f32[512]{0:T(512)S(1)} %fusion.13), kind=kLoop, calls=%fused_computation.14 | loop fusion | flops 3145728 | bytes 6293504 | tf_op jit(solution)/shard_map/convert_element_type | solution.py:155
  153.3 43.1 %collective-permute-done.8 = f32[3,48,1536]{2,1,0:T(8,128)S(1)} collective-permute-done((f32[3,48,1536]{2,1,0:T(8,128)S(1)}, f32[3,48,1536]{2,1,0:T(8,128)S(1)}, u32[]{:S(2)}, u32[]{:S(2)}) %collective-permute-start.8) | collective-permute-done | bytes 884768 | tf_op jit(solution)/shard_map/ppermute | solution.py:89
  (78 shorter events, 39.2 us)
Async XLA Ops:
  7.2 190.3 %reduce-scatter.2.cloned.1.call-start = ((), (), s32[]{:S(2)}) async-start(), calls=%async_computation.1 | async-start | bytes 5308416 | tf_op jit(solution)/shard_map/reduce_scatter | solution.py:126
  10.4 18.7 %collective-permute-start.1 = (bf16[1,64,1536]{2,1,0:T(8,128)(2,1)}, bf16[1,64,1536]{2,1,0:T(8,128)(2,1)}, u32[]{:S(2)}, u32[]{:S(2)}) collective-permute-start(bf16[1,64,1536]{2,1,0:T(8,128)(2,1)} %get-tuple-element.12), channel_id=1, source_target_pairs={{2,0},{4,2},{6,4},{8,6},{10,8},{12,10},{14,12},{3,1},{5,3},{7,5},{... | collective-permute-start | bytes 589832 | tf_op jit(solution)/shard_map/ppermute | solution.py:22
  11.7 17.4 %collective-permute-start = (bf16[1,64,1536]{2,1,0:T(8,128)(2,1)}, bf16[1,64,1536]{2,1,0:T(8,128)(2,1)}, u32[]{:S(2)}, u32[]{:S(2)}) collective-permute-start(bf16[1,64,1536]{2,1,0:T(8,128)(2,1)} %get-tuple-element.13), channel_id=1, source_target_pairs={{0,2},{2,4},{4,6},{6,8},{8,10},{10,12},{12,14},{1,3},{3,5},{5,7},{... | collective-permute-start | bytes 589832 | tf_op jit(solution)/shard_map/ppermute | solution.py:20
  18.6 10.5 %copy-start.2 = (bf16[1,512,1536]{1,2,0:T(8,128)(2,1)}, bf16[1,512,1536]{1,2,0:T(8,128)(2,1)S(1)}, u32[]{:S(2)}) copy-start(bf16[1,512,1536]{1,2,0:T(8,128)(2,1)S(1)} %copy.36) | copy-start | bytes 4718596
  22.1 14.8 %copy-start.13 = (bf16[1,48,1536]{1,2,0:T(8,128)(2,1)}, bf16[1,48,1536]{1,2,0:T(8,128)(2,1)S(1)}, u32[]{:S(2)}) copy-start(bf16[1,48,1536]{1,2,0:T(8,128)(2,1)S(1)} %copy.39) | copy-start | bytes 442372
  41.2 8.0 %collective-permute-start.4 = (f32[768,1536]{1,0:T(8,128)S(1)}, f32[768,1536]{1,0:T(8,128)S(1)}, u32[]{:S(2)}, u32[]{:S(2)}) collective-permute-start(f32[768,1536]{1,0:T(8,128)S(1)} %fusion.8), channel_id=1, source_target_pairs={{0,1},{1,0},{2,3},{3,2},{4,5},{5,4},{6,7},{7,6},{8,9},{9,8},{10,11... | collective-permute-start | bytes 14155784 | tf_op jit(solution)/shard_map/ppermute | solution.py:89
  64.1 4.3 %copy-start.3 = (bf16[1,512,1536]{1,2,0:T(8,128)(2,1)S(1)}, bf16[1,512,1536]{1,2,0:T(8,128)(2,1)}, u32[]{:S(2)}) copy-start(bf16[1,512,1536]{1,2,0:T(8,128)(2,1)} %copy-done.2) | copy-start | bytes 4718596
  74.8 9.5 %copy-start.9 = (bf16[512,1536]{1,0:T(8,128)(2,1)S(1)}, bf16[512,1536]{1,0:T(8,128)(2,1)}, u32[]{:S(2)}) copy-start(bf16[512,1536]{1,0:T(8,128)(2,1)} %copy-done.8) | copy-start | bytes 4718596
  77.1 10.8 %copy-start.17 = (f32[512,1536]{1,0:T(8,128)S(1)}, f32[512,1536]{1,0:T(8,128)}, u32[]{:S(2)}) copy-start(f32[512,1536]{1,0:T(8,128)} %copy.41) | copy-start | bytes 9437188
  77.1 10.9 %copy-start.18 = (bf16[1,512,1536]{2,1,0:T(8,128)(2,1)S(1)}, bf16[1,512,1536]{2,1,0:T(8,128)(2,1)}, u32[]{:S(2)}) copy-start(bf16[1,512,1536]{2,1,0:T(8,128)(2,1)} %param.5) | copy-start | bytes 4718596
  78.4 2.5 %collective-permute-start.5 = (f32[3,48,1536]{2,1,0:T(8,128)S(1)}, f32[3,48,1536]{2,1,0:T(8,128)S(1)}, u32[]{:S(2)}, u32[]{:S(2)}) collective-permute-start(f32[3,48,1536]{2,1,0:T(8,128)S(1)} %pad_maximum_fusion.4), channel_id=1, source_target_pairs={{0,1},{1,0},{2,3},{3,2},{4,5},{5,4},{6,7},{7,6},{8,9},{9,8},{10,11... | collective-permute-start | bytes 2654216 | tf_op jit(solution)/shard_map/ppermute | solution.py:89
  82.0 33.3 %collective-permute-start.6 = (f32[3,48,1536]{2,1,0:T(8,128)S(1)}, f32[3,48,1536]{2,1,0:T(8,128)S(1)}, u32[]{:S(2)}, u32[]{:S(2)}) collective-permute-start(f32[3,48,1536]{2,1,0:T(8,128)S(1)} %fusion.14), channel_id=1, source_target_pairs={{0,2},{2,0},{4,6},{6,4},{8,10},{10,8},{12,14},{14,12},{1,3},{3,1},... | collective-permute-start | bytes 2654216 | tf_op jit(solution)/shard_map/ppermute | solution.py:89
  84.3 37.1 %collective-permute-start.3 = (bf16[1,64,1536]{2,1,0:T(8,128)(2,1)S(1)}, bf16[1,64,1536]{2,1,0:T(8,128)(2,1)S(1)}, u32[]{:S(2)}, u32[]{:S(2)}) collective-permute-start(bf16[1,64,1536]{2,1,0:T(8,128)(2,1)S(1)} %get-tuple-element.8), channel_id=1, source_target_pairs={{0,2},{2,4},{4,6},{6,8},{8,10},{10,12},{12,14},{1,3},{3,5},{5,7},{... | collective-permute-start | bytes 589832 | tf_op jit(solution)/shard_map/ppermute | solution.py:20
  86.3 29.0 %copy-start.11 = (f32[1,48,1536]{2,1,0:T(8,128)S(1)}, f32[1,48,1536]{2,1,0:T(8,128)}, u32[]{:S(2)}) copy-start(f32[1,48,1536]{2,1,0:T(8,128)} %copy.53) | copy-start | bytes 884740
  86.3 29.0 %copy-start.12 = (f32[1,48,1536]{2,1,0:T(8,128)S(1)}, f32[1,48,1536]{2,1,0:T(8,128)}, u32[]{:S(2)}) copy-start(f32[1,48,1536]{2,1,0:T(8,128)} %copy.54) | copy-start | bytes 884740
  86.3 35.1 %collective-permute-start.2 = (bf16[1,64,1536]{2,1,0:T(8,128)(2,1)S(1)}, bf16[1,64,1536]{2,1,0:T(8,128)(2,1)S(1)}, u32[]{:S(2)}, u32[]{:S(2)}) collective-permute-start(bf16[1,64,1536]{2,1,0:T(8,128)(2,1)S(1)} %get-tuple-element.9), channel_id=1, source_target_pairs={{2,0},{4,2},{6,4},{8,6},{10,8},{12,10},{14,12},{3,1},{5,3},{7,5},{... | collective-permute-start | bytes 589832 | tf_op jit(solution)/shard_map/ppermute | solution.py:22
  94.2 24.9 %copy-start.16 = (bf16[1,48,1536]{1,2,0:T(8,128)(2,1)S(1)}, bf16[1,48,1536]{1,2,0:T(8,128)(2,1)}, u32[]{:S(2)}) copy-start(bf16[1,48,1536]{1,2,0:T(8,128)(2,1)} %copy.37) | copy-start | bytes 442372
  116.4 24.6 %collective-permute-start.7 = (f32[3,48,1536]{2,1,0:T(8,128)}, f32[3,48,1536]{2,1,0:T(8,128)}, u32[]{:S(2)}, u32[]{:S(2)}) collective-permute-start(f32[3,48,1536]{2,1,0:T(8,128)} %fusion.47), channel_id=1, source_target_pairs={{0,4},{2,6},{4,0},{6,2},{8,12},{10,14},{12,8},{14,10},{1,5},{3,7},... | collective-permute-start | bytes 2654216 | tf_op jit(solution)/shard_map/ppermute | solution.py:89
  122.8 3.4 %copy-start.15 = (bf16[1,48,1536]{1,2,0:T(8,128)(2,1)S(1)}, bf16[1,48,1536]{1,2,0:T(8,128)(2,1)}, u32[]{:S(2)}) copy-start(bf16[1,48,1536]{1,2,0:T(8,128)(2,1)} %copy.35) | copy-start | bytes 442372
  126.2 17.6 %copy-start.6 = (f32[32,512,48]{1,2,0:T(8,128)S(1)}, f32[32,512,48]{1,2,0:T(8,128)}, u32[]{:S(2)}) copy-start(f32[32,512,48]{1,2,0:T(8,128)} %fusion.19) | copy-start | bytes 9437188
  126.2 17.6 %copy-start.10 = (bf16[1,512,1536]{1,2,0:T(8,128)(2,1)S(1)}, bf16[1,512,1536]{1,2,0:T(8,128)(2,1)}, u32[]{:S(2)}) copy-start(bf16[1,512,1536]{1,2,0:T(8,128)(2,1)} %copy.49) | copy-start | bytes 4718596
  126.2 17.6 %copy-start.14 = (bf16[1,48,1536]{1,2,0:T(8,128)(2,1)S(1)}, bf16[1,48,1536]{1,2,0:T(8,128)(2,1)}, u32[]{:S(2)}) copy-start(bf16[1,48,1536]{1,2,0:T(8,128)(2,1)} %copy-done.13) | copy-start | bytes 442372
  142.5 53.9 %collective-permute-start.8 = (f32[3,48,1536]{2,1,0:T(8,128)S(1)}, f32[3,48,1536]{2,1,0:T(8,128)S(1)}, u32[]{:S(2)}, u32[]{:S(2)}) collective-permute-start(f32[3,48,1536]{2,1,0:T(8,128)S(1)} %add.120), channel_id=1, source_target_pairs={{0,8},{2,10},{4,12},{6,14},{8,0},{10,2},{12,4},{14,6},{1,9},{3,11}... | collective-permute-start | bytes 2654216 | tf_op jit(solution)/shard_map/ppermute | solution.py:89
  146.1 3.8 %copy-start.1 = (bf16[1,512,1536]{2,1,0:T(8,128)(2,1)S(1)}, bf16[1,512,1536]{2,1,0:T(8,128)(2,1)}, u32[]{:S(2)}) copy-start(bf16[1,512,1536]{2,1,0:T(8,128)(2,1)} %param.9) | copy-start | bytes 4718596
  (5 other events, 9.7 us)
Sparse Core Ops, SparseCore 0:
  52.9 132.6 reduce-scatter.1

commit v2 on v1

--- a/solution.py
+++ b/solution.py
@@ -32,55 +32,52 @@
     return (pre * cdf, cdf + pre * dens)
 
 
-def conv_taps(padded_input, weight, sequence_length):
-    group_count = weight.shape[2] // GROUP_CHANNELS
-    total = jnp.zeros(
-        (padded_input.shape[0], sequence_length, group_count, GROUP_CHANNELS), jnp.float32
-    )
-    for kernel_offset in range(3):
-        segment_window = padded_input[
-            :, kernel_offset * DILATION_STEP : kernel_offset * DILATION_STEP + sequence_length
-        ].reshape(padded_input.shape[0], sequence_length, group_count, GROUP_CHANNELS)
-        wk = weight[kernel_offset].reshape(GROUP_CHANNELS, group_count, GROUP_CHANNELS)
-        total = total + jnp.einsum(
-            "slgi,igj->slgj", segment_window, wk, preferred_element_type=jnp.float32
-        )
-    return total.reshape(padded_input.shape[0], sequence_length, group_count * GROUP_CHANNELS)
+CHUNK = 384
 
 
-def transpose_taps(padded_input, weight, sequence_length):
-    group_count = weight.shape[2] // GROUP_CHANNELS
-    total = jnp.zeros(
-        (padded_input.shape[0], sequence_length, group_count, GROUP_CHANNELS), jnp.float32
-    )
-    for kernel_offset in range(3):
-        segment_window = padded_input[
-            :,
-            (2 - kernel_offset) * DILATION_STEP : (2 - kernel_offset) * DILATION_STEP
-            + sequence_length,
-        ].reshape(padded_input.shape[0], sequence_length, group_count, GROUP_CHANNELS)
-        wk = weight[kernel_offset].reshape(GROUP_CHANNELS, group_count, GROUP_CHANNELS)
-        total = total + jnp.einsum(
-            "slgj,igj->slgi", segment_window, wk, preferred_element_type=jnp.float32
-        )
-    return total.reshape(padded_input.shape[0], sequence_length, group_count * GROUP_CHANNELS)
+def dense_weight(weight):
+    taps, width, chans = weight.shape
+    chunks = chans // CHUNK
+    groups = CHUNK // width
+    cells = weight.reshape(taps, width, chunks, groups, width).transpose(0, 2, 1, 3, 4)
+    eye = jnp.eye(groups, dtype=weight.dtype)
+    dense = cells[:, :, None, :, :, :] * eye[None, None, :, None, :, None]
+    return dense.reshape(taps, chunks, CHUNK, CHUNK)
+
+
+def conv_taps(padded_input, dense, sequence_length, transpose=False):
+    rows = padded_input[0]
+    parts = []
+    for c in range(dense.shape[1]):
+        total = None
+        for k in range(3):
+            start = (2 - k if transpose else k) * DILATION_STEP
+            window = rows[start : start + sequence_length, c * CHUNK : (c + 1) * CHUNK]
+            dims = (((1,), (1,)), ((), ())) if transpose else (((1,), (0,)), ((), ()))
+            term = lax.dot_general(window, dense[k, c], dims, preferred_element_type=jnp.float32)
+            total = term if total is None else total + term
+        parts.append(total)
+    return jnp.concatenate(parts, axis=1)[None]
 
 
 def weight_taps(input_padded, output_gradient, sequence_length):
-    group_count = output_gradient.shape[2] // GROUP_CHANNELS
-    grouped = output_gradient.reshape(
-        output_gradient.shape[0], sequence_length, group_count, GROUP_CHANNELS
-    )
+    rows = input_padded[0]
+    grads = output_gradient[0]
+    chans = grads.shape[1]
+    chunks = chans // CHUNK
+    groups = CHUNK // GROUP_CHANNELS
+    eye = jnp.eye(groups, dtype=jnp.float32)
     taps = []
-    for kernel_offset in range(3):
-        segment_window = input_padded[
-            :, kernel_offset * DILATION_STEP : kernel_offset * DILATION_STEP + sequence_length
-        ].reshape(output_gradient.shape[0], sequence_length, group_count, GROUP_CHANNELS)
-        taps.append(
-            jnp.einsum(
-                "slgi,slgj->igj", segment_window, grouped, preferred_element_type=jnp.float32
-            ).reshape(GROUP_CHANNELS, group_count * GROUP_CHANNELS)
+    for k in range(3):
+        window = rows[k * DILATION_STEP : k * DILATION_STEP + sequence_length].reshape(
+            sequence_length, chunks, CHUNK
         )
+        full = jnp.einsum(
+            "tci,tcj->cij", window, grads.reshape(sequence_length, chunks, CHUNK),
+            preferred_element_type=jnp.float32,
+        ).reshape(chunks, groups, GROUP_CHANNELS, groups, GROUP_CHANNELS)
+        diag = jnp.einsum("caibj,ab->icbj", full, eye)
+        taps.append(diag.reshape(GROUP_CHANNELS, chans))
     return jnp.stack(taps)
 
 
@@ -137,7 +134,8 @@
     masked_input = (inputs.astype(jnp.float32) * mask3).astype(jnp.bfloat16)
     scale = 1.0 / math.sqrt(rep_count * seq_count * local_bins)
     padded_input = with_halo(masked_input, (("seq", 1),), DILATION_STEP)
-    pre = conv_taps(padded_input, conv_weight, local_bins)
+    dense = dense_weight(conv_weight)
+    pre = conv_taps(padded_input, dense, local_bins)
     act_val, slope = gelu_pair(pre)
     act = (act_val * mask3).astype(jnp.bfloat16)
     act_rows = act.reshape(local_bins, chans)
@@ -149,7 +147,7 @@
     )
     preactivation_gradient = (back.reshape(inputs.shape) * slope * mask3).astype(jnp.bfloat16)
     padded_gradient = with_halo(preactivation_gradient, (("seq", 1),), DILATION_STEP)
-    spread = transpose_taps(padded_gradient, conv_weight, local_bins)
+    spread = conv_taps(padded_gradient, dense, local_bins, transpose=True)
     conv_local = weight_taps(padded_input, preactivation_gradient, local_bins)
     grad_conv = tree_sum(conv_local) * scale
     grad_inputs = (cotangent.astype(jnp.float32) + mask3 * spread).astype(jnp.bfloat16)

time: 207 us -> 263 us (1.27); the launches traced: 206 us -> 258 us
  local copies, waits for them, and re-layouts: 30.8 us -> 63.7 us
  matrix products: 36.4 us -> 65.2 us
  waiting for transfers between devices: 88.6 us -> 76.1 us
  starting transfers between devices: 17.6 us -> 20.9 us
    dot_general x9 -> x30, matrix products: 18.2 us -> 40.7 us  [the longest x3 17 us: weight_taps(): diag = jnp.einsum('caibj,ab->icbj', full, eye)]
    mul x0 -> x4, local copies, waits for them, and re-layouts: none -> 20.5 us  [dense_weight(): dense = cells[:, :, None, :, :, :] * eye[None, None, :, None, :, None]]
    reshape x2 -> x7, local copies, waits for them, and re-layouts: 6.12 us -> 25.1 us  [the longest x3 15.8 us: weight_taps(): full = jnp.einsum('tci,tcj->cij', window, grads.reshape(sequence_length,...]
    slice x9 -> x0, local copies, waits for them, and re-layouts: 14.8 us -> none  [the longest x4 7.33 us: conv_taps(): weight[kernel_offset].reshape(GROUP_CHANNELS, group_count, GROUP_CHANNELS)]
    ppermute x5, waiting for transfers between devices: 88.5 us -> 76.1 us  [swap(): return lax.ppermute(value, axis, [(i, i ^ distance) for i in range(count)])]
    dot_general x2, matrix products: 4.9 us -> 10.1 us  [rows_of(): lax.dot_general(cols, cot_rows, (((0,), (0,)), ((), ())), preferred_eleme...]
    dot_general x0 -> x3, local copies, waits for them, and re-layouts: none -> 4.01 us  [weight_taps(): diag = jnp.einsum('caibj,ab->icbj', full, eye)]
    squeeze x0 -> x2, other arithmetic: none -> 3.98 us  [conv_taps(): rows = padded_input[0]]
  transfers between devices with their start and end apart: 10 -> 10, of which waited for: 5 -> 4; matrix products, arithmetic and copies ran while one was open for 31% -> 47% of each run, Pallas kernels for 0% -> 0%
where the time goes in v2:
time: 263 us; the launch traced here: 258 us
  waiting for transfers between devices  76.1 us (29%)
  matrix products  65.2 us (25%)
  local copies, waits for them, and re-layouts  63.7 us (24%)
  starting transfers between devices  20.9 us (8%)
  other arithmetic  17 us (6%)
  between operations  15.4 us (6%)
    ppermute x5, waiting for transfers between devices, swap(): return lax.ppermute(value, axis, [(i, i ^ distance) for i in range(count)])  76.1 us
    mul x4, local copies, waits for them, and re-layouts, dense_weight(): dense = cells[:, :, None, :, :, :] * eye[None, None, :, None, :, None]  20.5 us
    dot_general x3, matrix products, weight_taps(): diag = jnp.einsum('caibj,ab->icbj', full, eye)  17 us
    reshape x3, local copies, waits for them, and re-layouts, weight_taps(): full = jnp.einsum('tci,tcj->cij', window, grads.reshape(sequence_length,...  15.8 us
    dot_general x3, matrix products, weight_taps(): jnp.einsum('tci,tcj->cij', window, grads.reshape(sequence_length, chunks,...  11.9 us
    dot_general x24, matrix products, conv_taps(): lax.dot_general(window, dense[k, c], dims, preferred_element_type=jnp.flo...  11.8 us
    ppermute x2, starting transfers between devices, with_halo(): lax.ppermute(tail, axis, [(i, (i + 1) % count) for i in range(ends)])  11.8 us
    dot_general x2, matrix products, rows_of(): lax.dot_general(cols, cot_rows, (((0,), (0,)), ((), ())), preferred_eleme...  10.1 us
  transfers between devices with their start and end apart: 10, of which 4 were waited for; matrix products, arithmetic and copies ran while one was open for 47% of the time, Pallas kernels for 0%

profile of v2, /device:TPU:0, one launch (start us, length us, event | category | flops | bytes accessed | tf_op | source)
XLA Modules:
  0.0 258.3 jit_solution(2541442776275549258)
XLA Ops:
  11.8 6.2 %collective-permute-start = (bf16[1,64,1536]{2,1,0:T(8,128)(2,1)}, bf16[1,64,1536]{2,1,0:T(8,128)(2,1)}, u32[]{:S(2)}, u32[]{:S(2)}) collective-permute-start(bf16[1,64,1536]{2,1,0:T(8,128)(2,1)} %get-tuple-element.10), channel_id=1, source_target_pairs={{0,2},{2,4},{4,6},{6,8},{8,10},{10,12},{12,14},{1,3},{3,5},{5,7},{... | collective-permute-start | bytes 589832 | tf_op jit(solution)/shard_map/ppermute | solution.py:20
  19.5 6.0 %mul.146 = bf16[3,4,8,48,8,48]{5,4,3,2,1,0:T(8,128)(2,1)} broadcast(bf16[3,4,48,8,48]{4,3,2,1,0:T(8,128)(2,1)S(1)} %copy.9), dimensions={0,1,3,4,5} | broadcast | bytes 3981312 | tf_op jit(solution)/shard_map/mul | solution.py:44
  25.5 13.1 %mul.147 = bf16[3,4,384,384]{3,2,1,0:T(8,128)(2,1)} reshape(bf16[3,4,8,48,8,48]{5,4,3,2,1,0:T(8,128)(2,1)} %mul.146) | data formatting | bytes 7077888 | tf_op jit(solution)/shard_map/mul | solution.py:44
  52.0 3.5 %fusion.16 = f32[768,1536]{1,0:T(8,128)} fusion(bf16[512,768]{0,1:T(8,128)(2,1)S(1)} %bitcast.138, bf16[1,512,1536]{2,1,0:T(8,128)(2,1)S(1)} %copy-done.2), kind=kOutput, calls=%fused_computation.33 | convolution fusion | flops 1207959552 | bytes 7077888 | tf_op jit(solution)/shard_map/dot_general | solution.py:111
  58.2 5.6 %collective-permute-done.4 = f32[768,1536]{1,0:T(8,128)} collective-permute-done((f32[768,1536]{1,0:T(8,128)}, f32[768,1536]{1,0:T(8,128)}, u32[]{:S(2)}, u32[]{:S(2)}) %collective-permute-start.4) | collective-permute-done | bytes 4718624 | tf_op jit(solution)/shard_map/ppermute | solution.py:86
  63.8 6.6 %convolution_add_fusion = f32[768,1536]{1,0:T(8,128)} fusion(f32[768,1536]{1,0:T(8,128)} %collective-permute-done.4, bf16[512,768]{0,1:T(8,128)(2,1)} %bitcast.127, bf16[1,512,1536]{2,1,0:T(8,128)(2,1)} %param.9), kind=kOutput, calls=%fused_computation.7 | convolution fusion | flops 1209139200 | bytes 11796480 | tf_op jit(solution)/shard_map/dot_general | solution.py:111
  70.4 6.8 %fusion.15 = bf16[512,1536]{0,1:T(8,128)(2,1)S(1)} fusion(bf16[1536,1536]{1,0:T(8,128)(2,1)} %param.8, bf16[1,512,1536]{2,1,0:T(8,128)(2,1)} %param.9, f32[512]{0:T(512)S(1)} %fusion.75, f32[512,384]{0,1:T(8,128)} %copy-done.6, f32[512,384]{0,1:T(8,128)} %copy-done.7, f32[512,384]{0,1:T(8,128)} %copy-done.8, f32[512,384]{0,1:T(8,128)} %copy-done.9), kind=kOutput, calls=%fused_computation.27 | convolution fusion | flops 2426929152 | bytes 11012096 | tf_op jit(solution)/shard_map/dot_general | solution.py:145
  79.7 5.6 %collective-permute-start.2 = (bf16[1,64,1536]{1,2,0:T(8,128)(2,1)}, bf16[1,64,1536]{1,2,0:T(8,128)(2,1)}, u32[]{:S(2)}, u32[]{:S(2)}) collective-permute-start(bf16[1,64,1536]{1,2,0:T(8,128)(2,1)} %get-tuple-element.8), channel_id=1, source_target_pairs={{0,2},{2,4},{4,6},{6,8},{8,10},{10,12},{12,14},{1,3},{3,5},{5,7},{... | collective-permute-start | bytes 589832 | tf_op jit(solution)/shard_map/ppermute | solution.py:20
  85.3 2.9 %pad_maximum_fusion.2 = (bf16[1,512,1536]{2,1,0:T(8,128)(2,1)}, bf16[1,512,1536]{2,1,0:T(8,128)(2,1)}) fusion(bf16[1,64,1536]{2,1,0:T(8,128)(2,1)} %collective-permute-done.1, bf16[1,512,1536]{2,1,0:T(8,128)(2,1)S(1)} %copy-done.1, bf16[1,64,1536]{2,1,0:T(8,128)(2,1)} %collective-permute-done), kind=kLoop, calls=%fused_computation.31 | loop fusion | flops 6291456 | bytes 5111808 | tf_op jit(solution)/shard_map/concatenate | solution.py:18
  88.2 3.0 %copy.52 = bf16[1,512,1536]{1,2,0:T(8,128)(2,1)} copy(bf16[1,512,1536]{2,1,0:T(8,128)(2,1)} %get-tuple-element.5) | data formatting | bytes 3145728 | tf_op jit(solution)/shard_map/reshape | solution.py:72
  91.2 4.0 %fusion.79 = bf16[4,384,384]{2,1,0:T(8,128)(2,1)} fusion(bf16[512,4,384]{0,2,1:T(8,128)(2,1)} %bitcast.143, bf16[512,4,384]{0,2,1:T(8,128)(2,1)} %bitcast.130), kind=kOutput, calls=%fused_computation.128 | convolution fusion | flops 603979776 | bytes 4325376 | tf_op jit(solution)/shard_map/tci,tcj->cij/dot_general | solution.py:75
  95.2 5.2 %reshape.196 = bf16[4,8,48,8,48]{4,3,2,1,0:T(8,128)(2,1)} reshape(bf16[4,384,384]{2,1,0:T(8,128)(2,1)} %fusion.79) | data formatting | bytes 2359296 | tf_op jit(solution)/shard_map/reshape | solution.py:78
  100.4 5.7 %fusion.4 = f32[8,1,4,48,48]{4,1,3,2,0:T(1,128)S(1)} fusion(pred[8,8,1,1,1]{0,2,4,3,1:T(4,128)(4,1)S(1)} %copy.43, bf16[4,8,48,8,48]{4,3,2,1,0:T(8,128)(2,1)} %reshape.196), kind=kOutput, calls=%fused_computation.4 | convolution fusion | flops 1179648 | bytes 1474624 | tf_op jit(solution)/shard_map/caibj,ab->icbj/dot_general | solution.py:79
  109.7 4.0 %fusion.80 = bf16[4,384,384]{2,1,0:T(8,128)(2,1)} fusion(bf16[512,4,384]{0,2,1:T(8,128)(2,1)} %bitcast.142, bf16[512,4,384]{0,2,1:T(8,128)(2,1)} %bitcast.131), kind=kOutput, calls=%fused_computation.129 | convolution fusion | flops 603979776 | bytes 4325376 | tf_op jit(solution)/shard_map/tci,tcj->cij/dot_general | solution.py:75
  113.7 5.2 %reshape.198 = bf16[4,8,48,8,48]{4,3,2,1,0:T(8,128)(2,1)} reshape(bf16[4,384,384]{2,1,0:T(8,128)(2,1)} %fusion.80) | data formatting | bytes 2359296 | tf_op jit(solution)/shard_map/reshape | solution.py:78
  119.0 5.7 %fusion.2 = f32[8,1,4,48,48]{4,1,3,2,0:T(1,128)S(1)} fusion(pred[8,8,1,1,1]{0,2,4,3,1:T(4,128)(4,1)S(1)} %copy.43, bf16[4,8,48,8,48]{4,3,2,1,0:T(8,128)(2,1)} %reshape.198), kind=kOutput, calls=%fused_computation.2 | convolution fusion | flops 1179648 | bytes 1474624 | tf_op jit(solution)/shard_map/caibj,ab->icbj/dot_general | solution.py:79
  130.9 3.9 %fusion.81 = bf16[4,384,384]{2,1,0:T(8,128)(2,1)} fusion(bf16[512,4,384]{0,2,1:T(8,128)(2,1)} %bitcast.144, bf16[512,4,384]{0,2,1:T(8,128)(2,1)} %bitcast.132), kind=kOutput, calls=%fused_computation.130 | convolution fusion | flops 603979776 | bytes 4325376 | tf_op jit(solution)/shard_map/tci,tcj->cij/dot_general | solution.py:75
  134.8 5.4 %reshape.200 = bf16[4,8,48,8,48]{4,3,2,1,0:T(8,128)(2,1)} reshape(bf16[4,384,384]{2,1,0:T(8,128)(2,1)} %fusion.81) | data formatting | bytes 2359296 | tf_op jit(solution)/shard_map/reshape | solution.py:78
  140.2 5.6 %fusion = f32[8,1,4,48,48]{4,1,3,2,0:T(1,128)S(1)} fusion(pred[8,8,1,1,1]{0,2,4,3,1:T(4,128)(4,1)S(1)} %copy.43, bf16[4,8,48,8,48]{4,3,2,1,0:T(8,128)(2,1)} %reshape.200), kind=kOutput, calls=%fused_computation | convolution fusion | flops 1179648 | bytes 1474624 | tf_op jit(solution)/shard_map/caibj,ab->icbj/dot_general | solution.py:79
  152.5 7.7 %fusion.8 = bf16[1,512,1536]{2,1,0:T(8,128)(2,1)} fusion(bf16[1,512,1536]{2,1,0:T(8,128)(2,1)} %param.5, bf16[1536,1536]{1,0:T(8,128)(2,1)} %param.8, f32[512]{0:T(512)S(1)} %fusion.75, f32[512,384]{0,1:T(8,128)} %copy-done.6, f32[512,384]{0,1:T(8,128)} %copy-done.7, f32[512,384]{0,1:T(8,128)} %copy-done.8, f32[512,384]{0,1:T(8,128)} %copy-done.9), kind=kOutput, calls=%fused_computation.14 | convolution fusion | flops 2425356288 | bytes 11012096 | tf_op jit(solution)/shard_map/dot_general | solution.py:143
  167.9 18.1 %collective-permute-done.6 = f32[3,48,1536]{2,1,0:T(8,128)S(1)} collective-permute-done((f32[3,48,1536]{2,1,0:T(8,128)S(1)}, f32[3,48,1536]{2,1,0:T(8,128)S(1)}, u32[]{:S(2)}, u32[]{:S(2)}) %collective-permute-start.6) | collective-permute-done | bytes 884768 | tf_op jit(solution)/shard_map/ppermute | solution.py:86
  190.6 17.0 %collective-permute-done.7 = f32[3,48,1536]{2,1,0:T(8,128)S(1)} collective-permute-done((f32[3,48,1536]{2,1,0:T(8,128)S(1)}, f32[3,48,1536]{2,1,0:T(8,128)S(1)}, u32[]{:S(2)}, u32[]{:S(2)}) %collective-permute-start.7) | collective-permute-done | bytes 884768 | tf_op jit(solution)/shard_map/ppermute | solution.py:86
  207.7 2.6 %collective-permute-start.8 = (f32[3,48,1536]{2,1,0:T(8,128)S(1)}, f32[3,48,1536]{2,1,0:T(8,128)S(1)}, u32[]{:S(2)}, u32[]{:S(2)}) collective-permute-start(f32[3,48,1536]{2,1,0:T(8,128)S(1)} %add.138), channel_id=1, source_target_pairs={{0,8},{2,10},{4,12},{6,14},{8,0},{10,2},{12,4},{14,6},{1,9},{3,11}... | collective-permute-start | bytes 2654216 | tf_op jit(solution)/shard_map/ppermute | solution.py:86
  212.9 35.4 %collective-permute-done.8 = f32[3,48,1536]{2,1,0:T(8,128)S(1)} collective-permute-done((f32[3,48,1536]{2,1,0:T(8,128)S(1)}, f32[3,48,1536]{2,1,0:T(8,128)S(1)}, u32[]{:S(2)}, u32[]{:S(2)}) %collective-permute-start.8) | collective-permute-done | bytes 884768 | tf_op jit(solution)/shard_map/ppermute | solution.py:86
  (94 shorter events, 58.1 us)
Async XLA Ops:
  7.2 10.9 %copy-start.10 = (bf16[3,48,1536]{2,1,0:T(8,128)(2,1)S(1)}, bf16[3,48,1536]{2,1,0:T(8,128)(2,1)}, u32[]{:S(2)}) copy-start(bf16[3,48,1536]{2,1,0:T(8,128)(2,1)} %param.7) | copy-start | bytes 1327108
  7.2 242.1 %reduce-scatter.2.cloned.1.call-start = ((), (), s32[]{:S(2)}) async-start(), calls=%async_computation.1 | async-start | bytes 5308416 | tf_op jit(solution)/shard_map/reduce_scatter | solution.py:123
  9.7 29.0 %copy-start = (bf16[1,512,1536]{2,1,0:T(8,128)(2,1)}, bf16[1,512,1536]{2,1,0:T(8,128)(2,1)S(1)}, u32[]{:S(2)}) copy-start(bf16[1,512,1536]{2,1,0:T(8,128)(2,1)S(1)} %fusion.7) | copy-start | bytes 4718596
  10.5 31.9 %collective-permute-start.1 = (bf16[1,64,1536]{2,1,0:T(8,128)(2,1)}, bf16[1,64,1536]{2,1,0:T(8,128)(2,1)}, u32[]{:S(2)}, u32[]{:S(2)}) collective-permute-start(bf16[1,64,1536]{2,1,0:T(8,128)(2,1)} %get-tuple-element.11), channel_id=1, source_target_pairs={{2,0},{4,2},{6,4},{8,6},{10,8},{12,10},{14,12},{3,1},{5,3},{7,5},{... | collective-permute-start | bytes 589832 | tf_op jit(solution)/shard_map/ppermute | solution.py:22
  11.8 30.7 %collective-permute-start = (bf16[1,64,1536]{2,1,0:T(8,128)(2,1)}, bf16[1,64,1536]{2,1,0:T(8,128)(2,1)}, u32[]{:S(2)}, u32[]{:S(2)}) collective-permute-start(bf16[1,64,1536]{2,1,0:T(8,128)(2,1)} %get-tuple-element.10), channel_id=1, source_target_pairs={{0,2},{2,4},{4,6},{6,8},{8,10},{10,12},{12,14},{1,3},{3,5},{5,7},{... | collective-permute-start | bytes 589832 | tf_op jit(solution)/shard_map/ppermute | solution.py:20
  48.0 1.3 copy-start.6
  48.4 1.2 copy-start.7
  48.9 0.9 copy-start.8
  49.3 0.9 copy-start.9
  50.2 1.8 copy-start.2
  55.5 8.3 %collective-permute-start.4 = (f32[768,1536]{1,0:T(8,128)}, f32[768,1536]{1,0:T(8,128)}, u32[]{:S(2)}, u32[]{:S(2)}) collective-permute-start(f32[768,1536]{1,0:T(8,128)} %fusion.16), channel_id=1, source_target_pairs={{0,1},{1,0},{2,3},{3,2},{4,5},{5,4},{6,7},{7,6},{8,9},{9,8},{10,11... | collective-permute-start | bytes 14155784 | tf_op jit(solution)/shard_map/ppermute | solution.py:86
  70.4 14.9 %copy-start.1 = (bf16[1,512,1536]{2,1,0:T(8,128)(2,1)S(1)}, bf16[1,512,1536]{2,1,0:T(8,128)(2,1)}, u32[]{:S(2)}) copy-start(bf16[1,512,1536]{2,1,0:T(8,128)(2,1)} %copy-done) | copy-start | bytes 4718596
  77.2 11.0 %copy-start.4 = (bf16[512,1536]{0,1:T(8,128)(2,1)}, bf16[512,1536]{0,1:T(8,128)(2,1)S(1)}, u32[]{:S(2)}) copy-start(bf16[512,1536]{0,1:T(8,128)(2,1)S(1)} %fusion.15) | copy-start | bytes 4718596
  78.5 81.8 %collective-permute-start.3 = (bf16[1,64,1536]{1,2,0:T(8,128)(2,1)}, bf16[1,64,1536]{1,2,0:T(8,128)(2,1)}, u32[]{:S(2)}, u32[]{:S(2)}) collective-permute-start(bf16[1,64,1536]{1,2,0:T(8,128)(2,1)} %get-tuple-element.9), channel_id=1, source_target_pairs={{2,0},{4,2},{6,4},{8,6},{10,8},{12,10},{14,12},{3,1},{5,3},{7,5},{... | collective-permute-start | bytes 589832 | tf_op jit(solution)/shard_map/ppermute | solution.py:22
  79.7 80.5 %collective-permute-start.2 = (bf16[1,64,1536]{1,2,0:T(8,128)(2,1)}, bf16[1,64,1536]{1,2,0:T(8,128)(2,1)}, u32[]{:S(2)}, u32[]{:S(2)}) collective-permute-start(bf16[1,64,1536]{1,2,0:T(8,128)(2,1)} %get-tuple-element.8), channel_id=1, source_target_pairs={{0,2},{2,4},{4,6},{6,8},{8,10},{10,12},{12,14},{1,3},{3,5},{5,7},{... | collective-permute-start | bytes 589832 | tf_op jit(solution)/shard_map/ppermute | solution.py:20
  152.4 7.8 %copy-start.5 = (bf16[512,1536]{0,1:T(8,128)(2,1)S(1)}, bf16[512,1536]{0,1:T(8,128)(2,1)}, u32[]{:S(2)}) copy-start(bf16[512,1536]{0,1:T(8,128)(2,1)} %copy-done.4) | copy-start | bytes 4718596
  152.4 11.3 %collective-permute-start.5 = (f32[3,48,1536]{2,1,0:T(8,128)S(1)}, f32[3,48,1536]{2,1,0:T(8,128)S(1)}, u32[]{:S(2)}, u32[]{:S(2)}) collective-permute-start(f32[3,48,1536]{2,1,0:T(8,128)S(1)} %constant_dynamic-update-slice_fusion), channel_id=1, source_target_pairs={{0,1},{1,0},{2,3},{3,2},{4,5},{5,4},{6,7},{7,6},{8,9},{9,8},{10,11... | collective-permute-start | bytes 2654216 | tf_op jit(solution)/shard_map/ppermute | solution.py:86
  163.9 22.1 %collective-permute-start.6 = (f32[3,48,1536]{2,1,0:T(8,128)S(1)}, f32[3,48,1536]{2,1,0:T(8,128)S(1)}, u32[]{:S(2)}, u32[]{:S(2)}) collective-permute-start(f32[3,48,1536]{2,1,0:T(8,128)S(1)} %add.136), channel_id=1, source_target_pairs={{0,2},{2,0},{4,6},{6,4},{8,10},{10,8},{12,14},{14,12},{1,3},{3,1},... | collective-permute-start | bytes 2654216 | tf_op jit(solution)/shard_map/ppermute | solution.py:86
  186.1 21.5 %collective-permute-start.7 = (f32[3,48,1536]{2,1,0:T(8,128)S(1)}, f32[3,48,1536]{2,1,0:T(8,128)S(1)}, u32[]{:S(2)}, u32[]{:S(2)}) collective-permute-start(f32[3,48,1536]{2,1,0:T(8,128)S(1)} %add.137), channel_id=1, source_target_pairs={{0,4},{2,6},{4,0},{6,2},{8,12},{10,14},{12,8},{14,10},{1,5},{3,7},... | collective-permute-start | bytes 2654216 | tf_op jit(solution)/shard_map/ppermute | solution.py:86
  207.7 3.6 %copy-start.3 = (bf16[1,512,1536]{2,1,0:T(8,128)(2,1)S(1)}, bf16[1,512,1536]{2,1,0:T(8,128)(2,1)}, u32[]{:S(2)}) copy-start(bf16[1,512,1536]{2,1,0:T(8,128)(2,1)} %param.9) | copy-start | bytes 4718596
  207.7 40.5 %collective-permute-start.8 = (f32[3,48,1536]{2,1,0:T(8,128)S(1)}, f32[3,48,1536]{2,1,0:T(8,128)S(1)}, u32[]{:S(2)}, u32[]{:S(2)}) collective-permute-start(f32[3,48,1536]{2,1,0:T(8,128)S(1)} %add.138), channel_id=1, source_target_pairs={{0,8},{2,10},{4,12},{6,14},{8,0},{10,2},{12,4},{14,6},{1,9},{3,11}... | collective-permute-start | bytes 2654216 | tf_op jit(solution)/shard_map/ppermute | solution.py:86
Sparse Core Ops, SparseCore 0:
  70.5 104.4 reduce-scatter.1

commit v3 on v2

--- a/solution.py
+++ b/solution.py
@@ -35,26 +35,33 @@
 CHUNK = 384
 
 
+def group_mask(rows, chans, dtype):
+    row_group = lax.broadcasted_iota(jnp.int32, (rows, chans), 0) // GROUP_CHANNELS
+    col_group = (lax.broadcasted_iota(jnp.int32, (rows, chans), 1) % CHUNK) // GROUP_CHANNELS
+    return (row_group == col_group).astype(dtype)
+
+
 def dense_weight(weight):
     taps, width, chans = weight.shape
-    chunks = chans // CHUNK
     groups = CHUNK // width
-    cells = weight.reshape(taps, width, chunks, groups, width).transpose(0, 2, 1, 3, 4)
-    eye = jnp.eye(groups, dtype=weight.dtype)
-    dense = cells[:, :, None, :, :, :] * eye[None, None, :, None, :, None]
-    return dense.reshape(taps, chunks, CHUNK, CHUNK)
+    tiled = jnp.tile(weight, (1, groups, 1))
+    return tiled * group_mask(CHUNK, chans, weight.dtype)[None]
 
 
 def conv_taps(padded_input, dense, sequence_length, transpose=False):
     rows = padded_input[0]
+    chunks = dense.shape[2] // CHUNK
     parts = []
-    for c in range(dense.shape[1]):
+    for c in range(chunks):
+        cols = slice(c * CHUNK, (c + 1) * CHUNK)
         total = None
         for k in range(3):
             start = (2 - k if transpose else k) * DILATION_STEP
-            window = rows[start : start + sequence_length, c * CHUNK : (c + 1) * CHUNK]
+            window = rows[start : start + sequence_length, cols]
             dims = (((1,), (1,)), ((), ())) if transpose else (((1,), (0,)), ((), ()))
-            term = lax.dot_general(window, dense[k, c], dims, preferred_element_type=jnp.float32)
+            term = lax.dot_general(
+                window, dense[k, :, cols], dims, preferred_element_type=jnp.float32
+            )
             total = term if total is None else total + term
         parts.append(total)
     return jnp.concatenate(parts, axis=1)[None]
@@ -66,18 +73,19 @@
     chans = grads.shape[1]
     chunks = chans // CHUNK
     groups = CHUNK // GROUP_CHANNELS
-    eye = jnp.eye(groups, dtype=jnp.float32)
+    mask = group_mask(CHUNK, CHUNK, jnp.float32).reshape(groups, GROUP_CHANNELS, CHUNK)
     taps = []
     for k in range(3):
-        window = rows[k * DILATION_STEP : k * DILATION_STEP + sequence_length].reshape(
-            sequence_length, chunks, CHUNK
-        )
-        full = jnp.einsum(
-            "tci,tcj->cij", window, grads.reshape(sequence_length, chunks, CHUNK),
-            preferred_element_type=jnp.float32,
-        ).reshape(chunks, groups, GROUP_CHANNELS, groups, GROUP_CHANNELS)
-        diag = jnp.einsum("caibj,ab->icbj", full, eye)
-        taps.append(diag.reshape(GROUP_CHANNELS, chans))
+        parts = []
+        for c in range(chunks):
+            cols = slice(c * CHUNK, (c + 1) * CHUNK)
+            window = rows[k * DILATION_STEP : k * DILATION_STEP + sequence_length, cols]
+            full = lax.dot_general(
+                window, grads[:, cols], (((0,), (0,)), ((), ())),
+                preferred_element_type=jnp.float32,
+            ).reshape(groups, GROUP_CHANNELS, CHUNK)
+            parts.append(jnp.sum(full * mask, axis=0))
+        taps.append(jnp.concatenate(parts, axis=1))
     return jnp.stack(taps)
 
 

time: 263 us -> 203 us (0.77); the launches traced: 258 us -> 203 us
  local copies, waits for them, and re-layouts: 63.7 us -> 3.9 us
  waiting for transfers between devices: 76.1 us -> 108 us
  matrix products: 65.2 us -> 34.6 us
  starting transfers between devices: 20.9 us -> 26.9 us
  other arithmetic: 17 us -> 13.4 us
    reshape x7 -> x0, local copies, waits for them, and re-layouts: 25.1 us -> none  [the longest x3 15.8 us: weight_taps(): full = jnp.einsum('tci,tcj->cij', window, grads.reshape(sequence_length,...]
    dot_general x30 -> x36, matrix products: 40.7 us -> 19.8 us  [the longest x24 11.6 us: conv_taps(): lax.dot_general(window, dense[k, :, cols], dims, preferred_element_type=j...]
    mul x4 -> x0, local copies, waits for them, and re-layouts: 20.5 us -> none  [dense_weight(): dense = cells[:, :, None, :, :, :] * eye[None, None, :, None, :, None]]
    ppermute x5, waiting for transfers between devices: 76.1 us -> 95.5 us  [swap(): return lax.ppermute(value, axis, [(i, i ^ distance) for i in range(count)])]
    ppermute x2, waiting for transfers between devices: 0.01 us -> 10 us  [with_halo(): lax.ppermute(tail, axis, [(i, (i + 1) % count) for i in range(ends)])]
    ppermute x5, starting transfers between devices: 6.54 us -> 14.5 us  [swap(): return lax.ppermute(value, axis, [(i, i ^ distance) for i in range(count)])]
    another operation x4 -> x0, local copies, waits for them, and re-layouts: 7.89 us -> none  [weight_taps(): return jnp.stack(taps)]
    dot_general x2, matrix products: 10.1 us -> 4.88 us  [rows_of(): lax.dot_general(cols, cot_rows, (((0,), (0,)), ((), ())), preferred_eleme...]
  transfers between devices with their start and end apart: 10 -> 10, of which waited for: 4 -> 7; matrix products, arithmetic and copies ran while one was open for 47% -> 16% of each run, Pallas kernels for 0% -> 0%
where the time goes in v3:
time: 203 us
  waiting for transfers between devices  108 us (53%)
  matrix products  34.6 us (17%)
  starting transfers between devices  26.9 us (13%)
  between operations  15.5 us (8%)
  other arithmetic  13.4 us (7%)
  local copies, waits for them, and re-layouts  3.9 us (2%)
    ppermute x5, waiting for transfers between devices, swap(): return lax.ppermute(value, axis, [(i, i ^ distance) for i in range(count)])  95.5 us
    ppermute x5, starting transfers between devices, swap(): return lax.ppermute(value, axis, [(i, i ^ distance) for i in range(count)])  14.5 us
    dot_general x24, matrix products, conv_taps(): lax.dot_general(window, dense[k, :, cols], dims, preferred_element_type=j...  11.6 us
    ppermute x2, waiting for transfers between devices, with_halo(): lax.ppermute(tail, axis, [(i, (i + 1) % count) for i in range(ends)])  10 us
    ppermute x2, starting transfers between devices, with_halo(): lax.ppermute(tail, axis, [(i, (i + 1) % count) for i in range(ends)])  9.61 us
    dot_general x12, matrix products, weight_taps(): lax.dot_general(window, grads[:, cols], (((0,), (0,)), ((), ())), preferr...  8.23 us
    dot_general x1, matrix products, on_device(): jnp.dot(act_rows, point_weight, preferred_element_type=jnp.float32)  6.15 us
    dot_general x2, matrix products, rows_of(): lax.dot_general(cols, cot_rows, (((0,), (0,)), ((), ())), preferred_eleme...  4.88 us
  transfers between devices with their start and end apart: 10, of which 7 were waited for; matrix products, arithmetic and copies ran while one was open for 16% of the time, Pallas kernels for 0%

profile of v3, /device:TPU:0, one launch (start us, length us, event | category | flops | bytes accessed | tf_op | source)
XLA Modules:
  0.0 202.5 jit_solution(4858945216565617482)
XLA Ops:
  7.9 1.7 fusion.1
  10.4 5.6 %collective-permute-start = (bf16[1,64,1536]{2,1,0:T(8,128)(2,1)}, bf16[1,64,1536]{2,1,0:T(8,128)(2,1)}, u32[]{:S(2)}, u32[]{:S(2)}) collective-permute-start(bf16[1,64,1536]{2,1,0:T(8,128)(2,1)} %get-tuple-element.20), channel_id=1, source_target_pairs={{0,2},{2,4},{4,6},{6,8},{8,10},{10,12},{12,14},{1,3},{3,5},{5,7},{... | collective-permute-start | bytes 589832 | tf_op jit(solution)/shard_map/ppermute | solution.py:20
  15.9 1.3 collective-permute-start.1
  18.2 5.7 %collective-permute-done = bf16[1,64,1536]{2,1,0:T(8,128)(2,1)} collective-permute-done((bf16[1,64,1536]{2,1,0:T(8,128)(2,1)}, bf16[1,64,1536]{2,1,0:T(8,128)(2,1)}, u32[]{:S(2)}, u32[]{:S(2)}) %collective-permute-start) | collective-permute-done | bytes 196640 | tf_op jit(solution)/shard_map/ppermute | solution.py:20
  32.4 1.4 fusion.15
  35.1 3.7 %fusion.9 = bf16[512,1536]{0,1:T(8,128)(2,1)S(1)} fusion(bf16[1536,1536]{1,0:T(8,128)(2,1)S(1)} %bitcast.127, bf16[1,512,1536]{2,1,0:T(8,128)(2,1)S(1)} %copy-done.2, f32[512]{0:T(512)S(1)} %fusion.116, f32[512,384]{0,1:T(8,128)S(1)} %fusion.23, f32[512,384]{0,1:T(8,128)S(1)} %fusion.22, f32[512,384]{0,1:T(8,128)S(1)} %fusion.21, f32[512,384]{0,1:T(8,128)S(1)} %fusion.20), kind=kOutput, calls=%fused_computation.26 | convolution fusion | flops 2426929152 | bytes 11012096 | tf_op jit(solution)/shard_map/dot_general | solution.py:153
  38.8 1.2 fusion.89
  40.0 1.3 fusion.85
  41.3 1.2 fusion.78
  42.5 1.3 fusion.74
  44.8 3.5 %convolution_add_fusion = f32[768,1536]{1,0:T(8,128)} fusion(f32[768,1536]{1,0:T(8,128)S(1)} %collective-permute-done.4, bf16[512,768]{0,1:T(8,128)(2,1)S(1)} %bitcast.108, bf16[1,512,1536]{2,1,0:T(8,128)(2,1)S(1)} %copy-done.2), kind=kOutput, calls=%fused_computation.4 | convolution fusion | flops 1209139200 | bytes 11796480 | tf_op jit(solution)/shard_map/dot_general | solution.py:119
  48.8 4.1 %collective-permute-start.2 = (bf16[1,64,1536]{1,2,0:T(8,128)(2,1)}, bf16[1,64,1536]{1,2,0:T(8,128)(2,1)S(1)}, u32[]{:S(2)}, u32[]{:S(2)}) collective-permute-start(bf16[1,64,1536]{1,2,0:T(8,128)(2,1)} %get-tuple-element.18), channel_id=1, source_target_pairs={{0,2},{2,4},{4,6},{6,8},{8,10},{10,12},{12,14},{1,3},{3,5},{5,7},{... | collective-permute-start | bytes 589832 | tf_op jit(solution)/shard_map/ppermute | solution.py:20
  52.8 1.5 collective-permute-start.3
  60.3 6.1 %fusion.2 = bf16[1,512,1536]{2,1,0:T(8,128)(2,1)} fusion(bf16[1,512,1536]{2,1,0:T(8,128)(2,1)S(1)} %copy-done.16, bf16[1536,1536]{1,0:T(8,128)(2,1)} %param.8, f32[512]{0:T(512)S(1)} %fusion.116, f32[512,384]{0,1:T(8,128)S(1)} %copy-done.5, f32[512,384]{0,1:T(8,128)S(1)} %copy-done.7, f32[512,384]{0,1:T(8,128)S(1)} %copy-done.9, f32[512,384]{0,1:T(8,128)S(1)} %copy-done.11), kind=kOutput, calls=%fused_computation.13 | convolution fusion | flops 2425356288 | bytes 11012096 | tf_op jit(solution)/shard_map/dot_general | solution.py:151
  66.4 4.3 %collective-permute-done.2 = bf16[1,64,1536]{1,2,0:T(8,128)(2,1)S(1)} collective-permute-done((bf16[1,64,1536]{1,2,0:T(8,128)(2,1)}, bf16[1,64,1536]{1,2,0:T(8,128)(2,1)S(1)}, u32[]{:S(2)}, u32[]{:S(2)}) %collective-permute-start.2) | collective-permute-done | bytes 196640 | tf_op jit(solution)/shard_map/ppermute | solution.py:20
  70.8 2.4 %collective-permute-done.3 = bf16[1,64,1536]{1,2,0:T(8,128)(2,1)S(1)} collective-permute-done((bf16[1,64,1536]{1,2,0:T(8,128)(2,1)}, bf16[1,64,1536]{1,2,0:T(8,128)(2,1)S(1)}, u32[]{:S(2)}, u32[]{:S(2)}) %collective-permute-start.3) | collective-permute-done | bytes 196640 | tf_op jit(solution)/shard_map/ppermute | solution.py:22
  75.7 5.9 %collective-permute-start.6 = (f32[3,48,1536]{2,1,0:T(8,128)S(1)}, f32[3,48,1536]{2,1,0:T(8,128)S(1)}, u32[]{:S(2)}, u32[]{:S(2)}) collective-permute-start(f32[3,48,1536]{2,1,0:T(8,128)S(1)} %fusion.119), channel_id=1, source_target_pairs={{0,2},{2,0},{4,6},{6,4},{8,10},{10,8},{12,14},{14,12},{1,3},{3,1},... | collective-permute-start | bytes 2654216 | tf_op jit(solution)/shard_map/ppermute | solution.py:94
  83.7 25.7 %collective-permute-done.6 = f32[3,48,1536]{2,1,0:T(8,128)S(1)} collective-permute-done((f32[3,48,1536]{2,1,0:T(8,128)S(1)}, f32[3,48,1536]{2,1,0:T(8,128)S(1)}, u32[]{:S(2)}, u32[]{:S(2)}) %collective-permute-start.6) | collective-permute-done | bytes 884768 | tf_op jit(solution)/shard_map/ppermute | solution.py:94
  109.5 5.2 %collective-permute-start.7 = (f32[3,48,1536]{2,1,0:T(8,128)S(1)}, f32[3,48,1536]{2,1,0:T(8,128)S(1)}, u32[]{:S(2)}, u32[]{:S(2)}) collective-permute-start(f32[3,48,1536]{2,1,0:T(8,128)S(1)} %fusion.126), channel_id=1, source_target_pairs={{0,4},{2,6},{4,0},{6,2},{8,12},{10,14},{12,8},{14,10},{1,5},{3,7},... | collective-permute-start | bytes 2654216 | tf_op jit(solution)/shard_map/ppermute | solution.py:94
  117.1 16.6 %collective-permute-done.7 = f32[3,48,1536]{2,1,0:T(8,128)S(1)} collective-permute-done((f32[3,48,1536]{2,1,0:T(8,128)S(1)}, f32[3,48,1536]{2,1,0:T(8,128)S(1)}, u32[]{:S(2)}, u32[]{:S(2)}) %collective-permute-start.7) | collective-permute-done | bytes 884768 | tf_op jit(solution)/shard_map/ppermute | solution.py:94
  133.8 3.1 %collective-permute-start.8 = (f32[3,48,1536]{2,1,0:T(8,128)S(1)}, f32[3,48,1536]{2,1,0:T(8,128)S(1)}, u32[]{:S(2)}, u32[]{:S(2)}) collective-permute-start(f32[3,48,1536]{2,1,0:T(8,128)S(1)} %add.168), channel_id=1, source_target_pairs={{0,8},{2,10},{4,12},{6,14},{8,0},{10,2},{12,4},{14,6},{1,9},{3,11}... | collective-permute-start | bytes 2654216 | tf_op jit(solution)/shard_map/ppermute | solution.py:94
  137.9 1.6 fusion.8
  139.5 53.3 %collective-permute-done.8 = f32[3,48,1536]{2,1,0:T(8,128)S(1)} collective-permute-done((f32[3,48,1536]{2,1,0:T(8,128)S(1)}, f32[3,48,1536]{2,1,0:T(8,128)S(1)}, u32[]{:S(2)}, u32[]{:S(2)}) %collective-permute-start.8) | collective-permute-done | bytes 884768 | tf_op jit(solution)/shard_map/ppermute | solution.py:94
  193.8 1.9 broadcast_multiply_fusion
  (114 shorter events, 27.5 us)
Async XLA Ops:
  7.2 10.8 %copy-start.17 = (bf16[3,48,1536]{2,1,0:T(8,128)(2,1)S(1)}, bf16[3,48,1536]{2,1,0:T(8,128)(2,1)}, u32[]{:S(2)}) copy-start(bf16[3,48,1536]{2,1,0:T(8,128)(2,1)} %param.7) | copy-start | bytes 1327108
  7.2 186.6 %reduce-scatter.2.cloned.1.call-start = ((), (), s32[]{:S(2)}) async-start(), calls=%async_computation.1 | async-start | bytes 5308416 | tf_op jit(solution)/shard_map/reduce_scatter | solution.py:131
  10.4 13.6 %collective-permute-start = (bf16[1,64,1536]{2,1,0:T(8,128)(2,1)}, bf16[1,64,1536]{2,1,0:T(8,128)(2,1)}, u32[]{:S(2)}, u32[]{:S(2)}) collective-permute-start(bf16[1,64,1536]{2,1,0:T(8,128)(2,1)} %get-tuple-element.20), channel_id=1, source_target_pairs={{0,2},{2,4},{4,6},{6,8},{8,10},{10,12},{12,14},{1,3},{3,5},{5,7},{... | collective-permute-start | bytes 589832 | tf_op jit(solution)/shard_map/ppermute | solution.py:20
  15.9 8.3 %collective-permute-start.1 = (bf16[1,64,1536]{2,1,0:T(8,128)(2,1)S(1)}, bf16[1,64,1536]{2,1,0:T(8,128)(2,1)}, u32[]{:S(2)}, u32[]{:S(2)}) collective-permute-start(bf16[1,64,1536]{2,1,0:T(8,128)(2,1)S(1)} %get-tuple-element.21), channel_id=1, source_target_pairs={{2,0},{4,2},{6,4},{8,6},{10,8},{12,10},{14,12},{3,1},{5,3},{7,5},{... | collective-permute-start | bytes 589832 | tf_op jit(solution)/shard_map/ppermute | solution.py:22
  18.2 11.9 %copy-start = (bf16[3,384,1536]{2,1,0:T(8,128)(2,1)}, bf16[3,384,1536]{2,1,0:T(8,128)(2,1)S(1)}, u32[]{:S(2)}) copy-start(bf16[3,384,1536]{2,1,0:T(8,128)(2,1)S(1)} %bitcast_multiply_fusion) | copy-start | bytes 10616836
  29.3 5.8 %copy-start.4 = (f32[512,384]{0,1:T(8,128)}, f32[512,384]{0,1:T(8,128)S(1)}, u32[]{:S(2)}) copy-start(f32[512,384]{0,1:T(8,128)S(1)} %fusion.23) | copy-start | bytes 2359300
  29.7 5.3 %copy-start.6 = (f32[512,384]{0,1:T(8,128)}, f32[512,384]{0,1:T(8,128)S(1)}, u32[]{:S(2)}) copy-start(f32[512,384]{0,1:T(8,128)S(1)} %fusion.22) | copy-start | bytes 2359300
  30.2 4.8 %copy-start.8 = (f32[512,384]{0,1:T(8,128)}, f32[512,384]{0,1:T(8,128)S(1)}, u32[]{:S(2)}) copy-start(f32[512,384]{0,1:T(8,128)S(1)} %fusion.21) | copy-start | bytes 2359300
  30.6 4.4 %copy-start.10 = (f32[512,384]{0,1:T(8,128)}, f32[512,384]{0,1:T(8,128)S(1)}, u32[]{:S(2)}) copy-start(f32[512,384]{0,1:T(8,128)S(1)} %fusion.20) | copy-start | bytes 2359300
  31.0 4.1 %slice-start = ((s8[4718592]{0:T(1024)(128)(4,1)}), s8[4194304]{0:T(1024)(128)(4,1)S(1)}, s32[]{:S(2)}) async-start(s8[4718592]{0:T(1024)(128)(4,1)} %bitcast.126), calls=%async_computation.2 | async-start | bytes 8388608
  31.8 3.3 %slice-start.1 = ((s8[4718592]{0:T(1024)(128)(4,1)}), s8[524288]{0:T(1024)(128)(4,1)S(1)}, s32[]{:S(2)}) async-start(s8[4718592]{0:T(1024)(128)(4,1)} %bitcast.126), calls=%async_computation.3 | async-start | bytes 1048576
  33.7 11.1 %collective-permute-start.4 = (f32[768,1536]{1,0:T(8,128)S(1)}, f32[768,1536]{1,0:T(8,128)S(1)}, u32[]{:S(2)}, u32[]{:S(2)}) collective-permute-start(f32[768,1536]{1,0:T(8,128)S(1)} %fusion.15), channel_id=1, source_target_pairs={{0,1},{1,0},{2,3},{3,2},{4,5},{5,4},{6,7},{7,6},{8,9},{9,8},{10,11... | collective-permute-start | bytes 14155784 | tf_op jit(solution)/shard_map/ppermute | solution.py:94
  48.8 22.0 %collective-permute-start.2 = (bf16[1,64,1536]{1,2,0:T(8,128)(2,1)}, bf16[1,64,1536]{1,2,0:T(8,128)(2,1)S(1)}, u32[]{:S(2)}, u32[]{:S(2)}) collective-permute-start(bf16[1,64,1536]{1,2,0:T(8,128)(2,1)} %get-tuple-element.18), channel_id=1, source_target_pairs={{0,2},{2,4},{4,6},{6,8},{8,10},{10,12},{12,14},{1,3},{3,5},{5,7},{... | collective-permute-start | bytes 589832 | tf_op jit(solution)/shard_map/ppermute | solution.py:20
  52.8 20.3 %collective-permute-start.3 = (bf16[1,64,1536]{1,2,0:T(8,128)(2,1)}, bf16[1,64,1536]{1,2,0:T(8,128)(2,1)S(1)}, u32[]{:S(2)}, u32[]{:S(2)}) collective-permute-start(bf16[1,64,1536]{1,2,0:T(8,128)(2,1)} %get-tuple-element.19), channel_id=1, source_target_pairs={{2,0},{4,2},{6,4},{8,6},{10,8},{12,10},{14,12},{3,1},{5,3},{7,5},{... | collective-permute-start | bytes 589832 | tf_op jit(solution)/shard_map/ppermute | solution.py:22
  55.1 2.1 %copy-start.12 = (f32[384,384]{1,0:T(8,128)S(1)}, f32[384,384]{1,0:T(8,128)}, u32[]{:S(2)}) copy-start(f32[384,384]{1,0:T(8,128)} %fusion.89) | copy-start | bytes 1769476
  55.2 2.1 %copy-start.13 = (f32[384,384]{1,0:T(8,128)S(1)}, f32[384,384]{1,0:T(8,128)}, u32[]{:S(2)}) copy-start(f32[384,384]{1,0:T(8,128)} %fusion.85) | copy-start | bytes 1769476
  55.2 2.1 %copy-start.14 = (f32[384,384]{1,0:T(8,128)S(1)}, f32[384,384]{1,0:T(8,128)}, u32[]{:S(2)}) copy-start(f32[384,384]{1,0:T(8,128)} %fusion.78) | copy-start | bytes 1769476
  55.2 2.1 %copy-start.15 = (f32[384,384]{1,0:T(8,128)S(1)}, f32[384,384]{1,0:T(8,128)}, u32[]{:S(2)}) copy-start(f32[384,384]{1,0:T(8,128)} %fusion.74) | copy-start | bytes 1769476
  58.5 17.0 %collective-permute-start.5 = (f32[3,48,1536]{2,1,0:T(8,128)S(1)}, f32[3,48,1536]{2,1,0:T(8,128)S(1)}, u32[]{:S(2)}, u32[]{:S(2)}) collective-permute-start(f32[3,48,1536]{2,1,0:T(8,128)S(1)} %pad_maximum_fusion.2), channel_id=1, source_target_pairs={{0,1},{1,0},{2,3},{3,2},{4,5},{5,4},{6,7},{7,6},{8,9},{9,8},{10,11... | collective-permute-start | bytes 2654216 | tf_op jit(solution)/shard_map/ppermute | solution.py:94
  66.4 7.9 %copy-start.1 = (bf16[3,384,1536]{2,1,0:T(8,128)(2,1)S(1)}, bf16[3,384,1536]{2,1,0:T(8,128)(2,1)}, u32[]{:S(2)}) copy-start(bf16[3,384,1536]{2,1,0:T(8,128)(2,1)} %copy-done) | copy-start | bytes 10616836
  75.7 33.7 %collective-permute-start.6 = (f32[3,48,1536]{2,1,0:T(8,128)S(1)}, f32[3,48,1536]{2,1,0:T(8,128)S(1)}, u32[]{:S(2)}, u32[]{:S(2)}) collective-permute-start(f32[3,48,1536]{2,1,0:T(8,128)S(1)} %fusion.119), channel_id=1, source_target_pairs={{0,2},{2,0},{4,6},{6,4},{8,10},{10,8},{12,14},{14,12},{1,3},{3,1},... | collective-permute-start | bytes 2654216 | tf_op jit(solution)/shard_map/ppermute | solution.py:94
  109.5 24.2 %collective-permute-start.7 = (f32[3,48,1536]{2,1,0:T(8,128)S(1)}, f32[3,48,1536]{2,1,0:T(8,128)S(1)}, u32[]{:S(2)}, u32[]{:S(2)}) collective-permute-start(f32[3,48,1536]{2,1,0:T(8,128)S(1)} %fusion.126), channel_id=1, source_target_pairs={{0,4},{2,6},{4,0},{6,2},{8,12},{10,14},{12,8},{14,10},{1,5},{3,7},... | collective-permute-start | bytes 2654216 | tf_op jit(solution)/shard_map/ppermute | solution.py:94
  133.8 4.1 %copy-start.3 = (bf16[1,512,1536]{2,1,0:T(8,128)(2,1)S(1)}, bf16[1,512,1536]{2,1,0:T(8,128)(2,1)}, u32[]{:S(2)}) copy-start(bf16[1,512,1536]{2,1,0:T(8,128)(2,1)} %param.9) | copy-start | bytes 4718596
  133.8 58.9 %collective-permute-start.8 = (f32[3,48,1536]{2,1,0:T(8,128)S(1)}, f32[3,48,1536]{2,1,0:T(8,128)S(1)}, u32[]{:S(2)}, u32[]{:S(2)}) collective-permute-start(f32[3,48,1536]{2,1,0:T(8,128)S(1)} %add.168), channel_id=1, source_target_pairs={{0,8},{2,10},{4,12},{6,14},{8,0},{10,2},{12,4},{14,6},{1,9},{3,11}... | collective-permute-start | bytes 2654216 | tf_op jit(solution)/shard_map/ppermute | solution.py:94
  (10 other events, 16.7 us)
Sparse Core Ops, SparseCore 0:
  48.5 136.8 reduce-scatter.1

commit v4 on v3

--- a/solution.py
+++ b/solution.py
@@ -1,3 +1,4 @@
+import functools
 import math
 
 import jax
@@ -94,43 +95,85 @@
     return lax.ppermute(value, axis, [(i, i ^ distance) for i in range(count)])
 
 
-def tree_sum(value):
-    for axis in ("rep", "seq"):
-        count = lax.axis_size(axis)
-        if count & (count - 1):
-            value = lax.psum(value, axis)
-            continue
-        distance = 1
-        while distance < count:
-            value = value + swap(value, axis, distance)
-            distance *= 2
-    return value
-
-
-def point_gradient(act_rows, cot_rows, seq_count, rep_count):
+def ring_order(mesh):
+    count = mesh.shape["seq"]
+    names = mesh.axis_names
+    index = [0] * len(names)
+    cells = []
+    for s in range(count):
+        index[names.index("seq")] = s
+        device = mesh.devices[tuple(index)]
+        coords = getattr(device, "coords", None)
+        if coords is None:
+            return list(range(count))
+        cells.append((tuple(coords), s))
+    cells.sort(key=lambda cell: (cell[0][1], cell[0][2] if cell[0][1] % 2 == 0 else -cell[0][2]))
+    return [s for _, s in cells]
+
+
+def ring_reduce_scatter(blocks, ring):
+    count = blocks.shape[0]
+    if count == 1:
+        return blocks[0]
+    position = [0] * count
+    for p, s in enumerate(ring):
+        position[s] = p
+    ring_table = jnp.array(ring, jnp.int32)
+    here = jnp.array(position, jnp.int32)[lax.axis_index("seq")]
+    half = blocks.shape[2] // 2
+    forward = [(ring[i], ring[(i + 1) % count]) for i in range(count)]
+    backward = [(ring[i], ring[(i - 1) % count]) for i in range(count)]
+
+    def block(offset, low):
+        owner = ring_table[(here + offset) % count]
+        rows = lax.dynamic_index_in_dim(blocks, owner, axis=0, keepdims=False)
+        return rows[:, :half] if low else rows[:, half:]
+
+    ahead = block(-1, True)
+    behind = block(1, False)
+    for step in range(count - 1):
+        ahead = lax.ppermute(ahead, "seq", forward) + block(-2 - step, True)
+        behind = lax.ppermute(behind, "seq", backward) + block(2 + step, False)
+    return jnp.concatenate([ahead, behind], axis=1)
+
+
+def reduce_gradients(act_rows, cot_rows, conv_local, seq_count, rep_count, ring):
     chans = act_rows.shape[1]
-    block = chans // (seq_count * rep_count)
+    devices = seq_count * rep_count
+    block = chans // devices
     blocks = act_rows.reshape(act_rows.shape[0], seq_count, rep_count, block)
-    rep_index = lax.axis_index("rep")
+    conv_rows = conv_local.reshape(-1, chans)
+    conv_count = conv_rows.shape[0]
+    share = -(-conv_count // devices)
+    conv_rows = jnp.pad(conv_rows, ((0, share * devices - conv_count), (0, 0)))
+    conv_cells = conv_rows.reshape(seq_count, rep_count, share, chans)
 
     def rows_of(owner):
         cols = lax.dynamic_index_in_dim(blocks, owner, axis=2, keepdims=False)
         cols = cols.reshape(act_rows.shape[0], seq_count * block)
-        return lax.dot_general(
+        point = lax.dot_general(
             cols, cot_rows, (((0,), (0,)), ((), ())), preferred_element_type=jnp.float32
-        )
-
+        ).reshape(seq_count, block, chans)
+        conv = lax.dynamic_index_in_dim(conv_cells, owner, axis=1, keepdims=False)
+        return jnp.concatenate([point, conv], axis=1)
+
+    rep_index = lax.axis_index("rep")
     if rep_count == 2:
         mine = rows_of(rep_index) + swap(rows_of(1 - rep_index), "rep", 1)
     else:
-        full = lax.dot_general(
-            act_rows, cot_rows, (((0,), (0,)), ((), ())), preferred_element_type=jnp.float32
-        ).reshape(seq_count, rep_count, block, chans)
-        mine = lax.psum_scatter(full, "rep", scatter_dimension=1, tiled=True)
-        mine = mine.reshape(seq_count * block, chans)
-    return lax.psum_scatter(mine, "seq", scatter_dimension=0, tiled=True)
-
-def on_device(inputs, lengths, conv_weight, point_weight, cotangent):
+        mine = rows_of(0)
+        for other in range(1, rep_count):
+            mine = mine + lax.ppermute(
+                rows_of((rep_index + other) % rep_count), "rep",
+                [(i, (i + other) % rep_count) for i in range(rep_count)],
+            )
+    summed = ring_reduce_scatter(mine, ring)
+    point = summed[:block]
+    conv = lax.all_gather(summed[block:], ("seq", "rep"), axis=0, tiled=True)
+    return point, conv[:conv_count].reshape(conv_local.shape)
+
+
+def on_device(ring, inputs, lengths, conv_weight, point_weight, cotangent):
     local_bins = inputs.shape[1]
     chans = inputs.shape[2]
     seq_count = lax.axis_size("seq")
@@ -157,15 +200,18 @@
     padded_gradient = with_halo(preactivation_gradient, (("seq", 1),), DILATION_STEP)
     spread = conv_taps(padded_gradient, dense, local_bins, transpose=True)
     conv_local = weight_taps(padded_input, preactivation_gradient, local_bins)
-    grad_conv = tree_sum(conv_local) * scale
     grad_inputs = (cotangent.astype(jnp.float32) + mask3 * spread).astype(jnp.bfloat16)
-    grad_point = point_gradient(act_rows, cot_rows, seq_count, rep_count) * scale
+    grad_point, grad_conv = reduce_gradients(
+        act_rows, cot_rows, conv_local, seq_count, rep_count, ring
+    )
+    grad_point = grad_point * scale
+    grad_conv = grad_conv * scale
     return (output, grad_inputs, grad_point, grad_conv)
 
 
 def solution(mesh):
     return jax.shard_map(
-        on_device,
+        functools.partial(on_device, ring_order(mesh)),
         mesh=mesh,
         in_specs=(
             P(("groups", "rep"), "seq", None),

time: 203 us -> 238 us (1.17)
  waiting for transfers between devices: 108 us -> 47.3 us
  blocking collectives: 0 us -> 28.7 us
  between operations: 15.5 us -> 42.6 us
  local copies, waits for them, and re-layouts: 3.9 us -> 23 us
  other arithmetic: 13.4 us -> 22.4 us
  starting transfers between devices: 26.9 us -> 35.4 us
  matrix products: 34.6 us -> 37 us
    ppermute x5 -> x1, waiting for transfers between devices: 95.5 us -> 0.01 us  [swap(): return lax.ppermute(value, axis, [(i, i ^ distance) for i in range(count)])]
    ppermute x0 -> x14, waiting for transfers between devices: none -> 37.6 us  [the longest x7 24.7 us: ring_reduce_scatter(): ahead = lax.ppermute(ahead, 'seq', forward) + block(-2 - step, True)]
    all_gather x0 -> x1, blocking collectives: none -> 28.7 us  [reduce_gradients(): conv = lax.all_gather(summed[block:], ('seq', 'rep'), axis=0, tiled=True)]
    ppermute x0 -> x14, starting transfers between devices: none -> 23.2 us  [the longest x7 19.5 us: ring_reduce_scatter(): ahead = lax.ppermute(ahead, 'seq', forward) + block(-2 - step, True)]
    ppermute x5 -> x1, starting transfers between devices: 14.5 us -> 0.01 us  [swap(): return lax.ppermute(value, axis, [(i, i ^ distance) for i in range(count)])]
    add x3 -> x15, other arithmetic: 0.35 us -> 7.87 us  [the longest x1 7.25 us: reduce_gradients(): mine = rows_of(rep_index) + swap(rows_of(1 - rep_index), 'rep', 1)]
    concatenate x0 -> x1, local copies, waits for them, and re-layouts: none -> 5.33 us  [rows_of(): return jnp.concatenate([point, conv], axis=1)]
    squeeze x0 -> x2, local copies, waits for them, and re-layouts: none -> 5.3 us  [the longest x1 4.28 us: block(): rows = lax.dynamic_index_in_dim(blocks, owner, axis=0, keepdims=False)]
  transfers between devices with their start and end apart: 10 -> 19, of which waited for: 7 -> 17; matrix products, arithmetic and copies ran while one was open for 16% -> 13% of each run, Pallas kernels for 0% -> 0%
where the time goes in v4:
time: 238 us; the launch traced here: 237 us
  waiting for transfers between devices  47.3 us (20%)
  between operations  42.6 us (18%)
  matrix products  37 us (16%)
  starting transfers between devices  35.4 us (15%)
  blocking collectives  28.7 us (12%)
  local copies, waits for them, and re-layouts  23 us (10%)
  other arithmetic  22.4 us (9%)
    all_gather x1, blocking collectives, reduce_gradients(): conv = lax.all_gather(summed[block:], ('seq', 'rep'), axis=0, tiled=True)  28.7 us
    ppermute x7, waiting for transfers between devices, ring_reduce_scatter(): ahead = lax.ppermute(ahead, 'seq', forward) + block(-2 - step, True)  24.7 us
    ppermute x7, starting transfers between devices, ring_reduce_scatter(): ahead = lax.ppermute(ahead, 'seq', forward) + block(-2 - step, True)  19.5 us
    dot_general x24, matrix products, conv_taps(): lax.dot_general(window, dense[k, :, cols], dims, preferred_element_type=j...  15.9 us
    ppermute x7, waiting for transfers between devices, ring_reduce_scatter(): behind = lax.ppermute(behind, 'seq', backward) + block(2 + step, False)  12.9 us
    ppermute x2, starting transfers between devices, with_halo(): lax.ppermute(tail, axis, [(i, (i + 1) % count) for i in range(ends)])  9.39 us
    dot_general x1, matrix products, on_device(): jnp.dot(act_rows, point_weight, preferred_element_type=jnp.float32)  7.58 us
    add x1, other arithmetic, reduce_gradients(): mine = rows_of(rep_index) + swap(rows_of(1 - rep_index), 'rep', 1)  7.25 us
  transfers between devices with their start and end apart: 19, of which 17 were waited for; matrix products, arithmetic and copies ran while one was open for 13% of the time, Pallas kernels for 0%

profile of v4, /device:TPU:0, one launch (start us, length us, event | category | flops | bytes accessed | tf_op | source)
XLA Modules:
  0.0 236.6 jit_solution(1271054350265331045)
XLA Ops:
  3.9 5.5 %collective-permute-start = (bf16[1,64,1536]{2,1,0:T(8,128)(2,1)}, bf16[1,64,1536]{2,1,0:T(8,128)(2,1)}, u32[]{:S(2)}, u32[]{:S(2)}) collective-permute-start(bf16[1,64,1536]{2,1,0:T(8,128)(2,1)} %get-tuple-element.36), channel_id=1, source_target_pairs={{0,2},{2,4},{4,6},{6,8},{8,10},{10,12},{12,14},{1,3},{3,5},{5,7},{... | collective-permute-start | bytes 589832 | tf_op jit(solution)/shard_map/ppermute | solution.py:21
  13.3 4.7 %collective-permute-done.1 = bf16[1,64,1536]{2,1,0:T(8,128)(2,1)} collective-permute-done((bf16[1,64,1536]{2,1,0:T(8,128)(2,1)}, bf16[1,64,1536]{2,1,0:T(8,128)(2,1)}, u32[]{:S(2)}, u32[]{:S(2)}) %collective-permute-start.1) | collective-permute-done | bytes 196640 | tf_op jit(solution)/shard_map/ppermute | solution.py:23
  26.3 3.7 %fusion.9 = bf16[512,1536]{0,1:T(8,128)(2,1)S(1)} fusion(bf16[1536,1536]{1,0:T(8,128)(2,1)S(1)} %bitcast.206, bf16[1,512,1536]{2,1,0:T(8,128)(2,1)S(1)} %copy-done.2, f32[512]{0:T(512)S(1)} %fusion.126, f32[512,384]{0,1:T(8,128)S(1)} %fusion.24, f32[512,384]{0,1:T(8,128)S(1)} %fusion.23, f32[512,384]{0,1:T(8,128)S(1)} %fusion.22, f32[512,384]{0,1:T(8,128)S(1)} %fusion.21), kind=kOutput, calls=%fused_computation.27 | convolution fusion | flops 2426929152 | bytes 11012096 | tf_op jit(solution)/shard_map/dot_general | solution.py:196
  46.7 5.3 %copy.50 = f32[8,105,1536]{2,0,1:T(8,128)} copy(f32[8,105,1536]{2,1,0:T(8,128)S(1)} %pad_maximum_fusion) | data formatting | bytes 10321920 | tf_op jit(solution)/shard_map/concatenate | solution.py:158
  95.2 3.8 %collective-permute-start.2 = (bf16[1,64,1536]{1,2,0:T(8,128)(2,1)S(1)}, bf16[1,64,1536]{1,2,0:T(8,128)(2,1)S(1)}, u32[]{:S(2)}, u32[]{:S(2)}) collective-permute-start(bf16[1,64,1536]{1,2,0:T(8,128)(2,1)S(1)} %get-tuple-element.34), channel_id=1, source_target_pairs={{0,2},{2,4},{4,6},{6,8},{8,10},{10,12},{12,14},{1,3},{3,5},{5,7},{... | collective-permute-start | bytes 589832 | tf_op jit(solution)/shard_map/ppermute | solution.py:21
  100.7 7.6 %fusion.2 = bf16[1,512,1536]{2,1,0:T(8,128)(2,1)} fusion(bf16[1,512,1536]{2,1,0:T(8,128)(2,1)} %param.7, bf16[1536,1536]{1,0:T(8,128)(2,1)} %param.10, f32[512]{0:T(512)S(1)} %fusion.126, f32[512,384]{0,1:T(8,128)} %copy-done.11, f32[512,384]{0,1:T(8,128)} %copy-done.12, f32[512,384]{0,1:T(8,128)} %copy-done.13, f32[512,384]{0,1:T(8,128)} %copy-done.14), kind=kOutput, calls=%fused_computation.14 | convolution fusion | flops 2425356288 | bytes 11012096 | tf_op jit(solution)/shard_map/dot_general | solution.py:194
  108.3 3.6 %fusion.17 = f32[8,96,1536]{2,1,0:T(8,128)} fusion(bf16[1,512,1536]{2,1,0:T(8,128)(2,1)S(1)} %copy-done.4, bf16[512,8,2,96]{0,3,2,1:T(8,128)(2,1)S(1)} %copy-done.8, s32[]{:T(128)S(6)} %select_n.266), kind=kOutput, calls=%fused_computation.37 | convolution fusion | flops 1207959552 | bytes 7077892 | tf_op jit(solution)/shard_map/dot_general | solution.py:154
  111.9 4.6 %collective-permute-done.2 = bf16[1,64,1536]{1,2,0:T(8,128)(2,1)S(1)} collective-permute-done((bf16[1,64,1536]{1,2,0:T(8,128)(2,1)S(1)}, bf16[1,64,1536]{1,2,0:T(8,128)(2,1)S(1)}, u32[]{:S(2)}, u32[]{:S(2)}) %collective-permute-start.2) | collective-permute-done | bytes 196640 | tf_op jit(solution)/shard_map/ppermute | solution.py:21
  124.9 7.2 %maximum_add_fusion = f32[8,105,1536]{2,1,0:T(8,128)S(1)} fusion(f32[8,9,1536]{2,1,0:T(8,128)S(1)} %copy-done.10, f32[8,96,1536]{2,1,0:T(8,128)} %fusion.17, f32[8,105,1536]{2,0,1:T(8,128)} %collective-permute-done.4), kind=kLoop, calls=%fused_computation | loop fusion | flops 2580480 | bytes 15482880 | tf_op jit(solution)/shard_map/add | solution.py:162
  132.2 4.3 %dynamic-slice_bitcast_fusion.2 = (f32[105,1536]{1,0:T(8,128)}, f32[105,1536]{1,0:T(8,128)}, f32[105,1536]{1,0:T(8,128)}, f32[105,1536]{1,0:T(8,128)}, f32[105,1...) fusion(f32[8,105,1536]{2,1,0:T(8,128)S(1)} %maximum_add_fusion,, ...), kind=kLoop, calls=%fused_computation.71 | loop fusion | bytes 20643904 | tf_op jit(solution)/shard_map/jit(dynamic_index_in_dim)/squeeze | solution.py:129
  137.6 4.3 %collective-permute-start.5 = (f32[105,768]{1,0:T(8,128)S(1)}, f32[105,768]{1,0:T(8,128)S(1)}, u32[]{:S(2)}, u32[]{:S(2)}) collective-permute-start(f32[105,768]{1,0:T(8,128)S(1)} %slice.324), channel_id=1, source_target_pairs={{0,4},{4,8},{8,12},{12,14},{14,10},{10,6},{6,2},{2,0},{1,5},{5,9},... | collective-permute-start | bytes 967688 | tf_op jit(solution)/shard_map/ppermute | solution.py:135
  144.5 5.0 %collective-permute-done.5 = f32[105,768]{1,0:T(8,128)S(1)} collective-permute-done((f32[105,768]{1,0:T(8,128)S(1)}, f32[105,768]{1,0:T(8,128)S(1)}, u32[]{:S(2)}, u32[]{:S(2)}) %collective-permute-start.5) | collective-permute-done | bytes 322592 | tf_op jit(solution)/shard_map/ppermute | solution.py:135
  149.5 2.5 %collective-permute-start.6 = (f32[105,768]{1,0:T(8,128)S(1)}, f32[105,768]{1,0:T(8,128)S(1)}, u32[]{:S(2)}, u32[]{:S(2)}) collective-permute-start(f32[105,768]{1,0:T(8,128)S(1)} %slice_add_fusion.13), channel_id=1, source_target_pairs={{0,4},{4,8},{8,12},{12,14},{14,10},{10,6},{6,2},{2,0},{1,5},{5,9},... | collective-permute-start | bytes 967688 | tf_op jit(solution)/shard_map/ppermute | solution.py:135
  154.9 3.9 %collective-permute-done.6 = f32[105,768]{1,0:T(8,128)S(1)} collective-permute-done((f32[105,768]{1,0:T(8,128)S(1)}, f32[105,768]{1,0:T(8,128)S(1)}, u32[]{:S(2)}, u32[]{:S(2)}) %collective-permute-start.6) | collective-permute-done | bytes 322592 | tf_op jit(solution)/shard_map/ppermute | solution.py:135
  164.0 3.2 %collective-permute-done.7 = f32[105,768]{1,0:T(8,128)S(1)} collective-permute-done((f32[105,768]{1,0:T(8,128)S(1)}, f32[105,768]{1,0:T(8,128)S(1)}, u32[]{:S(2)}, u32[]{:S(2)}) %collective-permute-start.7) | collective-permute-done | bytes 322592 | tf_op jit(solution)/shard_map/ppermute | solution.py:135
  167.2 2.5 %collective-permute-start.8 = (f32[105,768]{1,0:T(8,128)S(1)}, f32[105,768]{1,0:T(8,128)S(1)}, u32[]{:S(2)}, u32[]{:S(2)}) collective-permute-start(f32[105,768]{1,0:T(8,128)S(1)} %slice_add_fusion.11), channel_id=1, source_target_pairs={{0,4},{4,8},{8,12},{12,14},{14,10},{10,6},{6,2},{2,0},{1,5},{5,9},... | collective-permute-start | bytes 967688 | tf_op jit(solution)/shard_map/ppermute | solution.py:135
  172.3 3.1 %collective-permute-done.8 = f32[105,768]{1,0:T(8,128)S(1)} collective-permute-done((f32[105,768]{1,0:T(8,128)S(1)}, f32[105,768]{1,0:T(8,128)S(1)}, u32[]{:S(2)}, u32[]{:S(2)}) %collective-permute-start.8) | collective-permute-done | bytes 322592 | tf_op jit(solution)/shard_map/ppermute | solution.py:135
  175.5 2.5 %collective-permute-start.9 = (f32[105,768]{1,0:T(8,128)S(1)}, f32[105,768]{1,0:T(8,128)S(1)}, u32[]{:S(2)}, u32[]{:S(2)}) collective-permute-start(f32[105,768]{1,0:T(8,128)S(1)} %slice_add_fusion.10), channel_id=1, source_target_pairs={{0,4},{4,8},{8,12},{12,14},{14,10},{10,6},{6,2},{2,0},{1,5},{5,9},... | collective-permute-start | bytes 967688 | tf_op jit(solution)/shard_map/ppermute | solution.py:135
  180.5 3.8 %collective-permute-done.9 = f32[105,768]{1,0:T(8,128)S(1)} collective-permute-done((f32[105,768]{1,0:T(8,128)S(1)}, f32[105,768]{1,0:T(8,128)S(1)}, u32[]{:S(2)}, u32[]{:S(2)}) %collective-permute-start.9) | collective-permute-done | bytes 322592 | tf_op jit(solution)/shard_map/ppermute | solution.py:135
  184.4 2.5 %collective-permute-start.10 = (f32[105,768]{1,0:T(8,128)S(1)}, f32[105,768]{1,0:T(8,128)S(1)}, u32[]{:S(2)}, u32[]{:S(2)}) collective-permute-start(f32[105,768]{1,0:T(8,128)S(1)} %slice_add_fusion.9), channel_id=1, source_target_pairs={{0,4},{4,8},{8,12},{12,14},{14,10},{10,6},{6,2},{2,0},{1,5},{5,9},... | collective-permute-start | bytes 967688 | tf_op jit(solution)/shard_map/ppermute | solution.py:135
  189.4 4.6 %collective-permute-done.10 = f32[105,768]{1,0:T(8,128)S(1)} collective-permute-done((f32[105,768]{1,0:T(8,128)S(1)}, f32[105,768]{1,0:T(8,128)S(1)}, u32[]{:S(2)}, u32[]{:S(2)}) %collective-permute-start.10) | collective-permute-done | bytes 322592 | tf_op jit(solution)/shard_map/ppermute | solution.py:135
  194.1 2.5 %collective-permute-start.11 = (f32[105,768]{1,0:T(8,128)S(1)}, f32[105,768]{1,0:T(8,128)S(1)}, u32[]{:S(2)}, u32[]{:S(2)}) collective-permute-start(f32[105,768]{1,0:T(8,128)S(1)} %slice_add_fusion.8), channel_id=1, source_target_pairs={{0,4},{4,8},{8,12},{12,14},{14,10},{10,6},{6,2},{2,0},{1,5},{5,9},... | collective-permute-start | bytes 967688 | tf_op jit(solution)/shard_map/ppermute | solution.py:135
  201.4 4.2 %collective-permute-done.18 = f32[105,768]{1,0:T(8,128)S(1)} collective-permute-done((f32[105,768]{1,0:T(8,128)S(1)}, f32[105,768]{1,0:T(8,128)S(1)}, u32[]{:S(2)}, u32[]{:S(2)}) %collective-permute-start.18) | collective-permute-done | bytes 322592 | tf_op jit(solution)/shard_map/ppermute | solution.py:136
  206.6 28.7 %all-gather = f32[16,9,1536]{2,1,0:T(8,128)S(1)} all-gather(f32[1,9,1536]{2,1,0:T(8,128)S(1)} %fusion.115), channel_id=1, replica_groups=mesh['groups'=2,'seq'=8,'rep'=2] {'seq','rep'}, dimensions={0}, use_global_device_ids=true | all-gather | bytes 940032 | tf_op jit(solution)/shard_map/all_gather | solution.py:172
  (182 shorter events, 69.9 us)
Async XLA Ops:
  3.9 9.4 %collective-permute-start = (bf16[1,64,1536]{2,1,0:T(8,128)(2,1)}, bf16[1,64,1536]{2,1,0:T(8,128)(2,1)}, u32[]{:S(2)}, u32[]{:S(2)}) collective-permute-start(bf16[1,64,1536]{2,1,0:T(8,128)(2,1)} %get-tuple-element.36), channel_id=1, source_target_pairs={{0,2},{2,4},{4,6},{6,8},{8,10},{10,12},{12,14},{1,3},{3,5},{5,7},{... | collective-permute-start | bytes 589832 | tf_op jit(solution)/shard_map/ppermute | solution.py:21
  9.4 8.6 %collective-permute-start.1 = (bf16[1,64,1536]{2,1,0:T(8,128)(2,1)}, bf16[1,64,1536]{2,1,0:T(8,128)(2,1)}, u32[]{:S(2)}, u32[]{:S(2)}) collective-permute-start(bf16[1,64,1536]{2,1,0:T(8,128)(2,1)} %get-tuple-element.37), channel_id=1, source_target_pairs={{2,0},{4,2},{6,4},{8,6},{10,8},{12,10},{14,12},{3,1},{5,3},{7,5},{... | collective-permute-start | bytes 589832 | tf_op jit(solution)/shard_map/ppermute | solution.py:23
  52.0 72.9 %collective-permute-start.4 = (f32[8,105,1536]{2,0,1:T(8,128)}, f32[8,105,1536]{2,0,1:T(8,128)}, u32[]{:S(2)}, u32[]{:S(2)}) collective-permute-start(f32[8,105,1536]{2,0,1:T(8,128)} %copy.50), channel_id=1, source_target_pairs={{0,1},{1,0},{2,3},{3,2},{4,5},{5,4},{6,7},{7,6},{8,9},{9,8},{10,11... | collective-permute-start | bytes 15482888 | tf_op jit(solution)/shard_map/ppermute | solution.py:95
  95.2 21.3 %collective-permute-start.2 = (bf16[1,64,1536]{1,2,0:T(8,128)(2,1)S(1)}, bf16[1,64,1536]{1,2,0:T(8,128)(2,1)S(1)}, u32[]{:S(2)}, u32[]{:S(2)}) collective-permute-start(bf16[1,64,1536]{1,2,0:T(8,128)(2,1)S(1)} %get-tuple-element.34), channel_id=1, source_target_pairs={{0,2},{2,4},{4,6},{6,8},{8,10},{10,12},{12,14},{1,3},{3,5},{5,7},{... | collective-permute-start | bytes 589832 | tf_op jit(solution)/shard_map/ppermute | solution.py:21
  99.1 17.4 %collective-permute-start.3 = (bf16[1,64,1536]{1,2,0:T(8,128)(2,1)S(1)}, bf16[1,64,1536]{1,2,0:T(8,128)(2,1)S(1)}, u32[]{:S(2)}, u32[]{:S(2)}) collective-permute-start(bf16[1,64,1536]{1,2,0:T(8,128)(2,1)S(1)} %get-tuple-element.35), channel_id=1, source_target_pairs={{2,0},{4,2},{6,4},{8,6},{10,8},{12,10},{14,12},{3,1},{5,3},{7,5},{... | collective-permute-start | bytes 589832 | tf_op jit(solution)/shard_map/ppermute | solution.py:23
  136.5 17.3 %copy-start.32 = (f32[105,1536]{1,0:T(8,128)S(1)}, f32[105,1536]{1,0:T(8,128)}, u32[]{:S(2)}) copy-start(f32[105,1536]{1,0:T(8,128)} %get-tuple-element.22) | copy-start | bytes 1935364
  137.6 11.9 %collective-permute-start.5 = (f32[105,768]{1,0:T(8,128)S(1)}, f32[105,768]{1,0:T(8,128)S(1)}, u32[]{:S(2)}, u32[]{:S(2)}) collective-permute-start(f32[105,768]{1,0:T(8,128)S(1)} %slice.324), channel_id=1, source_target_pairs={{0,4},{4,8},{8,12},{12,14},{14,10},{10,6},{6,2},{2,0},{1,5},{5,9},... | collective-permute-start | bytes 967688 | tf_op jit(solution)/shard_map/ppermute | solution.py:135
  143.7 19.0 %copy-start.30 = (f32[105,1536]{1,0:T(8,128)S(1)}, f32[105,1536]{1,0:T(8,128)}, u32[]{:S(2)}) copy-start(f32[105,1536]{1,0:T(8,128)} %get-tuple-element.21) | copy-start | bytes 1935364
  143.7 10.0 %collective-permute-start.12 = (f32[105,768]{1,0:T(8,128)S(1)}, f32[105,768]{1,0:T(8,128)S(1)}, u32[]{:S(2)}, u32[]{:S(2)}) collective-permute-start(f32[105,768]{1,0:T(8,128)S(1)} %slice.332), channel_id=1, source_target_pairs={{0,2},{4,0},{8,4},{12,8},{14,12},{10,14},{6,10},{2,6},{1,3},{5,1},... | collective-permute-start | bytes 967688 | tf_op jit(solution)/shard_map/ppermute | solution.py:136
  144.5 19.0 %copy-start.18 = (f32[512,384]{1,0:T(8,128)S(1)}, f32[512,384]{1,0:T(8,128)}, u32[]{:S(2)}) copy-start(f32[512,384]{1,0:T(8,128)} %fusion.39) | copy-start | bytes 2359300
  144.5 19.0 %copy-start.19 = (f32[512,384]{1,0:T(8,128)S(1)}, f32[512,384]{1,0:T(8,128)}, u32[]{:S(2)}) copy-start(f32[512,384]{1,0:T(8,128)} %fusion.41) | copy-start | bytes 2359300
  149.5 9.3 %collective-permute-start.6 = (f32[105,768]{1,0:T(8,128)S(1)}, f32[105,768]{1,0:T(8,128)S(1)}, u32[]{:S(2)}, u32[]{:S(2)}) collective-permute-start(f32[105,768]{1,0:T(8,128)S(1)} %slice_add_fusion.13), channel_id=1, source_target_pairs={{0,4},{4,8},{8,12},{12,14},{14,10},{10,6},{6,2},{2,0},{1,5},{5,9},... | collective-permute-start | bytes 967688 | tf_op jit(solution)/shard_map/ppermute | solution.py:135
  153.8 8.9 %collective-permute-start.13 = (f32[105,768]{1,0:T(8,128)S(1)}, f32[105,768]{1,0:T(8,128)S(1)}, u32[]{:S(2)}, u32[]{:S(2)}) collective-permute-start(f32[105,768]{1,0:T(8,128)S(1)} %slice_add_fusion.6), channel_id=1, source_target_pairs={{0,2},{4,0},{8,4},{12,8},{14,12},{10,14},{6,10},{2,6},{1,3},{5,1},... | collective-permute-start | bytes 967688 | tf_op jit(solution)/shard_map/ppermute | solution.py:136
  158.9 8.3 %collective-permute-start.7 = (f32[105,768]{1,0:T(8,128)S(1)}, f32[105,768]{1,0:T(8,128)S(1)}, u32[]{:S(2)}, u32[]{:S(2)}) collective-permute-start(f32[105,768]{1,0:T(8,128)S(1)} %slice_add_fusion.12), channel_id=1, source_target_pairs={{0,4},{4,8},{8,12},{12,14},{14,10},{10,6},{6,2},{2,0},{1,5},{5,9},... | collective-permute-start | bytes 967688 | tf_op jit(solution)/shard_map/ppermute | solution.py:135
  162.8 8.2 %collective-permute-start.14 = (f32[105,768]{1,0:T(8,128)S(1)}, f32[105,768]{1,0:T(8,128)S(1)}, u32[]{:S(2)}, u32[]{:S(2)}) collective-permute-start(f32[105,768]{1,0:T(8,128)S(1)} %slice_add_fusion.5), channel_id=1, source_target_pairs={{0,2},{4,0},{8,4},{12,8},{14,12},{10,14},{6,10},{2,6},{1,3},{5,1},... | collective-permute-start | bytes 967688 | tf_op jit(solution)/shard_map/ppermute | solution.py:136
  167.2 8.2 %collective-permute-start.8 = (f32[105,768]{1,0:T(8,128)S(1)}, f32[105,768]{1,0:T(8,128)S(1)}, u32[]{:S(2)}, u32[]{:S(2)}) collective-permute-start(f32[105,768]{1,0:T(8,128)S(1)} %slice_add_fusion.11), channel_id=1, source_target_pairs={{0,4},{4,8},{8,12},{12,14},{14,10},{10,6},{6,2},{2,0},{1,5},{5,9},... | collective-permute-start | bytes 967688 | tf_op jit(solution)/shard_map/ppermute | solution.py:135
  171.0 8.2 %collective-permute-start.15 = (f32[105,768]{1,0:T(8,128)S(1)}, f32[105,768]{1,0:T(8,128)S(1)}, u32[]{:S(2)}, u32[]{:S(2)}) collective-permute-start(f32[105,768]{1,0:T(8,128)S(1)} %slice_add_fusion.4), channel_id=1, source_target_pairs={{0,2},{4,0},{8,4},{12,8},{14,12},{10,14},{6,10},{2,6},{1,3},{5,1},... | collective-permute-start | bytes 967688 | tf_op jit(solution)/shard_map/ppermute | solution.py:136
  175.5 8.8 %collective-permute-start.9 = (f32[105,768]{1,0:T(8,128)S(1)}, f32[105,768]{1,0:T(8,128)S(1)}, u32[]{:S(2)}, u32[]{:S(2)}) collective-permute-start(f32[105,768]{1,0:T(8,128)S(1)} %slice_add_fusion.10), channel_id=1, source_target_pairs={{0,4},{4,8},{8,12},{12,14},{14,10},{10,6},{6,2},{2,0},{1,5},{5,9},... | collective-permute-start | bytes 967688 | tf_op jit(solution)/shard_map/ppermute | solution.py:135
  179.3 9.0 %collective-permute-start.16 = (f32[105,768]{1,0:T(8,128)S(1)}, f32[105,768]{1,0:T(8,128)S(1)}, u32[]{:S(2)}, u32[]{:S(2)}) collective-permute-start(f32[105,768]{1,0:T(8,128)S(1)} %slice_add_fusion.3), channel_id=1, source_target_pairs={{0,2},{4,0},{8,4},{12,8},{14,12},{10,14},{6,10},{2,6},{1,3},{5,1},... | collective-permute-start | bytes 967688 | tf_op jit(solution)/shard_map/ppermute | solution.py:136
  180.5 17.8 %copy-start.22 = (f32[105,1536]{1,0:T(8,128)S(1)}, f32[105,1536]{1,0:T(8,128)}, u32[]{:S(2)}) copy-start(f32[105,1536]{1,0:T(8,128)} %get-tuple-element.17) | copy-start | bytes 1935364
  184.4 9.7 %collective-permute-start.10 = (f32[105,768]{1,0:T(8,128)S(1)}, f32[105,768]{1,0:T(8,128)S(1)}, u32[]{:S(2)}, u32[]{:S(2)}) collective-permute-start(f32[105,768]{1,0:T(8,128)S(1)} %slice_add_fusion.9), channel_id=1, source_target_pairs={{0,4},{4,8},{8,12},{12,14},{14,10},{10,6},{6,2},{2,0},{1,5},{5,9},... | collective-permute-start | bytes 967688 | tf_op jit(solution)/shard_map/ppermute | solution.py:135
  188.4 9.9 %collective-permute-start.17 = (f32[105,768]{1,0:T(8,128)S(1)}, f32[105,768]{1,0:T(8,128)S(1)}, u32[]{:S(2)}, u32[]{:S(2)}) collective-permute-start(f32[105,768]{1,0:T(8,128)S(1)} %slice_add_fusion.2), channel_id=1, source_target_pairs={{0,2},{4,0},{8,4},{12,8},{14,12},{10,14},{6,10},{2,6},{1,3},{5,1},... | collective-permute-start | bytes 967688 | tf_op jit(solution)/shard_map/ppermute | solution.py:136
  194.1 7.3 %collective-permute-start.11 = (f32[105,768]{1,0:T(8,128)S(1)}, f32[105,768]{1,0:T(8,128)S(1)}, u32[]{:S(2)}, u32[]{:S(2)}) collective-permute-start(f32[105,768]{1,0:T(8,128)S(1)} %slice_add_fusion.8), channel_id=1, source_target_pairs={{0,4},{4,8},{8,12},{12,14},{14,10},{10,6},{6,2},{2,0},{1,5},{5,9},... | collective-permute-start | bytes 967688 | tf_op jit(solution)/shard_map/ppermute | solution.py:135
  198.4 7.3 %collective-permute-start.18 = (f32[105,768]{1,0:T(8,128)S(1)}, f32[105,768]{1,0:T(8,128)S(1)}, u32[]{:S(2)}, u32[]{:S(2)}) collective-permute-start(f32[105,768]{1,0:T(8,128)S(1)} %slice_add_fusion.1), channel_id=1, source_target_pairs={{0,2},{4,0},{8,4},{12,8},{14,12},{10,14},{6,10},{2,6},{1,3},{5,1},... | collective-permute-start | bytes 967688 | tf_op jit(solution)/shard_map/ppermute | solution.py:136
  (33 other events, 280.7 us)

commit v5 on v3

--- a/solution.py
+++ b/solution.py
@@ -94,17 +94,43 @@
     return lax.ppermute(value, axis, [(i, i ^ distance) for i in range(count)])
 
 
+def halving_plan(rows, cols, steps):
+    plan = []
+    for _ in range(steps):
+        if cols % 256 == 0:
+            plan.append(1)
+            cols //= 2
+        else:
+            plan.append(0)
+            rows //= 2
+    return plan
+
+
 def tree_sum(value):
+    shape = value.shape
+    cells = value.reshape(-1, shape[-1])
+    stages = []
     for axis in ("rep", "seq"):
-        count = lax.axis_size(axis)
-        if count & (count - 1):
-            value = lax.psum(value, axis)
-            continue
         distance = 1
-        while distance < count:
-            value = value + swap(value, axis, distance)
+        while distance < lax.axis_size(axis):
+            stages.append((axis, distance))
             distance *= 2
-    return value
+    plan = halving_plan(cells.shape[0], cells.shape[1], len(stages))
+    held = cells
+    for (axis, distance), dim in zip(stages, plan):
+        bit = (lax.axis_index(axis) // distance) % 2
+        size = held.shape[dim] // 2
+        keep = lax.dynamic_slice_in_dim(held, bit * size, size, axis=dim)
+        give = lax.dynamic_slice_in_dim(held, (1 - bit) * size, size, axis=dim)
+        held = keep + swap(give, axis, distance)
+    for (axis, distance), dim in reversed(list(zip(stages, plan))):
+        bit = (lax.axis_index(axis) // distance) % 2
+        size = held.shape[dim]
+        other = swap(held, axis, distance)
+        full = jnp.concatenate([held, held], axis=dim)
+        full = lax.dynamic_update_slice_in_dim(full, held, bit * size, axis=dim)
+        held = lax.dynamic_update_slice_in_dim(full, other, (1 - bit) * size, axis=dim)
+    return held.reshape(shape)
 
 
 def point_gradient(act_rows, cot_rows, seq_count, rep_count):

time: 203 us -> 187 us (0.921)
  waiting for transfers between devices: 108 us -> 74.2 us
  matrix products: 34.6 us -> 51.3 us
  other arithmetic: 13.4 us -> 19 us
  starting transfers between devices: 26.9 us -> 22.1 us
    ppermute x5 -> x9, waiting for transfers between devices: 95.5 us -> 40.6 us  [swap(): return lax.ppermute(value, axis, [(i, i ^ distance) for i in range(count)])]
    reduce_scatter x1, waiting for transfers between devices: 0.01 us -> 27.6 us  [point_gradient(): return lax.psum_scatter(mine, 'seq', scatter_dimension=0, tiled=True)]
    dot_general x12, matrix products: 8.23 us -> 14 us  [weight_taps(): lax.dot_general(window, grads[:, cols], (((0,), (0,)), ((), ())), preferr...]
    ppermute x5 -> x9, starting transfers between devices: 14.5 us -> 8.92 us  [swap(): return lax.ppermute(value, axis, [(i, i ^ distance) for i in range(count)])]
    dot_general x2, matrix products: 4.88 us -> 9.34 us  [rows_of(): lax.dot_general(cols, cot_rows, (((0,), (0,)), ((), ())), preferred_eleme...]
    ppermute x2, waiting for transfers between devices: 10 us -> 5.7 us  [with_halo(): lax.ppermute(tail, axis, [(i, (i + 1) % count) for i in range(ends)])]
    dot_general x24, matrix products: 11.6 us -> 15.1 us  [conv_taps(): lax.dot_general(window, dense[k, :, cols], dims, preferred_element_type=j...]
    reduce_sum x1, other arithmetic: 0.96 us -> 3.94 us  [weight_taps(): parts.append(jnp.sum(full * mask, axis=0))]
  transfers between devices with their start and end apart: 10 -> 14, of which waited for: 7 -> 9; matrix products, arithmetic and copies ran while one was open for 16% -> 31% of each run, Pallas kernels for 0% -> 0%
where the time goes in v5:
time: 187 us
  waiting for transfers between devices  74.2 us (40%)
  matrix products  51.3 us (27%)
  starting transfers between devices  22.1 us (12%)
  other arithmetic  19 us (10%)
  between operations  15.4 us (8%)
  local copies, waits for them, and re-layouts  4.69 us (3%)
    ppermute x9, waiting for transfers between devices, swap(): return lax.ppermute(value, axis, [(i, i ^ distance) for i in range(count)])  40.6 us
    reduce_scatter x1, waiting for transfers between devices, point_gradient(): return lax.psum_scatter(mine, 'seq', scatter_dimension=0, tiled=True)  27.6 us
    dot_general x24, matrix products, conv_taps(): lax.dot_general(window, dense[k, :, cols], dims, preferred_element_type=j...  15.1 us
    dot_general x12, matrix products, weight_taps(): lax.dot_general(window, grads[:, cols], (((0,), (0,)), ((), ())), preferr...  14 us
    ppermute x2, starting transfers between devices, with_halo(): lax.ppermute(tail, axis, [(i, (i + 1) % count) for i in range(ends)])  10.4 us
    dot_general x2, matrix products, rows_of(): lax.dot_general(cols, cot_rows, (((0,), (0,)), ((), ())), preferred_eleme...  9.34 us
    ppermute x9, starting transfers between devices, swap(): return lax.ppermute(value, axis, [(i, i ^ distance) for i in range(count)])  8.92 us
    dot_general x1, matrix products, on_device(): lax.dot_general(cot_rows, point_weight, (((1,), (1,)), ((), ())), preferr...  6.65 us
  transfers between devices with their start and end apart: 14, of which 9 were waited for; matrix products, arithmetic and copies ran while one was open for 31% of the time, Pallas kernels for 0%

profile of v5, /device:TPU:0, one launch (start us, length us, event | category | flops | bytes accessed | tf_op | source)
XLA Modules:
  0.0 186.7 jit_solution(13822512825292006062)
XLA Ops:
  7.9 1.7 fusion.1
  10.4 5.6 %collective-permute-start = (bf16[1,64,1536]{2,1,0:T(8,128)(2,1)}, bf16[1,64,1536]{2,1,0:T(8,128)(2,1)}, u32[]{:S(2)}, u32[]{:S(2)}) collective-permute-start(bf16[1,64,1536]{2,1,0:T(8,128)(2,1)} %get-tuple-element.20), channel_id=1, source_target_pairs={{0,2},{2,4},{4,6},{6,8},{8,10},{10,12},{12,14},{1,3},{3,5},{5,7},{... | collective-permute-start | bytes 589832 | tf_op jit(solution)/shard_map/ppermute | solution.py:20
  18.2 5.7 %collective-permute-done = bf16[1,64,1536]{2,1,0:T(8,128)(2,1)} collective-permute-done((bf16[1,64,1536]{2,1,0:T(8,128)(2,1)}, bf16[1,64,1536]{2,1,0:T(8,128)(2,1)}, u32[]{:S(2)}, u32[]{:S(2)}) %collective-permute-start) | collective-permute-done | bytes 196640 | tf_op jit(solution)/shard_map/ppermute | solution.py:20
  33.4 3.5 %fusion.15 = f32[768,1536]{1,0:T(8,128)} fusion(bf16[512,768]{0,1:T(8,128)(2,1)S(1)} %bitcast.117, bf16[1,512,1536]{2,1,0:T(8,128)(2,1)S(1)} %copy-done.2), kind=kOutput, calls=%fused_computation.34 | convolution fusion | flops 1207959552 | bytes 7077888 | tf_op jit(solution)/shard_map/dot_general | solution.py:145
  38.0 6.6 %fusion.9 = bf16[512,1536]{0,1:T(8,128)(2,1)S(1)} fusion(bf16[1536,1536]{1,0:T(8,128)(2,1)} %param.8, bf16[1,512,1536]{2,1,0:T(8,128)(2,1)} %param.9, f32[512]{0:T(512)S(1)} %fusion.116, f32[512,384]{0,1:T(8,128)} %copy-done.6, f32[512,384]{0,1:T(8,128)} %copy-done.8, f32[512,384]{0,1:T(8,128)} %copy-done.10, f32[512,384]{0,1:T(8,128)} %copy-done.12), kind=kOutput, calls=%fused_computation.26 | convolution fusion | flops 2426929152 | bytes 11012096 | tf_op jit(solution)/shard_map/dot_general | solution.py:179
  45.7 4.8 %collective-permute-start.2 = (bf16[1,64,1536]{1,2,0:T(8,128)(2,1)}, bf16[1,64,1536]{1,2,0:T(8,128)(2,1)}, u32[]{:S(2)}, u32[]{:S(2)}) collective-permute-start(bf16[1,64,1536]{1,2,0:T(8,128)(2,1)} %get-tuple-element.18), channel_id=1, source_target_pairs={{0,2},{2,4},{4,6},{6,8},{8,10},{10,12},{12,14},{1,3},{3,5},{5,7},{... | collective-permute-start | bytes 589832 | tf_op jit(solution)/shard_map/ppermute | solution.py:20
  50.5 1.5 collective-permute-start.3
  65.6 5.8 %convolution_add_fusion = f32[768,1536]{1,0:T(8,128)} fusion(f32[768,1536]{1,0:T(8,128)} %collective-permute-done.4, bf16[512,768]{0,1:T(8,128)(2,1)S(1)} %bitcast.110, bf16[1,512,1536]{2,1,0:T(8,128)(2,1)S(1)} %copy-done.3), kind=kOutput, calls=%fused_computation.4 | convolution fusion | flops 1209139200 | bytes 11796480 | tf_op jit(solution)/shard_map/dot_general | solution.py:145
  72.0 3.9 %select_reduce_fusion.11 = (f32[48,384]{1,0:T(8,128)S(1)}, f32[48,384]{1,0:T(8,128)S(1)}, f32[48,384]{1,0:T(8,128)S(1)}, f32[48,384]{1,0:T(8,128)S(1)}, f32[48,3...) fusion(f32[8,48,384]{2,1,0:T(8,128)S(1)} %bitcast.129, ...), kind=kLoop, calls=%fused_computation.72 | loop fusion | flops 3760128 | bytes 7969536 | tf_op jit(solution)/shard_map/reduce_sum | solution.py:87
  76.2 6.2 %fusion.2 = bf16[1,512,1536]{2,1,0:T(8,128)(2,1)} fusion(bf16[1,512,1536]{2,1,0:T(8,128)(2,1)S(1)} %copy-done.15, bf16[1536,1536]{1,0:T(8,128)(2,1)} %param.8, f32[512]{0:T(512)S(1)} %fusion.116, f32[512,384]{0,1:T(8,128)S(1)} %copy-done.7, f32[512,384]{0,1:T(8,128)S(1)} %copy-done.9, f32[512,384]{0,1:T(8,128)S(1)} %copy-done.11, f32[512,384]{0,1:T(8,128)S(1)} %copy-done.13), kind=kOutput, calls=%fused_computation.13 | convolution fusion | flops 2425356288 | bytes 11012096 | tf_op jit(solution)/shard_map/dot_general | solution.py:177
  82.9 2.5 %maximum_bitcast_fusion.1 = bf16[640,1536]{0,1:T(8,128)(2,1)S(1)} fusion(bf16[1,64,1536]{1,2,0:T(8,128)(2,1)} %collective-permute-done.3, bf16[1,512,1536]{1,2,0:T(8,128)(2,1)S(1)} %bitcast.108, bf16[1,64,1536]{1,2,0:T(8,128)(2,1)} %collective-permute-done.2), kind=kLoop, calls=%fused_computation.33 | loop fusion | flops 5898240 | bytes 3932160 | tf_op jit(solution)/shard_map/squeeze | solution.py:52
  90.2 2.4 %collective-permute-start.6 = (f32[144,384]{1,0:T(8,128)S(1)}, f32[144,384]{1,0:T(8,128)S(1)}, u32[]{:S(2)}, u32[]{:S(2)}) collective-permute-start(f32[144,384]{1,0:T(8,128)S(1)} %constant_dynamic-slice_fusion.2), channel_id=1, source_target_pairs={{0,2},{2,0},{4,6},{6,4},{8,10},{10,8},{12,14},{14,12},{1,3},{3,1},... | collective-permute-start | bytes 663560 | tf_op jit(solution)/shard_map/ppermute | solution.py:94
  95.3 3.6 %collective-permute-done.6 = f32[144,384]{1,0:T(8,128)S(1)} collective-permute-done((f32[144,384]{1,0:T(8,128)S(1)}, f32[144,384]{1,0:T(8,128)S(1)}, u32[]{:S(2)}, u32[]{:S(2)}) %collective-permute-start.6) | collective-permute-done | bytes 221216 | tf_op jit(solution)/shard_map/ppermute | solution.py:94
  98.9 2.9 %collective-permute-start.7 = (f32[72,384]{1,0:T(8,128)S(1)}, f32[72,384]{1,0:T(8,128)S(1)}, u32[]{:S(2)}, u32[]{:S(2)}) collective-permute-start(f32[72,384]{1,0:T(8,128)S(1)} %constant_dynamic-slice_fusion.1), channel_id=1, source_target_pairs={{0,4},{2,6},{4,0},{6,2},{8,12},{10,14},{12,8},{14,10},{1,5},{3,7},... | collective-permute-start | bytes 331784 | tf_op jit(solution)/shard_map/ppermute | solution.py:94
  103.2 8.8 %collective-permute-done.7 = f32[72,384]{1,0:T(8,128)S(1)} collective-permute-done((f32[72,384]{1,0:T(8,128)S(1)}, f32[72,384]{1,0:T(8,128)S(1)}, u32[]{:S(2)}, u32[]{:S(2)}) %collective-permute-start.7) | collective-permute-done | bytes 110624 | tf_op jit(solution)/shard_map/ppermute | solution.py:94
  112.0 1.5 collective-permute-start.8
  114.8 7.2 %collective-permute-done.8 = f32[36,384]{1,0:T(8,128)S(1)} collective-permute-done((f32[36,384]{1,0:T(8,128)S(1)}, f32[36,384]{1,0:T(8,128)S(1)}, u32[]{:S(2)}, u32[]{:S(2)}) %collective-permute-start.8) | collective-permute-done | bytes 55328 | tf_op jit(solution)/shard_map/ppermute | solution.py:94
  122.6 6.5 %collective-permute-done.9 = f32[36,384]{1,0:T(8,128)S(1)} collective-permute-done((f32[36,384]{1,0:T(8,128)S(1)}, f32[36,384]{1,0:T(8,128)S(1)}, u32[]{:S(2)}, u32[]{:S(2)}) %collective-permute-start.9) | collective-permute-done | bytes 55328 | tf_op jit(solution)/shard_map/ppermute | solution.py:94
  129.6 4.7 %collective-permute-done.10 = f32[72,384]{1,0:T(8,128)S(1)} collective-permute-done((f32[72,384]{1,0:T(8,128)S(1)}, f32[72,384]{1,0:T(8,128)S(1)}, u32[]{:S(2)}, u32[]{:S(2)}) %collective-permute-start.10) | collective-permute-done | bytes 110624 | tf_op jit(solution)/shard_map/ppermute | solution.py:94
  134.3 1.6 collective-permute-start.11
  136.0 9.8 %collective-permute-done.11 = f32[144,384]{1,0:T(8,128)S(1)} collective-permute-done((f32[144,384]{1,0:T(8,128)S(1)}, f32[144,384]{1,0:T(8,128)S(1)}, u32[]{:S(2)}, u32[]{:S(2)}) %collective-permute-start.11) | collective-permute-done | bytes 221216 | tf_op jit(solution)/shard_map/ppermute | solution.py:94
  145.9 3.2 %fusion.8 = bf16[1,512,1536]{2,1,0:T(8,128)(2,1)} fusion(f32[1,512,384]{2,1,0:T(8,128)} %fusion.31, f32[1,512,384]{2,1,0:T(8,128)} %fusion.29, f32[1,512,384]{2,1,0:T(8,128)S(1)} %copy-done.14, f32[1,512,384]{2,1,0:T(8,128)} %fusion.25, bf16[1,512,1536]{2,1,0:T(8,128)(2,1)S(1)} %copy-done.4, f32[512]{0:T(512)S(1)} %fusion.116), kind=kLoop, calls=%fused_computation.21 | loop fusion | flops 5505024 | bytes 6293504 | tf_op jit(solution)/shard_map/convert_element_type | solution.py:187
  150.3 27.6 %reduce-scatter.2.cloned.1.call-done = f32[96,1536]{1,0:T(8,128)} async-done(((f32[768,1536]{1,0:T(8,128)}), f32[96,1536]{1,0:T(8,128)}) %reduce-scatter.2.cloned.1.call-update) | async-done | bytes 589840 | tf_op jit(solution)/shard_map/reduce_scatter | solution.py:157
  177.9 1.9 %broadcast_multiply_fusion.1 = f32[96,1536]{1,0:T(8,128)} fusion(f32[96,1536]{1,0:T(8,128)} %reduce-scatter.2.cloned.1.call-done), kind=kLoop, calls=%fused_computation.168 | loop fusion | flops 147456 | bytes 1179648 | tf_op jit(solution)/shard_map/mul | solution.py:188
  (126 shorter events, 41.7 us)
Async XLA Ops:
  7.2 10.8 %copy-start.16 = (bf16[3,48,1536]{2,1,0:T(8,128)(2,1)S(1)}, bf16[3,48,1536]{2,1,0:T(8,128)(2,1)}, u32[]{:S(2)}) copy-start(bf16[3,48,1536]{2,1,0:T(8,128)(2,1)} %param.7) | copy-start | bytes 1327108
  7.2 170.7 %reduce-scatter.2.cloned.1.call-start = ((), (), s32[]{:S(2)}) async-start(), calls=%async_computation.1 | async-start | bytes 5308416 | tf_op jit(solution)/shard_map/reduce_scatter | solution.py:157
  10.4 13.6 %collective-permute-start = (bf16[1,64,1536]{2,1,0:T(8,128)(2,1)}, bf16[1,64,1536]{2,1,0:T(8,128)(2,1)}, u32[]{:S(2)}, u32[]{:S(2)}) collective-permute-start(bf16[1,64,1536]{2,1,0:T(8,128)(2,1)} %get-tuple-element.20), channel_id=1, source_target_pairs={{0,2},{2,4},{4,6},{6,8},{8,10},{10,12},{12,14},{1,3},{3,5},{5,7},{... | collective-permute-start | bytes 589832 | tf_op jit(solution)/shard_map/ppermute | solution.py:20
  15.9 8.3 %collective-permute-start.1 = (bf16[1,64,1536]{2,1,0:T(8,128)(2,1)S(1)}, bf16[1,64,1536]{2,1,0:T(8,128)(2,1)}, u32[]{:S(2)}, u32[]{:S(2)}) collective-permute-start(bf16[1,64,1536]{2,1,0:T(8,128)(2,1)S(1)} %get-tuple-element.21), channel_id=1, source_target_pairs={{2,0},{4,2},{6,4},{8,6},{10,8},{12,10},{14,12},{3,1},{5,3},{7,5},{... | collective-permute-start | bytes 589832 | tf_op jit(solution)/shard_map/ppermute | solution.py:22
  18.2 11.9 %copy-start = (bf16[3,384,1536]{2,1,0:T(8,128)(2,1)}, bf16[3,384,1536]{2,1,0:T(8,128)(2,1)S(1)}, u32[]{:S(2)}) copy-start(bf16[3,384,1536]{2,1,0:T(8,128)(2,1)S(1)} %bitcast_multiply_fusion) | copy-start | bytes 10616836
  36.9 28.8 %collective-permute-start.4 = (f32[768,1536]{1,0:T(8,128)}, f32[768,1536]{1,0:T(8,128)}, u32[]{:S(2)}, u32[]{:S(2)}) collective-permute-start(f32[768,1536]{1,0:T(8,128)} %fusion.15), channel_id=1, source_target_pairs={{0,1},{1,0},{2,3},{3,2},{4,5},{5,4},{6,7},{7,6},{8,9},{9,8},{10,11... | collective-permute-start | bytes 14155784 | tf_op jit(solution)/shard_map/ppermute | solution.py:94
  45.7 37.1 %collective-permute-start.2 = (bf16[1,64,1536]{1,2,0:T(8,128)(2,1)}, bf16[1,64,1536]{1,2,0:T(8,128)(2,1)}, u32[]{:S(2)}, u32[]{:S(2)}) collective-permute-start(bf16[1,64,1536]{1,2,0:T(8,128)(2,1)} %get-tuple-element.18), channel_id=1, source_target_pairs={{0,2},{2,4},{4,6},{6,8},{8,10},{10,12},{12,14},{1,3},{3,5},{5,7},{... | collective-permute-start | bytes 589832 | tf_op jit(solution)/shard_map/ppermute | solution.py:20
  50.5 32.3 %collective-permute-start.3 = (bf16[1,64,1536]{1,2,0:T(8,128)(2,1)}, bf16[1,64,1536]{1,2,0:T(8,128)(2,1)}, u32[]{:S(2)}, u32[]{:S(2)}) collective-permute-start(bf16[1,64,1536]{1,2,0:T(8,128)(2,1)} %get-tuple-element.19), channel_id=1, source_target_pairs={{2,0},{4,2},{6,4},{8,6},{10,8},{12,10},{14,12},{3,1},{5,3},{7,5},{... | collective-permute-start | bytes 589832 | tf_op jit(solution)/shard_map/ppermute | solution.py:22
  59.4 6.2 %copy-start.3 = (bf16[1,512,1536]{2,1,0:T(8,128)(2,1)S(1)}, bf16[1,512,1536]{2,1,0:T(8,128)(2,1)}, u32[]{:S(2)}) copy-start(bf16[1,512,1536]{2,1,0:T(8,128)(2,1)} %param.9) | copy-start | bytes 4718596
  59.4 6.2 %copy-start.5 = (bf16[512,8,1,96]{0,3,2,1:T(8,128)(2,1)S(1)}, bf16[512,8,1,96]{0,3,2,1:T(8,128)(2,1)}, u32[]{:S(2)}) copy-start(bf16[512,8,1,96]{0,3,2,1:T(8,128)(2,1)} %get-tuple-element.16) | copy-start | bytes 2359300
  71.9 4.1 %copy-start.7 = (f32[512,384]{0,1:T(8,128)S(1)}, f32[512,384]{0,1:T(8,128)}, u32[]{:S(2)}) copy-start(f32[512,384]{0,1:T(8,128)} %copy-done.6) | copy-start | bytes 2359300
  71.9 4.1 %copy-start.9 = (f32[512,384]{0,1:T(8,128)S(1)}, f32[512,384]{0,1:T(8,128)}, u32[]{:S(2)}) copy-start(f32[512,384]{0,1:T(8,128)} %copy-done.8) | copy-start | bytes 2359300
  71.9 4.1 %copy-start.11 = (f32[512,384]{0,1:T(8,128)S(1)}, f32[512,384]{0,1:T(8,128)}, u32[]{:S(2)}) copy-start(f32[512,384]{0,1:T(8,128)} %copy-done.10) | copy-start | bytes 2359300
  72.0 4.3 %copy-start.15 = (bf16[1,512,1536]{2,1,0:T(8,128)(2,1)S(1)}, bf16[1,512,1536]{2,1,0:T(8,128)(2,1)}, u32[]{:S(2)}) copy-start(bf16[1,512,1536]{2,1,0:T(8,128)(2,1)} %param.5) | copy-start | bytes 4718596
  82.5 7.5 %collective-permute-start.5 = (f32[144,768]{1,0:T(8,128)S(1)}, f32[144,768]{1,0:T(8,128)S(1)}, u32[]{:S(2)}, u32[]{:S(2)}) collective-permute-start(f32[144,768]{1,0:T(8,128)S(1)} %constant_dynamic-slice_fusion.3), channel_id=1, source_target_pairs={{0,1},{1,0},{2,3},{3,2},{4,5},{5,4},{6,7},{7,6},{8,9},{9,8},{10,11... | collective-permute-start | bytes 1327112 | tf_op jit(solution)/shard_map/ppermute | solution.py:94
  90.2 8.7 %collective-permute-start.6 = (f32[144,384]{1,0:T(8,128)S(1)}, f32[144,384]{1,0:T(8,128)S(1)}, u32[]{:S(2)}, u32[]{:S(2)}) collective-permute-start(f32[144,384]{1,0:T(8,128)S(1)} %constant_dynamic-slice_fusion.2), channel_id=1, source_target_pairs={{0,2},{2,0},{4,6},{6,4},{8,10},{10,8},{12,14},{14,12},{1,3},{3,1},... | collective-permute-start | bytes 663560 | tf_op jit(solution)/shard_map/ppermute | solution.py:94
  98.9 13.0 %collective-permute-start.7 = (f32[72,384]{1,0:T(8,128)S(1)}, f32[72,384]{1,0:T(8,128)S(1)}, u32[]{:S(2)}, u32[]{:S(2)}) collective-permute-start(f32[72,384]{1,0:T(8,128)S(1)} %constant_dynamic-slice_fusion.1), channel_id=1, source_target_pairs={{0,4},{2,6},{4,0},{6,2},{8,12},{10,14},{12,8},{14,10},{1,5},{3,7},... | collective-permute-start | bytes 331784 | tf_op jit(solution)/shard_map/ppermute | solution.py:94
  103.2 42.7 %copy-start.4 = (bf16[1,512,1536]{2,1,0:T(8,128)(2,1)S(1)}, bf16[1,512,1536]{2,1,0:T(8,128)(2,1)}, u32[]{:S(2)}) copy-start(bf16[1,512,1536]{2,1,0:T(8,128)(2,1)} %param.9) | copy-start | bytes 4718596
  112.0 10.0 %collective-permute-start.8 = (f32[36,384]{1,0:T(8,128)S(1)}, f32[36,384]{1,0:T(8,128)S(1)}, u32[]{:S(2)}, u32[]{:S(2)}) collective-permute-start(f32[36,384]{1,0:T(8,128)S(1)} %constant_dynamic-slice_fusion), channel_id=1, source_target_pairs={{0,8},{2,10},{4,12},{6,14},{8,0},{10,2},{12,4},{14,6},{1,9},{3,11}... | collective-permute-start | bytes 165896 | tf_op jit(solution)/shard_map/ppermute | solution.py:94
  114.8 31.1 %copy-start.14 = (f32[1,512,384]{2,1,0:T(8,128)S(1)}, f32[1,512,384]{2,1,0:T(8,128)}, u32[]{:S(2)}) copy-start(f32[1,512,384]{2,1,0:T(8,128)} %fusion.27) | copy-start | bytes 2359300
  122.0 7.1 %collective-permute-start.9 = (f32[36,384]{1,0:T(8,128)S(1)}, f32[36,384]{1,0:T(8,128)S(1)}, u32[]{:S(2)}, u32[]{:S(2)}) collective-permute-start(f32[36,384]{1,0:T(8,128)S(1)} %dynamic-slice_add_fusion.3), channel_id=1, source_target_pairs={{0,8},{2,10},{4,12},{6,14},{8,0},{10,2},{12,4},{14,6},{1,9},{3,11}... | collective-permute-start | bytes 165896 | tf_op jit(solution)/shard_map/ppermute | solution.py:94
  129.5 4.8 %collective-permute-start.10 = (f32[72,384]{1,0:T(8,128)S(1)}, f32[72,384]{1,0:T(8,128)S(1)}, u32[]{:S(2)}, u32[]{:S(2)}) collective-permute-start(f32[72,384]{1,0:T(8,128)S(1)} %dynamic_update_slice.25), channel_id=1, source_target_pairs={{0,4},{2,6},{4,0},{6,2},{8,12},{10,14},{12,8},{14,10},{1,5},{3,7},... | collective-permute-start | bytes 331784 | tf_op jit(solution)/shard_map/ppermute | solution.py:94
  134.3 11.4 %collective-permute-start.11 = (f32[144,384]{1,0:T(8,128)S(1)}, f32[144,384]{1,0:T(8,128)S(1)}, u32[]{:S(2)}, u32[]{:S(2)}) collective-permute-start(f32[144,384]{1,0:T(8,128)S(1)} %constant_dynamic-update-slice_fusion.4), channel_id=1, source_target_pairs={{0,2},{2,0},{4,6},{6,4},{8,10},{10,8},{12,14},{14,12},{1,3},{3,1},... | collective-permute-start | bytes 663560 | tf_op jit(solution)/shard_map/ppermute | solution.py:94
  145.8 3.4 %collective-permute-start.12 = (f32[144,768]{1,0:T(8,128)S(1)}, f32[144,768]{1,0:T(8,128)S(1)}, u32[]{:S(2)}, u32[]{:S(2)}) collective-permute-start(f32[144,768]{1,0:T(8,128)S(1)} %constant_dynamic-update-slice_fusion.2), channel_id=1, source_target_pairs={{0,1},{1,0},{2,3},{3,2},{4,5},{5,4},{6,7},{7,6},{8,9},{9,8},{10,11... | collective-permute-start | bytes 1327112 | tf_op jit(solution)/shard_map/ppermute | solution.py:94
  (8 other events, 14.3 us)
Sparse Core Ops, SparseCore 0:
  71.6 106.2 reduce-scatter.1

commit v6 on v5

--- a/solution.py
+++ b/solution.py
@@ -133,28 +133,11 @@
     return held.reshape(shape)
 
 
-def point_gradient(act_rows, cot_rows, seq_count, rep_count):
-    chans = act_rows.shape[1]
-    block = chans // (seq_count * rep_count)
-    blocks = act_rows.reshape(act_rows.shape[0], seq_count, rep_count, block)
-    rep_index = lax.axis_index("rep")
+def point_gradient(act_rows, cot_rows):
+    return lax.dot_general(
+        act_rows, cot_rows, (((0,), (0,)), ((), ())), preferred_element_type=jnp.float32
+    )
 
-    def rows_of(owner):
-        cols = lax.dynamic_index_in_dim(blocks, owner, axis=2, keepdims=False)
-        cols = cols.reshape(act_rows.shape[0], seq_count * block)
-        return lax.dot_general(
-            cols, cot_rows, (((0,), (0,)), ((), ())), preferred_element_type=jnp.float32
-        )
-
-    if rep_count == 2:
-        mine = rows_of(rep_index) + swap(rows_of(1 - rep_index), "rep", 1)
-    else:
-        full = lax.dot_general(
-            act_rows, cot_rows, (((0,), (0,)), ((), ())), preferred_element_type=jnp.float32
-        ).reshape(seq_count, rep_count, block, chans)
-        mine = lax.psum_scatter(full, "rep", scatter_dimension=1, tiled=True)
-        mine = mine.reshape(seq_count * block, chans)
-    return lax.psum_scatter(mine, "seq", scatter_dimension=0, tiled=True)
 
 def on_device(inputs, lengths, conv_weight, point_weight, cotangent):
     local_bins = inputs.shape[1]
@@ -176,6 +159,11 @@
     cot_rows = cotangent.reshape(local_bins, chans)
     proj = jnp.dot(act_rows, point_weight, preferred_element_type=jnp.float32).reshape(inputs.shape)
     output = (inputs.astype(jnp.float32) + proj).astype(jnp.bfloat16)
+    point_partial = point_gradient(act_rows, cot_rows)
+    point_partial, cot_rows = lax.optimization_barrier((point_partial, cot_rows))
+    grad_point = lax.psum_scatter(
+        point_partial, ("seq", "rep"), scatter_dimension=0, tiled=True
+    )
     back = lax.dot_general(
         cot_rows, point_weight, (((1,), (1,)), ((), ())), preferred_element_type=jnp.float32
     )
@@ -185,7 +173,7 @@
     conv_local = weight_taps(padded_input, preactivation_gradient, local_bins)
     grad_conv = tree_sum(conv_local) * scale
     grad_inputs = (cotangent.astype(jnp.float32) + mask3 * spread).astype(jnp.bfloat16)
-    grad_point = point_gradient(act_rows, cot_rows, seq_count, rep_count) * scale
+    grad_point = grad_point * scale
     return (output, grad_inputs, grad_point, grad_conv)
 
 

time: 187 us -> 163 us (0.87)
  matrix products: 51.3 us -> 32.5 us
  other arithmetic: 19 us -> 9.99 us
  starting transfers between devices: 22.1 us -> 27.2 us
    dot_general x12, matrix products: 14 us -> 4.96 us  [weight_taps(): lax.dot_general(window, grads[:, cols], (((0,), (0,)), ((), ())), preferr...]
    ppermute x9 -> x8, starting transfers between devices: 8.92 us -> 15.1 us  [swap(): return lax.ppermute(value, axis, [(i, i ^ distance) for i in range(count)])]
    reduce_scatter x1, waiting for transfers between devices: 27.6 us -> 22.8 us  [on_device(): lax.psum_scatter(point_partial, ('seq', 'rep'), scatter_dimension=0, tile...]
    ppermute x2, waiting for transfers between devices: 0.33 us -> 4.07 us  [with_halo(): lax.ppermute(head, axis, [((i + 1) % count, i) for i in range(ends)])]
    dot_general x24, matrix products: 15.1 us -> 11.5 us  [conv_taps(): lax.dot_general(window, dense[k, :, cols], dims, preferred_element_type=j...]
    dot_general x2 -> x1, matrix products: 9.34 us -> 5.78 us  [point_gradient(): lax.dot_general(act_rows, cot_rows, (((0,), (0,)), ((), ())), preferred_e...]
    reduce_sum x1, other arithmetic: 3.94 us -> 0.99 us  [weight_taps(): parts.append(jnp.sum(full * mask, axis=0))]
    dot_general x1, matrix products: 6.18 us -> 3.77 us  [on_device(): jnp.dot(act_rows, point_weight, preferred_element_type=jnp.float32)]
  transfers between devices with their start and end apart: 14 -> 13, of which waited for: 9 -> 10; matrix products, arithmetic and copies ran while one was open for 31% -> 18% of each run, Pallas kernels for 0% -> 0%
where the time goes in v6:
time: 163 us
  waiting for transfers between devices  73.4 us (45%)
  matrix products  32.5 us (20%)
  starting transfers between devices  27.2 us (17%)
  between operations  15.6 us (10%)
  other arithmetic  9.99 us (6%)
  local copies, waits for them, and re-layouts  4.4 us (3%)
    ppermute x8, waiting for transfers between devices, swap(): return lax.ppermute(value, axis, [(i, i ^ distance) for i in range(count)])  42.5 us
    reduce_scatter x1, waiting for transfers between devices, on_device(): lax.psum_scatter(point_partial, ('seq', 'rep'), scatter_dimension=0, tile...  22.8 us
    ppermute x8, starting transfers between devices, swap(): return lax.ppermute(value, axis, [(i, i ^ distance) for i in range(count)])  15.1 us
    dot_general x24, matrix products, conv_taps(): lax.dot_general(window, dense[k, :, cols], dims, preferred_element_type=j...  11.5 us
    ppermute x2, starting transfers between devices, with_halo(): lax.ppermute(tail, axis, [(i, (i + 1) % count) for i in range(ends)])  9.35 us
    dot_general x1, matrix products, on_device(): lax.dot_general(cot_rows, point_weight, (((1,), (1,)), ((), ())), preferr...  6.45 us
    dot_general x1, matrix products, point_gradient(): lax.dot_general(act_rows, cot_rows, (((0,), (0,)), ((), ())), preferred_e...  5.78 us
    dot_general x12, matrix products, weight_taps(): lax.dot_general(window, grads[:, cols], (((0,), (0,)), ((), ())), preferr...  4.96 us
  transfers between devices with their start and end apart: 13, of which 10 were waited for; matrix products, arithmetic and copies ran while one was open for 18% of the time, Pallas kernels for 0%

profile of v6, /device:TPU:0, one launch (start us, length us, event | category | flops | bytes accessed | tf_op | source)
XLA Modules:
  0.0 163.1 jit_solution(5285829355739857193)
XLA Ops:
  7.9 1.8 %fusion.1 = bf16[1,512,1536]{2,1,0:T(8,128)(2,1)S(1)} fusion(bf16[1,512,1536]{2,1,0:T(8,128)(2,1)} %param.5, f32[512]{0:T(512)S(1)} %fusion.117), kind=kLoop, calls=%fused_computation.11 | loop fusion | flops 2359296 | bytes 3147776 | tf_op jit(solution)/shard_map/convert_element_type | solution.py:151
  9.7 4.9 %collective-permute-start = (bf16[1,64,1536]{2,1,0:T(8,128)(2,1)S(1)}, bf16[1,64,1536]{2,1,0:T(8,128)(2,1)S(1)}, u32[]{:S(2)}, u32[]{:S(2)}) collective-permute-start(bf16[1,64,1536]{2,1,0:T(8,128)(2,1)S(1)} %get-tuple-element.22), channel_id=1, source_target_pairs={{0,2},{2,4},{4,6},{6,8},{8,10},{10,12},{12,14},{1,3},{3,5},{5,7},{... | collective-permute-start | bytes 589832 | tf_op jit(solution)/shard_map/ppermute | solution.py:20
  16.9 1.9 %collective-permute-done = bf16[1,64,1536]{2,1,0:T(8,128)(2,1)S(1)} collective-permute-done((bf16[1,64,1536]{2,1,0:T(8,128)(2,1)S(1)}, bf16[1,64,1536]{2,1,0:T(8,128)(2,1)S(1)}, u32[]{:S(2)}, u32[]{:S(2)}) %collective-permute-start) | collective-permute-done | bytes 196640 | tf_op jit(solution)/shard_map/ppermute | solution.py:20
  18.8 4.1 %collective-permute-done.1 = bf16[1,64,1536]{2,1,0:T(8,128)(2,1)S(1)} collective-permute-done((bf16[1,64,1536]{2,1,0:T(8,128)(2,1)S(1)}, bf16[1,64,1536]{2,1,0:T(8,128)(2,1)S(1)}, u32[]{:S(2)}, u32[]{:S(2)}) %collective-permute-start.1) | collective-permute-done | bytes 196640 | tf_op jit(solution)/shard_map/ppermute | solution.py:22
  29.6 5.8 %fusion.15 = f32[1536,1536]{1,0:T(8,128)} fusion(f32[1,512,1,1,1,1,384]{1,6,5,4,3,2,0:T(8,128)S(1)} %bitcast.120, f32[1,512,1,1,1,1,384]{1,6,5,4,3,2,0:T(8,128)S(1)} %bitcast.121, f32[1,512,1,1,1,1,384]{1,6,5,4,3,2,0:T(8,128)S(1)} %bitcast.122, f32[1,512,1,1,1,1,384]{1,6,5,4,3,2,0:T(8,128)S(1)} %bitcast.123, f32[512]{0:T(512)S(1)} %fusion.117, ...), kind=kOutput, calls=%fused_computation.33 | convolution fusion | flops 2422996992 | bytes 14157824 | tf_op jit(solution)/shard_map/dot_general | solution.py:137
  35.5 6.5 %fusion.9 = bf16[512,1536]{0,1:T(8,128)(2,1)S(1)} fusion(bf16[512,1536]{1,0:T(8,128)(2,1)S(1)} %bitcast.118, bf16[1536,1536]{1,0:T(8,128)(2,1)} %param.8, f32[512]{0:T(512)S(1)} %fusion.117, f32[512,384]{0,1:T(8,128)} %copy-done.5, f32[512,384]{0,1:T(8,128)} %copy-done.7, f32[512,384]{0,1:T(8,128)} %copy-done.9, f32[512,384]{0,1:T(8,128)} %copy-done.11), kind=kOutput, calls=%fused_computation.25 | convolution fusion | flops 2426929152 | bytes 11012096 | tf_op jit(solution)/shard_map/dot_general | solution.py:167
  42.2 4.5 %collective-permute-start.2 = (bf16[1,64,1536]{1,2,0:T(8,128)(2,1)S(1)}, bf16[1,64,1536]{1,2,0:T(8,128)(2,1)S(1)}, u32[]{:S(2)}, u32[]{:S(2)}) collective-permute-start(bf16[1,64,1536]{1,2,0:T(8,128)(2,1)S(1)} %get-tuple-element.20), channel_id=1, source_target_pairs={{0,2},{2,4},{4,6},{6,8},{8,10},{10,12},{12,14},{1,3},{3,5},{5,7},{... | collective-permute-start | bytes 589832 | tf_op jit(solution)/shard_map/ppermute | solution.py:20
  46.6 1.5 collective-permute-start.3
  56.1 3.8 %fusion.2 = bf16[1,512,1536]{2,1,0:T(8,128)(2,1)} fusion(bf16[1,512,1536]{2,1,0:T(8,128)(2,1)S(1)} %copy-done.2, bf16[1536,1536]{1,0:T(8,128)(2,1)S(1)} %bitcast.125, f32[512]{0:T(512)S(1)} %fusion.117, f32[512,384]{0,1:T(8,128)S(1)} %copy-done.6, f32[512,384]{0,1:T(8,128)S(1)} %copy-done.8, f32[512,384]{0,1:T(8,128)S(1)} %copy-done.10, ...), kind=kOutput, calls=%fused_computation.12 | convolution fusion | flops 2425356288 | bytes 11012096 | tf_op jit(solution)/shard_map/dot_general | solution.py:160
  60.1 2.1 %collective-permute-done.2 = bf16[1,64,1536]{1,2,0:T(8,128)(2,1)S(1)} collective-permute-done((bf16[1,64,1536]{1,2,0:T(8,128)(2,1)S(1)}, bf16[1,64,1536]{1,2,0:T(8,128)(2,1)S(1)}, u32[]{:S(2)}, u32[]{:S(2)}) %collective-permute-start.2) | collective-permute-done | bytes 196640 | tf_op jit(solution)/shard_map/ppermute | solution.py:20
  68.2 2.6 %collective-permute-start.5 = (f32[144,384]{1,0:T(8,128)S(1)}, f32[144,384]{1,0:T(8,128)S(1)}, u32[]{:S(2)}, u32[]{:S(2)}) collective-permute-start(f32[144,384]{1,0:T(8,128)S(1)} %constant_dynamic-slice_fusion.2), channel_id=1, source_target_pairs={{0,2},{2,0},{4,6},{6,4},{8,10},{10,8},{12,14},{14,12},{1,3},{3,1},... | collective-permute-start | bytes 663560 | tf_op jit(solution)/shard_map/ppermute | solution.py:94
  71.7 8.9 %collective-permute-done.5 = f32[144,384]{1,0:T(8,128)S(1)} collective-permute-done((f32[144,384]{1,0:T(8,128)S(1)}, f32[144,384]{1,0:T(8,128)S(1)}, u32[]{:S(2)}, u32[]{:S(2)}) %collective-permute-start.5) | collective-permute-done | bytes 221216 | tf_op jit(solution)/shard_map/ppermute | solution.py:94
  80.7 6.2 %collective-permute-start.6 = (f32[72,384]{1,0:T(8,128)S(1)}, f32[72,384]{1,0:T(8,128)S(1)}, u32[]{:S(2)}, u32[]{:S(2)}) collective-permute-start(f32[72,384]{1,0:T(8,128)S(1)} %constant_dynamic-slice_fusion.1), channel_id=1, source_target_pairs={{0,4},{2,6},{4,0},{6,2},{8,12},{10,14},{12,8},{14,10},{1,5},{3,7},... | collective-permute-start | bytes 331784 | tf_op jit(solution)/shard_map/ppermute | solution.py:94
  87.3 12.5 %collective-permute-done.6 = f32[72,384]{1,0:T(8,128)S(1)} collective-permute-done((f32[72,384]{1,0:T(8,128)S(1)}, f32[72,384]{1,0:T(8,128)S(1)}, u32[]{:S(2)}, u32[]{:S(2)}) %collective-permute-start.6) | collective-permute-done | bytes 110624 | tf_op jit(solution)/shard_map/ppermute | solution.py:94
  99.9 1.6 collective-permute-start.7
  102.0 7.6 %collective-permute-done.7 = f32[36,384]{1,0:T(8,128)S(1)} collective-permute-done((f32[36,384]{1,0:T(8,128)S(1)}, f32[36,384]{1,0:T(8,128)S(1)}, u32[]{:S(2)}, u32[]{:S(2)}) %collective-permute-start.7) | collective-permute-done | bytes 55328 | tf_op jit(solution)/shard_map/ppermute | solution.py:94
  110.2 5.6 %collective-permute-done.8 = f32[36,384]{1,0:T(8,128)S(1)} collective-permute-done((f32[36,384]{1,0:T(8,128)S(1)}, f32[36,384]{1,0:T(8,128)S(1)}, u32[]{:S(2)}, u32[]{:S(2)}) %collective-permute-start.8) | collective-permute-done | bytes 55328 | tf_op jit(solution)/shard_map/ppermute | solution.py:94
  116.2 1.9 %collective-permute-start.9 = (f32[72,384]{1,0:T(8,128)S(1)}, f32[72,384]{1,0:T(8,128)S(1)}, u32[]{:S(2)}, u32[]{:S(2)}) collective-permute-start(f32[72,384]{1,0:T(8,128)S(1)} %dynamic_update_slice.25), channel_id=1, source_target_pairs={{0,4},{2,6},{4,0},{6,2},{8,12},{10,14},{12,8},{14,10},{1,5},{3,7},... | collective-permute-start | bytes 331784 | tf_op jit(solution)/shard_map/ppermute | solution.py:94
  118.1 3.1 %collective-permute-done.9 = f32[72,384]{1,0:T(8,128)S(1)} collective-permute-done((f32[72,384]{1,0:T(8,128)S(1)}, f32[72,384]{1,0:T(8,128)S(1)}, u32[]{:S(2)}, u32[]{:S(2)}) %collective-permute-start.9) | collective-permute-done | bytes 110624 | tf_op jit(solution)/shard_map/ppermute | solution.py:94
  121.2 2.6 %collective-permute-start.10 = (f32[144,384]{1,0:T(8,128)S(1)}, f32[144,384]{1,0:T(8,128)S(1)}, u32[]{:S(2)}, u32[]{:S(2)}) collective-permute-start(f32[144,384]{1,0:T(8,128)S(1)} %constant_dynamic-update-slice_fusion.4), channel_id=1, source_target_pairs={{0,2},{2,0},{4,6},{6,4},{8,10},{10,8},{12,14},{14,12},{1,3},{3,1},... | collective-permute-start | bytes 663560 | tf_op jit(solution)/shard_map/ppermute | solution.py:94
  123.9 4.7 %collective-permute-done.10 = f32[144,384]{1,0:T(8,128)S(1)} collective-permute-done((f32[144,384]{1,0:T(8,128)S(1)}, f32[144,384]{1,0:T(8,128)S(1)}, u32[]{:S(2)}, u32[]{:S(2)}) %collective-permute-start.10) | collective-permute-done | bytes 221216 | tf_op jit(solution)/shard_map/ppermute | solution.py:94
  128.7 1.6 fusion.8
  131.5 22.8 %reduce-scatter.2.cloned.1.call-done = f32[96,1536]{1,0:T(8,128)} async-done(((f32[1536,1536]{1,0:T(8,128)}), f32[96,1536]{1,0:T(8,128)}) %reduce-scatter.2.cloned.1.call-update) | async-done | bytes 589840 | tf_op jit(solution)/shard_map/reduce_scatter | solution.py:164
  154.3 1.9 %broadcast_multiply_fusion.1 = f32[96,1536]{1,0:T(8,128)} fusion(f32[96,1536]{1,0:T(8,128)} %reduce-scatter.2.cloned.1.call-done), kind=kLoop, calls=%fused_computation.168 | loop fusion | flops 147456 | bytes 1179648 | tf_op jit(solution)/shard_map/mul | solution.py:176
  (117 shorter events, 27.1 us)
Async XLA Ops:
  7.2 147.2 %reduce-scatter.2.cloned.1.call-start = ((), (), s32[]{:S(2)}) async-start(), calls=%async_computation.1 | async-start | bytes 10027008 | tf_op jit(solution)/shard_map/reduce_scatter | solution.py:164
  7.9 8.7 %copy-start.13 = (bf16[3,48,1536]{2,1,0:T(8,128)(2,1)S(1)}, bf16[3,48,1536]{2,1,0:T(8,128)(2,1)}, u32[]{:S(2)}) copy-start(bf16[3,48,1536]{2,1,0:T(8,128)(2,1)} %param.7) | copy-start | bytes 1327108
  9.7 9.1 %collective-permute-start = (bf16[1,64,1536]{2,1,0:T(8,128)(2,1)S(1)}, bf16[1,64,1536]{2,1,0:T(8,128)(2,1)S(1)}, u32[]{:S(2)}, u32[]{:S(2)}) collective-permute-start(bf16[1,64,1536]{2,1,0:T(8,128)(2,1)S(1)} %get-tuple-element.22), channel_id=1, source_target_pairs={{0,2},{2,4},{4,6},{6,8},{8,10},{10,12},{12,14},{1,3},{3,5},{5,7},{... | collective-permute-start | bytes 589832 | tf_op jit(solution)/shard_map/ppermute | solution.py:20
  14.6 8.3 %collective-permute-start.1 = (bf16[1,64,1536]{2,1,0:T(8,128)(2,1)S(1)}, bf16[1,64,1536]{2,1,0:T(8,128)(2,1)S(1)}, u32[]{:S(2)}, u32[]{:S(2)}) collective-permute-start(bf16[1,64,1536]{2,1,0:T(8,128)(2,1)S(1)} %get-tuple-element.23), channel_id=1, source_target_pairs={{2,0},{4,2},{6,4},{8,6},{10,8},{12,10},{14,12},{3,1},{5,3},{7,5},{... | collective-permute-start | bytes 589832 | tf_op jit(solution)/shard_map/ppermute | solution.py:22
  16.9 10.8 %copy-start = (bf16[3,384,1536]{2,1,0:T(8,128)(2,1)}, bf16[3,384,1536]{2,1,0:T(8,128)(2,1)S(1)}, u32[]{:S(2)}) copy-start(bf16[3,384,1536]{2,1,0:T(8,128)(2,1)S(1)} %bitcast_multiply_fusion) | copy-start | bytes 10616836
  27.3 2.3 %copy-start.3 = (bf16[1,512,1536]{2,1,0:T(8,128)(2,1)S(1)}, bf16[1,512,1536]{2,1,0:T(8,128)(2,1)}, u32[]{:S(2)}) copy-start(bf16[1,512,1536]{2,1,0:T(8,128)(2,1)} %param.9) | copy-start | bytes 4718596
  42.2 20.0 %collective-permute-start.2 = (bf16[1,64,1536]{1,2,0:T(8,128)(2,1)S(1)}, bf16[1,64,1536]{1,2,0:T(8,128)(2,1)S(1)}, u32[]{:S(2)}, u32[]{:S(2)}) collective-permute-start(bf16[1,64,1536]{1,2,0:T(8,128)(2,1)S(1)} %get-tuple-element.20), channel_id=1, source_target_pairs={{0,2},{2,4},{4,6},{6,8},{8,10},{10,12},{12,14},{1,3},{3,5},{5,7},{... | collective-permute-start | bytes 589832 | tf_op jit(solution)/shard_map/ppermute | solution.py:20
  46.6 15.5 %collective-permute-start.3 = (bf16[1,64,1536]{1,2,0:T(8,128)(2,1)S(1)}, bf16[1,64,1536]{1,2,0:T(8,128)(2,1)S(1)}, u32[]{:S(2)}, u32[]{:S(2)}) collective-permute-start(bf16[1,64,1536]{1,2,0:T(8,128)(2,1)S(1)} %get-tuple-element.21), channel_id=1, source_target_pairs={{2,0},{4,2},{6,4},{8,6},{10,8},{12,10},{14,12},{3,1},{5,3},{7,5},{... | collective-permute-start | bytes 589832 | tf_op jit(solution)/shard_map/ppermute | solution.py:22
  49.0 5.4 %slice-start = ((s8[4718592]{0:T(1024)(128)(4,1)}), s8[4194304]{0:T(1024)(128)(4,1)S(1)}, s32[]{:S(2)}) async-start(s8[4718592]{0:T(1024)(128)(4,1)} %bitcast.124), calls=%async_computation.2 | async-start | bytes 8388608
  52.4 2.0 %slice-start.1 = ((s8[4718592]{0:T(1024)(128)(4,1)}), s8[524288]{0:T(1024)(128)(4,1)S(1)}, s32[]{:S(2)}) async-start(s8[4718592]{0:T(1024)(128)(4,1)} %bitcast.124), calls=%async_computation.3 | async-start | bytes 1048576
  53.2 1.9 %copy-start.6 = (f32[512,384]{0,1:T(8,128)S(1)}, f32[512,384]{0,1:T(8,128)}, u32[]{:S(2)}) copy-start(f32[512,384]{0,1:T(8,128)} %copy-done.5) | copy-start | bytes 2359300
  53.2 2.2 %copy-start.8 = (f32[512,384]{0,1:T(8,128)S(1)}, f32[512,384]{0,1:T(8,128)}, u32[]{:S(2)}) copy-start(f32[512,384]{0,1:T(8,128)} %copy-done.7) | copy-start | bytes 2359300
  53.2 2.5 %copy-start.10 = (f32[512,384]{0,1:T(8,128)S(1)}, f32[512,384]{0,1:T(8,128)}, u32[]{:S(2)}) copy-start(f32[512,384]{0,1:T(8,128)} %copy-done.9) | copy-start | bytes 2359300
  53.3 2.8 %copy-start.12 = (f32[512,384]{0,1:T(8,128)S(1)}, f32[512,384]{0,1:T(8,128)}, u32[]{:S(2)}) copy-start(f32[512,384]{0,1:T(8,128)} %copy-done.11) | copy-start | bytes 2359300
  60.0 3.4 %copy-start.1 = (bf16[3,384,1536]{2,1,0:T(8,128)(2,1)S(1)}, bf16[3,384,1536]{2,1,0:T(8,128)(2,1)}, u32[]{:S(2)}) copy-start(bf16[3,384,1536]{2,1,0:T(8,128)(2,1)} %copy-done) | copy-start | bytes 10616836
  60.0 8.1 %collective-permute-start.4 = (f32[144,768]{1,0:T(8,128)S(1)}, f32[144,768]{1,0:T(8,128)S(1)}, u32[]{:S(2)}, u32[]{:S(2)}) collective-permute-start(f32[144,768]{1,0:T(8,128)S(1)} %constant_dynamic-slice_fusion.3), channel_id=1, source_target_pairs={{0,1},{1,0},{2,3},{3,2},{4,5},{5,4},{6,7},{7,6},{8,9},{9,8},{10,11... | collective-permute-start | bytes 1327112 | tf_op jit(solution)/shard_map/ppermute | solution.py:94
  68.2 12.4 %collective-permute-start.5 = (f32[144,384]{1,0:T(8,128)S(1)}, f32[144,384]{1,0:T(8,128)S(1)}, u32[]{:S(2)}, u32[]{:S(2)}) collective-permute-start(f32[144,384]{1,0:T(8,128)S(1)} %constant_dynamic-slice_fusion.2), channel_id=1, source_target_pairs={{0,2},{2,0},{4,6},{6,4},{8,10},{10,8},{12,14},{14,12},{1,3},{3,1},... | collective-permute-start | bytes 663560 | tf_op jit(solution)/shard_map/ppermute | solution.py:94
  80.7 19.2 %collective-permute-start.6 = (f32[72,384]{1,0:T(8,128)S(1)}, f32[72,384]{1,0:T(8,128)S(1)}, u32[]{:S(2)}, u32[]{:S(2)}) collective-permute-start(f32[72,384]{1,0:T(8,128)S(1)} %constant_dynamic-slice_fusion.1), channel_id=1, source_target_pairs={{0,4},{2,6},{4,0},{6,2},{8,12},{10,14},{12,8},{14,10},{1,5},{3,7},... | collective-permute-start | bytes 331784 | tf_op jit(solution)/shard_map/ppermute | solution.py:94
  99.9 9.7 %collective-permute-start.7 = (f32[36,384]{1,0:T(8,128)S(1)}, f32[36,384]{1,0:T(8,128)S(1)}, u32[]{:S(2)}, u32[]{:S(2)}) collective-permute-start(f32[36,384]{1,0:T(8,128)S(1)} %constant_dynamic-slice_fusion), channel_id=1, source_target_pairs={{0,8},{2,10},{4,12},{6,14},{8,0},{10,2},{12,4},{14,6},{1,9},{3,11}... | collective-permute-start | bytes 165896 | tf_op jit(solution)/shard_map/ppermute | solution.py:94
  109.6 6.2 %collective-permute-start.8 = (f32[36,384]{1,0:T(8,128)S(1)}, f32[36,384]{1,0:T(8,128)S(1)}, u32[]{:S(2)}, u32[]{:S(2)}) collective-permute-start(f32[36,384]{1,0:T(8,128)S(1)} %dynamic-slice_add_fusion.3), channel_id=1, source_target_pairs={{0,8},{2,10},{4,12},{6,14},{8,0},{10,2},{12,4},{14,6},{1,9},{3,11}... | collective-permute-start | bytes 165896 | tf_op jit(solution)/shard_map/ppermute | solution.py:94
  116.2 12.5 %copy-start.4 = (bf16[1,512,1536]{2,1,0:T(8,128)(2,1)S(1)}, bf16[1,512,1536]{2,1,0:T(8,128)(2,1)}, u32[]{:S(2)}) copy-start(bf16[1,512,1536]{2,1,0:T(8,128)(2,1)} %param.9) | copy-start | bytes 4718596
  116.2 5.0 %collective-permute-start.9 = (f32[72,384]{1,0:T(8,128)S(1)}, f32[72,384]{1,0:T(8,128)S(1)}, u32[]{:S(2)}, u32[]{:S(2)}) collective-permute-start(f32[72,384]{1,0:T(8,128)S(1)} %dynamic_update_slice.25), channel_id=1, source_target_pairs={{0,4},{2,6},{4,0},{6,2},{8,12},{10,14},{12,8},{14,10},{1,5},{3,7},... | collective-permute-start | bytes 331784 | tf_op jit(solution)/shard_map/ppermute | solution.py:94
  121.2 7.3 %collective-permute-start.10 = (f32[144,384]{1,0:T(8,128)S(1)}, f32[144,384]{1,0:T(8,128)S(1)}, u32[]{:S(2)}, u32[]{:S(2)}) collective-permute-start(f32[144,384]{1,0:T(8,128)S(1)} %constant_dynamic-update-slice_fusion.4), channel_id=1, source_target_pairs={{0,2},{2,0},{4,6},{6,4},{8,10},{10,8},{12,14},{14,12},{1,3},{3,1},... | collective-permute-start | bytes 663560 | tf_op jit(solution)/shard_map/ppermute | solution.py:94
  128.6 1.9 %collective-permute-start.11 = (f32[144,768]{1,0:T(8,128)S(1)}, f32[144,768]{1,0:T(8,128)S(1)}, u32[]{:S(2)}, u32[]{:S(2)}) collective-permute-start(f32[144,768]{1,0:T(8,128)S(1)} %constant_dynamic-update-slice_fusion.2), channel_id=1, source_target_pairs={{0,1},{1,0},{2,3},{3,2},{4,5},{5,4},{6,7},{7,6},{8,9},{9,8},{10,11... | collective-permute-start | bytes 1327112 | tf_op jit(solution)/shard_map/ppermute | solution.py:94
  (5 other events, 5.8 us)
Sparse Core Ops, SparseCore 0:
  35.5 118.7 reduce-scatter.1

commit v7 on v5

--- a/solution.py
+++ b/solution.py
@@ -1,3 +1,4 @@
+import functools
 import math
 
 import jax
@@ -133,30 +134,80 @@
     return held.reshape(shape)
 
 
-def point_gradient(act_rows, cot_rows, seq_count, rep_count):
+def ring_order(mesh):
+    count = mesh.shape["seq"]
+    names = mesh.axis_names
+    index = [0] * len(names)
+    cells = []
+    for s in range(count):
+        index[names.index("seq")] = s
+        device = mesh.devices[tuple(index)]
+        coords = getattr(device, "coords", None)
+        if coords is None:
+            return list(range(count))
+        cells.append((tuple(coords), s))
+    cells.sort(key=lambda cell: (cell[0][1], cell[0][2] if cell[0][1] % 2 == 0 else -cell[0][2]))
+    return [s for _, s in cells]
+
+
+def ring_reduce_scatter(blocks, ring):
+    count = blocks.shape[0]
+    if count == 1:
+        return blocks[0]
+    position = [0] * count
+    for p, s in enumerate(ring):
+        position[s] = p
+    ring_table = jnp.array(ring, jnp.int32)
+    here = jnp.array(position, jnp.int32)[lax.axis_index("seq")]
+    half = blocks.shape[2] // 2
+    forward = [(ring[i], ring[(i + 1) % count]) for i in range(count)]
+    backward = [(ring[i], ring[(i - 1) % count]) for i in range(count)]
+
+    def block(offset, low):
+        owner = ring_table[(here + offset) % count]
+        rows = lax.dynamic_index_in_dim(blocks, owner, axis=0, keepdims=False)
+        return rows[:, :half] if low else rows[:, half:]
+
+    ahead = block(-1, True)
+    behind = block(1, False)
+    for step in range(count - 1):
+        ahead = lax.ppermute(ahead, "seq", forward) + block(-2 - step, True)
+        behind = lax.ppermute(behind, "seq", backward) + block(2 + step, False)
+    return jnp.concatenate([ahead, behind], axis=1)
+
+
+def point_gradient(act_rows, cot_rows, ring):
     chans = act_rows.shape[1]
+    seq_count = lax.axis_size("seq")
+    rep_count = lax.axis_size("rep")
     block = chans // (seq_count * rep_count)
+    split = chans // 2
+    product = lambda a, b: lax.dot_general(
+        a, b, (((0,), (0,)), ((), ())), preferred_element_type=jnp.float32
+    )
+    offload = product(act_rows, cot_rows[:, :split])
+    offload, cot_rows = lax.optimization_barrier((offload, cot_rows))
+    first = lax.psum_scatter(offload, ("seq", "rep"), scatter_dimension=0, tiled=True)
+    if rep_count != 2:
+        rest = lax.psum_scatter(
+            product(act_rows, cot_rows[:, split:]), ("seq", "rep"),
+            scatter_dimension=0, tiled=True,
+        )
+        return jnp.concatenate([first, rest], axis=1), cot_rows
     blocks = act_rows.reshape(act_rows.shape[0], seq_count, rep_count, block)
     rep_index = lax.axis_index("rep")
 
     def rows_of(owner):
         cols = lax.dynamic_index_in_dim(blocks, owner, axis=2, keepdims=False)
         cols = cols.reshape(act_rows.shape[0], seq_count * block)
-        return lax.dot_general(
-            cols, cot_rows, (((0,), (0,)), ((), ())), preferred_element_type=jnp.float32
-        )
-
-    if rep_count == 2:
-        mine = rows_of(rep_index) + swap(rows_of(1 - rep_index), "rep", 1)
-    else:
-        full = lax.dot_general(
-            act_rows, cot_rows, (((0,), (0,)), ((), ())), preferred_element_type=jnp.float32
-        ).reshape(seq_count, rep_count, block, chans)
-        mine = lax.psum_scatter(full, "rep", scatter_dimension=1, tiled=True)
-        mine = mine.reshape(seq_count * block, chans)
-    return lax.psum_scatter(mine, "seq", scatter_dimension=0, tiled=True)
-
-def on_device(inputs, lengths, conv_weight, point_weight, cotangent):
+        return product(cols, cot_rows[:, split:]).reshape(seq_count, block, chans - split)
+
+    mine = rows_of(rep_index) + swap(rows_of(1 - rep_index), "rep", 1)
+    rest = ring_reduce_scatter(mine, ring)
+    return jnp.concatenate([first, rest], axis=1), cot_rows
+
+
+def on_device(ring, inputs, lengths, conv_weight, point_weight, cotangent):
     local_bins = inputs.shape[1]
     chans = inputs.shape[2]
     seq_count = lax.axis_size("seq")
@@ -176,6 +227,7 @@
     cot_rows = cotangent.reshape(local_bins, chans)
     proj = jnp.dot(act_rows, point_weight, preferred_element_type=jnp.float32).reshape(inputs.shape)
     output = (inputs.astype(jnp.float32) + proj).astype(jnp.bfloat16)
+    grad_point, cot_rows = point_gradient(act_rows, cot_rows, ring)
     back = lax.dot_general(
         cot_rows, point_weight, (((1,), (1,)), ((), ())), preferred_element_type=jnp.float32
     )
@@ -185,13 +237,13 @@
     conv_local = weight_taps(padded_input, preactivation_gradient, local_bins)
     grad_conv = tree_sum(conv_local) * scale
     grad_inputs = (cotangent.astype(jnp.float32) + mask3 * spread).astype(jnp.bfloat16)
-    grad_point = point_gradient(act_rows, cot_rows, seq_count, rep_count) * scale
+    grad_point = grad_point * scale
     return (output, grad_inputs, grad_point, grad_conv)
 
 
 def solution(mesh):
     return jax.shard_map(
-        on_device,
+        functools.partial(on_device, ring_order(mesh)),
         mesh=mesh,
         in_specs=(
             P(("groups", "rep"), "seq", None),

time: 187 us -> 242 us (1.29)
  between operations: 15.4 us -> 56 us
  starting transfers between devices: 22.1 us -> 39.8 us
  waiting for transfers between devices: 74.2 us -> 68.4 us
  local copies, waits for them, and re-layouts: 4.69 us -> 9.24 us
    reduce_scatter x1, waiting for transfers between devices: 27.6 us -> 0.02 us  [point_gradient(): lax.psum_scatter(offload, ('seq', 'rep'), scatter_dimension=0, tiled=True)]
    ppermute x0 -> x14, waiting for transfers between devices: none -> 26.3 us  [the longest x7 21.7 us: ring_reduce_scatter(): ahead = lax.ppermute(ahead, 'seq', forward) + block(-2 - step, True)]
    ppermute x0 -> x14, starting transfers between devices: none -> 14.7 us  [the longest x7 10.8 us: ring_reduce_scatter(): ahead = lax.ppermute(ahead, 'seq', forward) + block(-2 - step, True)]
    ppermute x9, waiting for transfers between devices: 40.6 us -> 30.3 us  [swap(): return lax.ppermute(value, axis, [(i, i ^ distance) for i in range(count)])]
    ppermute x2, waiting for transfers between devices: 5.7 us -> 11.8 us  [with_halo(): lax.ppermute(tail, axis, [(i, (i + 1) % count) for i in range(ends)])]
    unnamed x36 -> x58, local copies, waits for them, and re-layouts: 0.87 us -> 6.06 us
    ppermute x9, starting transfers between devices: 8.92 us -> 12.8 us  [swap(): return lax.ppermute(value, axis, [(i, i ^ distance) for i in range(count)])]
    dot_general x2 -> x3, matrix products: 9.34 us -> 8.32 us  [point_gradient(): lax.dot_general(a, b, (((0,), (0,)), ((), ())), preferred_element_type=jn...]
  transfers between devices with their start and end apart: 14 -> 28, of which waited for: 9 -> 20; matrix products, arithmetic and copies ran while one was open for 31% -> 13% of each run, Pallas kernels for 0% -> 0%
where the time goes in v7:
time: 242 us; the launch traced here: 241 us
  waiting for transfers between devices  68.4 us (28%)
  between operations  56 us (23%)
  matrix products  49 us (20%)
  starting transfers between devices  39.8 us (16%)
  other arithmetic  18.8 us (8%)
  local copies, waits for them, and re-layouts  9.24 us (4%)
    ppermute x9, waiting for transfers between devices, swap(): return lax.ppermute(value, axis, [(i, i ^ distance) for i in range(count)])  30.3 us
    ppermute x7, waiting for transfers between devices, ring_reduce_scatter(): ahead = lax.ppermute(ahead, 'seq', forward) + block(-2 - step, True)  21.7 us
    dot_general x24, matrix products, conv_taps(): lax.dot_general(window, dense[k, :, cols], dims, preferred_element_type=j...  15.1 us
    dot_general x12, matrix products, weight_taps(): lax.dot_general(window, grads[:, cols], (((0,), (0,)), ((), ())), preferr...  14.9 us
    ppermute x9, starting transfers between devices, swap(): return lax.ppermute(value, axis, [(i, i ^ distance) for i in range(count)])  12.8 us
    ppermute x2, waiting for transfers between devices, with_halo(): lax.ppermute(tail, axis, [(i, (i + 1) % count) for i in range(ends)])  11.8 us
    ppermute x7, starting transfers between devices, ring_reduce_scatter(): ahead = lax.ppermute(ahead, 'seq', forward) + block(-2 - step, True)  10.8 us
    ppermute x2, starting transfers between devices, with_halo(): lax.ppermute(tail, axis, [(i, (i + 1) % count) for i in range(ends)])  9.6 us
  transfers between devices with their start and end apart: 28, of which 20 were waited for; matrix products, arithmetic and copies ran while one was open for 13% of the time, Pallas kernels for 0%

profile of v7, /device:TPU:0, one launch (start us, length us, event | category | flops | bytes accessed | tf_op | source)
XLA Modules:
  0.0 241.2 jit_solution(3213995918455359716)
XLA Ops:
  9.7 4.9 %collective-permute-start = (bf16[1,64,1536]{2,1,0:T(8,128)(2,1)S(1)}, bf16[1,64,1536]{2,1,0:T(8,128)(2,1)S(1)}, u32[]{:S(2)}, u32[]{:S(2)}) collective-permute-start(bf16[1,64,1536]{2,1,0:T(8,128)(2,1)S(1)} %get-tuple-element.38), channel_id=1, source_target_pairs={{0,2},{2,4},{4,6},{6,8},{8,10},{10,12},{12,14},{1,3},{3,5},{5,7},{... | collective-permute-start | bytes 589832 | tf_op jit(solution)/shard_map/ppermute | solution.py:21
  70.3 3.8 %fusion.2 = bf16[1,512,1536]{2,1,0:T(8,128)(2,1)} fusion(bf16[1,512,1536]{2,1,0:T(8,128)(2,1)S(1)} %copy-done.18, bf16[512,1536]{0,1:T(8,128)(2,1)S(1)} %multiply_convert_fusion.1, bf16[1536,1536]{1,0:T(8,128)(2,1)S(1)} %bitcast.210), kind=kOutput, calls=%fused_computation.12 | convolution fusion | flops 2418278400 | bytes 9437184 | tf_op jit(solution)/shard_map/dot_general | solution.py:228
  74.1 3.6 %fusion.27 = f32[1536,768]{1,0:T(8,128)} fusion(bf16[512,1536]{0,1:T(8,128)(2,1)S(1)} %multiply_convert_fusion.1, bf16[512,1536]{1,0:T(8,128)(2,1)S(1)} %bitcast.187), kind=kOutput, calls=%fused_computation.56 | convolution fusion | flops 1207959552 | bytes 7077888 | tf_op jit(solution)/shard_map/dot_general | solution.py:185
  77.7 6.8 %fusion.9 = bf16[512,1536]{0,1:T(8,128)(2,1)S(1)} fusion(bf16[512,1536]{1,0:T(8,128)(2,1)} %bitcast.186, bf16[1536,1536]{1,0:T(8,128)(2,1)} %param.10, f32[512]{0:T(512)S(1)} %fusion.124, f32[512,384]{0,1:T(8,128)} %copy-done.4, f32[512,384]{0,1:T(8,128)} %copy-done.6, f32[512,384]{0,1:T(8,128)} %copy-done.8, f32[512,384]{0,1:T(8,128)} %copy-done.10), kind=kOutput, calls=%fused_computation.25 | convolution fusion | flops 2426929152 | bytes 11012096 | tf_op jit(solution)/shard_map/dot_general | solution.py:231
  101.0 3.4 %select_reduce_fusion.11 = (f32[48,384]{1,0:T(8,128)S(1)}, f32[48,384]{1,0:T(8,128)S(1)}, f32[48,384]{1,0:T(8,128)S(1)}, f32[48,384]{1,0:T(8,128)S(1)}, f32[48,3...) fusion(f32[8,48,384]{2,1,0:T(8,128)} %bitcast.207, ...), kind=kLoop, calls=%fused_computation.79 | loop fusion | flops 3760128 | bytes 7969536 | tf_op jit(solution)/shard_map/reduce_sum | solution.py:88
  104.9 4.7 %collective-permute-start.2 = (bf16[1,64,1536]{1,2,0:T(8,128)(2,1)S(1)}, bf16[1,64,1536]{1,2,0:T(8,128)(2,1)S(1)}, u32[]{:S(2)}, u32[]{:S(2)}) collective-permute-start(bf16[1,64,1536]{1,2,0:T(8,128)(2,1)S(1)} %get-tuple-element.36), channel_id=1, source_target_pairs={{0,2},{2,4},{4,6},{6,8},{8,10},{10,12},{12,14},{1,3},{3,5},{5,7},{... | collective-permute-start | bytes 589832 | tf_op jit(solution)/shard_map/ppermute | solution.py:21
  115.1 11.8 %collective-permute-done.2 = bf16[1,64,1536]{1,2,0:T(8,128)(2,1)S(1)} collective-permute-done((bf16[1,64,1536]{1,2,0:T(8,128)(2,1)S(1)}, bf16[1,64,1536]{1,2,0:T(8,128)(2,1)S(1)}, u32[]{:S(2)}, u32[]{:S(2)}) %collective-permute-start.2) | collective-permute-done | bytes 196640 | tf_op jit(solution)/shard_map/ppermute | solution.py:21
  132.9 2.6 %collective-permute-start.20 = (f32[144,384]{1,0:T(8,128)S(1)}, f32[144,384]{1,0:T(8,128)S(1)}, u32[]{:S(2)}, u32[]{:S(2)}) collective-permute-start(f32[144,384]{1,0:T(8,128)S(1)} %constant_dynamic-slice_fusion.2), channel_id=1, source_target_pairs={{0,2},{2,0},{4,6},{6,4},{8,10},{10,8},{12,14},{14,12},{1,3},{3,1},... | collective-permute-start | bytes 663560 | tf_op jit(solution)/shard_map/ppermute | solution.py:95
  138.2 7.1 %collective-permute-done.20 = f32[144,384]{1,0:T(8,128)S(1)} collective-permute-done((f32[144,384]{1,0:T(8,128)S(1)}, f32[144,384]{1,0:T(8,128)S(1)}, u32[]{:S(2)}, u32[]{:S(2)}) %collective-permute-start.20) | collective-permute-done | bytes 221216 | tf_op jit(solution)/shard_map/ppermute | solution.py:95
  145.4 4.6 %collective-permute-start.21 = (f32[72,384]{1,0:T(8,128)S(1)}, f32[72,384]{1,0:T(8,128)S(1)}, u32[]{:S(2)}, u32[]{:S(2)}) collective-permute-start(f32[72,384]{1,0:T(8,128)S(1)} %constant_dynamic-slice_fusion.1), channel_id=1, source_target_pairs={{0,4},{2,6},{4,0},{6,2},{8,12},{10,14},{12,8},{14,10},{1,5},{3,7},... | collective-permute-start | bytes 331784 | tf_op jit(solution)/shard_map/ppermute | solution.py:95
  151.4 2.5 %collective-permute-done.21 = f32[72,384]{1,0:T(8,128)S(1)} collective-permute-done((f32[72,384]{1,0:T(8,128)S(1)}, f32[72,384]{1,0:T(8,128)S(1)}, u32[]{:S(2)}, u32[]{:S(2)}) %collective-permute-start.21) | collective-permute-done | bytes 110624 | tf_op jit(solution)/shard_map/ppermute | solution.py:95
  154.0 2.9 %collective-permute-start.22 = (f32[36,384]{1,0:T(8,128)S(1)}, f32[36,384]{1,0:T(8,128)S(1)}, u32[]{:S(2)}, u32[]{:S(2)}) collective-permute-start(f32[36,384]{1,0:T(8,128)S(1)} %constant_dynamic-slice_fusion), channel_id=1, source_target_pairs={{0,8},{2,10},{4,12},{6,14},{8,0},{10,2},{12,4},{14,6},{1,9},{3,11}... | collective-permute-start | bytes 165896 | tf_op jit(solution)/shard_map/ppermute | solution.py:95
  158.2 5.0 %collective-permute-done.22 = f32[36,384]{1,0:T(8,128)S(1)} collective-permute-done((f32[36,384]{1,0:T(8,128)S(1)}, f32[36,384]{1,0:T(8,128)S(1)}, u32[]{:S(2)}, u32[]{:S(2)}) %collective-permute-start.22) | collective-permute-done | bytes 55328 | tf_op jit(solution)/shard_map/ppermute | solution.py:95
  164.1 5.8 %collective-permute-done.23 = f32[36,384]{1,0:T(8,128)S(1)} collective-permute-done((f32[36,384]{1,0:T(8,128)S(1)}, f32[36,384]{1,0:T(8,128)S(1)}, u32[]{:S(2)}, u32[]{:S(2)}) %collective-permute-start.23) | collective-permute-done | bytes 55328 | tf_op jit(solution)/shard_map/ppermute | solution.py:95
  171.5 3.5 %collective-permute-done.24 = f32[72,384]{1,0:T(8,128)S(1)} collective-permute-done((f32[72,384]{1,0:T(8,128)S(1)}, f32[72,384]{1,0:T(8,128)S(1)}, u32[]{:S(2)}, u32[]{:S(2)}) %collective-permute-start.24) | collective-permute-done | bytes 110624 | tf_op jit(solution)/shard_map/ppermute | solution.py:95
  176.1 6.3 %collective-permute-done.25 = f32[144,384]{1,0:T(8,128)S(1)} collective-permute-done((f32[144,384]{1,0:T(8,128)S(1)}, f32[144,384]{1,0:T(8,128)S(1)}, u32[]{:S(2)}, u32[]{:S(2)}) %collective-permute-start.25) | collective-permute-done | bytes 221216 | tf_op jit(solution)/shard_map/ppermute | solution.py:95
  182.5 3.2 %fusion.8 = bf16[1,512,1536]{2,1,0:T(8,128)(2,1)} fusion(f32[1,512,384]{2,1,0:T(8,128)} %fusion.26, f32[1,512,384]{2,1,0:T(8,128)} %fusion.24, f32[1,512,384]{2,1,0:T(8,128)} %fusion.22, f32[1,512,384]{2,1,0:T(8,128)S(1)} %copy-done.14, bf16[1,512,1536]{2,1,0:T(8,128)(2,1)S(1)} %copy-done.3, f32[512]{0:T(512)S(1)} %fusion.124), kind=kLoop, calls=%fused_computation.20 | loop fusion | flops 5505024 | bytes 6293504 | tf_op jit(solution)/shard_map/convert_element_type | solution.py:239
  193.3 3.1 %collective-permute-done.5 = f32[96,384]{1,0:T(8,128)S(1)} collective-permute-done((f32[96,384]{1,0:T(8,128)S(1)}, f32[96,384]{1,0:T(8,128)S(1)}, u32[]{:S(2)}, u32[]{:S(2)}) %collective-permute-start.5) | collective-permute-done | bytes 147488 | tf_op jit(solution)/shard_map/ppermute | solution.py:174
  199.3 2.6 %collective-permute-done.6 = f32[96,384]{1,0:T(8,128)S(1)} collective-permute-done((f32[96,384]{1,0:T(8,128)S(1)}, f32[96,384]{1,0:T(8,128)S(1)}, u32[]{:S(2)}, u32[]{:S(2)}) %collective-permute-start.6) | collective-permute-done | bytes 147488 | tf_op jit(solution)/shard_map/ppermute | solution.py:174
  204.5 2.6 %collective-permute-done.7 = f32[96,384]{1,0:T(8,128)S(1)} collective-permute-done((f32[96,384]{1,0:T(8,128)S(1)}, f32[96,384]{1,0:T(8,128)S(1)}, u32[]{:S(2)}, u32[]{:S(2)}) %collective-permute-start.7) | collective-permute-done | bytes 147488 | tf_op jit(solution)/shard_map/ppermute | solution.py:174
  209.7 3.2 %collective-permute-done.8 = f32[96,384]{1,0:T(8,128)S(1)} collective-permute-done((f32[96,384]{1,0:T(8,128)S(1)}, f32[96,384]{1,0:T(8,128)S(1)}, u32[]{:S(2)}, u32[]{:S(2)}) %collective-permute-start.8) | collective-permute-done | bytes 147488 | tf_op jit(solution)/shard_map/ppermute | solution.py:174
  215.8 3.7 %collective-permute-done.9 = f32[96,384]{1,0:T(8,128)S(1)} collective-permute-done((f32[96,384]{1,0:T(8,128)S(1)}, f32[96,384]{1,0:T(8,128)S(1)}, u32[]{:S(2)}, u32[]{:S(2)}) %collective-permute-start.9) | collective-permute-done | bytes 147488 | tf_op jit(solution)/shard_map/ppermute | solution.py:174
  222.2 3.5 %collective-permute-done.10 = f32[96,384]{1,0:T(8,128)S(1)} collective-permute-done((f32[96,384]{1,0:T(8,128)S(1)}, f32[96,384]{1,0:T(8,128)S(1)}, u32[]{:S(2)}, u32[]{:S(2)}) %collective-permute-start.10) | collective-permute-done | bytes 147488 | tf_op jit(solution)/shard_map/ppermute | solution.py:174
  227.8 3.0 %collective-permute-done.11 = f32[96,384]{1,0:T(8,128)S(1)} collective-permute-done((f32[96,384]{1,0:T(8,128)S(1)}, f32[96,384]{1,0:T(8,128)S(1)}, u32[]{:S(2)}, u32[]{:S(2)}) %collective-permute-start.11) | collective-permute-done | bytes 147488 | tf_op jit(solution)/shard_map/ppermute | solution.py:174
  (197 shorter events, 80.8 us)
Async XLA Ops:
  7.2 225.3 %reduce-scatter.2.cloned.1.call-start = ((), (), s32[]{:S(2)}) async-start(), calls=%async_computation.1 | async-start | bytes 5013504 | tf_op jit(solution)/shard_map/reduce_scatter | solution.py:190
  9.7 50.7 %collective-permute-start = (bf16[1,64,1536]{2,1,0:T(8,128)(2,1)S(1)}, bf16[1,64,1536]{2,1,0:T(8,128)(2,1)S(1)}, u32[]{:S(2)}, u32[]{:S(2)}) collective-permute-start(bf16[1,64,1536]{2,1,0:T(8,128)(2,1)S(1)} %get-tuple-element.38), channel_id=1, source_target_pairs={{0,2},{2,4},{4,6},{6,8},{8,10},{10,12},{12,14},{1,3},{3,5},{5,7},{... | collective-permute-start | bytes 589832 | tf_op jit(solution)/shard_map/ppermute | solution.py:21
  14.6 46.5 %collective-permute-start.1 = (bf16[1,64,1536]{2,1,0:T(8,128)(2,1)S(1)}, bf16[1,64,1536]{2,1,0:T(8,128)(2,1)}, u32[]{:S(2)}, u32[]{:S(2)}) collective-permute-start(bf16[1,64,1536]{2,1,0:T(8,128)(2,1)S(1)} %get-tuple-element.39), channel_id=1, source_target_pairs={{2,0},{4,2},{6,4},{8,6},{10,8},{12,10},{14,12},{3,1},{5,3},{7,5},{... | collective-permute-start | bytes 589832 | tf_op jit(solution)/shard_map/ppermute | solution.py:23
  104.6 28.2 %collective-permute-start.19 = (f32[144,768]{1,0:T(8,128)S(1)}, f32[144,768]{1,0:T(8,128)S(1)}, u32[]{:S(2)}, u32[]{:S(2)}) collective-permute-start(f32[144,768]{1,0:T(8,128)S(1)} %constant_dynamic-slice_fusion.3), channel_id=1, source_target_pairs={{0,1},{1,0},{2,3},{3,2},{4,5},{5,4},{6,7},{7,6},{8,9},{9,8},{10,11... | collective-permute-start | bytes 1327112 | tf_op jit(solution)/shard_map/ppermute | solution.py:95
  104.9 22.0 %collective-permute-start.2 = (bf16[1,64,1536]{1,2,0:T(8,128)(2,1)S(1)}, bf16[1,64,1536]{1,2,0:T(8,128)(2,1)S(1)}, u32[]{:S(2)}, u32[]{:S(2)}) collective-permute-start(bf16[1,64,1536]{1,2,0:T(8,128)(2,1)S(1)} %get-tuple-element.36), channel_id=1, source_target_pairs={{0,2},{2,4},{4,6},{6,8},{8,10},{10,12},{12,14},{1,3},{3,5},{5,7},{... | collective-permute-start | bytes 589832 | tf_op jit(solution)/shard_map/ppermute | solution.py:21
  109.6 17.3 %collective-permute-start.3 = (bf16[1,64,1536]{1,2,0:T(8,128)(2,1)S(1)}, bf16[1,64,1536]{1,2,0:T(8,128)(2,1)S(1)}, u32[]{:S(2)}, u32[]{:S(2)}) collective-permute-start(bf16[1,64,1536]{1,2,0:T(8,128)(2,1)S(1)} %get-tuple-element.37), channel_id=1, source_target_pairs={{2,0},{4,2},{6,4},{8,6},{10,8},{12,10},{14,12},{3,1},{5,3},{7,5},{... | collective-permute-start | bytes 589832 | tf_op jit(solution)/shard_map/ppermute | solution.py:23
  115.1 70.8 %collective-permute-start.4 = (f32[8,96,768]{2,1,0:T(8,128)}, f32[8,96,768]{2,1,0:T(8,128)}, u32[]{:S(2)}, u32[]{:S(2)}) collective-permute-start(f32[8,96,768]{2,1,0:T(8,128)} %fusion.29), channel_id=1, source_target_pairs={{0,1},{1,0},{2,3},{3,2},{4,5},{5,4},{6,7},{7,6},{8,9},{9,8},{10,11... | collective-permute-start | bytes 7077896 | tf_op jit(solution)/shard_map/ppermute | solution.py:95
  132.9 12.4 %collective-permute-start.20 = (f32[144,384]{1,0:T(8,128)S(1)}, f32[144,384]{1,0:T(8,128)S(1)}, u32[]{:S(2)}, u32[]{:S(2)}) collective-permute-start(f32[144,384]{1,0:T(8,128)S(1)} %constant_dynamic-slice_fusion.2), channel_id=1, source_target_pairs={{0,2},{2,0},{4,6},{6,4},{8,10},{10,8},{12,14},{14,12},{1,3},{3,1},... | collective-permute-start | bytes 663560 | tf_op jit(solution)/shard_map/ppermute | solution.py:95
  145.4 8.6 %collective-permute-start.21 = (f32[72,384]{1,0:T(8,128)S(1)}, f32[72,384]{1,0:T(8,128)S(1)}, u32[]{:S(2)}, u32[]{:S(2)}) collective-permute-start(f32[72,384]{1,0:T(8,128)S(1)} %constant_dynamic-slice_fusion.1), channel_id=1, source_target_pairs={{0,4},{2,6},{4,0},{6,2},{8,12},{10,14},{12,8},{14,10},{1,5},{3,7},... | collective-permute-start | bytes 331784 | tf_op jit(solution)/shard_map/ppermute | solution.py:95
  154.0 9.2 %collective-permute-start.22 = (f32[36,384]{1,0:T(8,128)S(1)}, f32[36,384]{1,0:T(8,128)S(1)}, u32[]{:S(2)}, u32[]{:S(2)}) collective-permute-start(f32[36,384]{1,0:T(8,128)S(1)} %constant_dynamic-slice_fusion), channel_id=1, source_target_pairs={{0,8},{2,10},{4,12},{6,14},{8,0},{10,2},{12,4},{14,6},{1,9},{3,11}... | collective-permute-start | bytes 165896 | tf_op jit(solution)/shard_map/ppermute | solution.py:95
  163.2 6.7 %collective-permute-start.23 = (f32[36,384]{1,0:T(8,128)S(1)}, f32[36,384]{1,0:T(8,128)S(1)}, u32[]{:S(2)}, u32[]{:S(2)}) collective-permute-start(f32[36,384]{1,0:T(8,128)S(1)} %dynamic-slice_add_fusion.3), channel_id=1, source_target_pairs={{0,8},{2,10},{4,12},{6,14},{8,0},{10,2},{12,4},{14,6},{1,9},{3,11}... | collective-permute-start | bytes 165896 | tf_op jit(solution)/shard_map/ppermute | solution.py:95
  175.0 7.4 %collective-permute-start.25 = (f32[144,384]{1,0:T(8,128)S(1)}, f32[144,384]{1,0:T(8,128)S(1)}, u32[]{:S(2)}, u32[]{:S(2)}) collective-permute-start(f32[144,384]{1,0:T(8,128)S(1)} %constant_dynamic-update-slice_fusion.4), channel_id=1, source_target_pairs={{0,2},{2,0},{4,6},{6,4},{8,10},{10,8},{12,14},{14,12},{1,3},{3,1},... | collective-permute-start | bytes 663560 | tf_op jit(solution)/shard_map/ppermute | solution.py:95
  190.1 6.3 %collective-permute-start.5 = (f32[96,384]{1,0:T(8,128)S(1)}, f32[96,384]{1,0:T(8,128)S(1)}, u32[]{:S(2)}, u32[]{:S(2)}) collective-permute-start(f32[96,384]{1,0:T(8,128)S(1)} %slice.322), channel_id=1, source_target_pairs={{0,4},{4,8},{8,12},{12,14},{14,10},{10,6},{6,2},{2,0},{1,5},{5,9},... | collective-permute-start | bytes 442376 | tf_op jit(solution)/shard_map/ppermute | solution.py:174
  192.7 6.0 %collective-permute-start.12 = (f32[96,384]{1,0:T(8,128)S(1)}, f32[96,384]{1,0:T(8,128)S(1)}, u32[]{:S(2)}, u32[]{:S(2)}) collective-permute-start(f32[96,384]{1,0:T(8,128)S(1)} %slice.330), channel_id=1, source_target_pairs={{0,2},{4,0},{8,4},{12,8},{14,12},{10,14},{6,10},{2,6},{1,3},{5,1},... | collective-permute-start | bytes 442376 | tf_op jit(solution)/shard_map/ppermute | solution.py:175
  196.4 5.5 %collective-permute-start.6 = (f32[96,384]{1,0:T(8,128)S(1)}, f32[96,384]{1,0:T(8,128)S(1)}, u32[]{:S(2)}, u32[]{:S(2)}) collective-permute-start(f32[96,384]{1,0:T(8,128)S(1)} %slice_add_fusion.13), channel_id=1, source_target_pairs={{0,4},{4,8},{8,12},{12,14},{14,10},{10,6},{6,2},{2,0},{1,5},{5,9},... | collective-permute-start | bytes 442376 | tf_op jit(solution)/shard_map/ppermute | solution.py:174
  198.7 5.2 %collective-permute-start.13 = (f32[96,384]{1,0:T(8,128)S(1)}, f32[96,384]{1,0:T(8,128)S(1)}, u32[]{:S(2)}, u32[]{:S(2)}) collective-permute-start(f32[96,384]{1,0:T(8,128)S(1)} %slice_add_fusion.6), channel_id=1, source_target_pairs={{0,2},{4,0},{8,4},{12,8},{14,12},{10,14},{6,10},{2,6},{1,3},{5,1},... | collective-permute-start | bytes 442376 | tf_op jit(solution)/shard_map/ppermute | solution.py:175
  203.9 5.2 %collective-permute-start.14 = (f32[96,384]{1,0:T(8,128)S(1)}, f32[96,384]{1,0:T(8,128)S(1)}, u32[]{:S(2)}, u32[]{:S(2)}) collective-permute-start(f32[96,384]{1,0:T(8,128)S(1)} %slice_add_fusion.5), channel_id=1, source_target_pairs={{0,2},{4,0},{8,4},{12,8},{14,12},{10,14},{6,10},{2,6},{1,3},{5,1},... | collective-permute-start | bytes 442376 | tf_op jit(solution)/shard_map/ppermute | solution.py:175
  207.2 5.7 %collective-permute-start.8 = (f32[96,384]{1,0:T(8,128)S(1)}, f32[96,384]{1,0:T(8,128)S(1)}, u32[]{:S(2)}, u32[]{:S(2)}) collective-permute-start(f32[96,384]{1,0:T(8,128)S(1)} %slice_add_fusion.11), channel_id=1, source_target_pairs={{0,4},{4,8},{8,12},{12,14},{14,10},{10,6},{6,2},{2,0},{1,5},{5,9},... | collective-permute-start | bytes 442376 | tf_op jit(solution)/shard_map/ppermute | solution.py:174
  209.2 6.2 %collective-permute-start.15 = (f32[96,384]{1,0:T(8,128)S(1)}, f32[96,384]{1,0:T(8,128)S(1)}, u32[]{:S(2)}, u32[]{:S(2)}) collective-permute-start(f32[96,384]{1,0:T(8,128)S(1)} %slice_add_fusion.4), channel_id=1, source_target_pairs={{0,2},{4,0},{8,4},{12,8},{14,12},{10,14},{6,10},{2,6},{1,3},{5,1},... | collective-permute-start | bytes 442376 | tf_op jit(solution)/shard_map/ppermute | solution.py:175
  212.9 6.6 %collective-permute-start.9 = (f32[96,384]{1,0:T(8,128)S(1)}, f32[96,384]{1,0:T(8,128)S(1)}, u32[]{:S(2)}, u32[]{:S(2)}) collective-permute-start(f32[96,384]{1,0:T(8,128)S(1)} %slice_add_fusion.10), channel_id=1, source_target_pairs={{0,4},{4,8},{8,12},{12,14},{14,10},{10,6},{6,2},{2,0},{1,5},{5,9},... | collective-permute-start | bytes 442376 | tf_op jit(solution)/shard_map/ppermute | solution.py:174
  215.4 6.2 %collective-permute-start.16 = (f32[96,384]{1,0:T(8,128)S(1)}, f32[96,384]{1,0:T(8,128)S(1)}, u32[]{:S(2)}, u32[]{:S(2)}) collective-permute-start(f32[96,384]{1,0:T(8,128)S(1)} %slice_add_fusion.3), channel_id=1, source_target_pairs={{0,2},{4,0},{8,4},{12,8},{14,12},{10,14},{6,10},{2,6},{1,3},{5,1},... | collective-permute-start | bytes 442376 | tf_op jit(solution)/shard_map/ppermute | solution.py:175
  219.5 6.1 %collective-permute-start.10 = (f32[96,384]{1,0:T(8,128)S(1)}, f32[96,384]{1,0:T(8,128)S(1)}, u32[]{:S(2)}, u32[]{:S(2)}) collective-permute-start(f32[96,384]{1,0:T(8,128)S(1)} %slice_add_fusion.9), channel_id=1, source_target_pairs={{0,4},{4,8},{8,12},{12,14},{14,10},{10,6},{6,2},{2,0},{1,5},{5,9},... | collective-permute-start | bytes 442376 | tf_op jit(solution)/shard_map/ppermute | solution.py:174
  221.6 5.6 %collective-permute-start.17 = (f32[96,384]{1,0:T(8,128)S(1)}, f32[96,384]{1,0:T(8,128)S(1)}, u32[]{:S(2)}, u32[]{:S(2)}) collective-permute-start(f32[96,384]{1,0:T(8,128)S(1)} %slice_add_fusion.2), channel_id=1, source_target_pairs={{0,2},{4,0},{8,4},{12,8},{14,12},{10,14},{6,10},{2,6},{1,3},{5,1},... | collective-permute-start | bytes 442376 | tf_op jit(solution)/shard_map/ppermute | solution.py:175
  227.2 5.2 %collective-permute-start.18 = (f32[96,384]{1,0:T(8,128)S(1)}, f32[96,384]{1,0:T(8,128)S(1)}, u32[]{:S(2)}, u32[]{:S(2)}) collective-permute-start(f32[96,384]{1,0:T(8,128)S(1)} %slice_add_fusion.1), channel_id=1, source_target_pairs={{0,2},{4,0},{8,4},{12,8},{14,12},{10,14},{6,10},{2,6},{1,3},{5,1},... | collective-permute-start | bytes 442376 | tf_op jit(solution)/shard_map/ppermute | solution.py:175
  (33 other events, 222.8 us)
Sparse Core Ops, SparseCore 0:
  99.7 90.9 reduce-scatter.1

commit v8 on v6

--- a/solution.py
+++ b/solution.py
@@ -134,9 +134,29 @@
 
 
 def point_gradient(act_rows, cot_rows):
-    return lax.dot_general(
-        act_rows, cot_rows, (((0,), (0,)), ((), ())), preferred_element_type=jnp.float32
+    chans = act_rows.shape[1]
+    seq_count = lax.axis_size("seq")
+    rep_count = lax.axis_size("rep")
+    product = lambda a, b: lax.dot_general(
+        a, b, (((0,), (0,)), ((), ())), preferred_element_type=jnp.float32
     )
+    if rep_count != 2:
+        partial = product(act_rows, cot_rows)
+        partial, cot_rows = lax.optimization_barrier((partial, cot_rows))
+        total = lax.psum_scatter(partial, ("seq", "rep"), scatter_dimension=0, tiled=True)
+        return total, cot_rows
+    block = chans // (seq_count * rep_count)
+    blocks = act_rows.reshape(act_rows.shape[0], seq_count, rep_count, block)
+    rep_index = lax.axis_index("rep")
+
+    def rows_of(owner):
+        cols = lax.dynamic_index_in_dim(blocks, owner, axis=2, keepdims=False)
+        return product(cols.reshape(act_rows.shape[0], seq_count * block), cot_rows)
+
+    mine = rows_of(rep_index) + swap(rows_of(1 - rep_index), "rep", 1)
+    mine, cot_rows = lax.optimization_barrier((mine, cot_rows))
+    total = lax.psum_scatter(mine, "seq", scatter_dimension=0, tiled=True)
+    return total, cot_rows
 
 
 def on_device(inputs, lengths, conv_weight, point_weight, cotangent):
@@ -159,11 +179,7 @@
     cot_rows = cotangent.reshape(local_bins, chans)
     proj = jnp.dot(act_rows, point_weight, preferred_element_type=jnp.float32).reshape(inputs.shape)
     output = (inputs.astype(jnp.float32) + proj).astype(jnp.bfloat16)
-    point_partial = point_gradient(act_rows, cot_rows)
-    point_partial, cot_rows = lax.optimization_barrier((point_partial, cot_rows))
-    grad_point = lax.psum_scatter(
-        point_partial, ("seq", "rep"), scatter_dimension=0, tiled=True
-    )
+    grad_point, cot_rows = point_gradient(act_rows, cot_rows)
     back = lax.dot_general(
         cot_rows, point_weight, (((1,), (1,)), ((), ())), preferred_element_type=jnp.float32
     )

time: 163 us -> 190 us (1.17)
  matrix products: 32.5 us -> 49.7 us
  waiting for transfers between devices: 73.4 us -> 84.3 us
  starting transfers between devices: 27.2 us -> 19.7 us
  other arithmetic: 9.99 us -> 16.4 us
    ppermute x2, waiting for transfers between devices: 4 us -> 14.6 us  [with_halo(): lax.ppermute(tail, axis, [(i, (i + 1) % count) for i in range(ends)])]
    ppermute x8 -> x9, starting transfers between devices: 15.1 us -> 5.66 us  [swap(): return lax.ppermute(value, axis, [(i, i ^ distance) for i in range(count)])]
    ppermute x8 -> x9, waiting for transfers between devices: 42.5 us -> 34.6 us  [swap(): return lax.ppermute(value, axis, [(i, i ^ distance) for i in range(count)])]
    dot_general x12, matrix products: 4.96 us -> 10.7 us  [weight_taps(): lax.dot_general(window, grads[:, cols], (((0,), (0,)), ((), ())), preferr...]
    ppermute x2, waiting for transfers between devices: 4.07 us -> 9.3 us  [with_halo(): lax.ppermute(head, axis, [((i + 1) % count, i) for i in range(ends)])]
    dot_general x1, matrix products: 3.77 us -> 7.63 us  [on_device(): jnp.dot(act_rows, point_weight, preferred_element_type=jnp.float32)]
    dot_general x1 -> x2, matrix products: 5.78 us -> 9.41 us  [point_gradient(): lax.dot_general(a, b, (((0,), (0,)), ((), ())), preferred_element_type=jn...]
    dot_general x24, matrix products: 11.5 us -> 15.1 us  [conv_taps(): lax.dot_general(window, dense[k, :, cols], dims, preferred_element_type=j...]
  transfers between devices with their start and end apart: 13 -> 14, of which waited for: 10 -> 10; matrix products, arithmetic and copies ran while one was open for 18% -> 16% of each run, Pallas kernels for 0% -> 0%
where the time goes in v8:
time: 190 us
  waiting for transfers between devices  84.3 us (44%)
  matrix products  49.7 us (26%)
  starting transfers between devices  19.7 us (10%)
  other arithmetic  16.4 us (9%)
  between operations  15.5 us (8%)
  local copies, waits for them, and re-layouts  4.47 us (2%)
    ppermute x9, waiting for transfers between devices, swap(): return lax.ppermute(value, axis, [(i, i ^ distance) for i in range(count)])  34.6 us
    reduce_scatter x1, waiting for transfers between devices, point_gradient(): total = lax.psum_scatter(mine, 'seq', scatter_dimension=0, tiled=True)  25.8 us
    dot_general x24, matrix products, conv_taps(): lax.dot_general(window, dense[k, :, cols], dims, preferred_element_type=j...  15.1 us
    ppermute x2, waiting for transfers between devices, with_halo(): lax.ppermute(tail, axis, [(i, (i + 1) % count) for i in range(ends)])  14.6 us
    ppermute x2, starting transfers between devices, with_halo(): lax.ppermute(tail, axis, [(i, (i + 1) % count) for i in range(ends)])  11.3 us
    dot_general x12, matrix products, weight_taps(): lax.dot_general(window, grads[:, cols], (((0,), (0,)), ((), ())), preferr...  10.7 us
    dot_general x2, matrix products, point_gradient(): lax.dot_general(a, b, (((0,), (0,)), ((), ())), preferred_element_type=jn...  9.41 us
    ppermute x2, waiting for transfers between devices, with_halo(): lax.ppermute(head, axis, [((i + 1) % count, i) for i in range(ends)])  9.3 us
  transfers between devices with their start and end apart: 14, of which 10 were waited for; matrix products, arithmetic and copies ran while one was open for 16% of the time, Pallas kernels for 0%

profile of v8, /device:TPU:0, one launch (start us, length us, event | category | flops | bytes accessed | tf_op | source)
XLA Modules:
  0.0 190.1 jit_solution(9944998756055710939)
XLA Ops:
  7.9 1.7 fusion.1
  11.7 6.2 %collective-permute-start = (bf16[1,64,1536]{2,1,0:T(8,128)(2,1)S(1)}, bf16[1,64,1536]{2,1,0:T(8,128)(2,1)}, u32[]{:S(2)}, u32[]{:S(2)}) collective-permute-start(bf16[1,64,1536]{2,1,0:T(8,128)(2,1)S(1)} %get-tuple-element.24), channel_id=1, source_target_pairs={{0,2},{2,4},{4,6},{6,8},{8,10},{10,12},{12,14},{1,3},{3,5},{5,7},{... | collective-permute-start | bytes 589832 | tf_op jit(solution)/shard_map/ppermute | solution.py:20
  18.6 2.1 %bitcast_multiply_fusion = bf16[3,384,1536]{2,1,0:T(8,128)(2,1)} fusion(bf16[384,1536]{1,0:T(8,128)(2,1)S(1)} %fusion.13, bf16[3,48,1536]{2,1,0:T(8,128)(2,1)S(1)} %copy-done.17), kind=kLoop, calls=%fused_computation.7 | loop fusion | flops 1769472 | bytes 5160960 | tf_op jit(solution)/shard_map/mul | solution.py:48
  20.7 4.0 %collective-permute-done = bf16[1,64,1536]{2,1,0:T(8,128)(2,1)} collective-permute-done((bf16[1,64,1536]{2,1,0:T(8,128)(2,1)S(1)}, bf16[1,64,1536]{2,1,0:T(8,128)(2,1)}, u32[]{:S(2)}, u32[]{:S(2)}) %collective-permute-start) | collective-permute-done | bytes 196640 | tf_op jit(solution)/shard_map/ppermute | solution.py:20
  33.7 3.5 %fusion.115 = f32[768,1536]{1,0:T(8,128)} fusion(bf16[512,768]{0,1:T(8,128)(2,1)S(1)} %bitcast.117, bf16[1,512,1536]{2,1,0:T(8,128)(2,1)S(1)} %copy-done.2), kind=kOutput, calls=%fused_computation.203 | convolution fusion | flops 1207959552 | bytes 7077888 | tf_op jit(solution)/shard_map/dot_general | solution.py:140
  38.4 7.6 %fusion.2 = bf16[1,512,1536]{2,1,0:T(8,128)(2,1)} fusion(bf16[1,512,1536]{2,1,0:T(8,128)(2,1)} %param.5, bf16[1536,1536]{1,0:T(8,128)(2,1)} %param.8, f32[512]{0:T(512)S(1)} %fusion.112, f32[512,384]{0,1:T(8,128)} %copy-done.5, f32[512,384]{0,1:T(8,128)} %copy-done.6, f32[512,384]{0,1:T(8,128)} %copy-done.7, f32[512,384]{0,1:T(8,128)} %copy-done.8), kind=kOutput, calls=%fused_computation.13 | convolution fusion | flops 2425356288 | bytes 11012096 | tf_op jit(solution)/shard_map/dot_general | solution.py:180
  46.0 5.9 %convolution_add_fusion = f32[768,1536]{1,0:T(8,128)} fusion(f32[768,1536]{1,0:T(8,128)} %collective-permute-done.2, bf16[512,768]{0,1:T(8,128)(2,1)S(1)} %bitcast.110, bf16[1,512,1536]{2,1,0:T(8,128)(2,1)S(1)} %copy-done.2), kind=kOutput, calls=%fused_computation.4 | convolution fusion | flops 1209139200 | bytes 11796480 | tf_op jit(solution)/shard_map/dot_general | solution.py:140
  51.9 6.8 %fusion.9 = bf16[512,1536]{0,1:T(8,128)(2,1)S(1)} fusion(bf16[512,1536]{1,0:T(8,128)(2,1)} %bitcast.108, bf16[1536,1536]{1,0:T(8,128)(2,1)} %param.8, f32[512]{0:T(512)S(1)} %fusion.112, f32[512,384]{0,1:T(8,128)} %copy-done.5, f32[512,384]{0,1:T(8,128)} %copy-done.6, f32[512,384]{0,1:T(8,128)} %copy-done.7, f32[512,384]{0,1:T(8,128)} %copy-done.8), kind=kOutput, calls=%fused_computation.26 | convolution fusion | flops 2426929152 | bytes 11012096 | tf_op jit(solution)/shard_map/dot_general | solution.py:183
  69.0 1.4 collective-permute-start.4
  70.5 5.1 %collective-permute-start.3 = (bf16[1,64,1536]{1,2,0:T(8,128)(2,1)}, bf16[1,64,1536]{1,2,0:T(8,128)(2,1)S(1)}, u32[]{:S(2)}, u32[]{:S(2)}) collective-permute-start(bf16[1,64,1536]{1,2,0:T(8,128)(2,1)} %get-tuple-element.20), channel_id=1, source_target_pairs={{0,2},{2,4},{4,6},{6,8},{8,10},{10,12},{12,14},{1,3},{3,5},{5,7},{... | collective-permute-start | bytes 589832 | tf_op jit(solution)/shard_map/ppermute | solution.py:20
  78.8 9.3 %collective-permute-done.4 = bf16[1,64,1536]{1,2,0:T(8,128)(2,1)S(1)} collective-permute-done((bf16[1,64,1536]{1,2,0:T(8,128)(2,1)}, bf16[1,64,1536]{1,2,0:T(8,128)(2,1)S(1)}, u32[]{:S(2)}, u32[]{:S(2)}) %collective-permute-start.4) | collective-permute-done | bytes 196640 | tf_op jit(solution)/shard_map/ppermute | solution.py:22
  88.1 10.6 %collective-permute-done.3 = bf16[1,64,1536]{1,2,0:T(8,128)(2,1)S(1)} collective-permute-done((bf16[1,64,1536]{1,2,0:T(8,128)(2,1)}, bf16[1,64,1536]{1,2,0:T(8,128)(2,1)S(1)}, u32[]{:S(2)}, u32[]{:S(2)}) %collective-permute-start.3) | collective-permute-done | bytes 196640 | tf_op jit(solution)/shard_map/ppermute | solution.py:20
  104.7 2.4 %collective-permute-start.6 = (f32[144,384]{1,0:T(8,128)S(1)}, f32[144,384]{1,0:T(8,128)S(1)}, u32[]{:S(2)}, u32[]{:S(2)}) collective-permute-start(f32[144,384]{1,0:T(8,128)S(1)} %constant_dynamic-slice_fusion.2), channel_id=1, source_target_pairs={{0,2},{2,0},{4,6},{6,4},{8,10},{10,8},{12,14},{14,12},{1,3},{3,1},... | collective-permute-start | bytes 663560 | tf_op jit(solution)/shard_map/ppermute | solution.py:94
  108.5 1.4 fusion.25
  109.8 7.2 %collective-permute-done.6 = f32[144,384]{1,0:T(8,128)S(1)} collective-permute-done((f32[144,384]{1,0:T(8,128)S(1)}, f32[144,384]{1,0:T(8,128)S(1)}, u32[]{:S(2)}, u32[]{:S(2)}) %collective-permute-start.6) | collective-permute-done | bytes 221216 | tf_op jit(solution)/shard_map/ppermute | solution.py:94
  119.6 9.2 %collective-permute-done.7 = f32[72,384]{1,0:T(8,128)S(1)} collective-permute-done((f32[72,384]{1,0:T(8,128)S(1)}, f32[72,384]{1,0:T(8,128)S(1)}, u32[]{:S(2)}, u32[]{:S(2)}) %collective-permute-start.7) | collective-permute-done | bytes 110624 | tf_op jit(solution)/shard_map/ppermute | solution.py:94
  130.3 3.8 %collective-permute-done.8 = f32[36,384]{1,0:T(8,128)S(1)} collective-permute-done((f32[36,384]{1,0:T(8,128)S(1)}, f32[36,384]{1,0:T(8,128)S(1)}, u32[]{:S(2)}, u32[]{:S(2)}) %collective-permute-start.8) | collective-permute-done | bytes 55328 | tf_op jit(solution)/shard_map/ppermute | solution.py:94
  134.8 4.6 %collective-permute-done.9 = f32[36,384]{1,0:T(8,128)S(1)} collective-permute-done((f32[36,384]{1,0:T(8,128)S(1)}, f32[36,384]{1,0:T(8,128)S(1)}, u32[]{:S(2)}, u32[]{:S(2)}) %collective-permute-start.9) | collective-permute-done | bytes 55328 | tf_op jit(solution)/shard_map/ppermute | solution.py:94
  139.8 4.7 %collective-permute-done.10 = f32[72,384]{1,0:T(8,128)S(1)} collective-permute-done((f32[72,384]{1,0:T(8,128)S(1)}, f32[72,384]{1,0:T(8,128)S(1)}, u32[]{:S(2)}, u32[]{:S(2)}) %collective-permute-start.10) | collective-permute-done | bytes 110624 | tf_op jit(solution)/shard_map/ppermute | solution.py:94
  144.5 1.4 collective-permute-start.11
  146.0 5.0 %collective-permute-done.11 = f32[144,384]{1,0:T(8,128)S(1)} collective-permute-done((f32[144,384]{1,0:T(8,128)S(1)}, f32[144,384]{1,0:T(8,128)S(1)}, u32[]{:S(2)}, u32[]{:S(2)}) %collective-permute-start.11) | collective-permute-done | bytes 221216 | tf_op jit(solution)/shard_map/ppermute | solution.py:94
  151.1 3.2 %fusion.8 = bf16[1,512,1536]{2,1,0:T(8,128)(2,1)} fusion(f32[1,512,384]{2,1,0:T(8,128)} %fusion.27, f32[1,512,384]{2,1,0:T(8,128)} %fusion.25, f32[1,512,384]{2,1,0:T(8,128)S(1)} %copy-done.9, f32[1,512,384]{2,1,0:T(8,128)} %fusion.21, bf16[1,512,1536]{2,1,0:T(8,128)(2,1)S(1)} %copy-done.3, f32[512]{0:T(512)S(1)} %fusion.112), kind=kLoop, calls=%fused_computation.22 | loop fusion | flops 5505024 | bytes 6293504 | tf_op jit(solution)/shard_map/convert_element_type | solution.py:191
  155.5 25.8 %reduce-scatter.2.cloned.1.call-done = f32[96,1536]{1,0:T(8,128)} async-done(((f32[768,1536]{1,0:T(8,128)}), f32[96,1536]{1,0:T(8,128)}) %reduce-scatter.2.cloned.1.call-update) | async-done | bytes 589840 | tf_op jit(solution)/shard_map/reduce_scatter | solution.py:158
  181.3 1.9 %broadcast_multiply_fusion.1 = f32[96,1536]{1,0:T(8,128)} fusion(f32[96,1536]{1,0:T(8,128)} %reduce-scatter.2.cloned.1.call-done), kind=kLoop, calls=%fused_computation.164 | loop fusion | flops 147456 | bytes 1179648 | tf_op jit(solution)/shard_map/mul | solution.py:192
  (134 shorter events, 39.6 us)
Async XLA Ops:
  7.2 11.4 %copy-start.17 = (bf16[3,48,1536]{2,1,0:T(8,128)(2,1)S(1)}, bf16[3,48,1536]{2,1,0:T(8,128)(2,1)}, u32[]{:S(2)}) copy-start(bf16[3,48,1536]{2,1,0:T(8,128)(2,1)} %param.7) | copy-start | bytes 1327108
  7.2 174.1 %reduce-scatter.2.cloned.1.call-start = ((), (), s32[]{:S(2)}) async-start(), calls=%async_computation.1 | async-start | bytes 5308416 | tf_op jit(solution)/shard_map/reduce_scatter | solution.py:158
  10.4 10.3 %collective-permute-start.1 = (bf16[1,64,1536]{2,1,0:T(8,128)(2,1)}, bf16[1,64,1536]{2,1,0:T(8,128)(2,1)}, u32[]{:S(2)}, u32[]{:S(2)}) collective-permute-start(bf16[1,64,1536]{2,1,0:T(8,128)(2,1)} %get-tuple-element.25), channel_id=1, source_target_pairs={{2,0},{4,2},{6,4},{8,6},{10,8},{12,10},{14,12},{3,1},{5,3},{7,5},{... | collective-permute-start | bytes 589832 | tf_op jit(solution)/shard_map/ppermute | solution.py:22
  11.7 13.0 %collective-permute-start = (bf16[1,64,1536]{2,1,0:T(8,128)(2,1)S(1)}, bf16[1,64,1536]{2,1,0:T(8,128)(2,1)}, u32[]{:S(2)}, u32[]{:S(2)}) collective-permute-start(bf16[1,64,1536]{2,1,0:T(8,128)(2,1)S(1)} %get-tuple-element.24), channel_id=1, source_target_pairs={{0,2},{2,4},{4,6},{6,8},{8,10},{10,12},{12,14},{1,3},{3,5},{5,7},{... | collective-permute-start | bytes 589832 | tf_op jit(solution)/shard_map/ppermute | solution.py:20
  37.2 8.8 %collective-permute-start.2 = (f32[768,1536]{1,0:T(8,128)}, f32[768,1536]{1,0:T(8,128)}, u32[]{:S(2)}, u32[]{:S(2)}) collective-permute-start(f32[768,1536]{1,0:T(8,128)} %fusion.115), channel_id=1, source_target_pairs={{0,1},{1,0},{2,3},{3,2},{4,5},{5,4},{6,7},{7,6},{8,9},{9,8},{10,11... | collective-permute-start | bytes 14155784 | tf_op jit(solution)/shard_map/ppermute | solution.py:94
  68.5 8.8 %copy-start.10 = (f32[384,384]{1,0:T(8,128)S(1)}, f32[384,384]{1,0:T(8,128)}, u32[]{:S(2)}) copy-start(f32[384,384]{1,0:T(8,128)} %fusion.89) | copy-start | bytes 1769476
  68.5 8.8 %copy-start.11 = (f32[384,384]{1,0:T(8,128)S(1)}, f32[384,384]{1,0:T(8,128)}, u32[]{:S(2)}) copy-start(f32[384,384]{1,0:T(8,128)} %fusion.78) | copy-start | bytes 1769476
  68.6 8.8 %copy-start.12 = (f32[384,384]{1,0:T(8,128)S(1)}, f32[384,384]{1,0:T(8,128)}, u32[]{:S(2)}) copy-start(f32[384,384]{1,0:T(8,128)} %fusion.67) | copy-start | bytes 1769476
  68.6 8.7 %copy-start.13 = (f32[384,384]{1,0:T(8,128)S(1)}, f32[384,384]{1,0:T(8,128)}, u32[]{:S(2)}) copy-start(f32[384,384]{1,0:T(8,128)} %fusion.56) | copy-start | bytes 1769476
  68.6 8.7 %copy-start.14 = (f32[384,384]{1,0:T(8,128)S(1)}, f32[384,384]{1,0:T(8,128)}, u32[]{:S(2)}) copy-start(f32[384,384]{1,0:T(8,128)} %fusion.85) | copy-start | bytes 1769476
  68.6 8.7 %copy-start.15 = (f32[384,384]{1,0:T(8,128)S(1)}, f32[384,384]{1,0:T(8,128)}, u32[]{:S(2)}) copy-start(f32[384,384]{1,0:T(8,128)} %fusion.74) | copy-start | bytes 1769476
  69.0 19.0 %collective-permute-start.4 = (bf16[1,64,1536]{1,2,0:T(8,128)(2,1)}, bf16[1,64,1536]{1,2,0:T(8,128)(2,1)S(1)}, u32[]{:S(2)}, u32[]{:S(2)}) collective-permute-start(bf16[1,64,1536]{1,2,0:T(8,128)(2,1)} %get-tuple-element.21), channel_id=1, source_target_pairs={{2,0},{4,2},{6,4},{8,6},{10,8},{12,10},{14,12},{3,1},{5,3},{7,5},{... | collective-permute-start | bytes 589832 | tf_op jit(solution)/shard_map/ppermute | solution.py:22
  70.5 28.2 %collective-permute-start.3 = (bf16[1,64,1536]{1,2,0:T(8,128)(2,1)}, bf16[1,64,1536]{1,2,0:T(8,128)(2,1)S(1)}, u32[]{:S(2)}, u32[]{:S(2)}) collective-permute-start(bf16[1,64,1536]{1,2,0:T(8,128)(2,1)} %get-tuple-element.20), channel_id=1, source_target_pairs={{0,2},{2,4},{4,6},{6,8},{8,10},{10,12},{12,14},{1,3},{3,5},{5,7},{... | collective-permute-start | bytes 589832 | tf_op jit(solution)/shard_map/ppermute | solution.py:20
  78.4 21.5 %copy-start.1 = (bf16[3,384,1536]{2,1,0:T(8,128)(2,1)S(1)}, bf16[3,384,1536]{2,1,0:T(8,128)(2,1)}, u32[]{:S(2)}) copy-start(bf16[3,384,1536]{2,1,0:T(8,128)(2,1)} %bitcast_multiply_fusion) | copy-start | bytes 10616836
  78.5 26.1 %collective-permute-start.5 = (f32[144,768]{1,0:T(8,128)S(1)}, f32[144,768]{1,0:T(8,128)S(1)}, u32[]{:S(2)}, u32[]{:S(2)}) collective-permute-start(f32[144,768]{1,0:T(8,128)S(1)} %constant_dynamic-slice_fusion.3), channel_id=1, source_target_pairs={{0,1},{1,0},{2,3},{3,2},{4,5},{5,4},{6,7},{7,6},{8,9},{9,8},{10,11... | collective-permute-start | bytes 1327112 | tf_op jit(solution)/shard_map/ppermute | solution.py:94
  104.7 12.3 %collective-permute-start.6 = (f32[144,384]{1,0:T(8,128)S(1)}, f32[144,384]{1,0:T(8,128)S(1)}, u32[]{:S(2)}, u32[]{:S(2)}) collective-permute-start(f32[144,384]{1,0:T(8,128)S(1)} %constant_dynamic-slice_fusion.2), channel_id=1, source_target_pairs={{0,2},{2,0},{4,6},{6,4},{8,10},{10,8},{12,14},{14,12},{1,3},{3,1},... | collective-permute-start | bytes 663560 | tf_op jit(solution)/shard_map/ppermute | solution.py:94
  117.1 11.8 %collective-permute-start.7 = (f32[72,384]{1,0:T(8,128)S(1)}, f32[72,384]{1,0:T(8,128)S(1)}, u32[]{:S(2)}, u32[]{:S(2)}) collective-permute-start(f32[72,384]{1,0:T(8,128)S(1)} %constant_dynamic-slice_fusion.1), channel_id=1, source_target_pairs={{0,4},{2,6},{4,0},{6,2},{8,12},{10,14},{12,8},{14,10},{1,5},{3,7},... | collective-permute-start | bytes 331784 | tf_op jit(solution)/shard_map/ppermute | solution.py:94
  119.6 31.5 %copy-start.3 = (bf16[1,512,1536]{2,1,0:T(8,128)(2,1)S(1)}, bf16[1,512,1536]{2,1,0:T(8,128)(2,1)}, u32[]{:S(2)}) copy-start(bf16[1,512,1536]{2,1,0:T(8,128)(2,1)} %param.9) | copy-start | bytes 4718596
  128.9 5.2 %collective-permute-start.8 = (f32[36,384]{1,0:T(8,128)S(1)}, f32[36,384]{1,0:T(8,128)S(1)}, u32[]{:S(2)}, u32[]{:S(2)}) collective-permute-start(f32[36,384]{1,0:T(8,128)S(1)} %constant_dynamic-slice_fusion), channel_id=1, source_target_pairs={{0,8},{2,10},{4,12},{6,14},{8,0},{10,2},{12,4},{14,6},{1,9},{3,11}... | collective-permute-start | bytes 165896 | tf_op jit(solution)/shard_map/ppermute | solution.py:94
  130.3 20.8 %copy-start.9 = (f32[1,512,384]{2,1,0:T(8,128)S(1)}, f32[1,512,384]{2,1,0:T(8,128)}, u32[]{:S(2)}) copy-start(f32[1,512,384]{2,1,0:T(8,128)} %fusion.23) | copy-start | bytes 2359300
  134.2 5.3 %collective-permute-start.9 = (f32[36,384]{1,0:T(8,128)S(1)}, f32[36,384]{1,0:T(8,128)S(1)}, u32[]{:S(2)}, u32[]{:S(2)}) collective-permute-start(f32[36,384]{1,0:T(8,128)S(1)} %dynamic-slice_add_fusion.3), channel_id=1, source_target_pairs={{0,8},{2,10},{4,12},{6,14},{8,0},{10,2},{12,4},{14,6},{1,9},{3,11}... | collective-permute-start | bytes 165896 | tf_op jit(solution)/shard_map/ppermute | solution.py:94
  139.7 4.8 %collective-permute-start.10 = (f32[72,384]{1,0:T(8,128)S(1)}, f32[72,384]{1,0:T(8,128)S(1)}, u32[]{:S(2)}, u32[]{:S(2)}) collective-permute-start(f32[72,384]{1,0:T(8,128)S(1)} %dynamic_update_slice.25), channel_id=1, source_target_pairs={{0,4},{2,6},{4,0},{6,2},{8,12},{10,14},{12,8},{14,10},{1,5},{3,7},... | collective-permute-start | bytes 331784 | tf_op jit(solution)/shard_map/ppermute | solution.py:94
  144.5 6.5 %collective-permute-start.11 = (f32[144,384]{1,0:T(8,128)S(1)}, f32[144,384]{1,0:T(8,128)S(1)}, u32[]{:S(2)}, u32[]{:S(2)}) collective-permute-start(f32[144,384]{1,0:T(8,128)S(1)} %constant_dynamic-update-slice_fusion.4), channel_id=1, source_target_pairs={{0,2},{2,0},{4,6},{6,4},{8,10},{10,8},{12,14},{14,12},{1,3},{3,1},... | collective-permute-start | bytes 663560 | tf_op jit(solution)/shard_map/ppermute | solution.py:94
  151.0 3.4 %collective-permute-start.12 = (f32[144,768]{1,0:T(8,128)S(1)}, f32[144,768]{1,0:T(8,128)S(1)}, u32[]{:S(2)}, u32[]{:S(2)}) collective-permute-start(f32[144,768]{1,0:T(8,128)S(1)} %constant_dynamic-update-slice_fusion.2), channel_id=1, source_target_pairs={{0,1},{1,0},{2,3},{3,2},{4,5},{5,4},{6,7},{7,6},{8,9},{9,8},{10,11... | collective-permute-start | bytes 1327112 | tf_op jit(solution)/shard_map/ppermute | solution.py:94
  (12 other events, 56.8 us)
Sparse Core Ops, SparseCore 0:
  68.6 112.6 reduce-scatter.1

commit v9 on v6

--- a/solution.py
+++ b/solution.py
@@ -24,6 +24,37 @@
             axis=dim,
         )
     return cells
+
+
+def halos(cells, axis, width):
+    count = lax.axis_size(axis)
+    ends = count - 1
+    head = lax.slice_in_dim(cells, 0, width, axis=1)
+    tail = lax.slice_in_dim(cells, cells.shape[1] - width, cells.shape[1], axis=1)
+    left = lax.ppermute(tail, axis, [(i, (i + 1) % count) for i in range(ends)])
+    right = lax.ppermute(head, axis, [((i + 1) % count, i) for i in range(ends)])
+    return left, right
+
+
+def edge_taps(left, right, dense, sequence_length):
+    chunks = dense.shape[2] // CHUNK
+    width = left.shape[1]
+
+    def side(rows, k):
+        return jnp.concatenate(
+            [
+                jnp.dot(
+                    rows[0, :, c * CHUNK : (c + 1) * CHUNK],
+                    dense[k, :, c * CHUNK : (c + 1) * CHUNK],
+                    preferred_element_type=jnp.float32,
+                )
+                for c in range(chunks)
+            ],
+            axis=1,
+        )
+
+    middle = jnp.zeros((sequence_length - 2 * width, dense.shape[2]), jnp.float32)
+    return jnp.concatenate([side(left, 0), middle, side(right, 2)], axis=0)[None]
 
 
 def gelu_pair(pre):
@@ -150,16 +181,18 @@
     mask3 = mask[:, :, None]
     masked_input = (inputs.astype(jnp.float32) * mask3).astype(jnp.bfloat16)
     scale = 1.0 / math.sqrt(rep_count * seq_count * local_bins)
-    padded_input = with_halo(masked_input, (("seq", 1),), DILATION_STEP)
+    left, right = halos(masked_input, "seq", DILATION_STEP)
     dense = dense_weight(conv_weight)
-    pre = conv_taps(padded_input, dense, local_bins)
+    zero_padded = jnp.pad(masked_input, ((0, 0), (DILATION_STEP, DILATION_STEP), (0, 0)))
+    pre = conv_taps(zero_padded, dense, local_bins) + edge_taps(left, right, dense, local_bins)
+    padded_input = jnp.concatenate([left, masked_input, right], axis=1)
     act_val, slope = gelu_pair(pre)
     act = (act_val * mask3).astype(jnp.bfloat16)
     act_rows = act.reshape(local_bins, chans)
     cot_rows = cotangent.reshape(local_bins, chans)
     proj = jnp.dot(act_rows, point_weight, preferred_element_type=jnp.float32).reshape(inputs.shape)
     output = (inputs.astype(jnp.float32) + proj).astype(jnp.bfloat16)
-    point_partial = point_gradient(act_rows, cot_rows)
+    point_partial = point_gradient(act_rows, cot_rows) * scale
     point_partial, cot_rows = lax.optimization_barrier((point_partial, cot_rows))
     grad_point = lax.psum_scatter(
         point_partial, ("seq", "rep"), scatter_dimension=0, tiled=True
@@ -173,7 +206,6 @@
     conv_local = weight_taps(padded_input, preactivation_gradient, local_bins)
     grad_conv = tree_sum(conv_local) * scale
     grad_inputs = (cotangent.astype(jnp.float32) + mask3 * spread).astype(jnp.bfloat16)
-    grad_point = grad_point * scale
     return (output, grad_inputs, grad_point, grad_conv)
 
 

time: 163 us -> 175 us (1.074)
  matrix products: 32.5 us -> 49.9 us
  starting transfers between devices: 27.2 us -> 19.7 us
  waiting for transfers between devices: 73.4 us -> 67.7 us
  other arithmetic: 9.99 us -> 14.7 us
  local copies, waits for them, and re-layouts: 4.4 us -> 6.52 us
    dot_general x0 -> x8, matrix products: none -> 9.21 us  [side(): jnp.dot(rows[0, :, c * CHUNK:(c + 1) * CHUNK], dense[k, :, c * CHUNK:(c +...]
    ppermute x8, starting transfers between devices: 15.1 us -> 7.52 us  [swap(): return lax.ppermute(value, axis, [(i, i ^ distance) for i in range(count)])]
    ppermute x0 -> x2, starting transfers between devices: none -> 6.82 us  [the longest x1 5.54 us: halos(): left = lax.ppermute(tail, axis, [(i, (i + 1) % count) for i in range(ends)])]
    ppermute x2 -> x1, starting transfers between devices: 9.35 us -> 3.85 us  [with_halo(): lax.ppermute(tail, axis, [(i, (i + 1) % count) for i in range(ends)])]
    ppermute x2 -> x1, waiting for transfers between devices: 4.07 us -> 0.01 us  [with_halo(): lax.ppermute(head, axis, [((i + 1) % count, i) for i in range(ends)])]
    ppermute x2 -> x1, waiting for transfers between devices: 4 us -> 0.01 us  [with_halo(): lax.ppermute(tail, axis, [(i, (i + 1) % count) for i in range(ends)])]
    reduce_scatter x1, waiting for transfers between devices: 22.8 us -> 19.1 us  [on_device(): lax.psum_scatter(point_partial, ('seq', 'rep'), scatter_dimension=0, tile...]
    ppermute x0 -> x2, waiting for transfers between devices: none -> 3.49 us  [the longest x1 3.49 us: halos(): lax.ppermute(head, axis, [((i + 1) % count, i) for i in range(ends)])]
  transfers between devices with their start and end apart: 13 -> 13, of which waited for: 10 -> 8; matrix products, arithmetic and copies ran while one was open for 18% -> 23% of each run, Pallas kernels for 0% -> 0%
where the time goes in v9:
time: 175 us; the launch traced here: 174 us
  waiting for transfers between devices  67.7 us (39%)
  matrix products  49.9 us (29%)
  starting transfers between devices  19.7 us (11%)
  between operations  15.9 us (9%)
  other arithmetic  14.7 us (8%)
  local copies, waits for them, and re-layouts  6.52 us (4%)
    ppermute x8, waiting for transfers between devices, swap(): return lax.ppermute(value, axis, [(i, i ^ distance) for i in range(count)])  45.1 us
    reduce_scatter x1, waiting for transfers between devices, on_device(): lax.psum_scatter(point_partial, ('seq', 'rep'), scatter_dimension=0, tile...  19.1 us
    dot_general x24, matrix products, conv_taps(): lax.dot_general(window, dense[k, :, cols], dims, preferred_element_type=j...  15 us
    dot_general x8, matrix products, side(): jnp.dot(rows[0, :, c * CHUNK:(c + 1) * CHUNK], dense[k, :, c * CHUNK:(c +...  9.21 us
    dot_general x1, matrix products, on_device(): lax.dot_general(cot_rows, point_weight, (((1,), (1,)), ((), ())), preferr...  8.28 us
    ppermute x8, starting transfers between devices, swap(): return lax.ppermute(value, axis, [(i, i ^ distance) for i in range(count)])  7.52 us
    dot_general x1, matrix products, point_gradient(): lax.dot_general(act_rows, cot_rows, (((0,), (0,)), ((), ())), preferred_e...  6.44 us
    dot_general x1, matrix products, on_device(): jnp.dot(act_rows, point_weight, preferred_element_type=jnp.float32)  5.99 us
  transfers between devices with their start and end apart: 13, of which 8 were waited for; matrix products, arithmetic and copies ran while one was open for 23% of the time, Pallas kernels for 0%

profile of v9, /device:TPU:0, one launch (start us, length us, event | category | flops | bytes accessed | tf_op | source)
XLA Modules:
  0.0 174.4 jit_solution(4302713260511441687)
XLA Ops:
  7.9 1.7 fusion.1
  11.5 5.5 %collective-permute-start = (bf16[1,64,1536]{2,1,0:T(8,128)(2,1)}, bf16[1,64,1536]{2,1,0:T(8,128)(2,1)}, u32[]{:S(2)}, u32[]{:S(2)}) collective-permute-start(bf16[1,64,1536]{2,1,0:T(8,128)(2,1)} %get-tuple-element.24), channel_id=1, source_target_pairs={{0,2},{2,4},{4,6},{6,8},{8,10},{10,12},{12,14},{1,3},{3,5},{5,7},{... | collective-permute-start | bytes 589832 | tf_op jit(solution)/shard_map/ppermute | solution.py:34
  19.6 1.3 bitcast_multiply_fusion
  22.1 3.5 %collective-permute-done.1 = bf16[1,64,1536]{2,1,0:T(8,128)(2,1)} collective-permute-done((bf16[1,64,1536]{2,1,0:T(8,128)(2,1)}, bf16[1,64,1536]{2,1,0:T(8,128)(2,1)}, u32[]{:S(2)}, u32[]{:S(2)}) %collective-permute-start.1) | collective-permute-done | bytes 196640 | tf_op jit(solution)/shard_map/ppermute | solution.py:35
  25.6 2.5 %maximum_bitcast_fusion.1 = (bf16[640,1536]{1,0:T(8,128)(2,1)}, bf16[640,1536]{1,0:T(8,128)(2,1)S(1)}) fusion(bf16[1,64,1536]{2,1,0:T(8,128)(2,1)} %collective-permute-done.1, bf16[1,512,1536]{2,1,0:T(8,128)(2,1)S(1)} %copy-done.2, bf16[1,64,1536]{2,1,0:T(8,128)(2,1)} %collective-permute-done), kind=kLoop, calls=%fused_computation.33 | loop fusion | flops 5898240 | bytes 5898240 | tf_op jit(solution)/shard_map/squeeze | solution.py:102
  43.4 6.4 %convolution_multiply_fusion = f32[1536,1536]{1,0:T(8,128)} fusion(f32[1,64,1,1,1,1,1536]{1,6,5,4,3,2,0:T(8,128)S(1)} %maximum_bitcast_fusion.3, f32[1,64,1,1,1,1,1536]{1,6,5,4,3,2,0:T(8,128)S(1)} %maximum_bitcast_fusion.2, f32[1,512,1,1,1,1,384]{1,6,5,4,3,2,0:T(8,128)S(1)} %bitcast.158, f32[1,512,1,1,1,1,384]{1,6,5,4,3,2,0:T(8,128)S(1)} %bitcast.159, ...), kind=kOutput, calls=%fused_computation | convolution fusion | flops 2427715584 | bytes 14946304 | tf_op jit(solution)/shard_map/dot_general | solution.py:168
  49.9 8.3 %fusion.9 = bf16[512,1536]{0,1:T(8,128)(2,1)S(1)} fusion(bf16[512,1536]{1,0:T(8,128)(2,1)} %bitcast.156, bf16[1536,1536]{1,0:T(8,128)(2,1)} %param.8, f32[512]{0:T(512)S(1)} %fusion.116, f32[64,384]{0,1:T(8,128)} %copy-done.15, f32[64,384]{0,1:T(8,128)} %copy-done.17, f32[64,384]{0,1:T(8,128)} %copy-done.19, f32[64,384]{0,1:T(8,128)} %copy-done.21, ...), kind=kOutput, calls=%fused_computation.26 | convolution fusion | flops 2434007040 | bytes 11800576 | tf_op jit(solution)/shard_map/dot_general | solution.py:200
  58.4 3.9 %collective-permute-start.2 = (bf16[1,64,1536]{1,2,0:T(8,128)(2,1)S(1)}, bf16[1,64,1536]{1,2,0:T(8,128)(2,1)S(1)}, u32[]{:S(2)}, u32[]{:S(2)}) collective-permute-start(bf16[1,64,1536]{1,2,0:T(8,128)(2,1)S(1)} %get-tuple-element.22), channel_id=1, source_target_pairs={{0,2},{2,4},{4,6},{6,8},{8,10},{10,12},{12,14},{1,3},{3,5},{5,7},{... | collective-permute-start | bytes 589832 | tf_op jit(solution)/shard_map/ppermute | solution.py:20
  62.2 1.5 collective-permute-start.3
  72.3 6.0 %fusion.2 = bf16[1,512,1536]{2,1,0:T(8,128)(2,1)} fusion(bf16[1,512,1536]{2,1,0:T(8,128)(2,1)S(1)} %copy-done.5, bf16[1536,1536]{1,0:T(8,128)(2,1)S(1)} %bitcast.163, f32[512]{0:T(512)S(1)} %fusion.116, f32[512,384]{0,1:T(8,128)S(1)} %copy-done.24, f32[512,384]{0,1:T(8,128)S(1)} %copy-done.26, f32[512,384]{0,1:T(8,128)S(1)} %copy-done.28, ...), kind=kOutput, calls=%fused_computation.13 | convolution fusion | flops 2432434176 | bytes 11800576 | tf_op jit(solution)/shard_map/dot_general | solution.py:193
  84.5 3.1 %collective-permute-start.5 = (f32[144,384]{1,0:T(8,128)S(1)}, f32[144,384]{1,0:T(8,128)S(1)}, u32[]{:S(2)}, u32[]{:S(2)}) collective-permute-start(f32[144,384]{1,0:T(8,128)S(1)} %constant_dynamic-slice_fusion.2), channel_id=1, source_target_pairs={{0,2},{2,0},{4,6},{6,4},{8,10},{10,8},{12,14},{14,12},{1,3},{3,1},... | collective-permute-start | bytes 663560 | tf_op jit(solution)/shard_map/ppermute | solution.py:125
  87.7 1.3 fusion.27
  89.0 1.3 fusion.25
  90.3 8.3 %collective-permute-done.5 = f32[144,384]{1,0:T(8,128)S(1)} collective-permute-done((f32[144,384]{1,0:T(8,128)S(1)}, f32[144,384]{1,0:T(8,128)S(1)}, u32[]{:S(2)}, u32[]{:S(2)}) %collective-permute-start.5) | collective-permute-done | bytes 221216 | tf_op jit(solution)/shard_map/ppermute | solution.py:125
  98.7 3.7 %collective-permute-start.6 = (f32[72,384]{1,0:T(8,128)S(1)}, f32[72,384]{1,0:T(8,128)S(1)}, u32[]{:S(2)}, u32[]{:S(2)}) collective-permute-start(f32[72,384]{1,0:T(8,128)S(1)} %constant_dynamic-slice_fusion.1), channel_id=1, source_target_pairs={{0,4},{2,6},{4,0},{6,2},{8,12},{10,14},{12,8},{14,10},{1,5},{3,7},... | collective-permute-start | bytes 331784 | tf_op jit(solution)/shard_map/ppermute | solution.py:125
  102.4 1.3 fusion.23
  103.7 12.0 %collective-permute-done.6 = f32[72,384]{1,0:T(8,128)S(1)} collective-permute-done((f32[72,384]{1,0:T(8,128)S(1)}, f32[72,384]{1,0:T(8,128)S(1)}, u32[]{:S(2)}, u32[]{:S(2)}) %collective-permute-start.6) | collective-permute-done | bytes 110624 | tf_op jit(solution)/shard_map/ppermute | solution.py:125
  116.0 1.3 fusion.21
  117.3 8.8 %collective-permute-done.7 = f32[36,384]{1,0:T(8,128)S(1)} collective-permute-done((f32[36,384]{1,0:T(8,128)S(1)}, f32[36,384]{1,0:T(8,128)S(1)}, u32[]{:S(2)}, u32[]{:S(2)}) %collective-permute-start.7) | collective-permute-done | bytes 55328 | tf_op jit(solution)/shard_map/ppermute | solution.py:125
  126.7 5.6 %collective-permute-done.8 = f32[36,384]{1,0:T(8,128)S(1)} collective-permute-done((f32[36,384]{1,0:T(8,128)S(1)}, f32[36,384]{1,0:T(8,128)S(1)}, u32[]{:S(2)}, u32[]{:S(2)}) %collective-permute-start.8) | collective-permute-done | bytes 55328 | tf_op jit(solution)/shard_map/ppermute | solution.py:125
  132.7 4.7 %collective-permute-done.9 = f32[72,384]{1,0:T(8,128)S(1)} collective-permute-done((f32[72,384]{1,0:T(8,128)S(1)}, f32[72,384]{1,0:T(8,128)S(1)}, u32[]{:S(2)}, u32[]{:S(2)}) %collective-permute-start.9) | collective-permute-done | bytes 110624 | tf_op jit(solution)/shard_map/ppermute | solution.py:125
  137.7 5.7 %collective-permute-done.10 = f32[144,384]{1,0:T(8,128)S(1)} collective-permute-done((f32[144,384]{1,0:T(8,128)S(1)}, f32[144,384]{1,0:T(8,128)S(1)}, u32[]{:S(2)}, u32[]{:S(2)}) %collective-permute-start.10) | collective-permute-done | bytes 221216 | tf_op jit(solution)/shard_map/ppermute | solution.py:125
  143.6 3.7 %fusion.8 = bf16[1,512,1536]{2,1,0:T(8,128)(2,1)} fusion(f32[1,512,384]{2,1,0:T(8,128)} %fusion.27, f32[1,512,384]{2,1,0:T(8,128)} %fusion.25, f32[1,512,384]{2,1,0:T(8,128)S(1)} %copy-done.3, f32[1,512,384]{2,1,0:T(8,128)S(1)} %copy-done.4, bf16[1,512,1536]{2,1,0:T(8,128)(2,1)} %param.9, f32[512]{0:T(512)S(1)} %fusion.116), kind=kLoop, calls=%fused_computation.22 | loop fusion | flops 5505024 | bytes 6293504 | tf_op jit(solution)/shard_map/convert_element_type | solution.py:208
  148.4 19.1 %reduce-scatter.2.cloned.1.call-done = f32[96,1536]{1,0:T(8,128)} async-done(((f32[1536,1536]{1,0:T(8,128)}), f32[96,1536]{1,0:T(8,128)}) %reduce-scatter.2.cloned.1.call-update) | async-done | bytes 589840 | tf_op jit(solution)/shard_map/reduce_scatter | solution.py:197
  (174 shorter events, 37.7 us)
Async XLA Ops:
  7.2 160.4 %reduce-scatter.2.cloned.1.call-start = ((), (), s32[]{:S(2)}) async-start(), calls=%async_computation.1 | async-start | bytes 10027008 | tf_op jit(solution)/shard_map/reduce_scatter | solution.py:197
  11.5 10.6 %collective-permute-start = (bf16[1,64,1536]{2,1,0:T(8,128)(2,1)}, bf16[1,64,1536]{2,1,0:T(8,128)(2,1)}, u32[]{:S(2)}, u32[]{:S(2)}) collective-permute-start(bf16[1,64,1536]{2,1,0:T(8,128)(2,1)} %get-tuple-element.24), channel_id=1, source_target_pairs={{0,2},{2,4},{4,6},{6,8},{8,10},{10,12},{12,14},{1,3},{3,5},{5,7},{... | collective-permute-start | bytes 589832 | tf_op jit(solution)/shard_map/ppermute | solution.py:34
  17.1 8.6 %collective-permute-start.1 = (bf16[1,64,1536]{2,1,0:T(8,128)(2,1)}, bf16[1,64,1536]{2,1,0:T(8,128)(2,1)}, u32[]{:S(2)}, u32[]{:S(2)}) collective-permute-start(bf16[1,64,1536]{2,1,0:T(8,128)(2,1)} %get-tuple-element.25), channel_id=1, source_target_pairs={{2,0},{4,2},{6,4},{8,6},{10,8},{12,10},{14,12},{3,1},{5,3},{7,5},{... | collective-permute-start | bytes 589832 | tf_op jit(solution)/shard_map/ppermute | solution.py:35
  18.6 24.7 %copy-start.34 = (f32[512]{0:T(512)}, f32[512]{0:T(512)S(1)}, u32[]{:S(2)}) copy-start(f32[512]{0:T(512)S(1)} %pad.49.clone) | copy-start | bytes 6148
  30.7 12.7 %copy-start.23 = (f32[512,384]{0,1:T(8,128)}, f32[512,384]{0,1:T(8,128)S(1)}, u32[]{:S(2)}) copy-start(f32[512,384]{0,1:T(8,128)S(1)} %convolution_add_fusion.4) | copy-start | bytes 2359300
  31.6 11.8 %copy-start.25 = (f32[512,384]{0,1:T(8,128)}, f32[512,384]{0,1:T(8,128)S(1)}, u32[]{:S(2)}) copy-start(f32[512,384]{0,1:T(8,128)S(1)} %convolution_add_fusion.6) | copy-start | bytes 2359300
  32.4 11.0 %copy-start.27 = (f32[512,384]{0,1:T(8,128)}, f32[512,384]{0,1:T(8,128)S(1)}, u32[]{:S(2)}) copy-start(f32[512,384]{0,1:T(8,128)S(1)} %convolution_add_fusion.8) | copy-start | bytes 2359300
  33.3 10.1 %copy-start.29 = (f32[512,384]{0,1:T(8,128)}, f32[512,384]{0,1:T(8,128)S(1)}, u32[]{:S(2)}) copy-start(f32[512,384]{0,1:T(8,128)S(1)} %convolution_add_fusion.10) | copy-start | bytes 2359300
  34.4 8.3 %copy-start.7 = (f32[64,384]{0,1:T(8,128)}, f32[64,384]{0,1:T(8,128)S(1)}, u32[]{:S(2)}) copy-start(f32[64,384]{0,1:T(8,128)S(1)} %fusion.106) | copy-start | bytes 294916
  35.6 7.2 %copy-start.9 = (f32[64,384]{0,1:T(8,128)}, f32[64,384]{0,1:T(8,128)S(1)}, u32[]{:S(2)}) copy-start(f32[64,384]{0,1:T(8,128)S(1)} %fusion.104) | copy-start | bytes 294916
  35.6 7.8 %copy-start.6 = (bf16[1,512,1536]{2,1,0:T(8,128)(2,1)S(1)}, bf16[1,512,1536]{2,1,0:T(8,128)(2,1)}, u32[]{:S(2)}) copy-start(bf16[1,512,1536]{2,1,0:T(8,128)(2,1)} %param.9) | copy-start | bytes 4718596
  49.9 13.8 %copy-start = (bf16[640,1536]{1,0:T(8,128)(2,1)S(1)}, bf16[640,1536]{1,0:T(8,128)(2,1)}, u32[]{:S(2)}) copy-start(bf16[640,1536]{1,0:T(8,128)(2,1)} %get-tuple-element.20) | copy-start | bytes 5898244
  58.4 20.1 %collective-permute-start.2 = (bf16[1,64,1536]{1,2,0:T(8,128)(2,1)S(1)}, bf16[1,64,1536]{1,2,0:T(8,128)(2,1)S(1)}, u32[]{:S(2)}, u32[]{:S(2)}) collective-permute-start(bf16[1,64,1536]{1,2,0:T(8,128)(2,1)S(1)} %get-tuple-element.22), channel_id=1, source_target_pairs={{0,2},{2,4},{4,6},{6,8},{8,10},{10,12},{12,14},{1,3},{3,5},{5,7},{... | collective-permute-start | bytes 589832 | tf_op jit(solution)/shard_map/ppermute | solution.py:20
  62.2 16.3 %collective-permute-start.3 = (bf16[1,64,1536]{1,2,0:T(8,128)(2,1)S(1)}, bf16[1,64,1536]{1,2,0:T(8,128)(2,1)S(1)}, u32[]{:S(2)}, u32[]{:S(2)}) collective-permute-start(bf16[1,64,1536]{1,2,0:T(8,128)(2,1)S(1)} %get-tuple-element.23), channel_id=1, source_target_pairs={{2,0},{4,2},{6,4},{8,6},{10,8},{12,10},{14,12},{3,1},{5,3},{7,5},{... | collective-permute-start | bytes 589832 | tf_op jit(solution)/shard_map/ppermute | solution.py:22
  78.4 6.0 %collective-permute-start.4 = (f32[144,768]{1,0:T(8,128)S(1)}, f32[144,768]{1,0:T(8,128)S(1)}, u32[]{:S(2)}, u32[]{:S(2)}) collective-permute-start(f32[144,768]{1,0:T(8,128)S(1)} %constant_dynamic-slice_fusion.3), channel_id=1, source_target_pairs={{0,1},{1,0},{2,3},{3,2},{4,5},{5,4},{6,7},{7,6},{8,9},{9,8},{10,11... | collective-permute-start | bytes 1327112 | tf_op jit(solution)/shard_map/ppermute | solution.py:125
  84.5 14.1 %collective-permute-start.5 = (f32[144,384]{1,0:T(8,128)S(1)}, f32[144,384]{1,0:T(8,128)S(1)}, u32[]{:S(2)}, u32[]{:S(2)}) collective-permute-start(f32[144,384]{1,0:T(8,128)S(1)} %constant_dynamic-slice_fusion.2), channel_id=1, source_target_pairs={{0,2},{2,0},{4,6},{6,4},{8,10},{10,8},{12,14},{14,12},{1,3},{3,1},... | collective-permute-start | bytes 663560 | tf_op jit(solution)/shard_map/ppermute | solution.py:125
  98.7 17.1 %collective-permute-start.6 = (f32[72,384]{1,0:T(8,128)S(1)}, f32[72,384]{1,0:T(8,128)S(1)}, u32[]{:S(2)}, u32[]{:S(2)}) collective-permute-start(f32[72,384]{1,0:T(8,128)S(1)} %constant_dynamic-slice_fusion.1), channel_id=1, source_target_pairs={{0,4},{2,6},{4,0},{6,2},{8,12},{10,14},{12,8},{14,10},{1,5},{3,7},... | collective-permute-start | bytes 331784 | tf_op jit(solution)/shard_map/ppermute | solution.py:125
  115.8 10.3 %collective-permute-start.7 = (f32[36,384]{1,0:T(8,128)S(1)}, f32[36,384]{1,0:T(8,128)S(1)}, u32[]{:S(2)}, u32[]{:S(2)}) collective-permute-start(f32[36,384]{1,0:T(8,128)S(1)} %constant_dynamic-slice_fusion), channel_id=1, source_target_pairs={{0,8},{2,10},{4,12},{6,14},{8,0},{10,2},{12,4},{14,6},{1,9},{3,11}... | collective-permute-start | bytes 165896 | tf_op jit(solution)/shard_map/ppermute | solution.py:125
  117.3 26.2 %copy-start.3 = (f32[1,512,384]{2,1,0:T(8,128)S(1)}, f32[1,512,384]{2,1,0:T(8,128)}, u32[]{:S(2)}) copy-start(f32[1,512,384]{2,1,0:T(8,128)} %fusion.23) | copy-start | bytes 2359300
  117.3 26.3 %copy-start.4 = (f32[1,512,384]{2,1,0:T(8,128)S(1)}, f32[1,512,384]{2,1,0:T(8,128)}, u32[]{:S(2)}) copy-start(f32[1,512,384]{2,1,0:T(8,128)} %fusion.21) | copy-start | bytes 2359300
  126.1 6.2 %collective-permute-start.8 = (f32[36,384]{1,0:T(8,128)S(1)}, f32[36,384]{1,0:T(8,128)S(1)}, u32[]{:S(2)}, u32[]{:S(2)}) collective-permute-start(f32[36,384]{1,0:T(8,128)S(1)} %dynamic-slice_add_fusion.3), channel_id=1, source_target_pairs={{0,8},{2,10},{4,12},{6,14},{8,0},{10,2},{12,4},{14,6},{1,9},{3,11}... | collective-permute-start | bytes 165896 | tf_op jit(solution)/shard_map/ppermute | solution.py:125
  132.6 4.8 %collective-permute-start.9 = (f32[72,384]{1,0:T(8,128)S(1)}, f32[72,384]{1,0:T(8,128)S(1)}, u32[]{:S(2)}, u32[]{:S(2)}) collective-permute-start(f32[72,384]{1,0:T(8,128)S(1)} %dynamic_update_slice.25), channel_id=1, source_target_pairs={{0,4},{2,6},{4,0},{6,2},{8,12},{10,14},{12,8},{14,10},{1,5},{3,7},... | collective-permute-start | bytes 331784 | tf_op jit(solution)/shard_map/ppermute | solution.py:125
  137.4 6.0 %collective-permute-start.10 = (f32[144,384]{1,0:T(8,128)S(1)}, f32[144,384]{1,0:T(8,128)S(1)}, u32[]{:S(2)}, u32[]{:S(2)}) collective-permute-start(f32[144,384]{1,0:T(8,128)S(1)} %constant_dynamic-update-slice_fusion.4), channel_id=1, source_target_pairs={{0,2},{2,0},{4,6},{6,4},{8,10},{10,8},{12,14},{14,12},{1,3},{3,1},... | collective-permute-start | bytes 663560 | tf_op jit(solution)/shard_map/ppermute | solution.py:125
  143.5 3.9 %collective-permute-start.11 = (f32[144,768]{1,0:T(8,128)S(1)}, f32[144,768]{1,0:T(8,128)S(1)}, u32[]{:S(2)}, u32[]{:S(2)}) collective-permute-start(f32[144,768]{1,0:T(8,128)S(1)} %constant_dynamic-update-slice_fusion.2), channel_id=1, source_target_pairs={{0,1},{1,0},{2,3},{3,2},{4,5},{5,4},{6,7},{7,6},{8,9},{9,8},{10,11... | collective-permute-start | bytes 1327112 | tf_op jit(solution)/shard_map/ppermute | solution.py:125
  (28 other events, 73.3 us)
Sparse Core Ops, SparseCore 0:
  50.0 117.4 reduce-scatter.1

commit v10 on v6

--- a/solution.py
+++ b/solution.py
@@ -159,7 +159,7 @@
     cot_rows = cotangent.reshape(local_bins, chans)
     proj = jnp.dot(act_rows, point_weight, preferred_element_type=jnp.float32).reshape(inputs.shape)
     output = (inputs.astype(jnp.float32) + proj).astype(jnp.bfloat16)
-    point_partial = point_gradient(act_rows, cot_rows)
+    point_partial = point_gradient(act_rows, cot_rows) * scale
     point_partial, cot_rows = lax.optimization_barrier((point_partial, cot_rows))
     grad_point = lax.psum_scatter(
         point_partial, ("seq", "rep"), scatter_dimension=0, tiled=True
@@ -173,7 +173,6 @@
     conv_local = weight_taps(padded_input, preactivation_gradient, local_bins)
     grad_conv = tree_sum(conv_local) * scale
     grad_inputs = (cotangent.astype(jnp.float32) + mask3 * spread).astype(jnp.bfloat16)
-    grad_point = grad_point * scale
     return (output, grad_inputs, grad_point, grad_conv)
 
 

time: 163 us -> 162 us (level)
  other arithmetic: 9.99 us -> 8.06 us
    mul x1 -> x0, other arithmetic: 1.93 us -> none  [on_device(): grad_point = grad_point * scale]
where the time goes in v10:
time: 162 us; the launch traced here: 161 us
  waiting for transfers between devices  73.4 us (45%)
  matrix products  32.6 us (20%)
  starting transfers between devices  27.3 us (17%)
  between operations  15.6 us (10%)
  other arithmetic  8.06 us (5%)
  local copies, waits for them, and re-layouts  4.39 us (3%)
    ppermute x8, waiting for transfers between devices, swap(): return lax.ppermute(value, axis, [(i, i ^ distance) for i in range(count)])  42.5 us
    reduce_scatter x1, waiting for transfers between devices, on_device(): lax.psum_scatter(point_partial, ('seq', 'rep'), scatter_dimension=0, tile...  22.8 us
    ppermute x8, starting transfers between devices, swap(): return lax.ppermute(value, axis, [(i, i ^ distance) for i in range(count)])  15.1 us
    dot_general x24, matrix products, conv_taps(): lax.dot_general(window, dense[k, :, cols], dims, preferred_element_type=j...  11.5 us
    ppermute x2, starting transfers between devices, with_halo(): lax.ppermute(tail, axis, [(i, (i + 1) % count) for i in range(ends)])  9.39 us
    dot_general x1, matrix products, on_device(): lax.dot_general(cot_rows, point_weight, (((1,), (1,)), ((), ())), preferr...  6.46 us
    dot_general x1, matrix products, point_gradient(): lax.dot_general(act_rows, cot_rows, (((0,), (0,)), ((), ())), preferred_e...  5.88 us
    dot_general x12, matrix products, weight_taps(): lax.dot_general(window, grads[:, cols], (((0,), (0,)), ((), ())), preferr...  4.96 us
  transfers between devices with their start and end apart: 13, of which 10 were waited for; matrix products, arithmetic and copies ran while one was open for 18% of the time, Pallas kernels for 0%

profile of v10, /device:TPU:0, one launch (start us, length us, event | category | flops | bytes accessed | tf_op | source)
XLA Modules:
  0.0 161.2 jit_solution(4698975253825821762)
XLA Ops:
  7.9 1.8 %fusion.1 = bf16[1,512,1536]{2,1,0:T(8,128)(2,1)S(1)} fusion(bf16[1,512,1536]{2,1,0:T(8,128)(2,1)} %param.5, f32[512]{0:T(512)S(1)} %fusion.116), kind=kLoop, calls=%fused_computation.12 | loop fusion | flops 2359296 | bytes 3147776 | tf_op jit(solution)/shard_map/convert_element_type | solution.py:151
  9.7 4.9 %collective-permute-start = (bf16[1,64,1536]{2,1,0:T(8,128)(2,1)S(1)}, bf16[1,64,1536]{2,1,0:T(8,128)(2,1)S(1)}, u32[]{:S(2)}, u32[]{:S(2)}) collective-permute-start(bf16[1,64,1536]{2,1,0:T(8,128)(2,1)S(1)} %get-tuple-element.22), channel_id=1, source_target_pairs={{0,2},{2,4},{4,6},{6,8},{8,10},{10,12},{12,14},{1,3},{3,5},{5,7},{... | collective-permute-start | bytes 589832 | tf_op jit(solution)/shard_map/ppermute | solution.py:20
  14.6 1.3 collective-permute-start.1
  16.9 1.9 %collective-permute-done = bf16[1,64,1536]{2,1,0:T(8,128)(2,1)S(1)} collective-permute-done((bf16[1,64,1536]{2,1,0:T(8,128)(2,1)S(1)}, bf16[1,64,1536]{2,1,0:T(8,128)(2,1)S(1)}, u32[]{:S(2)}, u32[]{:S(2)}) %collective-permute-start) | collective-permute-done | bytes 196640 | tf_op jit(solution)/shard_map/ppermute | solution.py:20
  18.8 4.1 %collective-permute-done.1 = bf16[1,64,1536]{2,1,0:T(8,128)(2,1)S(1)} collective-permute-done((bf16[1,64,1536]{2,1,0:T(8,128)(2,1)S(1)}, bf16[1,64,1536]{2,1,0:T(8,128)(2,1)S(1)}, u32[]{:S(2)}, u32[]{:S(2)}) %collective-permute-start.1) | collective-permute-done | bytes 196640 | tf_op jit(solution)/shard_map/ppermute | solution.py:22
  29.6 5.9 %convolution_multiply_fusion = f32[1536,1536]{1,0:T(8,128)} fusion(f32[1,512,1,1,1,1,384]{1,6,5,4,3,2,0:T(8,128)S(1)} %bitcast.120, f32[1,512,1,1,1,1,384]{1,6,5,4,3,2,0:T(8,128)S(1)} %bitcast.121, f32[1,512,1,1,1,1,384]{1,6,5,4,3,2,0:T(8,128)S(1)} %bitcast.122, f32[1,512,1,1,1,1,384]{1,6,5,4,3,2,0:T(8,128)S(1)} %bitcast.123, f32[512]{0:T(512)S(1)} %fusion.116, ...), kind=kOutput, calls=%fused_computation | convolution fusion | flops 2425356288 | bytes 14157824 | tf_op jit(solution)/shard_map/dot_general | solution.py:137
  35.6 6.5 %fusion.9 = bf16[512,1536]{0,1:T(8,128)(2,1)S(1)} fusion(bf16[512,1536]{1,0:T(8,128)(2,1)S(1)} %bitcast.118, bf16[1536,1536]{1,0:T(8,128)(2,1)} %param.8, f32[512]{0:T(512)S(1)} %fusion.116, f32[512,384]{0,1:T(8,128)} %copy-done.5, f32[512,384]{0,1:T(8,128)} %copy-done.7, f32[512,384]{0,1:T(8,128)} %copy-done.9, f32[512,384]{0,1:T(8,128)} %copy-done.11), kind=kOutput, calls=%fused_computation.26 | convolution fusion | flops 2426929152 | bytes 11012096 | tf_op jit(solution)/shard_map/dot_general | solution.py:167
  42.3 4.5 %collective-permute-start.2 = (bf16[1,64,1536]{1,2,0:T(8,128)(2,1)S(1)}, bf16[1,64,1536]{1,2,0:T(8,128)(2,1)S(1)}, u32[]{:S(2)}, u32[]{:S(2)}) collective-permute-start(bf16[1,64,1536]{1,2,0:T(8,128)(2,1)S(1)} %get-tuple-element.20), channel_id=1, source_target_pairs={{0,2},{2,4},{4,6},{6,8},{8,10},{10,12},{12,14},{1,3},{3,5},{5,7},{... | collective-permute-start | bytes 589832 | tf_op jit(solution)/shard_map/ppermute | solution.py:20
  46.8 1.5 collective-permute-start.3
  56.2 3.8 %fusion.2 = bf16[1,512,1536]{2,1,0:T(8,128)(2,1)} fusion(bf16[1,512,1536]{2,1,0:T(8,128)(2,1)S(1)} %copy-done.2, bf16[1536,1536]{1,0:T(8,128)(2,1)S(1)} %bitcast.125, f32[512]{0:T(512)S(1)} %fusion.116, f32[512,384]{0,1:T(8,128)S(1)} %copy-done.6, f32[512,384]{0,1:T(8,128)S(1)} %copy-done.8, f32[512,384]{0,1:T(8,128)S(1)} %copy-done.10, ...), kind=kOutput, calls=%fused_computation.13 | convolution fusion | flops 2425356288 | bytes 11012096 | tf_op jit(solution)/shard_map/dot_general | solution.py:160
  60.2 2.1 %collective-permute-done.2 = bf16[1,64,1536]{1,2,0:T(8,128)(2,1)S(1)} collective-permute-done((bf16[1,64,1536]{1,2,0:T(8,128)(2,1)S(1)}, bf16[1,64,1536]{1,2,0:T(8,128)(2,1)S(1)}, u32[]{:S(2)}, u32[]{:S(2)}) %collective-permute-start.2) | collective-permute-done | bytes 196640 | tf_op jit(solution)/shard_map/ppermute | solution.py:20
  68.3 2.5 %collective-permute-start.5 = (f32[144,384]{1,0:T(8,128)S(1)}, f32[144,384]{1,0:T(8,128)S(1)}, u32[]{:S(2)}, u32[]{:S(2)}) collective-permute-start(f32[144,384]{1,0:T(8,128)S(1)} %constant_dynamic-slice_fusion.2), channel_id=1, source_target_pairs={{0,2},{2,0},{4,6},{6,4},{8,10},{10,8},{12,14},{14,12},{1,3},{3,1},... | collective-permute-start | bytes 663560 | tf_op jit(solution)/shard_map/ppermute | solution.py:94
  71.8 8.9 %collective-permute-done.5 = f32[144,384]{1,0:T(8,128)S(1)} collective-permute-done((f32[144,384]{1,0:T(8,128)S(1)}, f32[144,384]{1,0:T(8,128)S(1)}, u32[]{:S(2)}, u32[]{:S(2)}) %collective-permute-start.5) | collective-permute-done | bytes 221216 | tf_op jit(solution)/shard_map/ppermute | solution.py:94
  80.8 6.2 %collective-permute-start.6 = (f32[72,384]{1,0:T(8,128)S(1)}, f32[72,384]{1,0:T(8,128)S(1)}, u32[]{:S(2)}, u32[]{:S(2)}) collective-permute-start(f32[72,384]{1,0:T(8,128)S(1)} %constant_dynamic-slice_fusion.1), channel_id=1, source_target_pairs={{0,4},{2,6},{4,0},{6,2},{8,12},{10,14},{12,8},{14,10},{1,5},{3,7},... | collective-permute-start | bytes 331784 | tf_op jit(solution)/shard_map/ppermute | solution.py:94
  87.4 12.5 %collective-permute-done.6 = f32[72,384]{1,0:T(8,128)S(1)} collective-permute-done((f32[72,384]{1,0:T(8,128)S(1)}, f32[72,384]{1,0:T(8,128)S(1)}, u32[]{:S(2)}, u32[]{:S(2)}) %collective-permute-start.6) | collective-permute-done | bytes 110624 | tf_op jit(solution)/shard_map/ppermute | solution.py:94
  100.0 1.6 collective-permute-start.7
  102.1 7.7 %collective-permute-done.7 = f32[36,384]{1,0:T(8,128)S(1)} collective-permute-done((f32[36,384]{1,0:T(8,128)S(1)}, f32[36,384]{1,0:T(8,128)S(1)}, u32[]{:S(2)}, u32[]{:S(2)}) %collective-permute-start.7) | collective-permute-done | bytes 55328 | tf_op jit(solution)/shard_map/ppermute | solution.py:94
  110.3 5.6 %collective-permute-done.8 = f32[36,384]{1,0:T(8,128)S(1)} collective-permute-done((f32[36,384]{1,0:T(8,128)S(1)}, f32[36,384]{1,0:T(8,128)S(1)}, u32[]{:S(2)}, u32[]{:S(2)}) %collective-permute-start.8) | collective-permute-done | bytes 55328 | tf_op jit(solution)/shard_map/ppermute | solution.py:94
  116.3 1.9 %collective-permute-start.9 = (f32[72,384]{1,0:T(8,128)S(1)}, f32[72,384]{1,0:T(8,128)S(1)}, u32[]{:S(2)}, u32[]{:S(2)}) collective-permute-start(f32[72,384]{1,0:T(8,128)S(1)} %dynamic_update_slice.25), channel_id=1, source_target_pairs={{0,4},{2,6},{4,0},{6,2},{8,12},{10,14},{12,8},{14,10},{1,5},{3,7},... | collective-permute-start | bytes 331784 | tf_op jit(solution)/shard_map/ppermute | solution.py:94
  118.2 3.0 %collective-permute-done.9 = f32[72,384]{1,0:T(8,128)S(1)} collective-permute-done((f32[72,384]{1,0:T(8,128)S(1)}, f32[72,384]{1,0:T(8,128)S(1)}, u32[]{:S(2)}, u32[]{:S(2)}) %collective-permute-start.9) | collective-permute-done | bytes 110624 | tf_op jit(solution)/shard_map/ppermute | solution.py:94
  121.3 2.6 %collective-permute-start.10 = (f32[144,384]{1,0:T(8,128)S(1)}, f32[144,384]{1,0:T(8,128)S(1)}, u32[]{:S(2)}, u32[]{:S(2)}) collective-permute-start(f32[144,384]{1,0:T(8,128)S(1)} %constant_dynamic-update-slice_fusion.4), channel_id=1, source_target_pairs={{0,2},{2,0},{4,6},{6,4},{8,10},{10,8},{12,14},{14,12},{1,3},{3,1},... | collective-permute-start | bytes 663560 | tf_op jit(solution)/shard_map/ppermute | solution.py:94
  124.0 4.7 %collective-permute-done.10 = f32[144,384]{1,0:T(8,128)S(1)} collective-permute-done((f32[144,384]{1,0:T(8,128)S(1)}, f32[144,384]{1,0:T(8,128)S(1)}, u32[]{:S(2)}, u32[]{:S(2)}) %collective-permute-start.10) | collective-permute-done | bytes 221216 | tf_op jit(solution)/shard_map/ppermute | solution.py:94
  128.7 1.6 fusion.8
  131.6 22.8 %reduce-scatter.2.cloned.1.call-done = f32[96,1536]{1,0:T(8,128)} async-done(((f32[1536,1536]{1,0:T(8,128)}), f32[96,1536]{1,0:T(8,128)}) %reduce-scatter.2.cloned.1.call-update) | async-done | bytes 589840 | tf_op jit(solution)/shard_map/reduce_scatter | solution.py:164
  (116 shorter events, 25.9 us)
Async XLA Ops:
  7.2 147.2 %reduce-scatter.2.cloned.1.call-start = ((), (), s32[]{:S(2)}) async-start(), calls=%async_computation.1 | async-start | bytes 10027008 | tf_op jit(solution)/shard_map/reduce_scatter | solution.py:164
  7.9 8.7 %copy-start.13 = (bf16[3,48,1536]{2,1,0:T(8,128)(2,1)S(1)}, bf16[3,48,1536]{2,1,0:T(8,128)(2,1)}, u32[]{:S(2)}) copy-start(bf16[3,48,1536]{2,1,0:T(8,128)(2,1)} %param.7) | copy-start | bytes 1327108
  9.7 9.1 %collective-permute-start = (bf16[1,64,1536]{2,1,0:T(8,128)(2,1)S(1)}, bf16[1,64,1536]{2,1,0:T(8,128)(2,1)S(1)}, u32[]{:S(2)}, u32[]{:S(2)}) collective-permute-start(bf16[1,64,1536]{2,1,0:T(8,128)(2,1)S(1)} %get-tuple-element.22), channel_id=1, source_target_pairs={{0,2},{2,4},{4,6},{6,8},{8,10},{10,12},{12,14},{1,3},{3,5},{5,7},{... | collective-permute-start | bytes 589832 | tf_op jit(solution)/shard_map/ppermute | solution.py:20
  14.6 8.3 %collective-permute-start.1 = (bf16[1,64,1536]{2,1,0:T(8,128)(2,1)S(1)}, bf16[1,64,1536]{2,1,0:T(8,128)(2,1)S(1)}, u32[]{:S(2)}, u32[]{:S(2)}) collective-permute-start(bf16[1,64,1536]{2,1,0:T(8,128)(2,1)S(1)} %get-tuple-element.23), channel_id=1, source_target_pairs={{2,0},{4,2},{6,4},{8,6},{10,8},{12,10},{14,12},{3,1},{5,3},{7,5},{... | collective-permute-start | bytes 589832 | tf_op jit(solution)/shard_map/ppermute | solution.py:22
  16.9 10.8 %copy-start = (bf16[3,384,1536]{2,1,0:T(8,128)(2,1)}, bf16[3,384,1536]{2,1,0:T(8,128)(2,1)S(1)}, u32[]{:S(2)}) copy-start(bf16[3,384,1536]{2,1,0:T(8,128)(2,1)S(1)} %bitcast_multiply_fusion) | copy-start | bytes 10616836
  27.3 2.3 %copy-start.3 = (bf16[1,512,1536]{2,1,0:T(8,128)(2,1)S(1)}, bf16[1,512,1536]{2,1,0:T(8,128)(2,1)}, u32[]{:S(2)}) copy-start(bf16[1,512,1536]{2,1,0:T(8,128)(2,1)} %param.9) | copy-start | bytes 4718596
  42.3 20.0 %collective-permute-start.2 = (bf16[1,64,1536]{1,2,0:T(8,128)(2,1)S(1)}, bf16[1,64,1536]{1,2,0:T(8,128)(2,1)S(1)}, u32[]{:S(2)}, u32[]{:S(2)}) collective-permute-start(bf16[1,64,1536]{1,2,0:T(8,128)(2,1)S(1)} %get-tuple-element.20), channel_id=1, source_target_pairs={{0,2},{2,4},{4,6},{6,8},{8,10},{10,12},{12,14},{1,3},{3,5},{5,7},{... | collective-permute-start | bytes 589832 | tf_op jit(solution)/shard_map/ppermute | solution.py:20
  46.8 15.5 %collective-permute-start.3 = (bf16[1,64,1536]{1,2,0:T(8,128)(2,1)S(1)}, bf16[1,64,1536]{1,2,0:T(8,128)(2,1)S(1)}, u32[]{:S(2)}, u32[]{:S(2)}) collective-permute-start(bf16[1,64,1536]{1,2,0:T(8,128)(2,1)S(1)} %get-tuple-element.21), channel_id=1, source_target_pairs={{2,0},{4,2},{6,4},{8,6},{10,8},{12,10},{14,12},{3,1},{5,3},{7,5},{... | collective-permute-start | bytes 589832 | tf_op jit(solution)/shard_map/ppermute | solution.py:22
  49.1 5.4 %slice-start = ((s8[4718592]{0:T(1024)(128)(4,1)}), s8[4194304]{0:T(1024)(128)(4,1)S(1)}, s32[]{:S(2)}) async-start(s8[4718592]{0:T(1024)(128)(4,1)} %bitcast.124), calls=%async_computation.2 | async-start | bytes 8388608
  52.5 2.0 %slice-start.1 = ((s8[4718592]{0:T(1024)(128)(4,1)}), s8[524288]{0:T(1024)(128)(4,1)S(1)}, s32[]{:S(2)}) async-start(s8[4718592]{0:T(1024)(128)(4,1)} %bitcast.124), calls=%async_computation.3 | async-start | bytes 1048576
  53.4 1.9 %copy-start.6 = (f32[512,384]{0,1:T(8,128)S(1)}, f32[512,384]{0,1:T(8,128)}, u32[]{:S(2)}) copy-start(f32[512,384]{0,1:T(8,128)} %copy-done.5) | copy-start | bytes 2359300
  53.4 2.2 %copy-start.8 = (f32[512,384]{0,1:T(8,128)S(1)}, f32[512,384]{0,1:T(8,128)}, u32[]{:S(2)}) copy-start(f32[512,384]{0,1:T(8,128)} %copy-done.7) | copy-start | bytes 2359300
  53.4 2.5 %copy-start.10 = (f32[512,384]{0,1:T(8,128)S(1)}, f32[512,384]{0,1:T(8,128)}, u32[]{:S(2)}) copy-start(f32[512,384]{0,1:T(8,128)} %copy-done.9) | copy-start | bytes 2359300
  53.4 2.8 %copy-start.12 = (f32[512,384]{0,1:T(8,128)S(1)}, f32[512,384]{0,1:T(8,128)}, u32[]{:S(2)}) copy-start(f32[512,384]{0,1:T(8,128)} %copy-done.11) | copy-start | bytes 2359300
  60.1 3.4 %copy-start.1 = (bf16[3,384,1536]{2,1,0:T(8,128)(2,1)S(1)}, bf16[3,384,1536]{2,1,0:T(8,128)(2,1)}, u32[]{:S(2)}) copy-start(bf16[3,384,1536]{2,1,0:T(8,128)(2,1)} %copy-done) | copy-start | bytes 10616836
  60.1 8.1 %collective-permute-start.4 = (f32[144,768]{1,0:T(8,128)S(1)}, f32[144,768]{1,0:T(8,128)S(1)}, u32[]{:S(2)}, u32[]{:S(2)}) collective-permute-start(f32[144,768]{1,0:T(8,128)S(1)} %constant_dynamic-slice_fusion.3), channel_id=1, source_target_pairs={{0,1},{1,0},{2,3},{3,2},{4,5},{5,4},{6,7},{7,6},{8,9},{9,8},{10,11... | collective-permute-start | bytes 1327112 | tf_op jit(solution)/shard_map/ppermute | solution.py:94
  68.3 12.4 %collective-permute-start.5 = (f32[144,384]{1,0:T(8,128)S(1)}, f32[144,384]{1,0:T(8,128)S(1)}, u32[]{:S(2)}, u32[]{:S(2)}) collective-permute-start(f32[144,384]{1,0:T(8,128)S(1)} %constant_dynamic-slice_fusion.2), channel_id=1, source_target_pairs={{0,2},{2,0},{4,6},{6,4},{8,10},{10,8},{12,14},{14,12},{1,3},{3,1},... | collective-permute-start | bytes 663560 | tf_op jit(solution)/shard_map/ppermute | solution.py:94
  80.8 19.2 %collective-permute-start.6 = (f32[72,384]{1,0:T(8,128)S(1)}, f32[72,384]{1,0:T(8,128)S(1)}, u32[]{:S(2)}, u32[]{:S(2)}) collective-permute-start(f32[72,384]{1,0:T(8,128)S(1)} %constant_dynamic-slice_fusion.1), channel_id=1, source_target_pairs={{0,4},{2,6},{4,0},{6,2},{8,12},{10,14},{12,8},{14,10},{1,5},{3,7},... | collective-permute-start | bytes 331784 | tf_op jit(solution)/shard_map/ppermute | solution.py:94
  100.0 9.7 %collective-permute-start.7 = (f32[36,384]{1,0:T(8,128)S(1)}, f32[36,384]{1,0:T(8,128)S(1)}, u32[]{:S(2)}, u32[]{:S(2)}) collective-permute-start(f32[36,384]{1,0:T(8,128)S(1)} %constant_dynamic-slice_fusion), channel_id=1, source_target_pairs={{0,8},{2,10},{4,12},{6,14},{8,0},{10,2},{12,4},{14,6},{1,9},{3,11}... | collective-permute-start | bytes 165896 | tf_op jit(solution)/shard_map/ppermute | solution.py:94
  109.7 6.2 %collective-permute-start.8 = (f32[36,384]{1,0:T(8,128)S(1)}, f32[36,384]{1,0:T(8,128)S(1)}, u32[]{:S(2)}, u32[]{:S(2)}) collective-permute-start(f32[36,384]{1,0:T(8,128)S(1)} %dynamic-slice_add_fusion.3), channel_id=1, source_target_pairs={{0,8},{2,10},{4,12},{6,14},{8,0},{10,2},{12,4},{14,6},{1,9},{3,11}... | collective-permute-start | bytes 165896 | tf_op jit(solution)/shard_map/ppermute | solution.py:94
  116.2 12.5 %copy-start.4 = (bf16[1,512,1536]{2,1,0:T(8,128)(2,1)S(1)}, bf16[1,512,1536]{2,1,0:T(8,128)(2,1)}, u32[]{:S(2)}) copy-start(bf16[1,512,1536]{2,1,0:T(8,128)(2,1)} %param.9) | copy-start | bytes 4718596
  116.3 5.0 %collective-permute-start.9 = (f32[72,384]{1,0:T(8,128)S(1)}, f32[72,384]{1,0:T(8,128)S(1)}, u32[]{:S(2)}, u32[]{:S(2)}) collective-permute-start(f32[72,384]{1,0:T(8,128)S(1)} %dynamic_update_slice.25), channel_id=1, source_target_pairs={{0,4},{2,6},{4,0},{6,2},{8,12},{10,14},{12,8},{14,10},{1,5},{3,7},... | collective-permute-start | bytes 331784 | tf_op jit(solution)/shard_map/ppermute | solution.py:94
  121.3 7.4 %collective-permute-start.10 = (f32[144,384]{1,0:T(8,128)S(1)}, f32[144,384]{1,0:T(8,128)S(1)}, u32[]{:S(2)}, u32[]{:S(2)}) collective-permute-start(f32[144,384]{1,0:T(8,128)S(1)} %constant_dynamic-update-slice_fusion.4), channel_id=1, source_target_pairs={{0,2},{2,0},{4,6},{6,4},{8,10},{10,8},{12,14},{14,12},{1,3},{3,1},... | collective-permute-start | bytes 663560 | tf_op jit(solution)/shard_map/ppermute | solution.py:94
  128.7 1.9 %collective-permute-start.11 = (f32[144,768]{1,0:T(8,128)S(1)}, f32[144,768]{1,0:T(8,128)S(1)}, u32[]{:S(2)}, u32[]{:S(2)}) collective-permute-start(f32[144,768]{1,0:T(8,128)S(1)} %constant_dynamic-update-slice_fusion.2), channel_id=1, source_target_pairs={{0,1},{1,0},{2,3},{3,2},{4,5},{5,4},{6,7},{7,6},{8,9},{9,8},{10,11... | collective-permute-start | bytes 1327112 | tf_op jit(solution)/shard_map/ppermute | solution.py:94
  (5 other events, 5.8 us)
Sparse Core Ops, SparseCore 0:
  35.6 118.7 reduce-scatter.1

commit v11 on v8

--- a/solution.py
+++ b/solution.py
@@ -1,3 +1,4 @@
+import functools
 import math
 
 import jax
@@ -133,13 +134,63 @@
     return held.reshape(shape)
 
 
-def point_gradient(act_rows, cot_rows):
+def ring_order(mesh):
+    count = mesh.shape["seq"]
+    names = mesh.axis_names
+    index = [0] * len(names)
+    cells = []
+    for s in range(count):
+        index[names.index("seq")] = s
+        coords = getattr(mesh.devices[tuple(index)], "coords", None)
+        if coords is None:
+            return False
+        cells.append((tuple(coords), s))
+    cells.sort(key=lambda cell: (cell[0][1], cell[0][2] if cell[0][1] % 2 == 0 else -cell[0][2]))
+    half = count // 2
+    snake = [2 * p if p < half else 2 * (count - 1 - p) + 1 for p in range(count)]
+    return count % 2 == 0 and [s for _, s in cells] == snake
+
+
+def ring_reduce_scatter(blocks, snake):
+    count = blocks.shape[0]
+    half_count = count // 2
+    if snake:
+        ring = [2 * p if p < half_count else 2 * (count - 1 - p) + 1 for p in range(count)]
+    else:
+        ring = list(range(count))
+    seq_index = lax.axis_index("seq")
+    if snake:
+        here = jnp.where(seq_index % 2 == 0, seq_index // 2, count - 1 - seq_index // 2)
+    else:
+        here = seq_index
+    cols = blocks.shape[2] // 2
+    forward = [(ring[i], ring[(i + 1) % count]) for i in range(count)]
+    backward = [(ring[i], ring[(i - 1) % count]) for i in range(count)]
+
+    def block(offset, low):
+        spot = (here + offset + count) % count
+        if snake:
+            owner = jnp.where(spot < half_count, 2 * spot, 2 * (count - 1 - spot) + 1)
+        else:
+            owner = spot
+        rows = lax.dynamic_index_in_dim(blocks, owner, axis=0, keepdims=False)
+        return rows[:, :cols] if low else rows[:, cols:]
+
+    ahead = block(-1, True)
+    behind = block(1, False)
+    for step in range(count - 1):
+        ahead = lax.ppermute(ahead, "seq", forward) + block(-2 - step, True)
+        behind = lax.ppermute(behind, "seq", backward) + block(2 + step, False)
+    return jnp.concatenate([ahead, behind], axis=1)
+
+
+def point_gradient(act_rows, cot_rows, scale, snake):
     chans = act_rows.shape[1]
     seq_count = lax.axis_size("seq")
     rep_count = lax.axis_size("rep")
     product = lambda a, b: lax.dot_general(
         a, b, (((0,), (0,)), ((), ())), preferred_element_type=jnp.float32
-    )
+    ) * scale
     if rep_count != 2:
         partial = product(act_rows, cot_rows)
         partial, cot_rows = lax.optimization_barrier((partial, cot_rows))
@@ -151,15 +202,15 @@
 
     def rows_of(owner):
         cols = lax.dynamic_index_in_dim(blocks, owner, axis=2, keepdims=False)
-        return product(cols.reshape(act_rows.shape[0], seq_count * block), cot_rows)
+        cols = cols.reshape(act_rows.shape[0], seq_count * block)
+        return product(cols, cot_rows).reshape(seq_count, block, chans)
 
     mine = rows_of(rep_index) + swap(rows_of(1 - rep_index), "rep", 1)
     mine, cot_rows = lax.optimization_barrier((mine, cot_rows))
-    total = lax.psum_scatter(mine, "seq", scatter_dimension=0, tiled=True)
-    return total, cot_rows
-
-
-def on_device(inputs, lengths, conv_weight, point_weight, cotangent):
+    return ring_reduce_scatter(mine, snake), cot_rows
+
+
+def on_device(snake, inputs, lengths, conv_weight, point_weight, cotangent):
     local_bins = inputs.shape[1]
     chans = inputs.shape[2]
     seq_count = lax.axis_size("seq")
@@ -179,7 +230,7 @@
     cot_rows = cotangent.reshape(local_bins, chans)
     proj = jnp.dot(act_rows, point_weight, preferred_element_type=jnp.float32).reshape(inputs.shape)
     output = (inputs.astype(jnp.float32) + proj).astype(jnp.bfloat16)
-    grad_point, cot_rows = point_gradient(act_rows, cot_rows)
+    grad_point, cot_rows = point_gradient(act_rows, cot_rows, scale, snake)
     back = lax.dot_general(
         cot_rows, point_weight, (((1,), (1,)), ((), ())), preferred_element_type=jnp.float32
     )
@@ -189,13 +240,12 @@
     conv_local = weight_taps(padded_input, preactivation_gradient, local_bins)
     grad_conv = tree_sum(conv_local) * scale
     grad_inputs = (cotangent.astype(jnp.float32) + mask3 * spread).astype(jnp.bfloat16)
-    grad_point = grad_point * scale
     return (output, grad_inputs, grad_point, grad_conv)
 
 
 def solution(mesh):
     return jax.shard_map(
-        on_device,
+        functools.partial(on_device, ring_order(mesh)),
         mesh=mesh,
         in_specs=(
             P(("groups", "rep"), "seq", None),

time: 190 us -> 155 us (0.82)
  waiting for transfers between devices: 84.3 us -> 51 us
  starting transfers between devices: 19.7 us -> 43.4 us
  matrix products: 49.7 us -> 32.7 us
  between operations: 15.5 us -> 2.36 us
  other arithmetic: 16.4 us -> 19.3 us
    reduce_scatter x1 -> x0, waiting for transfers between devices: 25.8 us -> none  [point_gradient(): total = lax.psum_scatter(mine, 'seq', scatter_dimension=0, tiled=True)]
    ppermute x0 -> x14, starting transfers between devices: none -> 23.9 us  [the longest x7 12.4 us: ring_reduce_scatter(): ahead = lax.ppermute(ahead, 'seq', forward) + block(-2 - step, True)]
    ppermute x0 -> x14, waiting for transfers between devices: none -> 19 us  [the longest x7 17.1 us: ring_reduce_scatter(): ahead = lax.ppermute(ahead, 'seq', forward) + block(-2 - step, True)]
    ppermute x9, waiting for transfers between devices: 34.6 us -> 18.5 us  [swap(): return lax.ppermute(value, axis, [(i, i ^ distance) for i in range(count)])]
    ppermute x2, waiting for transfers between devices: 9.3 us -> 0.31 us  [with_halo(): lax.ppermute(head, axis, [((i + 1) % count, i) for i in range(ends)])]
    add x0 -> x15, other arithmetic: none -> 6.59 us  [the longest x1 3.32 us: point_gradient(): mine = rows_of(rep_index) + swap(rows_of(1 - rep_index), 'rep', 1)]
    dot_general x12, matrix products: 10.7 us -> 4.89 us  [weight_taps(): lax.dot_general(window, grads[:, cols], (((0,), (0,)), ((), ())), preferr...]
    dot_general x24, matrix products: 15.1 us -> 11.5 us  [conv_taps(): lax.dot_general(window, dense[k, :, cols], dims, preferred_element_type=j...]
  transfers between devices with their start and end apart: 14 -> 27, of which waited for: 10 -> 14; matrix products, arithmetic and copies ran while one was open for 16% -> 19% of each run, Pallas kernels for 0% -> 0%
where the time goes in v11:
time: 155 us
  waiting for transfers between devices  51 us (33%)
  starting transfers between devices  43.4 us (28%)
  matrix products  32.7 us (21%)
  other arithmetic  19.3 us (12%)
  local copies, waits for them, and re-layouts  6.31 us (4%)
  between operations  2.36 us (2%)
    ppermute x9, waiting for transfers between devices, swap(): return lax.ppermute(value, axis, [(i, i ^ distance) for i in range(count)])  18.5 us
    ppermute x7, waiting for transfers between devices, ring_reduce_scatter(): ahead = lax.ppermute(ahead, 'seq', forward) + block(-2 - step, True)  17.1 us
    ppermute x2, waiting for transfers between devices, with_halo(): lax.ppermute(tail, axis, [(i, (i + 1) % count) for i in range(ends)])  13.2 us
    ppermute x7, starting transfers between devices, ring_reduce_scatter(): ahead = lax.ppermute(ahead, 'seq', forward) + block(-2 - step, True)  12.4 us
    dot_general x24, matrix products, conv_taps(): lax.dot_general(window, dense[k, :, cols], dims, preferred_element_type=j...  11.5 us
    ppermute x7, starting transfers between devices, ring_reduce_scatter(): behind = lax.ppermute(behind, 'seq', backward) + block(2 + step, False)  11.5 us
    ppermute x2, starting transfers between devices, with_halo(): lax.ppermute(tail, axis, [(i, (i + 1) % count) for i in range(ends)])  9.6 us
    ppermute x9, starting transfers between devices, swap(): return lax.ppermute(value, axis, [(i, i ^ distance) for i in range(count)])  7.29 us
  transfers between devices with their start and end apart: 27, of which 14 were waited for; matrix products, arithmetic and copies ran while one was open for 19% of the time, Pallas kernels for 0%

profile of v11, /device:TPU:0, one launch (start us, length us, event | category | flops | bytes accessed | tf_op | source)
XLA Modules:
  0.0 155.1 jit_solution(17717294308730226831)
XLA Ops:
  3.8 5.5 %collective-permute-start = (bf16[1,64,1536]{2,1,0:T(8,128)(2,1)}, bf16[1,64,1536]{2,1,0:T(8,128)(2,1)}, u32[]{:S(2)}, u32[]{:S(2)}) collective-permute-start(bf16[1,64,1536]{2,1,0:T(8,128)(2,1)} %get-tuple-element.40), channel_id=1, source_target_pairs={{0,2},{2,4},{4,6},{6,8},{8,10},{10,12},{12,14},{1,3},{3,5},{5,7},{... | collective-permute-start | bytes 589832 | tf_op jit(solution)/shard_map/ppermute | solution.py:21
  11.4 2.1 %bitcast_multiply_fusion = bf16[3,384,1536]{2,1,0:T(8,128)(2,1)} fusion(bf16[384,1536]{1,0:T(8,128)(2,1)S(1)} %fusion.13, bf16[3,48,1536]{2,1,0:T(8,128)(2,1)S(1)} %copy-done.22), kind=kLoop, calls=%fused_computation.8 | loop fusion | flops 1769472 | bytes 5160960 | tf_op jit(solution)/shard_map/mul | solution.py:49
  13.5 3.9 %collective-permute-done = bf16[1,64,1536]{2,1,0:T(8,128)(2,1)} collective-permute-done((bf16[1,64,1536]{2,1,0:T(8,128)(2,1)}, bf16[1,64,1536]{2,1,0:T(8,128)(2,1)}, u32[]{:S(2)}, u32[]{:S(2)}) %collective-permute-start) | collective-permute-done | bytes 196640 | tf_op jit(solution)/shard_map/ppermute | solution.py:21
  26.7 3.6 %convolution_multiply_fusion = f32[768,1536]{1,0:T(8,128)} fusion(bf16[512,768]{0,1:T(8,128)(2,1)S(1)} %bitcast.152, bf16[1,512,1536]{2,1,0:T(8,128)(2,1)S(1)} %copy-done.2), kind=kOutput, calls=%fused_computation.4 | convolution fusion | flops 1209139200 | bytes 7077888 | tf_op jit(solution)/shard_map/dot_general | solution.py:191
  30.4 2.7 %convolution_multiply_fusion.1 = f32[768,1536]{1,0:T(8,128)S(1)} fusion(bf16[512,768]{0,1:T(8,128)(2,1)} %bitcast.151, bf16[1,512,1536]{2,1,0:T(8,128)(2,1)S(1)} %copy-done.2), kind=kOutput, calls=%fused_computation.5 | convolution fusion | flops 1209139200 | bytes 7077888 | tf_op jit(solution)/shard_map/dot_general | solution.py:191
  33.1 6.2 %fusion.2 = bf16[1,512,1536]{2,1,0:T(8,128)(2,1)} fusion(bf16[1,512,1536]{2,1,0:T(8,128)(2,1)S(1)} %copy-done.11, bf16[1536,1536]{1,0:T(8,128)(2,1)} %param.8, f32[512]{0:T(512)S(1)} %fusion.112, f32[512,384]{0,1:T(8,128)S(1)} %copy-done.10, f32[512,384]{0,1:T(8,128)S(1)} %copy-done.8, f32[512,384]{0,1:T(8,128)S(1)} %copy-done.6, f32[512,384]{0,1:T(8,128)S(1)} %copy-done.4), kind=kOutput, calls=%fused_computation.14 | convolution fusion | flops 2425356288 | bytes 11012096 | tf_op jit(solution)/shard_map/dot_general | solution.py:231
  39.3 3.3 %add.488 = f32[8,96,1536]{2,1,0:T(8,128)S(1)} add(f32[8,96,1536]{2,1,0:T(8,128)S(1)} %bitcast.142, f32[8,96,1536]{2,1,0:T(8,128)} %collective-permute-done.2) | non-fusion elementwise | flops 1179648 | bytes 14155776 | tf_op jit(solution)/shard_map/add | solution.py:208
  42.7 3.9 %fusion.9 = bf16[512,1536]{0,1:T(8,128)(2,1)S(1)} fusion(bf16[512,1536]{1,0:T(8,128)(2,1)S(1)} %bitcast.143, bf16[1536,1536]{1,0:T(8,128)(2,1)S(1)} %bitcast.167, f32[512]{0:T(512)S(1)} %fusion.112, f32[512,384]{0,1:T(8,128)S(1)} %copy-done.10, f32[512,384]{0,1:T(8,128)S(1)} %copy-done.8, f32[512,384]{0,1:T(8,128)S(1)} %copy-done.6, ...), kind=kOutput, calls=%fused_computation.27 | convolution fusion | flops 2426929152 | bytes 11012096 | tf_op jit(solution)/shard_map/dot_general | solution.py:234
  53.4 4.1 %collective-permute-start.3 = (bf16[1,64,1536]{1,2,0:T(8,128)(2,1)S(1)}, bf16[1,64,1536]{1,2,0:T(8,128)(2,1)S(1)}, u32[]{:S(2)}, u32[]{:S(2)}) collective-permute-start(bf16[1,64,1536]{1,2,0:T(8,128)(2,1)S(1)} %get-tuple-element.36), channel_id=1, source_target_pairs={{0,2},{2,4},{4,6},{6,8},{8,10},{10,12},{12,14},{1,3},{3,5},{5,7},{... | collective-permute-start | bytes 589832 | tf_op jit(solution)/shard_map/ppermute | solution.py:21
  58.8 2.7 %dynamic-slice_bitcast_fusion.8 = (f32[96,1536]{1,0:T(8,128)}, f32[96,1536]{1,0:T(8,128)}, f32[96,1536]{1,0:T(8,128)}, f32[96,1536]{1,0:T(8,128)}, f32[96,1536]{...) fusion(f32[8,96,1536]{2,1,0:T(8,128)S(1)} %add.488, ...), kind=kLoop, calls=%fused_computation.80 | loop fusion | bytes 18874432 | tf_op jit(solution)/shard_map/jit(dynamic_index_in_dim)/squeeze | solution.py:176
  61.5 4.5 %collective-permute-start.5 = (f32[96,768]{1,0:T(8,128)S(1)}, f32[96,768]{1,0:T(8,128)S(1)}, u32[]{:S(2)}, u32[]{:S(2)}) collective-permute-start(f32[96,768]{1,0:T(8,128)S(1)} %slice.312), channel_id=1, source_target_pairs={{0,4},{4,8},{8,12},{12,14},{14,10},{10,6},{6,2},{2,0},{1,5},{5,9},... | collective-permute-start | bytes 884744 | tf_op jit(solution)/shard_map/ppermute | solution.py:182
  66.1 9.3 %collective-permute-done.3 = bf16[1,64,1536]{1,2,0:T(8,128)(2,1)S(1)} collective-permute-done((bf16[1,64,1536]{1,2,0:T(8,128)(2,1)S(1)}, bf16[1,64,1536]{1,2,0:T(8,128)(2,1)S(1)}, u32[]{:S(2)}, u32[]{:S(2)}) %collective-permute-start.3) | collective-permute-done | bytes 196640 | tf_op jit(solution)/shard_map/ppermute | solution.py:21
  84.8 3.4 %collective-permute-start.6 = (f32[96,768]{1,0:T(8,128)S(1)}, f32[96,768]{1,0:T(8,128)S(1)}, u32[]{:S(2)}, u32[]{:S(2)}) collective-permute-start(f32[96,768]{1,0:T(8,128)S(1)} %slice_add_fusion.13), channel_id=1, source_target_pairs={{0,4},{4,8},{8,12},{12,14},{14,10},{10,6},{6,2},{2,0},{1,5},{5,9},... | collective-permute-start | bytes 884744 | tf_op jit(solution)/shard_map/ppermute | solution.py:182
  90.5 6.9 %collective-permute-done.20 = f32[144,384]{1,0:T(8,128)S(1)} collective-permute-done((f32[144,384]{1,0:T(8,128)S(1)}, f32[144,384]{1,0:T(8,128)S(1)}, u32[]{:S(2)}, u32[]{:S(2)}) %collective-permute-start.20) | collective-permute-done | bytes 221216 | tf_op jit(solution)/shard_map/ppermute | solution.py:95
  99.7 2.6 %collective-permute-done.21 = f32[72,384]{1,0:T(8,128)S(1)} collective-permute-done((f32[72,384]{1,0:T(8,128)S(1)}, f32[72,384]{1,0:T(8,128)S(1)}, u32[]{:S(2)}, u32[]{:S(2)}) %collective-permute-start.21) | collective-permute-done | bytes 110624 | tf_op jit(solution)/shard_map/ppermute | solution.py:95
  102.4 3.7 %collective-permute-start.22 = (f32[36,384]{1,0:T(8,128)S(1)}, f32[36,384]{1,0:T(8,128)S(1)}, u32[]{:S(2)}, u32[]{:S(2)}) collective-permute-start(f32[36,384]{1,0:T(8,128)S(1)} %constant_dynamic-slice_fusion), channel_id=1, source_target_pairs={{0,8},{2,10},{4,12},{6,14},{8,0},{10,2},{12,4},{14,6},{1,9},{3,11}... | collective-permute-start | bytes 165896 | tf_op jit(solution)/shard_map/ppermute | solution.py:95
  106.8 2.6 %collective-permute-start.14 = (f32[96,768]{1,0:T(8,128)}, f32[96,768]{1,0:T(8,128)}, u32[]{:S(2)}, u32[]{:S(2)}) collective-permute-start(f32[96,768]{1,0:T(8,128)} %slice_add_fusion.5), channel_id=1, source_target_pairs={{0,2},{4,0},{8,4},{12,8},{14,12},{10,14},{6,10},{2,6},{1,3},{5,1},... | collective-permute-start | bytes 884744 | tf_op jit(solution)/shard_map/ppermute | solution.py:183
  111.9 6.1 %collective-permute-done.23 = f32[36,384]{1,0:T(8,128)S(1)} collective-permute-done((f32[36,384]{1,0:T(8,128)S(1)}, f32[36,384]{1,0:T(8,128)S(1)}, u32[]{:S(2)}, u32[]{:S(2)}) %collective-permute-start.23) | collective-permute-done | bytes 55328 | tf_op jit(solution)/shard_map/ppermute | solution.py:95
  119.5 2.1 %collective-permute-start.8 = (f32[96,768]{1,0:T(8,128)S(1)}, f32[96,768]{1,0:T(8,128)S(1)}, u32[]{:S(2)}, u32[]{:S(2)}) collective-permute-start(f32[96,768]{1,0:T(8,128)S(1)} %slice_add_fusion.11), channel_id=1, source_target_pairs={{0,4},{4,8},{8,12},{12,14},{14,10},{10,6},{6,2},{2,0},{1,5},{5,9},... | collective-permute-start | bytes 884744 | tf_op jit(solution)/shard_map/ppermute | solution.py:182
  125.3 4.4 %collective-permute-done.8 = f32[96,768]{1,0:T(8,128)S(1)} collective-permute-done((f32[96,768]{1,0:T(8,128)S(1)}, f32[96,768]{1,0:T(8,128)S(1)}, u32[]{:S(2)}, u32[]{:S(2)}) %collective-permute-start.8) | collective-permute-done | bytes 294944 | tf_op jit(solution)/shard_map/ppermute | solution.py:182
  135.1 2.5 %collective-permute-done.9 = f32[96,768]{1,0:T(8,128)S(1)} collective-permute-done((f32[96,768]{1,0:T(8,128)S(1)}, f32[96,768]{1,0:T(8,128)S(1)}, u32[]{:S(2)}, u32[]{:S(2)}) %collective-permute-start.9) | collective-permute-done | bytes 294944 | tf_op jit(solution)/shard_map/ppermute | solution.py:182
  138.3 2.4 %collective-permute-start.17 = (f32[96,768]{1,0:T(8,128)S(1)}, f32[96,768]{1,0:T(8,128)S(1)}, u32[]{:S(2)}, u32[]{:S(2)}) collective-permute-start(f32[96,768]{1,0:T(8,128)S(1)} %slice_add_fusion.2), channel_id=1, source_target_pairs={{0,2},{4,0},{8,4},{12,8},{14,12},{10,14},{6,10},{2,6},{1,3},{5,1},... | collective-permute-start | bytes 884744 | tf_op jit(solution)/shard_map/ppermute | solution.py:183
  140.7 4.7 %collective-permute-done.10 = f32[96,768]{1,0:T(8,128)S(1)} collective-permute-done((f32[96,768]{1,0:T(8,128)S(1)}, f32[96,768]{1,0:T(8,128)S(1)}, u32[]{:S(2)}, u32[]{:S(2)}) %collective-permute-start.10) | collective-permute-done | bytes 294944 | tf_op jit(solution)/shard_map/ppermute | solution.py:182
  148.6 5.5 %collective-permute-done.11 = f32[96,768]{1,0:T(8,128)S(1)} collective-permute-done((f32[96,768]{1,0:T(8,128)S(1)}, f32[96,768]{1,0:T(8,128)S(1)}, u32[]{:S(2)}, u32[]{:S(2)}) %collective-permute-start.11) | collective-permute-done | bytes 294944 | tf_op jit(solution)/shard_map/ppermute | solution.py:182
  (184 shorter events, 54.1 us)
Async XLA Ops:
  3.8 13.6 %collective-permute-start = (bf16[1,64,1536]{2,1,0:T(8,128)(2,1)}, bf16[1,64,1536]{2,1,0:T(8,128)(2,1)}, u32[]{:S(2)}, u32[]{:S(2)}) collective-permute-start(bf16[1,64,1536]{2,1,0:T(8,128)(2,1)} %get-tuple-element.40), channel_id=1, source_target_pairs={{0,2},{2,4},{4,6},{6,8},{8,10},{10,12},{12,14},{1,3},{3,5},{5,7},{... | collective-permute-start | bytes 589832 | tf_op jit(solution)/shard_map/ppermute | solution.py:21
  9.3 8.3 %collective-permute-start.1 = (bf16[1,64,1536]{2,1,0:T(8,128)(2,1)S(1)}, bf16[1,64,1536]{2,1,0:T(8,128)(2,1)}, u32[]{:S(2)}, u32[]{:S(2)}) collective-permute-start(bf16[1,64,1536]{2,1,0:T(8,128)(2,1)S(1)} %get-tuple-element.41), channel_id=1, source_target_pairs={{2,0},{4,2},{6,4},{8,6},{10,8},{12,10},{14,12},{3,1},{5,3},{7,5},{... | collective-permute-start | bytes 589832 | tf_op jit(solution)/shard_map/ppermute | solution.py:23
  30.3 9.1 %collective-permute-start.2 = (f32[8,96,1536]{2,1,0:T(8,128)}, f32[8,96,1536]{2,1,0:T(8,128)}, u32[]{:S(2)}, u32[]{:S(2)}) collective-permute-start(f32[8,96,1536]{2,1,0:T(8,128)} %bitcast.25), channel_id=1, source_target_pairs={{0,1},{1,0},{2,3},{3,2},{4,5},{5,4},{6,7},{7,6},{8,9},{9,8},{10,11... | collective-permute-start | bytes 14155784 | tf_op jit(solution)/shard_map/ppermute | solution.py:95
  52.6 35.6 %collective-permute-start.19 = (f32[144,768]{1,0:T(8,128)S(1)}, f32[144,768]{1,0:T(8,128)S(1)}, u32[]{:S(2)}, u32[]{:S(2)}) collective-permute-start(f32[144,768]{1,0:T(8,128)S(1)} %constant_dynamic-slice_fusion.3), channel_id=1, source_target_pairs={{0,1},{1,0},{2,3},{3,2},{4,5},{5,4},{6,7},{7,6},{8,9},{9,8},{10,11... | collective-permute-start | bytes 1327112 | tf_op jit(solution)/shard_map/ppermute | solution.py:95
  53.4 22.0 %collective-permute-start.3 = (bf16[1,64,1536]{1,2,0:T(8,128)(2,1)S(1)}, bf16[1,64,1536]{1,2,0:T(8,128)(2,1)S(1)}, u32[]{:S(2)}, u32[]{:S(2)}) collective-permute-start(bf16[1,64,1536]{1,2,0:T(8,128)(2,1)S(1)} %get-tuple-element.36), channel_id=1, source_target_pairs={{0,2},{2,4},{4,6},{6,8},{8,10},{10,12},{12,14},{1,3},{3,5},{5,7},{... | collective-permute-start | bytes 589832 | tf_op jit(solution)/shard_map/ppermute | solution.py:21
  57.5 17.9 %collective-permute-start.4 = (bf16[1,64,1536]{1,2,0:T(8,128)(2,1)S(1)}, bf16[1,64,1536]{1,2,0:T(8,128)(2,1)S(1)}, u32[]{:S(2)}, u32[]{:S(2)}) collective-permute-start(bf16[1,64,1536]{1,2,0:T(8,128)(2,1)S(1)} %get-tuple-element.37), channel_id=1, source_target_pairs={{2,0},{4,2},{6,4},{8,6},{10,8},{12,10},{14,12},{3,1},{5,3},{7,5},{... | collective-permute-start | bytes 589832 | tf_op jit(solution)/shard_map/ppermute | solution.py:23
  61.5 23.3 %collective-permute-start.5 = (f32[96,768]{1,0:T(8,128)S(1)}, f32[96,768]{1,0:T(8,128)S(1)}, u32[]{:S(2)}, u32[]{:S(2)}) collective-permute-start(f32[96,768]{1,0:T(8,128)S(1)} %slice.312), channel_id=1, source_target_pairs={{0,4},{4,8},{8,12},{12,14},{14,10},{10,6},{6,2},{2,0},{1,5},{5,9},... | collective-permute-start | bytes 884744 | tf_op jit(solution)/shard_map/ppermute | solution.py:182
  66.0 22.4 %collective-permute-start.12 = (f32[96,768]{1,0:T(8,128)S(1)}, f32[96,768]{1,0:T(8,128)S(1)}, u32[]{:S(2)}, u32[]{:S(2)}) collective-permute-start(f32[96,768]{1,0:T(8,128)S(1)} %slice.320), channel_id=1, source_target_pairs={{0,2},{4,0},{8,4},{12,8},{14,12},{10,14},{6,10},{2,6},{1,3},{5,1},... | collective-permute-start | bytes 884744 | tf_op jit(solution)/shard_map/ppermute | solution.py:183
  84.8 12.8 %collective-permute-start.6 = (f32[96,768]{1,0:T(8,128)S(1)}, f32[96,768]{1,0:T(8,128)S(1)}, u32[]{:S(2)}, u32[]{:S(2)}) collective-permute-start(f32[96,768]{1,0:T(8,128)S(1)} %slice_add_fusion.13), channel_id=1, source_target_pairs={{0,4},{4,8},{8,12},{12,14},{14,10},{10,6},{6,2},{2,0},{1,5},{5,9},... | collective-permute-start | bytes 884744 | tf_op jit(solution)/shard_map/ppermute | solution.py:182
  88.4 9.1 %collective-permute-start.20 = (f32[144,384]{1,0:T(8,128)S(1)}, f32[144,384]{1,0:T(8,128)S(1)}, u32[]{:S(2)}, u32[]{:S(2)}) collective-permute-start(f32[144,384]{1,0:T(8,128)S(1)} %constant_dynamic-slice_fusion.2), channel_id=1, source_target_pairs={{0,2},{2,0},{4,6},{6,4},{8,10},{10,8},{12,14},{14,12},{1,3},{3,1},... | collective-permute-start | bytes 663560 | tf_op jit(solution)/shard_map/ppermute | solution.py:95
  88.5 17.6 %collective-permute-start.13 = (f32[96,768]{1,0:T(8,128)S(1)}, f32[96,768]{1,0:T(8,128)S(1)}, u32[]{:S(2)}, u32[]{:S(2)}) collective-permute-start(f32[96,768]{1,0:T(8,128)S(1)} %slice_add_fusion.6), channel_id=1, source_target_pairs={{0,2},{4,0},{8,4},{12,8},{14,12},{10,14},{6,10},{2,6},{1,3},{5,1},... | collective-permute-start | bytes 884744 | tf_op jit(solution)/shard_map/ppermute | solution.py:183
  97.7 20.8 %collective-permute-start.7 = (f32[96,768]{1,0:T(8,128)S(1)}, f32[96,768]{1,0:T(8,128)}, u32[]{:S(2)}, u32[]{:S(2)}) collective-permute-start(f32[96,768]{1,0:T(8,128)S(1)} %slice_add_fusion.12), channel_id=1, source_target_pairs={{0,4},{4,8},{8,12},{12,14},{14,10},{10,6},{6,2},{2,0},{1,5},{5,9},... | collective-permute-start | bytes 884744 | tf_op jit(solution)/shard_map/ppermute | solution.py:182
  102.4 7.1 %collective-permute-start.22 = (f32[36,384]{1,0:T(8,128)S(1)}, f32[36,384]{1,0:T(8,128)S(1)}, u32[]{:S(2)}, u32[]{:S(2)}) collective-permute-start(f32[36,384]{1,0:T(8,128)S(1)} %constant_dynamic-slice_fusion), channel_id=1, source_target_pairs={{0,8},{2,10},{4,12},{6,14},{8,0},{10,2},{12,4},{14,6},{1,9},{3,11}... | collective-permute-start | bytes 165896 | tf_op jit(solution)/shard_map/ppermute | solution.py:95
  106.8 14.7 %collective-permute-start.14 = (f32[96,768]{1,0:T(8,128)}, f32[96,768]{1,0:T(8,128)}, u32[]{:S(2)}, u32[]{:S(2)}) collective-permute-start(f32[96,768]{1,0:T(8,128)} %slice_add_fusion.5), channel_id=1, source_target_pairs={{0,2},{4,0},{8,4},{12,8},{14,12},{10,14},{6,10},{2,6},{1,3},{5,1},... | collective-permute-start | bytes 884744 | tf_op jit(solution)/shard_map/ppermute | solution.py:183
  109.5 8.5 %collective-permute-start.23 = (f32[36,384]{1,0:T(8,128)S(1)}, f32[36,384]{1,0:T(8,128)S(1)}, u32[]{:S(2)}, u32[]{:S(2)}) collective-permute-start(f32[36,384]{1,0:T(8,128)S(1)} %dynamic-slice_add_fusion.3), channel_id=1, source_target_pairs={{0,8},{2,10},{4,12},{6,14},{8,0},{10,2},{12,4},{14,6},{1,9},{3,11}... | collective-permute-start | bytes 165896 | tf_op jit(solution)/shard_map/ppermute | solution.py:95
  119.5 10.2 %collective-permute-start.8 = (f32[96,768]{1,0:T(8,128)S(1)}, f32[96,768]{1,0:T(8,128)S(1)}, u32[]{:S(2)}, u32[]{:S(2)}) collective-permute-start(f32[96,768]{1,0:T(8,128)S(1)} %slice_add_fusion.11), channel_id=1, source_target_pairs={{0,4},{4,8},{8,12},{12,14},{14,10},{10,6},{6,2},{2,0},{1,5},{5,9},... | collective-permute-start | bytes 884744 | tf_op jit(solution)/shard_map/ppermute | solution.py:182
  122.6 8.8 %collective-permute-start.15 = (f32[96,768]{1,0:T(8,128)S(1)}, f32[96,768]{1,0:T(8,128)S(1)}, u32[]{:S(2)}, u32[]{:S(2)}) collective-permute-start(f32[96,768]{1,0:T(8,128)S(1)} %slice_add_fusion.4), channel_id=1, source_target_pairs={{0,2},{4,0},{8,4},{12,8},{14,12},{10,14},{6,10},{2,6},{1,3},{5,1},... | collective-permute-start | bytes 884744 | tf_op jit(solution)/shard_map/ppermute | solution.py:183
  124.4 10.5 %collective-permute-start.25 = (f32[144,384]{1,0:T(8,128)S(1)}, f32[144,384]{1,0:T(8,128)S(1)}, u32[]{:S(2)}, u32[]{:S(2)}) collective-permute-start(f32[144,384]{1,0:T(8,128)S(1)} %constant_dynamic-update-slice_fusion.4), channel_id=1, source_target_pairs={{0,2},{2,0},{4,6},{6,4},{8,10},{10,8},{12,14},{14,12},{1,3},{3,1},... | collective-permute-start | bytes 663560 | tf_op jit(solution)/shard_map/ppermute | solution.py:95
  129.8 7.9 %collective-permute-start.9 = (f32[96,768]{1,0:T(8,128)S(1)}, f32[96,768]{1,0:T(8,128)S(1)}, u32[]{:S(2)}, u32[]{:S(2)}) collective-permute-start(f32[96,768]{1,0:T(8,128)S(1)} %slice_add_fusion.10), channel_id=1, source_target_pairs={{0,4},{4,8},{8,12},{12,14},{14,10},{10,6},{6,2},{2,0},{1,5},{5,9},... | collective-permute-start | bytes 884744 | tf_op jit(solution)/shard_map/ppermute | solution.py:182
  131.4 6.8 %collective-permute-start.16 = (f32[96,768]{1,0:T(8,128)S(1)}, f32[96,768]{1,0:T(8,128)S(1)}, u32[]{:S(2)}, u32[]{:S(2)}) collective-permute-start(f32[96,768]{1,0:T(8,128)S(1)} %slice_add_fusion.3), channel_id=1, source_target_pairs={{0,2},{4,0},{8,4},{12,8},{14,12},{10,14},{6,10},{2,6},{1,3},{5,1},... | collective-permute-start | bytes 884744 | tf_op jit(solution)/shard_map/ppermute | solution.py:183
  137.7 7.7 %collective-permute-start.10 = (f32[96,768]{1,0:T(8,128)S(1)}, f32[96,768]{1,0:T(8,128)S(1)}, u32[]{:S(2)}, u32[]{:S(2)}) collective-permute-start(f32[96,768]{1,0:T(8,128)S(1)} %slice_add_fusion.9), channel_id=1, source_target_pairs={{0,4},{4,8},{8,12},{12,14},{14,10},{10,6},{6,2},{2,0},{1,5},{5,9},... | collective-permute-start | bytes 884744 | tf_op jit(solution)/shard_map/ppermute | solution.py:182
  138.3 7.3 %collective-permute-start.17 = (f32[96,768]{1,0:T(8,128)S(1)}, f32[96,768]{1,0:T(8,128)S(1)}, u32[]{:S(2)}, u32[]{:S(2)}) collective-permute-start(f32[96,768]{1,0:T(8,128)S(1)} %slice_add_fusion.2), channel_id=1, source_target_pairs={{0,2},{4,0},{8,4},{12,8},{14,12},{10,14},{6,10},{2,6},{1,3},{5,1},... | collective-permute-start | bytes 884744 | tf_op jit(solution)/shard_map/ppermute | solution.py:183
  145.5 8.7 %collective-permute-start.11 = (f32[96,768]{1,0:T(8,128)S(1)}, f32[96,768]{1,0:T(8,128)S(1)}, u32[]{:S(2)}, u32[]{:S(2)}) collective-permute-start(f32[96,768]{1,0:T(8,128)S(1)} %slice_add_fusion.8), channel_id=1, source_target_pairs={{0,4},{4,8},{8,12},{12,14},{14,10},{10,6},{6,2},{2,0},{1,5},{5,9},... | collective-permute-start | bytes 884744 | tf_op jit(solution)/shard_map/ppermute | solution.py:182
  145.6 8.6 %collective-permute-start.18 = (f32[96,768]{1,0:T(8,128)S(1)}, f32[96,768]{1,0:T(8,128)S(1)}, u32[]{:S(2)}, u32[]{:S(2)}) collective-permute-start(f32[96,768]{1,0:T(8,128)S(1)} %slice_add_fusion.1), channel_id=1, source_target_pairs={{0,2},{4,0},{8,4},{12,8},{14,12},{10,14},{6,10},{2,6},{1,3},{5,1},... | collective-permute-start | bytes 884744 | tf_op jit(solution)/shard_map/ppermute | solution.py:183
  (28 other events, 312.8 us)

commit v12 on v11

--- a/solution.py
+++ b/solution.py
@@ -151,7 +151,7 @@
     return count % 2 == 0 and [s for _, s in cells] == snake
 
 
-def ring_reduce_scatter(blocks, snake):
+def ring_reduce_scatter(blocks, snake, hold):
     count = blocks.shape[0]
     half_count = count // 2
     if snake:
@@ -181,10 +181,12 @@
     for step in range(count - 1):
         ahead = lax.ppermute(ahead, "seq", forward) + block(-2 - step, True)
         behind = lax.ppermute(behind, "seq", backward) + block(2 + step, False)
-    return jnp.concatenate([ahead, behind], axis=1)
-
-
-def point_gradient(act_rows, cot_rows, scale, snake):
+        if step == 0:
+            ahead, behind, hold = lax.optimization_barrier((ahead, behind, hold))
+    return jnp.concatenate([ahead, behind], axis=1), hold
+
+
+def point_gradient(act_rows, cot_rows, scale, snake, hold):
     chans = act_rows.shape[1]
     seq_count = lax.axis_size("seq")
     rep_count = lax.axis_size("rep")
@@ -193,9 +195,9 @@
     ) * scale
     if rep_count != 2:
         partial = product(act_rows, cot_rows)
-        partial, cot_rows = lax.optimization_barrier((partial, cot_rows))
+        partial, hold = lax.optimization_barrier((partial, hold))
         total = lax.psum_scatter(partial, ("seq", "rep"), scatter_dimension=0, tiled=True)
-        return total, cot_rows
+        return total, hold
     block = chans // (seq_count * rep_count)
     blocks = act_rows.reshape(act_rows.shape[0], seq_count, rep_count, block)
     rep_index = lax.axis_index("rep")
@@ -206,8 +208,7 @@
         return product(cols, cot_rows).reshape(seq_count, block, chans)
 
     mine = rows_of(rep_index) + swap(rows_of(1 - rep_index), "rep", 1)
-    mine, cot_rows = lax.optimization_barrier((mine, cot_rows))
-    return ring_reduce_scatter(mine, snake), cot_rows
+    return ring_reduce_scatter(mine, snake, hold)
 
 
 def on_device(snake, inputs, lengths, conv_weight, point_weight, cotangent):
@@ -230,10 +231,10 @@
     cot_rows = cotangent.reshape(local_bins, chans)
     proj = jnp.dot(act_rows, point_weight, preferred_element_type=jnp.float32).reshape(inputs.shape)
     output = (inputs.astype(jnp.float32) + proj).astype(jnp.bfloat16)
-    grad_point, cot_rows = point_gradient(act_rows, cot_rows, scale, snake)
     back = lax.dot_general(
         cot_rows, point_weight, (((1,), (1,)), ((), ())), preferred_element_type=jnp.float32
     )
+    grad_point, back = point_gradient(act_rows, cot_rows, scale, snake, back)
     preactivation_gradient = (back.reshape(inputs.shape) * slope * mask3).astype(jnp.bfloat16)
     padded_gradient = with_halo(preactivation_gradient, (("seq", 1),), DILATION_STEP)
     spread = conv_taps(padded_gradient, dense, local_bins, transpose=True)

time: 155 us -> 162 us (1.045)
  other arithmetic: 19.3 us -> 24.5 us
  local copies, waits for them, and re-layouts: 6.31 us -> 10.7 us
  starting transfers between devices: 43.4 us -> 39.6 us
    ppermute x7, waiting for transfers between devices: 17.1 us -> 2.69 us  [ring_reduce_scatter(): ahead = lax.ppermute(ahead, 'seq', forward) + block(-2 - step, True)]
    ppermute x7, starting transfers between devices: 12.4 us -> 5.92 us  [ring_reduce_scatter(): ahead = lax.ppermute(ahead, 'seq', forward) + block(-2 - step, True)]
    ppermute x9, waiting for transfers between devices: 18.5 us -> 24.7 us  [swap(): return lax.ppermute(value, axis, [(i, i ^ distance) for i in range(count)])]
    ppermute x7, waiting for transfers between devices: 1.84 us -> 7.72 us  [ring_reduce_scatter(): behind = lax.ppermute(behind, 'seq', backward) + block(2 + step, False)]
    ppermute x2, waiting for transfers between devices: 0.31 us -> 4.11 us  [with_halo(): lax.ppermute(head, axis, [((i + 1) % count, i) for i in range(ends)])]
    optimization_barrier x0 -> x1, local copies, waits for them, and re-layouts: none -> 3.52 us  [ring_reduce_scatter(): ahead, behind, hold = lax.optimization_barrier((ahead, behind, hold))]
    ppermute x7, starting transfers between devices: 11.5 us -> 15 us  [ring_reduce_scatter(): behind = lax.ppermute(behind, 'seq', backward) + block(2 + step, False)]
    convert_element_type x0 -> x1, other arithmetic: none -> 3.47 us  [on_device(): (back.reshape(inputs.shape) * slope * mask3).astype(jnp.bfloat16)]
  transfers between devices with their start and end apart: 27 -> 27, of which waited for: 14 -> 16; matrix products, arithmetic and copies ran while one was open for 19% -> 21% of each run, Pallas kernels for 0% -> 0%
where the time goes in v12:
time: 162 us
  waiting for transfers between devices  50.7 us (31%)
  starting transfers between devices  39.6 us (24%)
  matrix products  34.1 us (21%)
  other arithmetic  24.5 us (15%)
  local copies, waits for them, and re-layouts  10.7 us (7%)
  between operations  2.38 us (1%)
    ppermute x9, waiting for transfers between devices, swap(): return lax.ppermute(value, axis, [(i, i ^ distance) for i in range(count)])  24.7 us
    ppermute x7, starting transfers between devices, ring_reduce_scatter(): behind = lax.ppermute(behind, 'seq', backward) + block(2 + step, False)  15 us
    dot_general x24, matrix products, conv_taps(): lax.dot_general(window, dense[k, :, cols], dims, preferred_element_type=j...  11.5 us
    ppermute x2, waiting for transfers between devices, with_halo(): lax.ppermute(tail, axis, [(i, (i + 1) % count) for i in range(ends)])  11.4 us
    ppermute x2, starting transfers between devices, with_halo(): lax.ppermute(tail, axis, [(i, (i + 1) % count) for i in range(ends)])  10.8 us
    ppermute x7, waiting for transfers between devices, ring_reduce_scatter(): behind = lax.ppermute(behind, 'seq', backward) + block(2 + step, False)  7.72 us
    dot_general x1, matrix products, on_device(): lax.dot_general(cot_rows, point_weight, (((1,), (1,)), ((), ())), preferr...  6.67 us
    dot_general x1, matrix products, on_device(): jnp.dot(act_rows, point_weight, preferred_element_type=jnp.float32)  6.1 us
  transfers between devices with their start and end apart: 27, of which 16 were waited for; matrix products, arithmetic and copies ran while one was open for 21% of the time, Pallas kernels for 0%

profile of v12, /device:TPU:0, one launch (start us, length us, event | category | flops | bytes accessed | tf_op | source)
XLA Modules:
  0.0 161.9 jit_solution(9544031246471562213)
XLA Ops:
  5.1 6.2 %collective-permute-start = (bf16[1,64,1536]{2,1,0:T(8,128)(2,1)S(1)}, bf16[1,64,1536]{2,1,0:T(8,128)(2,1)}, u32[]{:S(2)}, u32[]{:S(2)}) collective-permute-start(bf16[1,64,1536]{2,1,0:T(8,128)(2,1)S(1)} %get-tuple-element.42), channel_id=1, source_target_pairs={{0,2},{2,4},{4,6},{6,8},{8,10},{10,12},{12,14},{1,3},{3,5},{5,7},{... | collective-permute-start | bytes 589832 | tf_op jit(solution)/shard_map/ppermute | solution.py:21
  14.1 4.0 %collective-permute-done = bf16[1,64,1536]{2,1,0:T(8,128)(2,1)} collective-permute-done((bf16[1,64,1536]{2,1,0:T(8,128)(2,1)S(1)}, bf16[1,64,1536]{2,1,0:T(8,128)(2,1)}, u32[]{:S(2)}, u32[]{:S(2)}) %collective-permute-start) | collective-permute-done | bytes 196640 | tf_op jit(solution)/shard_map/ppermute | solution.py:21
  27.1 3.6 %convolution_multiply_fusion = f32[768,1536]{1,0:T(8,128)} fusion(bf16[512,768]{0,1:T(8,128)(2,1)S(1)} %bitcast.152, bf16[1,512,1536]{2,1,0:T(8,128)(2,1)S(1)} %copy-done.2), kind=kOutput, calls=%fused_computation.4 | convolution fusion | flops 1209139200 | bytes 7077888 | tf_op jit(solution)/shard_map/dot_general | solution.py:193
  31.9 6.7 %fusion.16 = f32[512,1536]{1,0:T(8,128)} fusion(bf16[1536,1536]{1,0:T(8,128)(2,1)} %param.8, bf16[1,512,1536]{2,1,0:T(8,128)(2,1)S(1)} %copy-done.2), kind=kOutput, calls=%fused_computation.35 | convolution fusion | flops 2415919104 | bytes 9437184 | tf_op jit(solution)/shard_map/dot_general | solution.py:234
  40.0 3.3 %add.488 = f32[8,96,1536]{2,1,0:T(8,128)S(1)} add(f32[8,96,1536]{2,1,0:T(8,128)S(1)} %bitcast.143, f32[8,96,1536]{2,1,0:T(8,128)} %collective-permute-done.2) | non-fusion elementwise | flops 1179648 | bytes 14155776 | tf_op jit(solution)/shard_map/add | solution.py:210
  43.4 3.6 %dynamic-slice_bitcast_fusion.6 = (f32[96,1536]{1,0:T(8,128)}, f32[96,1536]{1,0:T(8,128)}, f32[96,1536]{1,0:T(8,128)}, f32[96,1536]{1,0:T(8,128)}, f32[96,1536]{...) fusion(f32[8,96,1536]{2,1,0:T(8,128)S(1)} %add.488, ...), kind=kLoop, calls=%fused_computation.82 | loop fusion | bytes 18874432 | tf_op jit(solution)/shard_map/jit(dynamic_index_in_dim)/squeeze | solution.py:176
  50.0 6.1 %fusion.1 = bf16[1,512,1536]{2,1,0:T(8,128)(2,1)} fusion(bf16[1,512,1536]{2,1,0:T(8,128)(2,1)S(1)} %copy-done.12, bf16[1536,1536]{1,0:T(8,128)(2,1)} %param.8, f32[512]{0:T(512)S(1)} %fusion.117, f32[512,384]{0,1:T(8,128)S(1)} %copy-done.4, f32[512,384]{0,1:T(8,128)S(1)} %copy-done.6, f32[512,384]{0,1:T(8,128)S(1)} %copy-done.8, f32[512,384]{0,1:T(8,128)S(1)} %copy-done.10), kind=kOutput, calls=%fused_computation.12 | convolution fusion | flops 2425356288 | bytes 11012096 | tf_op jit(solution)/shard_map/dot_general | solution.py:232
  59.0 3.5 %copy.9 = f32[512,1536]{0,1:T(8,128)} copy(f32[512,1536]{1,0:T(8,128)} %fusion.16) | data formatting | bytes 6291456 | tf_op jit(solution)/shard_map/optimization_barrier | solution.py:185
  62.5 3.5 %fusion.8 = bf16[512,1536]{0,1:T(8,128)(2,1)S(1)} fusion(f32[512,1536]{0,1:T(8,128)} %copy.9, f32[512]{0:T(512)S(1)} %fusion.117, f32[512,384]{0,1:T(8,128)} %copy-done.3, f32[512,384]{0,1:T(8,128)} %copy-done.5, f32[512,384]{0,1:T(8,128)} %copy-done.7, f32[512,384]{0,1:T(8,128)} %copy-done.9), kind=kLoop, calls=%fused_computation.19 | loop fusion | flops 11010048 | bytes 7866368 | tf_op jit(solution)/shard_map/convert_element_type | solution.py:238
  72.5 4.6 %collective-permute-start.5 = (bf16[1,64,1536]{1,2,0:T(8,128)(2,1)S(1)}, bf16[1,64,1536]{1,2,0:T(8,128)(2,1)S(1)}, u32[]{:S(2)}, u32[]{:S(2)}) collective-permute-start(bf16[1,64,1536]{1,2,0:T(8,128)(2,1)S(1)} %get-tuple-element.38), channel_id=1, source_target_pairs={{0,2},{2,4},{4,6},{6,8},{8,10},{10,12},{12,14},{1,3},{3,5},{5,7},{... | collective-permute-start | bytes 589832 | tf_op jit(solution)/shard_map/ppermute | solution.py:21
  77.1 2.7 %collective-permute-start.13 = (f32[96,768]{1,0:T(8,128)S(1)}, f32[96,768]{1,0:T(8,128)S(1)}, u32[]{:S(2)}, u32[]{:S(2)}) collective-permute-start(f32[96,768]{1,0:T(8,128)S(1)} %copy-done.27), channel_id=1, source_target_pairs={{0,2},{4,0},{8,4},{12,8},{14,12},{10,14},{6,10},{2,6},{1,3},{5,1},... | collective-permute-start | bytes 884744 | tf_op jit(solution)/shard_map/ppermute | solution.py:183
  81.0 4.1 %collective-permute-done.6 = bf16[1,64,1536]{1,2,0:T(8,128)(2,1)S(1)} collective-permute-done((bf16[1,64,1536]{1,2,0:T(8,128)(2,1)S(1)}, bf16[1,64,1536]{1,2,0:T(8,128)(2,1)S(1)}, u32[]{:S(2)}, u32[]{:S(2)}) %collective-permute-start.6) | collective-permute-done | bytes 196640 | tf_op jit(solution)/shard_map/ppermute | solution.py:23
  85.1 7.4 %collective-permute-done.5 = bf16[1,64,1536]{1,2,0:T(8,128)(2,1)S(1)} collective-permute-done((bf16[1,64,1536]{1,2,0:T(8,128)(2,1)S(1)}, bf16[1,64,1536]{1,2,0:T(8,128)(2,1)S(1)}, u32[]{:S(2)}, u32[]{:S(2)}) %collective-permute-start.5) | collective-permute-done | bytes 196640 | tf_op jit(solution)/shard_map/ppermute | solution.py:21
  102.0 2.5 %collective-permute-start.14 = (f32[96,768]{1,0:T(8,128)S(1)}, f32[96,768]{1,0:T(8,128)S(1)}, u32[]{:S(2)}, u32[]{:S(2)}) collective-permute-start(f32[96,768]{1,0:T(8,128)S(1)} %slice_add_fusion.5), channel_id=1, source_target_pairs={{0,2},{4,0},{8,4},{12,8},{14,12},{10,14},{6,10},{2,6},{1,3},{5,1},... | collective-permute-start | bytes 884744 | tf_op jit(solution)/shard_map/ppermute | solution.py:183
  107.8 7.8 %collective-permute-done.20 = f32[144,384]{1,0:T(8,128)S(1)} collective-permute-done((f32[144,384]{1,0:T(8,128)S(1)}, f32[144,384]{1,0:T(8,128)S(1)}, u32[]{:S(2)}, u32[]{:S(2)}) %collective-permute-start.20) | collective-permute-done | bytes 221216 | tf_op jit(solution)/shard_map/ppermute | solution.py:95
  115.8 2.5 %collective-permute-start.15 = (f32[96,768]{1,0:T(8,128)S(1)}, f32[96,768]{1,0:T(8,128)S(1)}, u32[]{:S(2)}, u32[]{:S(2)}) collective-permute-start(f32[96,768]{1,0:T(8,128)S(1)} %slice_add_fusion.4), channel_id=1, source_target_pairs={{0,2},{4,0},{8,4},{12,8},{14,12},{10,14},{6,10},{2,6},{1,3},{5,1},... | collective-permute-start | bytes 884744 | tf_op jit(solution)/shard_map/ppermute | solution.py:183
  118.4 3.4 %collective-permute-done.21 = f32[72,384]{1,0:T(8,128)S(1)} collective-permute-done((f32[72,384]{1,0:T(8,128)S(1)}, f32[72,384]{1,0:T(8,128)S(1)}, u32[]{:S(2)}, u32[]{:S(2)}) %collective-permute-start.21) | collective-permute-done | bytes 110624 | tf_op jit(solution)/shard_map/ppermute | solution.py:95
  124.8 3.6 %collective-permute-done.22 = f32[36,384]{1,0:T(8,128)S(1)} collective-permute-done((f32[36,384]{1,0:T(8,128)S(1)}, f32[36,384]{1,0:T(8,128)S(1)}, u32[]{:S(2)}, u32[]{:S(2)}) %collective-permute-start.22) | collective-permute-done | bytes 55328 | tf_op jit(solution)/shard_map/ppermute | solution.py:95
  129.0 4.7 %collective-permute-done.23 = f32[36,384]{1,0:T(8,128)S(1)} collective-permute-done((f32[36,384]{1,0:T(8,128)S(1)}, f32[36,384]{1,0:T(8,128)S(1)}, u32[]{:S(2)}, u32[]{:S(2)}) %collective-permute-start.23) | collective-permute-done | bytes 55328 | tf_op jit(solution)/shard_map/ppermute | solution.py:95
  138.9 3.4 %collective-permute-start.25 = (f32[144,384]{1,0:T(8,128)S(1)}, f32[144,384]{1,0:T(8,128)S(1)}, u32[]{:S(2)}, u32[]{:S(2)}) collective-permute-start(f32[144,384]{1,0:T(8,128)S(1)} %constant_dynamic-update-slice_fusion.4), channel_id=1, source_target_pairs={{0,2},{2,0},{4,6},{6,4},{8,10},{10,8},{12,14},{14,12},{1,3},{3,1},... | collective-permute-start | bytes 663560 | tf_op jit(solution)/shard_map/ppermute | solution.py:95
  142.3 2.2 %collective-permute-done.16 = f32[96,768]{1,0:T(8,128)S(1)} collective-permute-done((f32[96,768]{1,0:T(8,128)S(1)}, f32[96,768]{1,0:T(8,128)S(1)}, u32[]{:S(2)}, u32[]{:S(2)}) %collective-permute-start.16) | collective-permute-done | bytes 294944 | tf_op jit(solution)/shard_map/ppermute | solution.py:183
  147.1 3.9 %collective-permute-done.25 = f32[144,384]{1,0:T(8,128)S(1)} collective-permute-done((f32[144,384]{1,0:T(8,128)S(1)}, f32[144,384]{1,0:T(8,128)S(1)}, u32[]{:S(2)}, u32[]{:S(2)}) %collective-permute-start.25) | collective-permute-done | bytes 221216 | tf_op jit(solution)/shard_map/ppermute | solution.py:95
  151.4 2.5 %collective-permute-start.18 = (f32[96,768]{1,0:T(8,128)S(1)}, f32[96,768]{1,0:T(8,128)S(1)}, u32[]{:S(2)}, u32[]{:S(2)}) collective-permute-start(f32[96,768]{1,0:T(8,128)S(1)} %slice_add_fusion.1), channel_id=1, source_target_pairs={{0,2},{4,0},{8,4},{12,8},{14,12},{10,14},{6,10},{2,6},{1,3},{5,1},... | collective-permute-start | bytes 884744 | tf_op jit(solution)/shard_map/ppermute | solution.py:183
  155.3 5.4 %collective-permute-done.18 = f32[96,768]{1,0:T(8,128)S(1)} collective-permute-done((f32[96,768]{1,0:T(8,128)S(1)}, f32[96,768]{1,0:T(8,128)S(1)}, u32[]{:S(2)}, u32[]{:S(2)}) %collective-permute-start.18) | collective-permute-done | bytes 294944 | tf_op jit(solution)/shard_map/ppermute | solution.py:183
  (199 shorter events, 58.4 us)
Async XLA Ops:
  3.8 10.3 %collective-permute-start.1 = (bf16[1,64,1536]{2,1,0:T(8,128)(2,1)}, bf16[1,64,1536]{2,1,0:T(8,128)(2,1)}, u32[]{:S(2)}, u32[]{:S(2)}) collective-permute-start(bf16[1,64,1536]{2,1,0:T(8,128)(2,1)} %get-tuple-element.43), channel_id=1, source_target_pairs={{2,0},{4,2},{6,4},{8,6},{10,8},{12,10},{14,12},{3,1},{5,3},{7,5},{... | collective-permute-start | bytes 589832 | tf_op jit(solution)/shard_map/ppermute | solution.py:23
  5.1 13.0 %collective-permute-start = (bf16[1,64,1536]{2,1,0:T(8,128)(2,1)S(1)}, bf16[1,64,1536]{2,1,0:T(8,128)(2,1)}, u32[]{:S(2)}, u32[]{:S(2)}) collective-permute-start(bf16[1,64,1536]{2,1,0:T(8,128)(2,1)S(1)} %get-tuple-element.42), channel_id=1, source_target_pairs={{0,2},{2,4},{4,6},{6,8},{8,10},{10,12},{12,14},{1,3},{3,5},{5,7},{... | collective-permute-start | bytes 589832 | tf_op jit(solution)/shard_map/ppermute | solution.py:21
  30.7 9.3 %collective-permute-start.2 = (f32[8,96,1536]{2,1,0:T(8,128)}, f32[8,96,1536]{2,1,0:T(8,128)}, u32[]{:S(2)}, u32[]{:S(2)}) collective-permute-start(f32[8,96,1536]{2,1,0:T(8,128)} %bitcast.25), channel_id=1, source_target_pairs={{0,1},{1,0},{2,3},{3,2},{4,5},{5,4},{6,7},{7,6},{8,9},{9,8},{10,11... | collective-permute-start | bytes 14155784 | tf_op jit(solution)/shard_map/ppermute | solution.py:95
  47.0 10.5 %collective-permute-start.3 = (f32[96,768]{1,0:T(8,128)S(1)}, f32[96,768]{1,0:T(8,128)S(1)}, u32[]{:S(2)}, u32[]{:S(2)}) collective-permute-start(f32[96,768]{1,0:T(8,128)S(1)} %slice.298), channel_id=1, source_target_pairs={{0,4},{4,8},{8,12},{12,14},{14,10},{10,6},{6,2},{2,0},{1,5},{5,9},... | collective-permute-start | bytes 884744 | tf_op jit(solution)/shard_map/ppermute | solution.py:182
  49.0 9.2 %collective-permute-start.4 = (f32[96,768]{1,0:T(8,128)S(1)}, f32[96,768]{1,0:T(8,128)S(1)}, u32[]{:S(2)}, u32[]{:S(2)}) collective-permute-start(f32[96,768]{1,0:T(8,128)S(1)} %slice.300), channel_id=1, source_target_pairs={{0,2},{4,0},{8,4},{12,8},{14,12},{10,14},{6,10},{2,6},{1,3},{5,1},... | collective-permute-start | bytes 884744 | tf_op jit(solution)/shard_map/ppermute | solution.py:183
  71.2 13.9 %collective-permute-start.6 = (bf16[1,64,1536]{1,2,0:T(8,128)(2,1)S(1)}, bf16[1,64,1536]{1,2,0:T(8,128)(2,1)S(1)}, u32[]{:S(2)}, u32[]{:S(2)}) collective-permute-start(bf16[1,64,1536]{1,2,0:T(8,128)(2,1)S(1)} %get-tuple-element.39), channel_id=1, source_target_pairs={{2,0},{4,2},{6,4},{8,6},{10,8},{12,10},{14,12},{3,1},{5,3},{7,5},{... | collective-permute-start | bytes 589832 | tf_op jit(solution)/shard_map/ppermute | solution.py:23
  72.5 20.0 %collective-permute-start.5 = (bf16[1,64,1536]{1,2,0:T(8,128)(2,1)S(1)}, bf16[1,64,1536]{1,2,0:T(8,128)(2,1)S(1)}, u32[]{:S(2)}, u32[]{:S(2)}) collective-permute-start(bf16[1,64,1536]{1,2,0:T(8,128)(2,1)S(1)} %get-tuple-element.38), channel_id=1, source_target_pairs={{0,2},{2,4},{4,6},{6,8},{8,10},{10,12},{12,14},{1,3},{3,5},{5,7},{... | collective-permute-start | bytes 589832 | tf_op jit(solution)/shard_map/ppermute | solution.py:21
  77.1 24.8 %collective-permute-start.13 = (f32[96,768]{1,0:T(8,128)S(1)}, f32[96,768]{1,0:T(8,128)S(1)}, u32[]{:S(2)}, u32[]{:S(2)}) collective-permute-start(f32[96,768]{1,0:T(8,128)S(1)} %copy-done.27), channel_id=1, source_target_pairs={{0,2},{4,0},{8,4},{12,8},{14,12},{10,14},{6,10},{2,6},{1,3},{5,1},... | collective-permute-start | bytes 884744 | tf_op jit(solution)/shard_map/ppermute | solution.py:183
  79.8 26.4 %collective-permute-start.7 = (f32[96,768]{1,0:T(8,128)S(1)}, f32[96,768]{1,0:T(8,128)S(1)}, u32[]{:S(2)}, u32[]{:S(2)}) collective-permute-start(f32[96,768]{1,0:T(8,128)S(1)} %copy-done.26), channel_id=1, source_target_pairs={{0,4},{4,8},{8,12},{12,14},{14,10},{10,6},{6,2},{2,0},{1,5},{5,9},... | collective-permute-start | bytes 884744 | tf_op jit(solution)/shard_map/ppermute | solution.py:182
  80.9 23.6 %collective-permute-start.19 = (f32[144,768]{1,0:T(8,128)S(1)}, f32[144,768]{1,0:T(8,128)S(1)}, u32[]{:S(2)}, u32[]{:S(2)}) collective-permute-start(f32[144,768]{1,0:T(8,128)S(1)} %constant_dynamic-slice_fusion.3), channel_id=1, source_target_pairs={{0,1},{1,0},{2,3},{3,2},{4,5},{5,4},{6,7},{7,6},{8,9},{9,8},{10,11... | collective-permute-start | bytes 1327112 | tf_op jit(solution)/shard_map/ppermute | solution.py:95
  102.0 13.8 %collective-permute-start.14 = (f32[96,768]{1,0:T(8,128)S(1)}, f32[96,768]{1,0:T(8,128)S(1)}, u32[]{:S(2)}, u32[]{:S(2)}) collective-permute-start(f32[96,768]{1,0:T(8,128)S(1)} %slice_add_fusion.5), channel_id=1, source_target_pairs={{0,2},{4,0},{8,4},{12,8},{14,12},{10,14},{6,10},{2,6},{1,3},{5,1},... | collective-permute-start | bytes 884744 | tf_op jit(solution)/shard_map/ppermute | solution.py:183
  104.6 11.0 %collective-permute-start.20 = (f32[144,384]{1,0:T(8,128)S(1)}, f32[144,384]{1,0:T(8,128)S(1)}, u32[]{:S(2)}, u32[]{:S(2)}) collective-permute-start(f32[144,384]{1,0:T(8,128)S(1)} %constant_dynamic-slice_fusion.2), channel_id=1, source_target_pairs={{0,2},{2,0},{4,6},{6,4},{8,10},{10,8},{12,14},{14,12},{1,3},{3,1},... | collective-permute-start | bytes 663560 | tf_op jit(solution)/shard_map/ppermute | solution.py:95
  106.2 15.7 %collective-permute-start.8 = (f32[96,768]{1,0:T(8,128)S(1)}, f32[96,768]{1,0:T(8,128)S(1)}, u32[]{:S(2)}, u32[]{:S(2)}) collective-permute-start(f32[96,768]{1,0:T(8,128)S(1)} %slice_add_fusion.11), channel_id=1, source_target_pairs={{0,4},{4,8},{8,12},{12,14},{14,10},{10,6},{6,2},{2,0},{1,5},{5,9},... | collective-permute-start | bytes 884744 | tf_op jit(solution)/shard_map/ppermute | solution.py:182
  115.7 6.1 %collective-permute-start.21 = (f32[72,384]{1,0:T(8,128)S(1)}, f32[72,384]{1,0:T(8,128)S(1)}, u32[]{:S(2)}, u32[]{:S(2)}) collective-permute-start(f32[72,384]{1,0:T(8,128)S(1)} %constant_dynamic-slice_fusion.1), channel_id=1, source_target_pairs={{0,4},{2,6},{4,0},{6,2},{8,12},{10,14},{12,8},{14,10},{1,5},{3,7},... | collective-permute-start | bytes 331784 | tf_op jit(solution)/shard_map/ppermute | solution.py:95
  115.8 18.3 %collective-permute-start.15 = (f32[96,768]{1,0:T(8,128)S(1)}, f32[96,768]{1,0:T(8,128)S(1)}, u32[]{:S(2)}, u32[]{:S(2)}) collective-permute-start(f32[96,768]{1,0:T(8,128)S(1)} %slice_add_fusion.4), channel_id=1, source_target_pairs={{0,2},{4,0},{8,4},{12,8},{14,12},{10,14},{6,10},{2,6},{1,3},{5,1},... | collective-permute-start | bytes 884744 | tf_op jit(solution)/shard_map/ppermute | solution.py:183
  121.8 6.6 %collective-permute-start.22 = (f32[36,384]{1,0:T(8,128)S(1)}, f32[36,384]{1,0:T(8,128)S(1)}, u32[]{:S(2)}, u32[]{:S(2)}) collective-permute-start(f32[36,384]{1,0:T(8,128)S(1)} %constant_dynamic-slice_fusion), channel_id=1, source_target_pairs={{0,8},{2,10},{4,12},{6,14},{8,0},{10,2},{12,4},{14,6},{1,9},{3,11}... | collective-permute-start | bytes 165896 | tf_op jit(solution)/shard_map/ppermute | solution.py:95
  122.6 13.7 %collective-permute-start.9 = (f32[96,768]{1,0:T(8,128)}, f32[96,768]{1,0:T(8,128)}, u32[]{:S(2)}, u32[]{:S(2)}) collective-permute-start(f32[96,768]{1,0:T(8,128)} %slice_add_fusion.10), channel_id=1, source_target_pairs={{0,4},{4,8},{8,12},{12,14},{14,10},{10,6},{6,2},{2,0},{1,5},{5,9},... | collective-permute-start | bytes 884744 | tf_op jit(solution)/shard_map/ppermute | solution.py:182
  134.2 10.3 %collective-permute-start.16 = (f32[96,768]{1,0:T(8,128)S(1)}, f32[96,768]{1,0:T(8,128)S(1)}, u32[]{:S(2)}, u32[]{:S(2)}) collective-permute-start(f32[96,768]{1,0:T(8,128)S(1)} %slice_add_fusion.3), channel_id=1, source_target_pairs={{0,2},{4,0},{8,4},{12,8},{14,12},{10,14},{6,10},{2,6},{1,3},{5,1},... | collective-permute-start | bytes 884744 | tf_op jit(solution)/shard_map/ppermute | solution.py:183
  137.4 9.5 %collective-permute-start.10 = (f32[96,768]{1,0:T(8,128)S(1)}, f32[96,768]{1,0:T(8,128)S(1)}, u32[]{:S(2)}, u32[]{:S(2)}) collective-permute-start(f32[96,768]{1,0:T(8,128)S(1)} %slice_add_fusion.9), channel_id=1, source_target_pairs={{0,4},{4,8},{8,12},{12,14},{14,10},{10,6},{6,2},{2,0},{1,5},{5,9},... | collective-permute-start | bytes 884744 | tf_op jit(solution)/shard_map/ppermute | solution.py:182
  138.9 12.2 %collective-permute-start.25 = (f32[144,384]{1,0:T(8,128)S(1)}, f32[144,384]{1,0:T(8,128)S(1)}, u32[]{:S(2)}, u32[]{:S(2)}) collective-permute-start(f32[144,384]{1,0:T(8,128)S(1)} %constant_dynamic-update-slice_fusion.4), channel_id=1, source_target_pairs={{0,2},{2,0},{4,6},{6,4},{8,10},{10,8},{12,14},{14,12},{1,3},{3,1},... | collective-permute-start | bytes 663560 | tf_op jit(solution)/shard_map/ppermute | solution.py:95
  144.5 6.8 %collective-permute-start.17 = (f32[96,768]{1,0:T(8,128)S(1)}, f32[96,768]{1,0:T(8,128)S(1)}, u32[]{:S(2)}, u32[]{:S(2)}) collective-permute-start(f32[96,768]{1,0:T(8,128)S(1)} %slice_add_fusion.2), channel_id=1, source_target_pairs={{0,2},{4,0},{8,4},{12,8},{14,12},{10,14},{6,10},{2,6},{1,3},{5,1},... | collective-permute-start | bytes 884744 | tf_op jit(solution)/shard_map/ppermute | solution.py:183
  147.0 7.2 %collective-permute-start.11 = (f32[96,768]{1,0:T(8,128)S(1)}, f32[96,768]{1,0:T(8,128)S(1)}, u32[]{:S(2)}, u32[]{:S(2)}) collective-permute-start(f32[96,768]{1,0:T(8,128)S(1)} %slice_add_fusion.8), channel_id=1, source_target_pairs={{0,4},{4,8},{8,12},{12,14},{14,10},{10,6},{6,2},{2,0},{1,5},{5,9},... | collective-permute-start | bytes 884744 | tf_op jit(solution)/shard_map/ppermute | solution.py:182
  151.4 9.4 %collective-permute-start.18 = (f32[96,768]{1,0:T(8,128)S(1)}, f32[96,768]{1,0:T(8,128)S(1)}, u32[]{:S(2)}, u32[]{:S(2)}) collective-permute-start(f32[96,768]{1,0:T(8,128)S(1)} %slice_add_fusion.1), channel_id=1, source_target_pairs={{0,2},{4,0},{8,4},{12,8},{14,12},{10,14},{6,10},{2,6},{1,3},{5,1},... | collective-permute-start | bytes 884744 | tf_op jit(solution)/shard_map/ppermute | solution.py:183
  154.2 6.8 %collective-permute-start.12 = (f32[96,768]{1,0:T(8,128)S(1)}, f32[96,768]{1,0:T(8,128)S(1)}, u32[]{:S(2)}, u32[]{:S(2)}) collective-permute-start(f32[96,768]{1,0:T(8,128)S(1)} %slice_add_fusion.7), channel_id=1, source_target_pairs={{0,4},{4,8},{8,12},{12,14},{14,10},{10,6},{6,2},{2,0},{1,5},{5,9},... | collective-permute-start | bytes 884744 | tf_op jit(solution)/shard_map/ppermute | solution.py:182
  (35 other events, 348.3 us)

commit v13 on v11

--- a/solution.py
+++ b/solution.py
@@ -238,6 +238,7 @@
     padded_gradient = with_halo(preactivation_gradient, (("seq", 1),), DILATION_STEP)
     spread = conv_taps(padded_gradient, dense, local_bins, transpose=True)
     conv_local = weight_taps(padded_input, preactivation_gradient, local_bins)
+    grad_point, conv_local = lax.optimization_barrier((grad_point, conv_local))
     grad_conv = tree_sum(conv_local) * scale
     grad_inputs = (cotangent.astype(jnp.float32) + mask3 * spread).astype(jnp.bfloat16)
     return (output, grad_inputs, grad_point, grad_conv)

time: 155 us -> 175 us (1.13)
  waiting for transfers between devices: 51 us -> 73.5 us
  starting transfers between devices: 43.4 us -> 38.4 us
  matrix products: 32.7 us -> 36.3 us
    ppermute x7, waiting for transfers between devices: 17.1 us -> 31.1 us  [ring_reduce_scatter(): ahead = lax.ppermute(ahead, 'seq', forward) + block(-2 - step, True)]
    ppermute x2, waiting for transfers between devices: 13.2 us -> 22 us  [with_halo(): lax.ppermute(tail, axis, [(i, (i + 1) % count) for i in range(ends)])]
    ppermute x7, starting transfers between devices: 11.5 us -> 3.95 us  [ring_reduce_scatter(): behind = lax.ppermute(behind, 'seq', backward) + block(2 + step, False)]
    dot_general x24, matrix products: 11.5 us -> 15.1 us  [conv_taps(): lax.dot_general(window, dense[k, :, cols], dims, preferred_element_type=j...]
    ppermute x9, starting transfers between devices: 7.29 us -> 10.7 us  [swap(): return lax.ppermute(value, axis, [(i, i ^ distance) for i in range(count)])]
    add x7, other arithmetic: 2.04 us -> 0.27 us  [ring_reduce_scatter(): behind = lax.ppermute(behind, 'seq', backward) + block(2 + step, False)]
  transfers between devices with their start and end apart: 27 -> 27, of which waited for: 14 -> 18; matrix products, arithmetic and copies ran while one was open for 19% -> 16% of each run, Pallas kernels for 0% -> 0%
where the time goes in v13:
time: 175 us
  waiting for transfers between devices  73.5 us (42%)
  starting transfers between devices  38.4 us (22%)
  matrix products  36.3 us (21%)
  other arithmetic  18.3 us (10%)
  local copies, waits for them, and re-layouts  6.28 us (4%)
  between operations  2.25 us (1%)
    ppermute x7, waiting for transfers between devices, ring_reduce_scatter(): ahead = lax.ppermute(ahead, 'seq', forward) + block(-2 - step, True)  31.1 us
    ppermute x2, waiting for transfers between devices, with_halo(): lax.ppermute(tail, axis, [(i, (i + 1) % count) for i in range(ends)])  22 us
    ppermute x9, waiting for transfers between devices, swap(): return lax.ppermute(value, axis, [(i, i ^ distance) for i in range(count)])  18 us
    dot_general x24, matrix products, conv_taps(): lax.dot_general(window, dense[k, :, cols], dims, preferred_element_type=j...  15.1 us
    ppermute x7, starting transfers between devices, ring_reduce_scatter(): ahead = lax.ppermute(ahead, 'seq', forward) + block(-2 - step, True)  12.7 us
    ppermute x9, starting transfers between devices, swap(): return lax.ppermute(value, axis, [(i, i ^ distance) for i in range(count)])  10.7 us
    ppermute x2, starting transfers between devices, with_halo(): lax.ppermute(tail, axis, [(i, (i + 1) % count) for i in range(ends)])  8.51 us
    dot_general x1, matrix products, on_device(): jnp.dot(act_rows, point_weight, preferred_element_type=jnp.float32)  6.24 us
  transfers between devices with their start and end apart: 27, of which 18 were waited for; matrix products, arithmetic and copies ran while one was open for 16% of the time, Pallas kernels for 0%

profile of v13, /device:TPU:0, one launch (start us, length us, event | category | flops | bytes accessed | tf_op | source)
XLA Modules:
  0.0 175.0 jit_solution(7040938822830473915)
XLA Ops:
  3.8 5.5 %collective-permute-start = (bf16[1,64,1536]{2,1,0:T(8,128)(2,1)}, bf16[1,64,1536]{2,1,0:T(8,128)(2,1)}, u32[]{:S(2)}, u32[]{:S(2)}) collective-permute-start(bf16[1,64,1536]{2,1,0:T(8,128)(2,1)} %get-tuple-element.44), channel_id=1, source_target_pairs={{0,2},{2,4},{4,6},{6,8},{8,10},{10,12},{12,14},{1,3},{3,5},{5,7},{... | collective-permute-start | bytes 589832 | tf_op jit(solution)/shard_map/ppermute | solution.py:21
  13.5 3.9 %collective-permute-done = bf16[1,64,1536]{2,1,0:T(8,128)(2,1)} collective-permute-done((bf16[1,64,1536]{2,1,0:T(8,128)(2,1)}, bf16[1,64,1536]{2,1,0:T(8,128)(2,1)}, u32[]{:S(2)}, u32[]{:S(2)}) %collective-permute-start) | collective-permute-done | bytes 196640 | tf_op jit(solution)/shard_map/ppermute | solution.py:21
  26.7 3.5 %convolution_multiply_fusion = f32[768,1536]{1,0:T(8,128)} fusion(bf16[512,768]{0,1:T(8,128)(2,1)S(1)} %bitcast.152, bf16[1,512,1536]{2,1,0:T(8,128)(2,1)S(1)} %copy-done.2), kind=kOutput, calls=%fused_computation.4 | convolution fusion | flops 1209139200 | bytes 7077888 | tf_op jit(solution)/shard_map/dot_general | solution.py:191
  30.4 2.7 %convolution_multiply_fusion.1 = f32[768,1536]{1,0:T(8,128)S(1)} fusion(bf16[512,768]{0,1:T(8,128)(2,1)} %bitcast.151, bf16[1,512,1536]{2,1,0:T(8,128)(2,1)S(1)} %copy-done.2), kind=kOutput, calls=%fused_computation.5 | convolution fusion | flops 1209139200 | bytes 7077888 | tf_op jit(solution)/shard_map/dot_general | solution.py:191
  33.1 6.2 %fusion.2 = bf16[1,512,1536]{2,1,0:T(8,128)(2,1)} fusion(bf16[1,512,1536]{2,1,0:T(8,128)(2,1)S(1)} %copy-done.12, bf16[1536,1536]{1,0:T(8,128)(2,1)} %param.8, f32[512]{0:T(512)S(1)} %fusion.112, f32[512,384]{0,1:T(8,128)S(1)} %copy-done.10, f32[512,384]{0,1:T(8,128)S(1)} %copy-done.8, f32[512,384]{0,1:T(8,128)S(1)} %copy-done.6, f32[512,384]{0,1:T(8,128)S(1)} %copy-done.4), kind=kOutput, calls=%fused_computation.14 | convolution fusion | flops 2425356288 | bytes 11012096 | tf_op jit(solution)/shard_map/dot_general | solution.py:231
  39.3 3.3 %add.488 = f32[8,96,1536]{2,1,0:T(8,128)S(1)} add(f32[8,96,1536]{2,1,0:T(8,128)S(1)} %bitcast.142, f32[8,96,1536]{2,1,0:T(8,128)} %collective-permute-done.2) | non-fusion elementwise | flops 1179648 | bytes 14155776 | tf_op jit(solution)/shard_map/add | solution.py:208
  42.7 3.9 %fusion.9 = bf16[512,1536]{0,1:T(8,128)(2,1)S(1)} fusion(bf16[512,1536]{1,0:T(8,128)(2,1)S(1)} %bitcast.143, bf16[1536,1536]{1,0:T(8,128)(2,1)S(1)} %bitcast.167, f32[512]{0:T(512)S(1)} %fusion.112, f32[512,384]{0,1:T(8,128)S(1)} %copy-done.10, f32[512,384]{0,1:T(8,128)S(1)} %copy-done.8, f32[512,384]{0,1:T(8,128)S(1)} %copy-done.6, ...), kind=kOutput, calls=%fused_computation.27 | convolution fusion | flops 2426929152 | bytes 11012096 | tf_op jit(solution)/shard_map/dot_general | solution.py:234
  51.5 2.7 %dynamic-slice_bitcast_fusion.8 = (f32[96,1536]{1,0:T(8,128)S(1)}, f32[96,1536]{1,0:T(8,128)S(1)}, f32[96,1536]{1,0:T(8,128)S(1)}, f32[96,1536]{1,0:T(8,128)}, f...) fusion(f32[8,96,1536]{2,1,0:T(8,128)S(1)} %add.488, ...), kind=kLoop, calls=%fused_computation.80 | loop fusion | bytes 18874432 | tf_op jit(solution)/shard_map/jit(dynamic_index_in_dim)/squeeze | solution.py:176
  54.2 3.2 %collective-permute-start.5 = (f32[96,768]{1,0:T(8,128)S(1)}, f32[96,768]{1,0:T(8,128)S(1)}, u32[]{:S(2)}, u32[]{:S(2)}) collective-permute-start(f32[96,768]{1,0:T(8,128)S(1)} %slice.312), channel_id=1, source_target_pairs={{0,4},{4,8},{8,12},{12,14},{14,10},{10,6},{6,2},{2,0},{1,5},{5,9},... | collective-permute-start | bytes 884744 | tf_op jit(solution)/shard_map/ppermute | solution.py:182
  57.6 3.0 %collective-permute-start.3 = (bf16[1,64,1536]{1,2,0:T(8,128)(2,1)S(1)}, bf16[1,64,1536]{1,2,0:T(8,128)(2,1)S(1)}, u32[]{:S(2)}, u32[]{:S(2)}) collective-permute-start(bf16[1,64,1536]{1,2,0:T(8,128)(2,1)S(1)} %get-tuple-element.40), channel_id=1, source_target_pairs={{0,2},{2,4},{4,6},{6,8},{8,10},{10,12},{12,14},{1,3},{3,5},{5,7},{... | collective-permute-start | bytes 589832 | tf_op jit(solution)/shard_map/ppermute | solution.py:21
  63.1 18.1 %collective-permute-done.3 = bf16[1,64,1536]{1,2,0:T(8,128)(2,1)S(1)} collective-permute-done((bf16[1,64,1536]{1,2,0:T(8,128)(2,1)S(1)}, bf16[1,64,1536]{1,2,0:T(8,128)(2,1)S(1)}, u32[]{:S(2)}, u32[]{:S(2)}) %collective-permute-start.3) | collective-permute-done | bytes 196640 | tf_op jit(solution)/shard_map/ppermute | solution.py:21
  85.6 6.3 %collective-permute-done.6 = f32[96,768]{1,0:T(8,128)S(1)} collective-permute-done((f32[96,768]{1,0:T(8,128)S(1)}, f32[96,768]{1,0:T(8,128)S(1)}, u32[]{:S(2)}, u32[]{:S(2)}) %collective-permute-start.6) | collective-permute-done | bytes 294944 | tf_op jit(solution)/shard_map/ppermute | solution.py:182
  94.9 5.2 %collective-permute-done.7 = f32[96,768]{1,0:T(8,128)S(1)} collective-permute-done((f32[96,768]{1,0:T(8,128)S(1)}, f32[96,768]{1,0:T(8,128)S(1)}, u32[]{:S(2)}, u32[]{:S(2)}) %collective-permute-start.7) | collective-permute-done | bytes 294944 | tf_op jit(solution)/shard_map/ppermute | solution.py:182
  103.0 4.3 %collective-permute-done.8 = f32[96,768]{1,0:T(8,128)S(1)} collective-permute-done((f32[96,768]{1,0:T(8,128)S(1)}, f32[96,768]{1,0:T(8,128)S(1)}, u32[]{:S(2)}, u32[]{:S(2)}) %collective-permute-start.8) | collective-permute-done | bytes 294944 | tf_op jit(solution)/shard_map/ppermute | solution.py:182
  110.0 5.2 %collective-permute-done.9 = f32[96,768]{1,0:T(8,128)S(1)} collective-permute-done((f32[96,768]{1,0:T(8,128)S(1)}, f32[96,768]{1,0:T(8,128)S(1)}, u32[]{:S(2)}, u32[]{:S(2)}) %collective-permute-start.9) | collective-permute-done | bytes 294944 | tf_op jit(solution)/shard_map/ppermute | solution.py:182
  118.1 6.1 %collective-permute-done.10 = f32[96,768]{1,0:T(8,128)S(1)} collective-permute-done((f32[96,768]{1,0:T(8,128)S(1)}, f32[96,768]{1,0:T(8,128)S(1)}, u32[]{:S(2)}, u32[]{:S(2)}) %collective-permute-start.10) | collective-permute-done | bytes 294944 | tf_op jit(solution)/shard_map/ppermute | solution.py:182
  127.2 3.9 %collective-permute-done.11 = f32[96,768]{1,0:T(8,128)S(1)} collective-permute-done((f32[96,768]{1,0:T(8,128)S(1)}, f32[96,768]{1,0:T(8,128)S(1)}, u32[]{:S(2)}, u32[]{:S(2)}) %collective-permute-start.11) | collective-permute-done | bytes 294944 | tf_op jit(solution)/shard_map/ppermute | solution.py:182
  139.1 4.5 %collective-permute-done.20 = f32[144,384]{1,0:T(8,128)S(1)} collective-permute-done((f32[144,384]{1,0:T(8,128)S(1)}, f32[144,384]{1,0:T(8,128)S(1)}, u32[]{:S(2)}, u32[]{:S(2)}) %collective-permute-start.20) | collective-permute-done | bytes 221216 | tf_op jit(solution)/shard_map/ppermute | solution.py:95
  148.6 2.8 %collective-permute-start.22 = (f32[36,384]{1,0:T(8,128)S(1)}, f32[36,384]{1,0:T(8,128)S(1)}, u32[]{:S(2)}, u32[]{:S(2)}) collective-permute-start(f32[36,384]{1,0:T(8,128)S(1)} %constant_dynamic-slice_fusion), channel_id=1, source_target_pairs={{0,8},{2,10},{4,12},{6,14},{8,0},{10,2},{12,4},{14,6},{1,9},{3,11}... | collective-permute-start | bytes 165896 | tf_op jit(solution)/shard_map/ppermute | solution.py:95
  153.8 2.8 %collective-permute-start.23 = (f32[36,384]{1,0:T(8,128)S(1)}, f32[36,384]{1,0:T(8,128)S(1)}, u32[]{:S(2)}, u32[]{:S(2)}) collective-permute-start(f32[36,384]{1,0:T(8,128)S(1)} %dynamic-slice_add_fusion.3), channel_id=1, source_target_pairs={{0,8},{2,10},{4,12},{6,14},{8,0},{10,2},{12,4},{14,6},{1,9},{3,11}... | collective-permute-start | bytes 165896 | tf_op jit(solution)/shard_map/ppermute | solution.py:95
  159.3 2.5 %collective-permute-start.24 = (f32[72,384]{1,0:T(8,128)S(1)}, f32[72,384]{1,0:T(8,128)S(1)}, u32[]{:S(2)}, u32[]{:S(2)}) collective-permute-start(f32[72,384]{1,0:T(8,128)S(1)} %dynamic_update_slice.25), channel_id=1, source_target_pairs={{0,4},{2,6},{4,0},{6,2},{8,12},{10,14},{12,8},{14,10},{1,5},{3,7},... | collective-permute-start | bytes 331784 | tf_op jit(solution)/shard_map/ppermute | solution.py:95
  161.8 2.7 %collective-permute-done.24 = f32[72,384]{1,0:T(8,128)S(1)} collective-permute-done((f32[72,384]{1,0:T(8,128)S(1)}, f32[72,384]{1,0:T(8,128)S(1)}, u32[]{:S(2)}, u32[]{:S(2)}) %collective-permute-start.24) | collective-permute-done | bytes 110624 | tf_op jit(solution)/shard_map/ppermute | solution.py:95
  164.7 5.9 %collective-permute-done.25 = f32[144,384]{1,0:T(8,128)S(1)} collective-permute-done((f32[144,384]{1,0:T(8,128)S(1)}, f32[144,384]{1,0:T(8,128)S(1)}, u32[]{:S(2)}, u32[]{:S(2)}) %collective-permute-start.25) | collective-permute-done | bytes 221216 | tf_op jit(solution)/shard_map/ppermute | solution.py:95
  170.6 3.2 %fusion.8 = bf16[1,512,1536]{2,1,0:T(8,128)(2,1)} fusion(f32[1,512,384]{2,1,0:T(8,128)} %fusion.27, f32[1,512,384]{2,1,0:T(8,128)S(1)} %copy-done.11, f32[1,512,384]{2,1,0:T(8,128)} %fusion.23, f32[1,512,384]{2,1,0:T(8,128)} %fusion.21, bf16[1,512,1536]{2,1,0:T(8,128)(2,1)S(1)} %copy-done.2, f32[512]{0:T(512)S(1)} %fusion.112), kind=kLoop, calls=%fused_computation.23 | loop fusion | flops 5505024 | bytes 6293504 | tf_op jit(solution)/shard_map/convert_element_type | solution.py:243
  (186 shorter events, 61.4 us)
Async XLA Ops:
  3.8 13.6 %collective-permute-start = (bf16[1,64,1536]{2,1,0:T(8,128)(2,1)}, bf16[1,64,1536]{2,1,0:T(8,128)(2,1)}, u32[]{:S(2)}, u32[]{:S(2)}) collective-permute-start(bf16[1,64,1536]{2,1,0:T(8,128)(2,1)} %get-tuple-element.44), channel_id=1, source_target_pairs={{0,2},{2,4},{4,6},{6,8},{8,10},{10,12},{12,14},{1,3},{3,5},{5,7},{... | collective-permute-start | bytes 589832 | tf_op jit(solution)/shard_map/ppermute | solution.py:21
  9.3 8.3 %collective-permute-start.1 = (bf16[1,64,1536]{2,1,0:T(8,128)(2,1)S(1)}, bf16[1,64,1536]{2,1,0:T(8,128)(2,1)}, u32[]{:S(2)}, u32[]{:S(2)}) collective-permute-start(bf16[1,64,1536]{2,1,0:T(8,128)(2,1)S(1)} %get-tuple-element.45), channel_id=1, source_target_pairs={{2,0},{4,2},{6,4},{8,6},{10,8},{12,10},{14,12},{3,1},{5,3},{7,5},{... | collective-permute-start | bytes 589832 | tf_op jit(solution)/shard_map/ppermute | solution.py:23
  30.2 9.1 %collective-permute-start.2 = (f32[8,96,1536]{2,1,0:T(8,128)}, f32[8,96,1536]{2,1,0:T(8,128)}, u32[]{:S(2)}, u32[]{:S(2)}) collective-permute-start(f32[8,96,1536]{2,1,0:T(8,128)} %bitcast.25), channel_id=1, source_target_pairs={{0,1},{1,0},{2,3},{3,2},{4,5},{5,4},{6,7},{7,6},{8,9},{9,8},{10,11... | collective-permute-start | bytes 14155784 | tf_op jit(solution)/shard_map/ppermute | solution.py:95
  54.2 28.2 %collective-permute-start.5 = (f32[96,768]{1,0:T(8,128)S(1)}, f32[96,768]{1,0:T(8,128)S(1)}, u32[]{:S(2)}, u32[]{:S(2)}) collective-permute-start(f32[96,768]{1,0:T(8,128)S(1)} %slice.312), channel_id=1, source_target_pairs={{0,4},{4,8},{8,12},{12,14},{14,10},{10,6},{6,2},{2,0},{1,5},{5,9},... | collective-permute-start | bytes 884744 | tf_op jit(solution)/shard_map/ppermute | solution.py:182
  57.4 27.5 %collective-permute-start.12 = (f32[96,768]{1,0:T(8,128)S(1)}, f32[96,768]{1,0:T(8,128)S(1)}, u32[]{:S(2)}, u32[]{:S(2)}) collective-permute-start(f32[96,768]{1,0:T(8,128)S(1)} %slice.320), channel_id=1, source_target_pairs={{0,2},{4,0},{8,4},{12,8},{14,12},{10,14},{6,10},{2,6},{1,3},{5,1},... | collective-permute-start | bytes 884744 | tf_op jit(solution)/shard_map/ppermute | solution.py:183
  57.6 23.6 %collective-permute-start.3 = (bf16[1,64,1536]{1,2,0:T(8,128)(2,1)S(1)}, bf16[1,64,1536]{1,2,0:T(8,128)(2,1)S(1)}, u32[]{:S(2)}, u32[]{:S(2)}) collective-permute-start(bf16[1,64,1536]{1,2,0:T(8,128)(2,1)S(1)} %get-tuple-element.40), channel_id=1, source_target_pairs={{0,2},{2,4},{4,6},{6,8},{8,10},{10,12},{12,14},{1,3},{3,5},{5,7},{... | collective-permute-start | bytes 589832 | tf_op jit(solution)/shard_map/ppermute | solution.py:21
  60.6 20.6 %collective-permute-start.4 = (bf16[1,64,1536]{1,2,0:T(8,128)(2,1)S(1)}, bf16[1,64,1536]{1,2,0:T(8,128)(2,1)S(1)}, u32[]{:S(2)}, u32[]{:S(2)}) collective-permute-start(bf16[1,64,1536]{1,2,0:T(8,128)(2,1)S(1)} %get-tuple-element.41), channel_id=1, source_target_pairs={{2,0},{4,2},{6,4},{8,6},{10,8},{12,10},{14,12},{3,1},{5,3},{7,5},{... | collective-permute-start | bytes 589832 | tf_op jit(solution)/shard_map/ppermute | solution.py:23
  82.5 9.4 %collective-permute-start.6 = (f32[96,768]{1,0:T(8,128)S(1)}, f32[96,768]{1,0:T(8,128)S(1)}, u32[]{:S(2)}, u32[]{:S(2)}) collective-permute-start(f32[96,768]{1,0:T(8,128)S(1)} %slice_add_fusion.13), channel_id=1, source_target_pairs={{0,4},{4,8},{8,12},{12,14},{14,10},{10,6},{6,2},{2,0},{1,5},{5,9},... | collective-permute-start | bytes 884744 | tf_op jit(solution)/shard_map/ppermute | solution.py:182
  84.9 8.6 %collective-permute-start.13 = (f32[96,768]{1,0:T(8,128)S(1)}, f32[96,768]{1,0:T(8,128)S(1)}, u32[]{:S(2)}, u32[]{:S(2)}) collective-permute-start(f32[96,768]{1,0:T(8,128)S(1)} %slice_add_fusion.6), channel_id=1, source_target_pairs={{0,2},{4,0},{8,4},{12,8},{14,12},{10,14},{6,10},{2,6},{1,3},{5,1},... | collective-permute-start | bytes 884744 | tf_op jit(solution)/shard_map/ppermute | solution.py:183
  92.0 8.1 %collective-permute-start.7 = (f32[96,768]{1,0:T(8,128)S(1)}, f32[96,768]{1,0:T(8,128)S(1)}, u32[]{:S(2)}, u32[]{:S(2)}) collective-permute-start(f32[96,768]{1,0:T(8,128)S(1)} %slice_add_fusion.12), channel_id=1, source_target_pairs={{0,4},{4,8},{8,12},{12,14},{14,10},{10,6},{6,2},{2,0},{1,5},{5,9},... | collective-permute-start | bytes 884744 | tf_op jit(solution)/shard_map/ppermute | solution.py:182
  93.6 7.7 %collective-permute-start.14 = (f32[96,768]{1,0:T(8,128)S(1)}, f32[96,768]{1,0:T(8,128)S(1)}, u32[]{:S(2)}, u32[]{:S(2)}) collective-permute-start(f32[96,768]{1,0:T(8,128)S(1)} %slice_add_fusion.5), channel_id=1, source_target_pairs={{0,2},{4,0},{8,4},{12,8},{14,12},{10,14},{6,10},{2,6},{1,3},{5,1},... | collective-permute-start | bytes 884744 | tf_op jit(solution)/shard_map/ppermute | solution.py:183
  100.1 7.2 %collective-permute-start.8 = (f32[96,768]{1,0:T(8,128)S(1)}, f32[96,768]{1,0:T(8,128)S(1)}, u32[]{:S(2)}, u32[]{:S(2)}) collective-permute-start(f32[96,768]{1,0:T(8,128)S(1)} %slice_add_fusion.11), channel_id=1, source_target_pairs={{0,4},{4,8},{8,12},{12,14},{14,10},{10,6},{6,2},{2,0},{1,5},{5,9},... | collective-permute-start | bytes 884744 | tf_op jit(solution)/shard_map/ppermute | solution.py:182
  101.3 7.3 %collective-permute-start.15 = (f32[96,768]{1,0:T(8,128)S(1)}, f32[96,768]{1,0:T(8,128)S(1)}, u32[]{:S(2)}, u32[]{:S(2)}) collective-permute-start(f32[96,768]{1,0:T(8,128)S(1)} %slice_add_fusion.4), channel_id=1, source_target_pairs={{0,2},{4,0},{8,4},{12,8},{14,12},{10,14},{6,10},{2,6},{1,3},{5,1},... | collective-permute-start | bytes 884744 | tf_op jit(solution)/shard_map/ppermute | solution.py:183
  107.4 7.9 %collective-permute-start.9 = (f32[96,768]{1,0:T(8,128)S(1)}, f32[96,768]{1,0:T(8,128)S(1)}, u32[]{:S(2)}, u32[]{:S(2)}) collective-permute-start(f32[96,768]{1,0:T(8,128)S(1)} %slice_add_fusion.10), channel_id=1, source_target_pairs={{0,4},{4,8},{8,12},{12,14},{14,10},{10,6},{6,2},{2,0},{1,5},{5,9},... | collective-permute-start | bytes 884744 | tf_op jit(solution)/shard_map/ppermute | solution.py:182
  108.6 8.1 %collective-permute-start.16 = (f32[96,768]{1,0:T(8,128)S(1)}, f32[96,768]{1,0:T(8,128)S(1)}, u32[]{:S(2)}, u32[]{:S(2)}) collective-permute-start(f32[96,768]{1,0:T(8,128)S(1)} %slice_add_fusion.3), channel_id=1, source_target_pairs={{0,2},{4,0},{8,4},{12,8},{14,12},{10,14},{6,10},{2,6},{1,3},{5,1},... | collective-permute-start | bytes 884744 | tf_op jit(solution)/shard_map/ppermute | solution.py:183
  115.3 9.0 %collective-permute-start.10 = (f32[96,768]{1,0:T(8,128)S(1)}, f32[96,768]{1,0:T(8,128)S(1)}, u32[]{:S(2)}, u32[]{:S(2)}) collective-permute-start(f32[96,768]{1,0:T(8,128)S(1)} %slice_add_fusion.9), channel_id=1, source_target_pairs={{0,4},{4,8},{8,12},{12,14},{14,10},{10,6},{6,2},{2,0},{1,5},{5,9},... | collective-permute-start | bytes 884744 | tf_op jit(solution)/shard_map/ppermute | solution.py:182
  116.8 9.3 %collective-permute-start.17 = (f32[96,768]{1,0:T(8,128)S(1)}, f32[96,768]{1,0:T(8,128)S(1)}, u32[]{:S(2)}, u32[]{:S(2)}) collective-permute-start(f32[96,768]{1,0:T(8,128)S(1)} %slice_add_fusion.2), channel_id=1, source_target_pairs={{0,2},{4,0},{8,4},{12,8},{14,12},{10,14},{6,10},{2,6},{1,3},{5,1},... | collective-permute-start | bytes 884744 | tf_op jit(solution)/shard_map/ppermute | solution.py:183
  124.3 6.8 %collective-permute-start.11 = (f32[96,768]{1,0:T(8,128)S(1)}, f32[96,768]{1,0:T(8,128)S(1)}, u32[]{:S(2)}, u32[]{:S(2)}) collective-permute-start(f32[96,768]{1,0:T(8,128)S(1)} %slice_add_fusion.8), channel_id=1, source_target_pairs={{0,4},{4,8},{8,12},{12,14},{14,10},{10,6},{6,2},{2,0},{1,5},{5,9},... | collective-permute-start | bytes 884744 | tf_op jit(solution)/shard_map/ppermute | solution.py:182
  126.1 7.1 %collective-permute-start.18 = (f32[96,768]{1,0:T(8,128)S(1)}, f32[96,768]{1,0:T(8,128)S(1)}, u32[]{:S(2)}, u32[]{:S(2)}) collective-permute-start(f32[96,768]{1,0:T(8,128)S(1)} %slice_add_fusion.1), channel_id=1, source_target_pairs={{0,2},{4,0},{8,4},{12,8},{14,12},{10,14},{6,10},{2,6},{1,3},{5,1},... | collective-permute-start | bytes 884744 | tf_op jit(solution)/shard_map/ppermute | solution.py:183
  136.1 7.5 %collective-permute-start.20 = (f32[144,384]{1,0:T(8,128)S(1)}, f32[144,384]{1,0:T(8,128)S(1)}, u32[]{:S(2)}, u32[]{:S(2)}) collective-permute-start(f32[144,384]{1,0:T(8,128)S(1)} %constant_dynamic-slice_fusion.2), channel_id=1, source_target_pairs={{0,2},{2,0},{4,6},{6,4},{8,10},{10,8},{12,14},{14,12},{1,3},{3,1},... | collective-permute-start | bytes 663560 | tf_op jit(solution)/shard_map/ppermute | solution.py:95
  148.6 5.2 %collective-permute-start.22 = (f32[36,384]{1,0:T(8,128)S(1)}, f32[36,384]{1,0:T(8,128)S(1)}, u32[]{:S(2)}, u32[]{:S(2)}) collective-permute-start(f32[36,384]{1,0:T(8,128)S(1)} %constant_dynamic-slice_fusion), channel_id=1, source_target_pairs={{0,8},{2,10},{4,12},{6,14},{8,0},{10,2},{12,4},{14,6},{1,9},{3,11}... | collective-permute-start | bytes 165896 | tf_op jit(solution)/shard_map/ppermute | solution.py:95
  153.8 5.2 %collective-permute-start.23 = (f32[36,384]{1,0:T(8,128)S(1)}, f32[36,384]{1,0:T(8,128)S(1)}, u32[]{:S(2)}, u32[]{:S(2)}) collective-permute-start(f32[36,384]{1,0:T(8,128)S(1)} %dynamic-slice_add_fusion.3), channel_id=1, source_target_pairs={{0,8},{2,10},{4,12},{6,14},{8,0},{10,2},{12,4},{14,6},{1,9},{3,11}... | collective-permute-start | bytes 165896 | tf_op jit(solution)/shard_map/ppermute | solution.py:95
  159.3 5.2 %collective-permute-start.24 = (f32[72,384]{1,0:T(8,128)S(1)}, f32[72,384]{1,0:T(8,128)S(1)}, u32[]{:S(2)}, u32[]{:S(2)}) collective-permute-start(f32[72,384]{1,0:T(8,128)S(1)} %dynamic_update_slice.25), channel_id=1, source_target_pairs={{0,4},{2,6},{4,0},{6,2},{8,12},{10,14},{12,8},{14,10},{1,5},{3,7},... | collective-permute-start | bytes 331784 | tf_op jit(solution)/shard_map/ppermute | solution.py:95
  164.5 6.0 %collective-permute-start.25 = (f32[144,384]{1,0:T(8,128)S(1)}, f32[144,384]{1,0:T(8,128)S(1)}, u32[]{:S(2)}, u32[]{:S(2)}) collective-permute-start(f32[144,384]{1,0:T(8,128)S(1)} %constant_dynamic-update-slice_fusion.4), channel_id=1, source_target_pairs={{0,2},{2,0},{4,6},{6,4},{8,10},{10,8},{12,14},{14,12},{1,3},{3,1},... | collective-permute-start | bytes 663560 | tf_op jit(solution)/shard_map/ppermute | solution.py:95
  (29 other events, 284.2 us)

commit v14 on v12

--- a/solution.py
+++ b/solution.py
@@ -151,7 +151,7 @@
     return count % 2 == 0 and [s for _, s in cells] == snake
 
 
-def ring_reduce_scatter(blocks, snake, hold):
+def ring_reduce_scatter(blocks, snake, hold=None):
     count = blocks.shape[0]
     half_count = count // 2
     if snake:
@@ -181,7 +181,7 @@
     for step in range(count - 1):
         ahead = lax.ppermute(ahead, "seq", forward) + block(-2 - step, True)
         behind = lax.ppermute(behind, "seq", backward) + block(2 + step, False)
-        if step == 0:
+        if step == 0 and hold is not None:
             ahead, behind, hold = lax.optimization_barrier((ahead, behind, hold))
     return jnp.concatenate([ahead, behind], axis=1), hold
 
@@ -195,7 +195,6 @@
     ) * scale
     if rep_count != 2:
         partial = product(act_rows, cot_rows)
-        partial, hold = lax.optimization_barrier((partial, hold))
         total = lax.psum_scatter(partial, ("seq", "rep"), scatter_dimension=0, tiled=True)
         return total, hold
     block = chans // (seq_count * rep_count)
@@ -234,8 +233,10 @@
     back = lax.dot_general(
         cot_rows, point_weight, (((1,), (1,)), ((), ())), preferred_element_type=jnp.float32
     )
-    grad_point, back = point_gradient(act_rows, cot_rows, scale, snake, back)
     preactivation_gradient = (back.reshape(inputs.shape) * slope * mask3).astype(jnp.bfloat16)
+    grad_point, preactivation_gradient = point_gradient(
+        act_rows, cot_rows, scale, snake, preactivation_gradient
+    )
     padded_gradient = with_halo(preactivation_gradient, (("seq", 1),), DILATION_STEP)
     spread = conv_taps(padded_gradient, dense, local_bins, transpose=True)
     conv_local = weight_taps(padded_input, preactivation_gradient, local_bins)

time: 162 us -> 157 us (0.969)
  waiting for transfers between devices: 50.7 us -> 63.7 us
  other arithmetic: 24.5 us -> 16.8 us
  starting transfers between devices: 39.6 us -> 32.8 us
  local copies, waits for them, and re-layouts: 10.7 us -> 5.96 us
    ppermute x2, waiting for transfers between devices: 11.4 us -> 23.4 us  [with_halo(): lax.ppermute(tail, axis, [(i, (i + 1) % count) for i in range(ends)])]
    ppermute x7, starting transfers between devices: 15 us -> 5.1 us  [ring_reduce_scatter(): behind = lax.ppermute(behind, 'seq', backward) + block(2 + step, False)]
    ppermute x7, starting transfers between devices: 5.92 us -> 14.1 us  [ring_reduce_scatter(): ahead = lax.ppermute(ahead, 'seq', forward) + block(-2 - step, True)]
    ppermute x7, waiting for transfers between devices: 2.69 us -> 8.88 us  [ring_reduce_scatter(): ahead = lax.ppermute(ahead, 'seq', forward) + block(-2 - step, True)]
    ppermute x2, waiting for transfers between devices: 4.11 us -> 0.32 us  [with_halo(): lax.ppermute(head, axis, [((i + 1) % count, i) for i in range(ends)])]
    ppermute x9, waiting for transfers between devices: 24.7 us -> 21 us  [swap(): return lax.ppermute(value, axis, [(i, i ^ distance) for i in range(count)])]
    optimization_barrier x1 -> x0, local copies, waits for them, and re-layouts: 3.52 us -> none  [ring_reduce_scatter(): ahead, behind, hold = lax.optimization_barrier((ahead, behind, hold))]
    convert_element_type x1 -> x0, other arithmetic: 3.47 us -> none  [on_device(): (back.reshape(inputs.shape) * slope * mask3).astype(jnp.bfloat16)]
  transfers between devices with their start and end apart: 27 -> 27, of which waited for: 16 -> 17; matrix products, arithmetic and copies ran while one was open for 21% -> 20% of each run, Pallas kernels for 0% -> 0%
where the time goes in v14:
time: 157 us; the launch traced here: 156 us
  waiting for transfers between devices  63.7 us (41%)
  matrix products  34.7 us (22%)
  starting transfers between devices  32.8 us (21%)
  other arithmetic  16.8 us (11%)
  local copies, waits for them, and re-layouts  5.96 us (4%)
  between operations  2.29 us (1%)
    ppermute x2, waiting for transfers between devices, with_halo(): lax.ppermute(tail, axis, [(i, (i + 1) % count) for i in range(ends)])  23.4 us
    ppermute x9, waiting for transfers between devices, swap(): return lax.ppermute(value, axis, [(i, i ^ distance) for i in range(count)])  21 us
    ppermute x7, starting transfers between devices, ring_reduce_scatter(): ahead = lax.ppermute(ahead, 'seq', forward) + block(-2 - step, True)  14.1 us
    dot_general x24, matrix products, conv_taps(): lax.dot_general(window, dense[k, :, cols], dims, preferred_element_type=j...  11.5 us
    ppermute x7, waiting for transfers between devices, ring_reduce_scatter(): behind = lax.ppermute(behind, 'seq', backward) + block(2 + step, False)  10 us
    ppermute x7, waiting for transfers between devices, ring_reduce_scatter(): ahead = lax.ppermute(ahead, 'seq', forward) + block(-2 - step, True)  8.88 us
    ppermute x2, starting transfers between devices, with_halo(): lax.ppermute(tail, axis, [(i, (i + 1) % count) for i in range(ends)])  7.74 us
    dot_general x2, matrix products, point_gradient(): lax.dot_general(a, b, (((0,), (0,)), ((), ())), preferred_element_type=jn...  6.19 us
  transfers between devices with their start and end apart: 27, of which 17 were waited for; matrix products, arithmetic and copies ran while one was open for 20% of the time, Pallas kernels for 0%

profile of v14, /device:TPU:0, one launch (start us, length us, event | category | flops | bytes accessed | tf_op | source)
XLA Modules:
  0.0 156.3 jit_solution(10933770416278349034)
XLA Ops:
  3.8 5.5 %collective-permute-start = (bf16[1,64,1536]{2,1,0:T(8,128)(2,1)}, bf16[1,64,1536]{2,1,0:T(8,128)(2,1)}, u32[]{:S(2)}, u32[]{:S(2)}) collective-permute-start(bf16[1,64,1536]{2,1,0:T(8,128)(2,1)} %get-tuple-element.42), channel_id=1, source_target_pairs={{0,2},{2,4},{4,6},{6,8},{8,10},{10,12},{12,14},{1,3},{3,5},{5,7},{... | collective-permute-start | bytes 589832 | tf_op jit(solution)/shard_map/ppermute | solution.py:21
  11.6 5.7 %collective-permute-done = bf16[1,64,1536]{2,1,0:T(8,128)(2,1)} collective-permute-done((bf16[1,64,1536]{2,1,0:T(8,128)(2,1)}, bf16[1,64,1536]{2,1,0:T(8,128)(2,1)}, u32[]{:S(2)}, u32[]{:S(2)}) %collective-permute-start) | collective-permute-done | bytes 196640 | tf_op jit(solution)/shard_map/ppermute | solution.py:21
  26.7 3.5 %convolution_multiply_fusion = f32[768,1536]{1,0:T(8,128)} fusion(bf16[512,768]{0,1:T(8,128)(2,1)S(1)} %bitcast.164, bf16[1,512,1536]{2,1,0:T(8,128)(2,1)S(1)} %copy-done.2), kind=kOutput, calls=%fused_computation.4 | convolution fusion | flops 1209139200 | bytes 7077888 | tf_op jit(solution)/shard_map/dot_general | solution.py:193
  30.3 2.7 %convolution_multiply_fusion.1 = f32[768,1536]{1,0:T(8,128)S(1)} fusion(bf16[512,768]{0,1:T(8,128)(2,1)} %bitcast.163, bf16[1,512,1536]{2,1,0:T(8,128)(2,1)S(1)} %copy-done.2), kind=kOutput, calls=%fused_computation.5 | convolution fusion | flops 1209139200 | bytes 7077888 | tf_op jit(solution)/shard_map/dot_general | solution.py:193
  33.0 6.0 %fusion.10 = bf16[1,512,1536]{1,2,0:T(8,128)(2,1)S(1)} fusion(bf16[1536,1536]{1,0:T(8,128)(2,1)} %param.8, bf16[1,512,1536]{2,1,0:T(8,128)(2,1)S(1)} %copy-done.2, f32[512]{0:T(512)S(1)} %fusion.116, f32[512,384]{0,1:T(8,128)S(1)} %copy-done.4, f32[512,384]{0,1:T(8,128)S(1)} %copy-done.6, f32[512,384]{0,1:T(8,128)S(1)} %copy-done.8, ...), kind=kOutput, calls=%fused_computation.28 | convolution fusion | flops 2426929152 | bytes 11012096 | tf_op jit(solution)/shard_map/dot_general | solution.py:233
  39.0 3.3 %add.488 = f32[8,96,1536]{2,1,0:T(8,128)S(1)} add(f32[8,96,1536]{2,1,0:T(8,128)S(1)} %bitcast.155, f32[8,96,1536]{2,1,0:T(8,128)} %collective-permute-done.2) | non-fusion elementwise | flops 1179648 | bytes 14155776 | tf_op jit(solution)/shard_map/add | solution.py:209
  42.4 2.4 %dynamic-slice_bitcast_fusion.6 = (f32[96,1536]{1,0:T(8,128)}, f32[96,1536]{1,0:T(8,128)}, f32[96,1536]{1,0:T(8,128)}, f32[96,1536]{1,0:T(8,128)}, f32[96,1536]{...) fusion(f32[8,96,1536]{2,1,0:T(8,128)S(1)} %add.488, ...), kind=kLoop, calls=%fused_computation.82 | loop fusion | bytes 18874432 | tf_op jit(solution)/shard_map/jit(dynamic_index_in_dim)/squeeze | solution.py:176
  44.9 3.2 %collective-permute-start.3 = (f32[96,768]{1,0:T(8,128)S(1)}, f32[96,768]{1,0:T(8,128)S(1)}, u32[]{:S(2)}, u32[]{:S(2)}) collective-permute-start(f32[96,768]{1,0:T(8,128)S(1)} %slice.298), channel_id=1, source_target_pairs={{0,4},{4,8},{8,12},{12,14},{14,10},{10,6},{6,2},{2,0},{1,5},{5,9},... | collective-permute-start | bytes 884744 | tf_op jit(solution)/shard_map/ppermute | solution.py:182
  48.0 6.1 %fusion.2 = bf16[1,512,1536]{2,1,0:T(8,128)(2,1)} fusion(bf16[1,512,1536]{2,1,0:T(8,128)(2,1)S(1)} %copy-done.11, bf16[1536,1536]{1,0:T(8,128)(2,1)} %param.8, f32[512]{0:T(512)S(1)} %fusion.116, f32[512,384]{0,1:T(8,128)S(1)} %copy-done.4, f32[512,384]{0,1:T(8,128)S(1)} %copy-done.6, f32[512,384]{0,1:T(8,128)S(1)} %copy-done.8, f32[512,384]{0,1:T(8,128)S(1)} %copy-done.10), kind=kOutput, calls=%fused_computation.14 | convolution fusion | flops 2425356288 | bytes 11012096 | tf_op jit(solution)/shard_map/dot_general | solution.py:231
  55.0 2.2 %collective-permute-done.4 = f32[96,768]{1,0:T(8,128)S(1)} collective-permute-done((f32[96,768]{1,0:T(8,128)S(1)}, f32[96,768]{1,0:T(8,128)S(1)}, u32[]{:S(2)}, u32[]{:S(2)}) %collective-permute-start.4) | collective-permute-done | bytes 294944 | tf_op jit(solution)/shard_map/ppermute | solution.py:183
  64.5 2.2 %collective-permute-start.5 = (bf16[1,64,1536]{1,2,0:T(8,128)(2,1)S(1)}, bf16[1,64,1536]{1,2,0:T(8,128)(2,1)S(1)}, u32[]{:S(2)}, u32[]{:S(2)}) collective-permute-start(bf16[1,64,1536]{1,2,0:T(8,128)(2,1)S(1)} %get-tuple-element.38), channel_id=1, source_target_pairs={{0,2},{2,4},{4,6},{6,8},{8,10},{10,12},{12,14},{1,3},{3,5},{5,7},{... | collective-permute-start | bytes 589832 | tf_op jit(solution)/shard_map/ppermute | solution.py:21
  69.2 17.7 %collective-permute-done.5 = bf16[1,64,1536]{1,2,0:T(8,128)(2,1)S(1)} collective-permute-done((bf16[1,64,1536]{1,2,0:T(8,128)(2,1)S(1)}, bf16[1,64,1536]{1,2,0:T(8,128)(2,1)S(1)}, u32[]{:S(2)}, u32[]{:S(2)}) %collective-permute-start.5) | collective-permute-done | bytes 196640 | tf_op jit(solution)/shard_map/ppermute | solution.py:21
  100.3 8.7 %collective-permute-done.20 = f32[144,384]{1,0:T(8,128)S(1)} collective-permute-done((f32[144,384]{1,0:T(8,128)S(1)}, f32[144,384]{1,0:T(8,128)S(1)}, u32[]{:S(2)}, u32[]{:S(2)}) %collective-permute-start.20) | collective-permute-done | bytes 221216 | tf_op jit(solution)/shard_map/ppermute | solution.py:95
  109.1 2.0 %collective-permute-start.9 = (f32[96,768]{1,0:T(8,128)S(1)}, f32[96,768]{1,0:T(8,128)}, u32[]{:S(2)}, u32[]{:S(2)}) collective-permute-start(f32[96,768]{1,0:T(8,128)S(1)} %slice_add_fusion.10), channel_id=1, source_target_pairs={{0,4},{4,8},{8,12},{12,14},{14,10},{10,6},{6,2},{2,0},{1,5},{5,9},... | collective-permute-start | bytes 884744 | tf_op jit(solution)/shard_map/ppermute | solution.py:182
  111.2 2.7 %collective-permute-done.21 = f32[72,384]{1,0:T(8,128)S(1)} collective-permute-done((f32[72,384]{1,0:T(8,128)S(1)}, f32[72,384]{1,0:T(8,128)S(1)}, u32[]{:S(2)}, u32[]{:S(2)}) %collective-permute-start.21) | collective-permute-done | bytes 110624 | tf_op jit(solution)/shard_map/ppermute | solution.py:95
  114.5 3.1 %collective-permute-start.15 = (f32[96,768]{1,0:T(8,128)S(1)}, f32[96,768]{1,0:T(8,128)}, u32[]{:S(2)}, u32[]{:S(2)}) collective-permute-start(f32[96,768]{1,0:T(8,128)S(1)} %slice_add_fusion.4), channel_id=1, source_target_pairs={{0,2},{4,0},{8,4},{12,8},{14,12},{10,14},{6,10},{2,6},{1,3},{5,1},... | collective-permute-start | bytes 884744 | tf_op jit(solution)/shard_map/ppermute | solution.py:183
  117.5 3.4 %collective-permute-done.22 = f32[36,384]{1,0:T(8,128)S(1)} collective-permute-done((f32[36,384]{1,0:T(8,128)S(1)}, f32[36,384]{1,0:T(8,128)S(1)}, u32[]{:S(2)}, u32[]{:S(2)}) %collective-permute-start.22) | collective-permute-done | bytes 55328 | tf_op jit(solution)/shard_map/ppermute | solution.py:95
  121.6 4.9 %collective-permute-done.23 = f32[36,384]{1,0:T(8,128)S(1)} collective-permute-done((f32[36,384]{1,0:T(8,128)S(1)}, f32[36,384]{1,0:T(8,128)S(1)}, u32[]{:S(2)}, u32[]{:S(2)}) %collective-permute-start.23) | collective-permute-done | bytes 55328 | tf_op jit(solution)/shard_map/ppermute | solution.py:95
  128.1 1.9 %collective-permute-start.10 = (f32[96,768]{1,0:T(8,128)S(1)}, f32[96,768]{1,0:T(8,128)S(1)}, u32[]{:S(2)}, u32[]{:S(2)}) collective-permute-start(f32[96,768]{1,0:T(8,128)S(1)} %slice_add_fusion.9), channel_id=1, source_target_pairs={{0,4},{4,8},{8,12},{12,14},{14,10},{10,6},{6,2},{2,0},{1,5},{5,9},... | collective-permute-start | bytes 884744 | tf_op jit(solution)/shard_map/ppermute | solution.py:182
  133.4 3.6 %collective-permute-done.10 = f32[96,768]{1,0:T(8,128)S(1)} collective-permute-done((f32[96,768]{1,0:T(8,128)S(1)}, f32[96,768]{1,0:T(8,128)S(1)}, u32[]{:S(2)}, u32[]{:S(2)}) %collective-permute-start.10) | collective-permute-done | bytes 294944 | tf_op jit(solution)/shard_map/ppermute | solution.py:182
  141.4 2.5 %collective-permute-done.11 = f32[96,768]{1,0:T(8,128)S(1)} collective-permute-done((f32[96,768]{1,0:T(8,128)S(1)}, f32[96,768]{1,0:T(8,128)S(1)}, u32[]{:S(2)}, u32[]{:S(2)}) %collective-permute-start.11) | collective-permute-done | bytes 294944 | tf_op jit(solution)/shard_map/ppermute | solution.py:182
  145.8 2.8 %collective-permute-done.17 = f32[96,768]{1,0:T(8,128)S(1)} collective-permute-done((f32[96,768]{1,0:T(8,128)S(1)}, f32[96,768]{1,0:T(8,128)S(1)}, u32[]{:S(2)}, u32[]{:S(2)}) %collective-permute-start.17) | collective-permute-done | bytes 294944 | tf_op jit(solution)/shard_map/ppermute | solution.py:183
  149.7 1.9 %collective-permute-done.12 = f32[96,768]{1,0:T(8,128)S(1)} collective-permute-done((f32[96,768]{1,0:T(8,128)S(1)}, f32[96,768]{1,0:T(8,128)S(1)}, u32[]{:S(2)}, u32[]{:S(2)}) %collective-permute-start.12) | collective-permute-done | bytes 294944 | tf_op jit(solution)/shard_map/ppermute | solution.py:182
  151.7 3.7 %collective-permute-done.18 = f32[96,768]{1,0:T(8,128)S(1)} collective-permute-done((f32[96,768]{1,0:T(8,128)S(1)}, f32[96,768]{1,0:T(8,128)S(1)}, u32[]{:S(2)}, u32[]{:S(2)}) %collective-permute-start.18) | collective-permute-done | bytes 294944 | tf_op jit(solution)/shard_map/ppermute | solution.py:183
  (175 shorter events, 52.3 us)
Async XLA Ops:
  3.8 13.6 %collective-permute-start = (bf16[1,64,1536]{2,1,0:T(8,128)(2,1)}, bf16[1,64,1536]{2,1,0:T(8,128)(2,1)}, u32[]{:S(2)}, u32[]{:S(2)}) collective-permute-start(bf16[1,64,1536]{2,1,0:T(8,128)(2,1)} %get-tuple-element.42), channel_id=1, source_target_pairs={{0,2},{2,4},{4,6},{6,8},{8,10},{10,12},{12,14},{1,3},{3,5},{5,7},{... | collective-permute-start | bytes 589832 | tf_op jit(solution)/shard_map/ppermute | solution.py:21
  9.3 8.3 %collective-permute-start.1 = (bf16[1,64,1536]{2,1,0:T(8,128)(2,1)S(1)}, bf16[1,64,1536]{2,1,0:T(8,128)(2,1)}, u32[]{:S(2)}, u32[]{:S(2)}) collective-permute-start(bf16[1,64,1536]{2,1,0:T(8,128)(2,1)S(1)} %get-tuple-element.43), channel_id=1, source_target_pairs={{2,0},{4,2},{6,4},{8,6},{10,8},{12,10},{14,12},{3,1},{5,3},{7,5},{... | collective-permute-start | bytes 589832 | tf_op jit(solution)/shard_map/ppermute | solution.py:23
  30.2 8.8 %collective-permute-start.2 = (f32[8,96,1536]{2,1,0:T(8,128)}, f32[8,96,1536]{2,1,0:T(8,128)}, u32[]{:S(2)}, u32[]{:S(2)}) collective-permute-start(f32[8,96,1536]{2,1,0:T(8,128)} %bitcast.25), channel_id=1, source_target_pairs={{0,1},{1,0},{2,3},{3,2},{4,5},{5,4},{6,7},{7,6},{8,9},{9,8},{10,11... | collective-permute-start | bytes 14155784 | tf_op jit(solution)/shard_map/ppermute | solution.py:95
  44.9 10.1 %collective-permute-start.3 = (f32[96,768]{1,0:T(8,128)S(1)}, f32[96,768]{1,0:T(8,128)S(1)}, u32[]{:S(2)}, u32[]{:S(2)}) collective-permute-start(f32[96,768]{1,0:T(8,128)S(1)} %slice.298), channel_id=1, source_target_pairs={{0,4},{4,8},{8,12},{12,14},{14,10},{10,6},{6,2},{2,0},{1,5},{5,9},... | collective-permute-start | bytes 884744 | tf_op jit(solution)/shard_map/ppermute | solution.py:182
  48.0 9.1 %collective-permute-start.4 = (f32[96,768]{1,0:T(8,128)S(1)}, f32[96,768]{1,0:T(8,128)S(1)}, u32[]{:S(2)}, u32[]{:S(2)}) collective-permute-start(f32[96,768]{1,0:T(8,128)S(1)} %slice.300), channel_id=1, source_target_pairs={{0,2},{4,0},{8,4},{12,8},{14,12},{10,14},{6,10},{2,6},{1,3},{5,1},... | collective-permute-start | bytes 884744 | tf_op jit(solution)/shard_map/ppermute | solution.py:183
  62.4 33.9 %collective-permute-start.7 = (f32[96,768]{1,0:T(8,128)S(1)}, f32[96,768]{1,0:T(8,128)S(1)}, u32[]{:S(2)}, u32[]{:S(2)}) collective-permute-start(f32[96,768]{1,0:T(8,128)S(1)} %slice_add_fusion.13), channel_id=1, source_target_pairs={{0,4},{4,8},{8,12},{12,14},{14,10},{10,6},{6,2},{2,0},{1,5},{5,9},... | collective-permute-start | bytes 884744 | tf_op jit(solution)/shard_map/ppermute | solution.py:182
  64.0 35.0 %collective-permute-start.13 = (f32[96,768]{1,0:T(8,128)S(1)}, f32[96,768]{1,0:T(8,128)S(1)}, u32[]{:S(2)}, u32[]{:S(2)}) collective-permute-start(f32[96,768]{1,0:T(8,128)S(1)} %slice_add_fusion.12), channel_id=1, source_target_pairs={{0,2},{4,0},{8,4},{12,8},{14,12},{10,14},{6,10},{2,6},{1,3},{5,1},... | collective-permute-start | bytes 884744 | tf_op jit(solution)/shard_map/ppermute | solution.py:183
  64.5 22.4 %collective-permute-start.5 = (bf16[1,64,1536]{1,2,0:T(8,128)(2,1)S(1)}, bf16[1,64,1536]{1,2,0:T(8,128)(2,1)S(1)}, u32[]{:S(2)}, u32[]{:S(2)}) collective-permute-start(bf16[1,64,1536]{1,2,0:T(8,128)(2,1)S(1)} %get-tuple-element.38), channel_id=1, source_target_pairs={{0,2},{2,4},{4,6},{6,8},{8,10},{10,12},{12,14},{1,3},{3,5},{5,7},{... | collective-permute-start | bytes 589832 | tf_op jit(solution)/shard_map/ppermute | solution.py:21
  66.7 20.2 %collective-permute-start.6 = (bf16[1,64,1536]{1,2,0:T(8,128)(2,1)S(1)}, bf16[1,64,1536]{1,2,0:T(8,128)(2,1)S(1)}, u32[]{:S(2)}, u32[]{:S(2)}) collective-permute-start(bf16[1,64,1536]{1,2,0:T(8,128)(2,1)S(1)} %get-tuple-element.39), channel_id=1, source_target_pairs={{2,0},{4,2},{6,4},{8,6},{10,8},{12,10},{14,12},{3,1},{5,3},{7,5},{... | collective-permute-start | bytes 589832 | tf_op jit(solution)/shard_map/ppermute | solution.py:23
  69.1 28.9 %collective-permute-start.19 = (f32[144,768]{1,0:T(8,128)S(1)}, f32[144,768]{1,0:T(8,128)S(1)}, u32[]{:S(2)}, u32[]{:S(2)}) collective-permute-start(f32[144,768]{1,0:T(8,128)S(1)} %constant_dynamic-slice_fusion.3), channel_id=1, source_target_pairs={{0,1},{1,0},{2,3},{3,2},{4,5},{5,4},{6,7},{7,6},{8,9},{9,8},{10,11... | collective-permute-start | bytes 1327112 | tf_op jit(solution)/shard_map/ppermute | solution.py:95
  96.3 12.8 %collective-permute-start.8 = (f32[96,768]{1,0:T(8,128)S(1)}, f32[96,768]{1,0:T(8,128)S(1)}, u32[]{:S(2)}, u32[]{:S(2)}) collective-permute-start(f32[96,768]{1,0:T(8,128)S(1)} %slice_add_fusion.11), channel_id=1, source_target_pairs={{0,4},{4,8},{8,12},{12,14},{14,10},{10,6},{6,2},{2,0},{1,5},{5,9},... | collective-permute-start | bytes 884744 | tf_op jit(solution)/shard_map/ppermute | solution.py:182
  98.1 10.9 %collective-permute-start.20 = (f32[144,384]{1,0:T(8,128)S(1)}, f32[144,384]{1,0:T(8,128)S(1)}, u32[]{:S(2)}, u32[]{:S(2)}) collective-permute-start(f32[144,384]{1,0:T(8,128)S(1)} %constant_dynamic-slice_fusion.2), channel_id=1, source_target_pairs={{0,2},{2,0},{4,6},{6,4},{8,10},{10,8},{12,14},{14,12},{1,3},{3,1},... | collective-permute-start | bytes 663560 | tf_op jit(solution)/shard_map/ppermute | solution.py:95
  99.1 15.4 %collective-permute-start.14 = (f32[96,768]{1,0:T(8,128)S(1)}, f32[96,768]{1,0:T(8,128)S(1)}, u32[]{:S(2)}, u32[]{:S(2)}) collective-permute-start(f32[96,768]{1,0:T(8,128)S(1)} %slice_add_fusion.5), channel_id=1, source_target_pairs={{0,2},{4,0},{8,4},{12,8},{14,12},{10,14},{6,10},{2,6},{1,3},{5,1},... | collective-permute-start | bytes 884744 | tf_op jit(solution)/shard_map/ppermute | solution.py:183
  109.1 18.0 %collective-permute-start.9 = (f32[96,768]{1,0:T(8,128)S(1)}, f32[96,768]{1,0:T(8,128)}, u32[]{:S(2)}, u32[]{:S(2)}) collective-permute-start(f32[96,768]{1,0:T(8,128)S(1)} %slice_add_fusion.10), channel_id=1, source_target_pairs={{0,4},{4,8},{8,12},{12,14},{14,10},{10,6},{6,2},{2,0},{1,5},{5,9},... | collective-permute-start | bytes 884744 | tf_op jit(solution)/shard_map/ppermute | solution.py:182
  113.9 7.1 %collective-permute-start.22 = (f32[36,384]{1,0:T(8,128)S(1)}, f32[36,384]{1,0:T(8,128)S(1)}, u32[]{:S(2)}, u32[]{:S(2)}) collective-permute-start(f32[36,384]{1,0:T(8,128)S(1)} %constant_dynamic-slice_fusion), channel_id=1, source_target_pairs={{0,8},{2,10},{4,12},{6,14},{8,0},{10,2},{12,4},{14,6},{1,9},{3,11}... | collective-permute-start | bytes 165896 | tf_op jit(solution)/shard_map/ppermute | solution.py:95
  114.5 15.5 %collective-permute-start.15 = (f32[96,768]{1,0:T(8,128)S(1)}, f32[96,768]{1,0:T(8,128)}, u32[]{:S(2)}, u32[]{:S(2)}) collective-permute-start(f32[96,768]{1,0:T(8,128)S(1)} %slice_add_fusion.4), channel_id=1, source_target_pairs={{0,2},{4,0},{8,4},{12,8},{14,12},{10,14},{6,10},{2,6},{1,3},{5,1},... | collective-permute-start | bytes 884744 | tf_op jit(solution)/shard_map/ppermute | solution.py:183
  128.1 8.9 %collective-permute-start.10 = (f32[96,768]{1,0:T(8,128)S(1)}, f32[96,768]{1,0:T(8,128)S(1)}, u32[]{:S(2)}, u32[]{:S(2)}) collective-permute-start(f32[96,768]{1,0:T(8,128)S(1)} %slice_add_fusion.9), channel_id=1, source_target_pairs={{0,4},{4,8},{8,12},{12,14},{14,10},{10,6},{6,2},{2,0},{1,5},{5,9},... | collective-permute-start | bytes 884744 | tf_op jit(solution)/shard_map/ppermute | solution.py:182
  131.1 9.3 %collective-permute-start.16 = (f32[96,768]{1,0:T(8,128)S(1)}, f32[96,768]{1,0:T(8,128)S(1)}, u32[]{:S(2)}, u32[]{:S(2)}) collective-permute-start(f32[96,768]{1,0:T(8,128)S(1)} %slice_add_fusion.3), channel_id=1, source_target_pairs={{0,2},{4,0},{8,4},{12,8},{14,12},{10,14},{6,10},{2,6},{1,3},{5,1},... | collective-permute-start | bytes 884744 | tf_op jit(solution)/shard_map/ppermute | solution.py:183
  132.1 9.1 %collective-permute-start.25 = (f32[144,384]{1,0:T(8,128)S(1)}, f32[144,384]{1,0:T(8,128)S(1)}, u32[]{:S(2)}, u32[]{:S(2)}) collective-permute-start(f32[144,384]{1,0:T(8,128)S(1)} %constant_dynamic-update-slice_fusion.4), channel_id=1, source_target_pairs={{0,2},{2,0},{4,6},{6,4},{8,10},{10,8},{12,14},{14,12},{1,3},{3,1},... | collective-permute-start | bytes 663560 | tf_op jit(solution)/shard_map/ppermute | solution.py:95
  137.1 6.8 %collective-permute-start.11 = (f32[96,768]{1,0:T(8,128)S(1)}, f32[96,768]{1,0:T(8,128)S(1)}, u32[]{:S(2)}, u32[]{:S(2)}) collective-permute-start(f32[96,768]{1,0:T(8,128)S(1)} %slice_add_fusion.8), channel_id=1, source_target_pairs={{0,4},{4,8},{8,12},{12,14},{14,10},{10,6},{6,2},{2,0},{1,5},{5,9},... | collective-permute-start | bytes 884744 | tf_op jit(solution)/shard_map/ppermute | solution.py:182
  140.4 8.1 %collective-permute-start.17 = (f32[96,768]{1,0:T(8,128)S(1)}, f32[96,768]{1,0:T(8,128)S(1)}, u32[]{:S(2)}, u32[]{:S(2)}) collective-permute-start(f32[96,768]{1,0:T(8,128)S(1)} %slice_add_fusion.2), channel_id=1, source_target_pairs={{0,2},{4,0},{8,4},{12,8},{14,12},{10,14},{6,10},{2,6},{1,3},{5,1},... | collective-permute-start | bytes 884744 | tf_op jit(solution)/shard_map/ppermute | solution.py:183
  141.2 7.5 %collective-permute-start.26 = (f32[144,768]{1,0:T(8,128)S(1)}, f32[144,768]{1,0:T(8,128)S(1)}, u32[]{:S(2)}, u32[]{:S(2)}) collective-permute-start(f32[144,768]{1,0:T(8,128)S(1)} %constant_dynamic-update-slice_fusion.2), channel_id=1, source_target_pairs={{0,1},{1,0},{2,3},{3,2},{4,5},{5,4},{6,7},{7,6},{8,9},{9,8},{10,11... | collective-permute-start | bytes 1327112 | tf_op jit(solution)/shard_map/ppermute | solution.py:95
  143.9 7.7 %collective-permute-start.12 = (f32[96,768]{1,0:T(8,128)S(1)}, f32[96,768]{1,0:T(8,128)S(1)}, u32[]{:S(2)}, u32[]{:S(2)}) collective-permute-start(f32[96,768]{1,0:T(8,128)S(1)} %slice_add_fusion.7), channel_id=1, source_target_pairs={{0,4},{4,8},{8,12},{12,14},{14,10},{10,6},{6,2},{2,0},{1,5},{5,9},... | collective-permute-start | bytes 884744 | tf_op jit(solution)/shard_map/ppermute | solution.py:182
  148.6 6.8 %collective-permute-start.18 = (f32[96,768]{1,0:T(8,128)S(1)}, f32[96,768]{1,0:T(8,128)S(1)}, u32[]{:S(2)}, u32[]{:S(2)}) collective-permute-start(f32[96,768]{1,0:T(8,128)S(1)} %slice_add_fusion.1), channel_id=1, source_target_pairs={{0,2},{4,0},{8,4},{12,8},{14,12},{10,14},{6,10},{2,6},{1,3},{5,1},... | collective-permute-start | bytes 884744 | tf_op jit(solution)/shard_map/ppermute | solution.py:183
  (24 other events, 252.4 us)

commit v15 on v11

--- a/solution.py
+++ b/solution.py
@@ -95,43 +95,42 @@
     return lax.ppermute(value, axis, [(i, i ^ distance) for i in range(count)])
 
 
-def halving_plan(rows, cols, steps):
-    plan = []
-    for _ in range(steps):
-        if cols % 256 == 0:
-            plan.append(1)
-            cols //= 2
-        else:
-            plan.append(0)
-            rows //= 2
-    return plan
-
-
 def tree_sum(value):
     shape = value.shape
     cells = value.reshape(-1, shape[-1])
-    stages = []
-    for axis in ("rep", "seq"):
-        distance = 1
-        while distance < lax.axis_size(axis):
-            stages.append((axis, distance))
-            distance *= 2
-    plan = halving_plan(cells.shape[0], cells.shape[1], len(stages))
-    held = cells
-    for (axis, distance), dim in zip(stages, plan):
-        bit = (lax.axis_index(axis) // distance) % 2
-        size = held.shape[dim] // 2
-        keep = lax.dynamic_slice_in_dim(held, bit * size, size, axis=dim)
-        give = lax.dynamic_slice_in_dim(held, (1 - bit) * size, size, axis=dim)
-        held = keep + swap(give, axis, distance)
-    for (axis, distance), dim in reversed(list(zip(stages, plan))):
-        bit = (lax.axis_index(axis) // distance) % 2
-        size = held.shape[dim]
-        other = swap(held, axis, distance)
-        full = jnp.concatenate([held, held], axis=dim)
-        full = lax.dynamic_update_slice_in_dim(full, held, bit * size, axis=dim)
-        held = lax.dynamic_update_slice_in_dim(full, other, (1 - bit) * size, axis=dim)
-    return held.reshape(shape)
+    rows, chans = cells.shape
+    rep_count = lax.axis_size("rep")
+    seq_count = lax.axis_size("seq")
+    if rep_count != 2 or chans % 2:
+        return lax.psum(value, ("seq", "rep"))
+    rep_bit = lax.axis_index("rep")
+    half = chans // 2
+    keep = lax.dynamic_slice_in_dim(cells, rep_bit * half, half, axis=1)
+    give = lax.dynamic_slice_in_dim(cells, (1 - rep_bit) * half, half, axis=1)
+    held = keep + swap(give, "rep", 1)
+    share = -(-rows // seq_count)
+    held = jnp.pad(held, ((0, share * seq_count - rows), (0, 0)))
+    pieces = held.reshape(seq_count, share, half)
+    here = lax.axis_index("seq")
+    total = lax.dynamic_index_in_dim(pieces, here, axis=0, keepdims=False)
+    for shift in range(1, seq_count):
+        perm = [(i, (i + shift) % seq_count) for i in range(seq_count)]
+        piece = lax.dynamic_index_in_dim(pieces, (here + shift) % seq_count, axis=0, keepdims=False)
+        total = total + lax.ppermute(piece, "seq", perm)
+    gathered = jnp.zeros_like(pieces)
+    gathered = lax.dynamic_update_index_in_dim(gathered, total, here, axis=0)
+    for shift in range(1, seq_count):
+        perm = [(i, (i + shift) % seq_count) for i in range(seq_count)]
+        source = (here - shift + seq_count) % seq_count
+        gathered = lax.dynamic_update_index_in_dim(
+            gathered, lax.ppermute(total, "seq", perm), source, axis=0
+        )
+    held = gathered.reshape(share * seq_count, half)[:rows]
+    other = swap(held, "rep", 1)
+    full = jnp.concatenate([held, held], axis=1)
+    full = lax.dynamic_update_slice_in_dim(full, held, rep_bit * half, axis=1)
+    full = lax.dynamic_update_slice_in_dim(full, other, (1 - rep_bit) * half, axis=1)
+    return full.reshape(shape)
 
 
 def ring_order(mesh):

time: 155 us -> 184 us (1.19)
  starting transfers between devices: 43.4 us -> 62.3 us
  other arithmetic: 19.3 us -> 24.3 us
  matrix products: 32.7 us -> 36.2 us
  local copies, waits for them, and re-layouts: 6.31 us -> 8.78 us
    ppermute x0 -> x14, starting transfers between devices: none -> 31.6 us  [the longest x7 17.4 us: tree_sum(): lax.ppermute(total, 'seq', perm)]
    ppermute x9 -> x3, waiting for transfers between devices: 18.5 us -> 0.01 us  [swap(): return lax.ppermute(value, axis, [(i, i ^ distance) for i in range(count)])]
    ppermute x7, waiting for transfers between devices: 17.1 us -> 28.9 us  [ring_reduce_scatter(): ahead = lax.ppermute(ahead, 'seq', forward) + block(-2 - step, True)]
    ppermute x0 -> x14, waiting for transfers between devices: none -> 8.03 us  [the longest x7 7.5 us: tree_sum(): lax.ppermute(total, 'seq', perm)]
    ppermute x9 -> x3, starting transfers between devices: 7.29 us -> 0.64 us  [swap(): return lax.ppermute(value, axis, [(i, i ^ distance) for i in range(count)])]
    ppermute x7, starting transfers between devices: 12.4 us -> 6.4 us  [ring_reduce_scatter(): ahead = lax.ppermute(ahead, 'seq', forward) + block(-2 - step, True)]
    dot_general x24, matrix products: 11.5 us -> 15 us  [conv_taps(): lax.dot_general(window, dense[k, :, cols], dims, preferred_element_type=j...]
    add x7, other arithmetic: 1.23 us -> 4.01 us  [ring_reduce_scatter(): ahead = lax.ppermute(ahead, 'seq', forward) + block(-2 - step, True)]
  transfers between devices with their start and end apart: 27 -> 35, of which waited for: 14 -> 15; matrix products, arithmetic and copies ran while one was open for 19% -> 22% of each run, Pallas kernels for 0% -> 0%
where the time goes in v15:
time: 184 us
  starting transfers between devices  62.3 us (34%)
  waiting for transfers between devices  49.7 us (27%)
  matrix products  36.2 us (20%)
  other arithmetic  24.3 us (13%)
  local copies, waits for them, and re-layouts  8.78 us (5%)
  between operations  2.27 us (1%)
    ppermute x7, waiting for transfers between devices, ring_reduce_scatter(): ahead = lax.ppermute(ahead, 'seq', forward) + block(-2 - step, True)  28.9 us
    ppermute x7, starting transfers between devices, tree_sum(): lax.ppermute(total, 'seq', perm)  17.4 us
    dot_general x24, matrix products, conv_taps(): lax.dot_general(window, dense[k, :, cols], dims, preferred_element_type=j...  15 us
    ppermute x7, starting transfers between devices, tree_sum(): total = total + lax.ppermute(piece, 'seq', perm)  14.2 us
    ppermute x7, starting transfers between devices, ring_reduce_scatter(): behind = lax.ppermute(behind, 'seq', backward) + block(2 + step, False)  11.5 us
    ppermute x2, waiting for transfers between devices, with_halo(): lax.ppermute(tail, axis, [(i, (i + 1) % count) for i in range(ends)])  11.2 us
    ppermute x2, starting transfers between devices, with_halo(): lax.ppermute(tail, axis, [(i, (i + 1) % count) for i in range(ends)])  9.6 us
    ppermute x7, waiting for transfers between devices, tree_sum(): lax.ppermute(total, 'seq', perm)  7.5 us
  transfers between devices with their start and end apart: 35, of which 15 were waited for; matrix products, arithmetic and copies ran while one was open for 22% of the time, Pallas kernels for 0%

profile of v15, /device:TPU:0, one launch (start us, length us, event | category | flops | bytes accessed | tf_op | source)
XLA Modules:
  0.0 183.5 jit_solution(17075681557349398476)
XLA Ops:
  3.8 5.5 %collective-permute-start = (bf16[1,64,1536]{2,1,0:T(8,128)(2,1)}, bf16[1,64,1536]{2,1,0:T(8,128)(2,1)}, u32[]{:S(2)}, u32[]{:S(2)}) collective-permute-start(bf16[1,64,1536]{2,1,0:T(8,128)(2,1)} %get-tuple-element.42), channel_id=1, source_target_pairs={{0,2},{2,4},{4,6},{6,8},{8,10},{10,12},{12,14},{1,3},{3,5},{5,7},{... | collective-permute-start | bytes 589832 | tf_op jit(solution)/shard_map/ppermute | solution.py:21
  13.5 3.9 %collective-permute-done = bf16[1,64,1536]{2,1,0:T(8,128)(2,1)} collective-permute-done((bf16[1,64,1536]{2,1,0:T(8,128)(2,1)}, bf16[1,64,1536]{2,1,0:T(8,128)(2,1)}, u32[]{:S(2)}, u32[]{:S(2)}) %collective-permute-start) | collective-permute-done | bytes 196640 | tf_op jit(solution)/shard_map/ppermute | solution.py:21
  26.7 3.6 %convolution_multiply_fusion = f32[768,1536]{1,0:T(8,128)} fusion(bf16[512,768]{0,1:T(8,128)(2,1)S(1)} %bitcast.197, bf16[1,512,1536]{2,1,0:T(8,128)(2,1)S(1)} %copy-done.2), kind=kOutput, calls=%fused_computation.4 | convolution fusion | flops 1209139200 | bytes 7077888 | tf_op jit(solution)/shard_map/dot_general | solution.py:190
  30.4 2.7 %convolution_multiply_fusion.1 = f32[768,1536]{1,0:T(8,128)S(1)} fusion(bf16[512,768]{0,1:T(8,128)(2,1)} %bitcast.196, bf16[1,512,1536]{2,1,0:T(8,128)(2,1)S(1)} %copy-done.2), kind=kOutput, calls=%fused_computation.5 | convolution fusion | flops 1209139200 | bytes 7077888 | tf_op jit(solution)/shard_map/dot_general | solution.py:190
  33.1 6.2 %fusion.2 = bf16[1,512,1536]{2,1,0:T(8,128)(2,1)} fusion(bf16[1,512,1536]{2,1,0:T(8,128)(2,1)S(1)} %copy-done.12, bf16[1536,1536]{1,0:T(8,128)(2,1)} %param.8, f32[512]{0:T(512)S(1)} %fusion.118, f32[512,384]{0,1:T(8,128)S(1)} %copy-done.10, f32[512,384]{0,1:T(8,128)S(1)} %copy-done.8, f32[512,384]{0,1:T(8,128)S(1)} %copy-done.6, f32[512,384]{0,1:T(8,128)S(1)} %copy-done.4), kind=kOutput, calls=%fused_computation.14 | convolution fusion | flops 2425356288 | bytes 11012096 | tf_op jit(solution)/shard_map/dot_general | solution.py:230
  39.4 3.3 %add.570 = f32[8,96,1536]{2,1,0:T(8,128)S(1)} add(f32[8,96,1536]{2,1,0:T(8,128)S(1)} %bitcast.187, f32[8,96,1536]{2,1,0:T(8,128)} %collective-permute-done.2) | non-fusion elementwise | flops 1179648 | bytes 14155776 | tf_op jit(solution)/shard_map/add | solution.py:207
  42.7 3.9 %fusion.9 = bf16[512,1536]{0,1:T(8,128)(2,1)S(1)} fusion(bf16[512,1536]{1,0:T(8,128)(2,1)S(1)} %bitcast.188, bf16[1536,1536]{1,0:T(8,128)(2,1)S(1)} %bitcast.212, f32[512]{0:T(512)S(1)} %fusion.118, f32[512,384]{0,1:T(8,128)S(1)} %copy-done.10, f32[512,384]{0,1:T(8,128)S(1)} %copy-done.8, f32[512,384]{0,1:T(8,128)S(1)} %copy-done.6, ...), kind=kOutput, calls=%fused_computation.27 | convolution fusion | flops 2426929152 | bytes 11012096 | tf_op jit(solution)/shard_map/dot_general | solution.py:233
  53.4 4.1 %collective-permute-start.3 = (bf16[1,64,1536]{1,2,0:T(8,128)(2,1)S(1)}, bf16[1,64,1536]{1,2,0:T(8,128)(2,1)S(1)}, u32[]{:S(2)}, u32[]{:S(2)}) collective-permute-start(bf16[1,64,1536]{1,2,0:T(8,128)(2,1)S(1)} %get-tuple-element.38), channel_id=1, source_target_pairs={{0,2},{2,4},{4,6},{6,8},{8,10},{10,12},{12,14},{1,3},{3,5},{5,7},{... | collective-permute-start | bytes 589832 | tf_op jit(solution)/shard_map/ppermute | solution.py:21
  58.8 3.4 %dynamic-slice_bitcast_fusion.8 = (f32[96,1536]{1,0:T(8,128)}, f32[96,1536]{1,0:T(8,128)}, f32[96,1536]{1,0:T(8,128)}, f32[96,1536]{1,0:T(8,128)}, f32[96,1536]{...) fusion(f32[8,96,1536]{2,1,0:T(8,128)S(1)} %add.570, ...), kind=kLoop, calls=%fused_computation.80 | loop fusion | bytes 18874432 | tf_op jit(solution)/shard_map/jit(dynamic_index_in_dim)/squeeze | solution.py:175
  62.9 4.5 %collective-permute-start.5 = (f32[96,768]{1,0:T(8,128)}, f32[96,768]{1,0:T(8,128)}, u32[]{:S(2)}, u32[]{:S(2)}) collective-permute-start(f32[96,768]{1,0:T(8,128)} %slice.312), channel_id=1, source_target_pairs={{0,4},{4,8},{8,12},{12,14},{14,10},{10,6},{6,2},{2,0},{1,5},{5,9},... | collective-permute-start | bytes 884744 | tf_op jit(solution)/shard_map/ppermute | solution.py:181
  68.1 7.3 %collective-permute-done.3 = bf16[1,64,1536]{1,2,0:T(8,128)(2,1)S(1)} collective-permute-done((bf16[1,64,1536]{1,2,0:T(8,128)(2,1)S(1)}, bf16[1,64,1536]{1,2,0:T(8,128)(2,1)S(1)}, u32[]{:S(2)}, u32[]{:S(2)}) %collective-permute-start.3) | collective-permute-done | bytes 196640 | tf_op jit(solution)/shard_map/ppermute | solution.py:21
  92.1 4.1 %collective-permute-start.22 = (f32[18,768]{1,0:T(8,128)S(1)}, f32[18,768]{1,0:T(8,128)S(1)}, u32[]{:S(2)}, u32[]{:S(2)}) collective-permute-start(f32[18,768]{1,0:T(8,128)S(1)} %get-tuple-element.49), channel_id=1, source_target_pairs={{0,6},{2,8},{4,10},{6,12},{8,14},{10,0},{12,2},{14,4},{1,7},{3,9},... | collective-permute-start | bytes 165896 | tf_op jit(solution)/shard_map/ppermute | solution.py:119
  96.2 3.2 %fusion.8 = bf16[1,512,1536]{2,1,0:T(8,128)(2,1)} fusion(f32[1,512,384]{2,1,0:T(8,128)} %fusion.27, f32[1,512,384]{2,1,0:T(8,128)} %fusion.25, f32[1,512,384]{2,1,0:T(8,128)} %fusion.23, f32[1,512,384]{2,1,0:T(8,128)S(1)} %copy-done.11, bf16[1,512,1536]{2,1,0:T(8,128)(2,1)S(1)} %copy-done.2, f32[512]{0:T(512)S(1)} %fusion.118), kind=kLoop, calls=%fused_computation.23 | loop fusion | flops 5505024 | bytes 6293504 | tf_op jit(solution)/shard_map/convert_element_type | solution.py:241
  103.3 2.8 %collective-permute-start.26 = (f32[18,768]{1,0:T(8,128)S(1)}, f32[18,768]{1,0:T(8,128)S(1)}, u32[]{:S(2)}, u32[]{:S(2)}) collective-permute-start(f32[18,768]{1,0:T(8,128)S(1)} %get-tuple-element.45), channel_id=1, source_target_pairs={{0,14},{2,0},{4,2},{6,4},{8,6},{10,8},{12,10},{14,12},{1,15},{3,1}... | collective-permute-start | bytes 165896 | tf_op jit(solution)/shard_map/ppermute | solution.py:119
  114.6 2.8 %collective-permute-start.29 = (f32[18,768]{1,0:T(8,128)S(1)}, f32[18,768]{1,0:T(8,128)S(1)}, u32[]{:S(2)}, u32[]{:S(2)}) collective-permute-start(f32[18,768]{1,0:T(8,128)S(1)} %get-tuple-element.21), channel_id=1, source_target_pairs={{0,6},{2,8},{4,10},{6,12},{8,14},{10,0},{12,2},{14,4},{1,7},{3,9},... | collective-permute-start | bytes 165896 | tf_op jit(solution)/shard_map/ppermute | solution.py:126
  117.5 2.7 %collective-permute-start.30 = (f32[18,768]{1,0:T(8,128)S(1)}, f32[18,768]{1,0:T(8,128)S(1)}, u32[]{:S(2)}, u32[]{:S(2)}) collective-permute-start(f32[18,768]{1,0:T(8,128)S(1)} %get-tuple-element.21), channel_id=1, source_target_pairs={{0,8},{2,10},{4,12},{6,14},{8,0},{10,2},{12,4},{14,6},{1,9},{3,11}... | collective-permute-start | bytes 165896 | tf_op jit(solution)/shard_map/ppermute | solution.py:126
  120.2 6.2 %collective-permute-done.28 = f32[18,768]{1,0:T(8,128)S(1)} collective-permute-done((f32[18,768]{1,0:T(8,128)S(1)}, f32[18,768]{1,0:T(8,128)S(1)}, u32[]{:S(2)}, u32[]{:S(2)}) %collective-permute-start.28) | collective-permute-done | bytes 55328 | tf_op jit(solution)/shard_map/ppermute | solution.py:126
  126.4 4.9 %collective-permute-start.31 = (f32[18,768]{1,0:T(8,128)S(1)}, f32[18,768]{1,0:T(8,128)S(1)}, u32[]{:S(2)}, u32[]{:S(2)}) collective-permute-start(f32[18,768]{1,0:T(8,128)S(1)} %get-tuple-element.21), channel_id=1, source_target_pairs={{0,10},{2,12},{4,14},{6,0},{8,2},{10,4},{12,6},{14,8},{1,11},{3,13... | collective-permute-start | bytes 165896 | tf_op jit(solution)/shard_map/ppermute | solution.py:126
  131.3 2.5 %collective-permute-start.32 = (f32[18,768]{1,0:T(8,128)S(1)}, f32[18,768]{1,0:T(8,128)S(1)}, u32[]{:S(2)}, u32[]{:S(2)}) collective-permute-start(f32[18,768]{1,0:T(8,128)S(1)} %get-tuple-element.21), channel_id=1, source_target_pairs={{0,12},{2,14},{4,0},{6,2},{8,4},{10,6},{12,8},{14,10},{1,13},{3,15... | collective-permute-start | bytes 165896 | tf_op jit(solution)/shard_map/ppermute | solution.py:126
  140.2 6.6 %collective-permute-done.7 = f32[96,768]{1,0:T(8,128)} collective-permute-done((f32[96,768]{1,0:T(8,128)}, f32[96,768]{1,0:T(8,128)}, u32[]{:S(2)}, u32[]{:S(2)}) %collective-permute-start.7) | collective-permute-done | bytes 294944 | tf_op jit(solution)/shard_map/ppermute | solution.py:181
  150.4 4.4 %collective-permute-done.8 = f32[96,768]{1,0:T(8,128)S(1)} collective-permute-done((f32[96,768]{1,0:T(8,128)S(1)}, f32[96,768]{1,0:T(8,128)S(1)}, u32[]{:S(2)}, u32[]{:S(2)}) %collective-permute-start.8) | collective-permute-done | bytes 294944 | tf_op jit(solution)/shard_map/ppermute | solution.py:181
  158.0 6.8 %collective-permute-done.9 = f32[96,768]{1,0:T(8,128)S(1)} collective-permute-done((f32[96,768]{1,0:T(8,128)S(1)}, f32[96,768]{1,0:T(8,128)S(1)}, u32[]{:S(2)}, u32[]{:S(2)}) %collective-permute-start.9) | collective-permute-done | bytes 294944 | tf_op jit(solution)/shard_map/ppermute | solution.py:181
  167.1 7.5 %collective-permute-done.10 = f32[96,768]{1,0:T(8,128)S(1)} collective-permute-done((f32[96,768]{1,0:T(8,128)S(1)}, f32[96,768]{1,0:T(8,128)S(1)}, u32[]{:S(2)}, u32[]{:S(2)}) %collective-permute-start.10) | collective-permute-done | bytes 294944 | tf_op jit(solution)/shard_map/ppermute | solution.py:181
  177.8 3.6 %collective-permute-done.11 = f32[96,768]{1,0:T(8,128)S(1)} collective-permute-done((f32[96,768]{1,0:T(8,128)S(1)}, f32[96,768]{1,0:T(8,128)S(1)}, u32[]{:S(2)}, u32[]{:S(2)}) %collective-permute-start.11) | collective-permute-done | bytes 294944 | tf_op jit(solution)/shard_map/ppermute | solution.py:181
  (203 shorter events, 75.1 us)
Async XLA Ops:
  3.8 13.6 %collective-permute-start = (bf16[1,64,1536]{2,1,0:T(8,128)(2,1)}, bf16[1,64,1536]{2,1,0:T(8,128)(2,1)}, u32[]{:S(2)}, u32[]{:S(2)}) collective-permute-start(bf16[1,64,1536]{2,1,0:T(8,128)(2,1)} %get-tuple-element.42), channel_id=1, source_target_pairs={{0,2},{2,4},{4,6},{6,8},{8,10},{10,12},{12,14},{1,3},{3,5},{5,7},{... | collective-permute-start | bytes 589832 | tf_op jit(solution)/shard_map/ppermute | solution.py:21
  9.3 8.3 %collective-permute-start.1 = (bf16[1,64,1536]{2,1,0:T(8,128)(2,1)S(1)}, bf16[1,64,1536]{2,1,0:T(8,128)(2,1)}, u32[]{:S(2)}, u32[]{:S(2)}) collective-permute-start(bf16[1,64,1536]{2,1,0:T(8,128)(2,1)S(1)} %get-tuple-element.43), channel_id=1, source_target_pairs={{2,0},{4,2},{6,4},{8,6},{10,8},{12,10},{14,12},{3,1},{5,3},{7,5},{... | collective-permute-start | bytes 589832 | tf_op jit(solution)/shard_map/ppermute | solution.py:23
  30.3 9.1 %collective-permute-start.2 = (f32[8,96,1536]{2,1,0:T(8,128)}, f32[8,96,1536]{2,1,0:T(8,128)}, u32[]{:S(2)}, u32[]{:S(2)}) collective-permute-start(f32[8,96,1536]{2,1,0:T(8,128)} %bitcast.25), channel_id=1, source_target_pairs={{0,1},{1,0},{2,3},{3,2},{4,5},{5,4},{6,7},{7,6},{8,9},{9,8},{10,11... | collective-permute-start | bytes 14155784 | tf_op jit(solution)/shard_map/ppermute | solution.py:95
  52.6 34.0 %collective-permute-start.19 = (f32[144,768]{1,0:T(8,128)S(1)}, f32[144,768]{1,0:T(8,128)S(1)}, u32[]{:S(2)}, u32[]{:S(2)}) collective-permute-start(f32[144,768]{1,0:T(8,128)S(1)} %constant_dynamic-slice_fusion), channel_id=1, source_target_pairs={{0,1},{1,0},{2,3},{3,2},{4,5},{5,4},{6,7},{7,6},{8,9},{9,8},{10,11... | collective-permute-start | bytes 1327112 | tf_op jit(solution)/shard_map/ppermute | solution.py:95
  53.4 21.9 %collective-permute-start.3 = (bf16[1,64,1536]{1,2,0:T(8,128)(2,1)S(1)}, bf16[1,64,1536]{1,2,0:T(8,128)(2,1)S(1)}, u32[]{:S(2)}, u32[]{:S(2)}) collective-permute-start(bf16[1,64,1536]{1,2,0:T(8,128)(2,1)S(1)} %get-tuple-element.38), channel_id=1, source_target_pairs={{0,2},{2,4},{4,6},{6,8},{8,10},{10,12},{12,14},{1,3},{3,5},{5,7},{... | collective-permute-start | bytes 589832 | tf_op jit(solution)/shard_map/ppermute | solution.py:21
  57.5 17.9 %collective-permute-start.4 = (bf16[1,64,1536]{1,2,0:T(8,128)(2,1)S(1)}, bf16[1,64,1536]{1,2,0:T(8,128)(2,1)S(1)}, u32[]{:S(2)}, u32[]{:S(2)}) collective-permute-start(bf16[1,64,1536]{1,2,0:T(8,128)(2,1)S(1)} %get-tuple-element.39), channel_id=1, source_target_pairs={{2,0},{4,2},{6,4},{8,6},{10,8},{12,10},{14,12},{3,1},{5,3},{7,5},{... | collective-permute-start | bytes 589832 | tf_op jit(solution)/shard_map/ppermute | solution.py:23
  62.9 36.5 %collective-permute-start.5 = (f32[96,768]{1,0:T(8,128)}, f32[96,768]{1,0:T(8,128)}, u32[]{:S(2)}, u32[]{:S(2)}) collective-permute-start(f32[96,768]{1,0:T(8,128)} %slice.312), channel_id=1, source_target_pairs={{0,4},{4,8},{8,12},{12,14},{14,10},{10,6},{6,2},{2,0},{1,5},{5,9},... | collective-permute-start | bytes 884744 | tf_op jit(solution)/shard_map/ppermute | solution.py:181
  68.1 43.5 %collective-permute-start.12 = (f32[96,768]{1,0:T(8,128)}, f32[96,768]{1,0:T(8,128)}, u32[]{:S(2)}, u32[]{:S(2)}) collective-permute-start(f32[96,768]{1,0:T(8,128)} %slice.320), channel_id=1, source_target_pairs={{0,2},{4,0},{8,4},{12,8},{14,12},{10,14},{6,10},{2,6},{1,3},{5,1},... | collective-permute-start | bytes 884744 | tf_op jit(solution)/shard_map/ppermute | solution.py:182
  88.6 12.0 %collective-permute-start.20 = (f32[18,768]{1,0:T(8,128)S(1)}, f32[18,768]{1,0:T(8,128)S(1)}, u32[]{:S(2)}, u32[]{:S(2)}) collective-permute-start(f32[18,768]{1,0:T(8,128)S(1)} %get-tuple-element.44), channel_id=1, source_target_pairs={{0,2},{2,4},{4,6},{6,8},{8,10},{10,12},{12,14},{14,0},{1,3},{3,5},... | collective-permute-start | bytes 165896 | tf_op jit(solution)/shard_map/ppermute | solution.py:119
  91.2 10.7 %collective-permute-start.21 = (f32[18,768]{1,0:T(8,128)S(1)}, f32[18,768]{1,0:T(8,128)S(1)}, u32[]{:S(2)}, u32[]{:S(2)}) collective-permute-start(f32[18,768]{1,0:T(8,128)S(1)} %get-tuple-element.50), channel_id=1, source_target_pairs={{0,4},{2,6},{4,8},{6,10},{8,12},{10,14},{12,0},{14,2},{1,5},{3,7},... | collective-permute-start | bytes 165896 | tf_op jit(solution)/shard_map/ppermute | solution.py:119
  92.1 11.1 %collective-permute-start.22 = (f32[18,768]{1,0:T(8,128)S(1)}, f32[18,768]{1,0:T(8,128)S(1)}, u32[]{:S(2)}, u32[]{:S(2)}) collective-permute-start(f32[18,768]{1,0:T(8,128)S(1)} %get-tuple-element.49), channel_id=1, source_target_pairs={{0,6},{2,8},{4,10},{6,12},{8,14},{10,0},{12,2},{14,4},{1,7},{3,9},... | collective-permute-start | bytes 165896 | tf_op jit(solution)/shard_map/ppermute | solution.py:119
  107.3 29.3 %collective-permute-start.6 = (f32[96,768]{1,0:T(8,128)S(1)}, f32[96,768]{1,0:T(8,128)S(1)}, u32[]{:S(2)}, u32[]{:S(2)}) collective-permute-start(f32[96,768]{1,0:T(8,128)S(1)} %slice_add_fusion.13), channel_id=1, source_target_pairs={{0,4},{4,8},{8,12},{12,14},{14,10},{10,6},{6,2},{2,0},{1,5},{5,9},... | collective-permute-start | bytes 884744 | tf_op jit(solution)/shard_map/ppermute | solution.py:181
  112.5 24.8 %collective-permute-start.13 = (f32[96,768]{1,0:T(8,128)S(1)}, f32[96,768]{1,0:T(8,128)S(1)}, u32[]{:S(2)}, u32[]{:S(2)}) collective-permute-start(f32[96,768]{1,0:T(8,128)S(1)} %slice_add_fusion.6), channel_id=1, source_target_pairs={{0,2},{4,0},{8,4},{12,8},{14,12},{10,14},{6,10},{2,6},{1,3},{5,1},... | collective-permute-start | bytes 884744 | tf_op jit(solution)/shard_map/ppermute | solution.py:182
  113.9 12.4 %collective-permute-start.28 = (f32[18,768]{1,0:T(8,128)S(1)}, f32[18,768]{1,0:T(8,128)S(1)}, u32[]{:S(2)}, u32[]{:S(2)}) collective-permute-start(f32[18,768]{1,0:T(8,128)S(1)} %get-tuple-element.21), channel_id=1, source_target_pairs={{0,4},{2,6},{4,8},{6,10},{8,12},{10,14},{12,0},{14,2},{1,5},{3,7},... | collective-permute-start | bytes 165896 | tf_op jit(solution)/shard_map/ppermute | solution.py:126
  114.6 16.6 %collective-permute-start.29 = (f32[18,768]{1,0:T(8,128)S(1)}, f32[18,768]{1,0:T(8,128)S(1)}, u32[]{:S(2)}, u32[]{:S(2)}) collective-permute-start(f32[18,768]{1,0:T(8,128)S(1)} %get-tuple-element.21), channel_id=1, source_target_pairs={{0,6},{2,8},{4,10},{6,12},{8,14},{10,0},{12,2},{14,4},{1,7},{3,9},... | collective-permute-start | bytes 165896 | tf_op jit(solution)/shard_map/ppermute | solution.py:126
  117.5 16.4 %collective-permute-start.30 = (f32[18,768]{1,0:T(8,128)S(1)}, f32[18,768]{1,0:T(8,128)S(1)}, u32[]{:S(2)}, u32[]{:S(2)}) collective-permute-start(f32[18,768]{1,0:T(8,128)S(1)} %get-tuple-element.21), channel_id=1, source_target_pairs={{0,8},{2,10},{4,12},{6,14},{8,0},{10,2},{12,4},{14,6},{1,9},{3,11}... | collective-permute-start | bytes 165896 | tf_op jit(solution)/shard_map/ppermute | solution.py:126
  126.4 8.9 %collective-permute-start.31 = (f32[18,768]{1,0:T(8,128)S(1)}, f32[18,768]{1,0:T(8,128)S(1)}, u32[]{:S(2)}, u32[]{:S(2)}) collective-permute-start(f32[18,768]{1,0:T(8,128)S(1)} %get-tuple-element.21), channel_id=1, source_target_pairs={{0,10},{2,12},{4,14},{6,0},{8,2},{10,4},{12,6},{14,8},{1,11},{3,13... | collective-permute-start | bytes 165896 | tf_op jit(solution)/shard_map/ppermute | solution.py:126
  137.3 9.5 %collective-permute-start.7 = (f32[96,768]{1,0:T(8,128)}, f32[96,768]{1,0:T(8,128)}, u32[]{:S(2)}, u32[]{:S(2)}) collective-permute-start(f32[96,768]{1,0:T(8,128)} %slice_add_fusion.12), channel_id=1, source_target_pairs={{0,4},{4,8},{8,12},{12,14},{14,10},{10,6},{6,2},{2,0},{1,5},{5,9},... | collective-permute-start | bytes 884744 | tf_op jit(solution)/shard_map/ppermute | solution.py:181
  138.1 9.9 %collective-permute-start.14 = (f32[96,768]{1,0:T(8,128)}, f32[96,768]{1,0:T(8,128)S(1)}, u32[]{:S(2)}, u32[]{:S(2)}) collective-permute-start(f32[96,768]{1,0:T(8,128)} %slice_add_fusion.5), channel_id=1, source_target_pairs={{0,2},{4,0},{8,4},{12,8},{14,12},{10,14},{6,10},{2,6},{1,3},{5,1},... | collective-permute-start | bytes 884744 | tf_op jit(solution)/shard_map/ppermute | solution.py:182
  150.3 16.7 %collective-permute-start.34 = (f32[144,768]{1,0:T(8,128)S(1)}, f32[144,768]{1,0:T(8,128)S(1)}, u32[]{:S(2)}, u32[]{:S(2)}) collective-permute-start(f32[144,768]{1,0:T(8,128)S(1)} %reshape.353), channel_id=1, source_target_pairs={{0,1},{1,0},{2,3},{3,2},{4,5},{5,4},{6,7},{7,6},{8,9},{9,8},{10,11... | collective-permute-start | bytes 1327112 | tf_op jit(solution)/shard_map/ppermute | solution.py:95
  155.8 9.0 %collective-permute-start.9 = (f32[96,768]{1,0:T(8,128)S(1)}, f32[96,768]{1,0:T(8,128)S(1)}, u32[]{:S(2)}, u32[]{:S(2)}) collective-permute-start(f32[96,768]{1,0:T(8,128)S(1)} %slice_add_fusion.10), channel_id=1, source_target_pairs={{0,4},{4,8},{8,12},{12,14},{14,10},{10,6},{6,2},{2,0},{1,5},{5,9},... | collective-permute-start | bytes 884744 | tf_op jit(solution)/shard_map/ppermute | solution.py:181
  156.0 8.9 %collective-permute-start.16 = (f32[96,768]{1,0:T(8,128)S(1)}, f32[96,768]{1,0:T(8,128)S(1)}, u32[]{:S(2)}, u32[]{:S(2)}) collective-permute-start(f32[96,768]{1,0:T(8,128)S(1)} %slice_add_fusion.3), channel_id=1, source_target_pairs={{0,2},{4,0},{8,4},{12,8},{14,12},{10,14},{6,10},{2,6},{1,3},{5,1},... | collective-permute-start | bytes 884744 | tf_op jit(solution)/shard_map/ppermute | solution.py:182
  164.9 9.7 %collective-permute-start.10 = (f32[96,768]{1,0:T(8,128)S(1)}, f32[96,768]{1,0:T(8,128)S(1)}, u32[]{:S(2)}, u32[]{:S(2)}) collective-permute-start(f32[96,768]{1,0:T(8,128)S(1)} %slice_add_fusion.9), channel_id=1, source_target_pairs={{0,4},{4,8},{8,12},{12,14},{14,10},{10,6},{6,2},{2,0},{1,5},{5,9},... | collective-permute-start | bytes 884744 | tf_op jit(solution)/shard_map/ppermute | solution.py:181
  165.0 9.9 %collective-permute-start.17 = (f32[96,768]{1,0:T(8,128)S(1)}, f32[96,768]{1,0:T(8,128)S(1)}, u32[]{:S(2)}, u32[]{:S(2)}) collective-permute-start(f32[96,768]{1,0:T(8,128)S(1)} %slice_add_fusion.2), channel_id=1, source_target_pairs={{0,2},{4,0},{8,4},{12,8},{14,12},{10,14},{6,10},{2,6},{1,3},{5,1},... | collective-permute-start | bytes 884744 | tf_op jit(solution)/shard_map/ppermute | solution.py:182
  (39 other events, 461.1 us)

commit v16 on v11

--- a/solution.py
+++ b/solution.py
@@ -151,7 +151,7 @@
     return count % 2 == 0 and [s for _, s in cells] == snake
 
 
-def ring_reduce_scatter(blocks, snake):
+def ring_reduce_scatter(blocks, snake, hold):
     count = blocks.shape[0]
     half_count = count // 2
     if snake:
@@ -181,10 +181,12 @@
     for step in range(count - 1):
         ahead = lax.ppermute(ahead, "seq", forward) + block(-2 - step, True)
         behind = lax.ppermute(behind, "seq", backward) + block(2 + step, False)
-    return jnp.concatenate([ahead, behind], axis=1)
-
-
-def point_gradient(act_rows, cot_rows, scale, snake):
+        if step == count // 2 - 1:
+            ahead, behind, hold = lax.optimization_barrier((ahead, behind, hold))
+    return jnp.concatenate([ahead, behind], axis=1), hold
+
+
+def point_gradient(act_rows, cot_rows, scale):
     chans = act_rows.shape[1]
     seq_count = lax.axis_size("seq")
     rep_count = lax.axis_size("rep")
@@ -207,7 +209,7 @@
 
     mine = rows_of(rep_index) + swap(rows_of(1 - rep_index), "rep", 1)
     mine, cot_rows = lax.optimization_barrier((mine, cot_rows))
-    return ring_reduce_scatter(mine, snake), cot_rows
+    return mine, cot_rows
 
 
 def on_device(snake, inputs, lengths, conv_weight, point_weight, cotangent):
@@ -230,7 +232,7 @@
     cot_rows = cotangent.reshape(local_bins, chans)
     proj = jnp.dot(act_rows, point_weight, preferred_element_type=jnp.float32).reshape(inputs.shape)
     output = (inputs.astype(jnp.float32) + proj).astype(jnp.bfloat16)
-    grad_point, cot_rows = point_gradient(act_rows, cot_rows, scale, snake)
+    mine, cot_rows = point_gradient(act_rows, cot_rows, scale)
     back = lax.dot_general(
         cot_rows, point_weight, (((1,), (1,)), ((), ())), preferred_element_type=jnp.float32
     )
@@ -238,6 +240,10 @@
     padded_gradient = with_halo(preactivation_gradient, (("seq", 1),), DILATION_STEP)
     spread = conv_taps(padded_gradient, dense, local_bins, transpose=True)
     conv_local = weight_taps(padded_input, preactivation_gradient, local_bins)
+    if lax.axis_size("rep") == 2:
+        grad_point, conv_local = ring_reduce_scatter(mine, snake, conv_local)
+    else:
+        grad_point = mine
     grad_conv = tree_sum(conv_local) * scale
     grad_inputs = (cotangent.astype(jnp.float32) + mask3 * spread).astype(jnp.bfloat16)
     return (output, grad_inputs, grad_point, grad_conv)

time: 155 us -> 168 us (1.084)
  waiting for transfers between devices: 51 us -> 72.9 us
  starting transfers between devices: 43.4 us -> 36.9 us
  other arithmetic: 19.3 us -> 16.7 us
    ppermute x7, waiting for transfers between devices: 1.84 us -> 18.1 us  [ring_reduce_scatter(): behind = lax.ppermute(behind, 'seq', backward) + block(2 + step, False)]
    ppermute x7, waiting for transfers between devices: 17.1 us -> 5.83 us  [ring_reduce_scatter(): ahead = lax.ppermute(ahead, 'seq', forward) + block(-2 - step, True)]
    ppermute x9, waiting for transfers between devices: 18.5 us -> 27.7 us  [swap(): return lax.ppermute(value, axis, [(i, i ^ distance) for i in range(count)])]
    ppermute x2, waiting for transfers between devices: 13.2 us -> 21 us  [with_halo(): lax.ppermute(tail, axis, [(i, (i + 1) % count) for i in range(ends)])]
    ppermute x9, starting transfers between devices: 7.29 us -> 4.75 us  [swap(): return lax.ppermute(value, axis, [(i, i ^ distance) for i in range(count)])]
    add x7, other arithmetic: 2.04 us -> 0.29 us  [ring_reduce_scatter(): behind = lax.ppermute(behind, 'seq', backward) + block(2 + step, False)]
  transfers between devices with their start and end apart: 27 -> 27, of which waited for: 14 -> 17; matrix products, arithmetic and copies ran while one was open for 19% -> 15% of each run, Pallas kernels for 0% -> 0%
where the time goes in v16:
time: 168 us
  waiting for transfers between devices  72.9 us (43%)
  starting transfers between devices  36.9 us (22%)
  matrix products  32.7 us (19%)
  other arithmetic  16.7 us (10%)
  local copies, waits for them, and re-layouts  6.25 us (4%)
  between operations  2.33 us (1%)
    ppermute x9, waiting for transfers between devices, swap(): return lax.ppermute(value, axis, [(i, i ^ distance) for i in range(count)])  27.7 us
    ppermute x2, waiting for transfers between devices, with_halo(): lax.ppermute(tail, axis, [(i, (i + 1) % count) for i in range(ends)])  21 us
    ppermute x7, waiting for transfers between devices, ring_reduce_scatter(): behind = lax.ppermute(behind, 'seq', backward) + block(2 + step, False)  18.1 us
    dot_general x24, matrix products, conv_taps(): lax.dot_general(window, dense[k, :, cols], dims, preferred_element_type=j...  11.5 us
    ppermute x7, starting transfers between devices, ring_reduce_scatter(): ahead = lax.ppermute(ahead, 'seq', forward) + block(-2 - step, True)  11.1 us
    ppermute x7, starting transfers between devices, ring_reduce_scatter(): behind = lax.ppermute(behind, 'seq', backward) + block(2 + step, False)  9.96 us
    ppermute x2, starting transfers between devices, with_halo(): lax.ppermute(tail, axis, [(i, (i + 1) % count) for i in range(ends)])  8.49 us
    dot_general x1, matrix products, on_device(): jnp.dot(act_rows, point_weight, preferred_element_type=jnp.float32)  6.24 us
  transfers between devices with their start and end apart: 27, of which 17 were waited for; matrix products, arithmetic and copies ran while one was open for 15% of the time, Pallas kernels for 0%

profile of v16, /device:TPU:0, one launch (start us, length us, event | category | flops | bytes accessed | tf_op | source)
XLA Modules:
  0.0 167.8 jit_solution(7937504394965054593)
XLA Ops:
  3.8 5.5 %collective-permute-start = (bf16[1,64,1536]{2,1,0:T(8,128)(2,1)}, bf16[1,64,1536]{2,1,0:T(8,128)(2,1)}, u32[]{:S(2)}, u32[]{:S(2)}) collective-permute-start(bf16[1,64,1536]{2,1,0:T(8,128)(2,1)} %get-tuple-element.46), channel_id=1, source_target_pairs={{0,2},{2,4},{4,6},{6,8},{8,10},{10,12},{12,14},{1,3},{3,5},{5,7},{... | collective-permute-start | bytes 589832 | tf_op jit(solution)/shard_map/ppermute | solution.py:21
  11.4 2.1 %bitcast_multiply_fusion = bf16[3,384,1536]{2,1,0:T(8,128)(2,1)} fusion(bf16[384,1536]{1,0:T(8,128)(2,1)S(1)} %fusion.13, bf16[3,48,1536]{2,1,0:T(8,128)(2,1)S(1)} %copy-done.22), kind=kLoop, calls=%fused_computation.8 | loop fusion | flops 1769472 | bytes 5160960 | tf_op jit(solution)/shard_map/mul | solution.py:49
  13.5 3.9 %collective-permute-done = bf16[1,64,1536]{2,1,0:T(8,128)(2,1)} collective-permute-done((bf16[1,64,1536]{2,1,0:T(8,128)(2,1)}, bf16[1,64,1536]{2,1,0:T(8,128)(2,1)}, u32[]{:S(2)}, u32[]{:S(2)}) %collective-permute-start) | collective-permute-done | bytes 196640 | tf_op jit(solution)/shard_map/ppermute | solution.py:21
  26.7 3.5 %convolution_multiply_fusion = f32[768,1536]{1,0:T(8,128)} fusion(bf16[512,768]{0,1:T(8,128)(2,1)S(1)} %bitcast.152, bf16[1,512,1536]{2,1,0:T(8,128)(2,1)S(1)} %copy-done.2), kind=kOutput, calls=%fused_computation.4 | convolution fusion | flops 1209139200 | bytes 7077888 | tf_op jit(solution)/shard_map/dot_general | solution.py:193
  30.4 2.7 %convolution_multiply_fusion.1 = f32[768,1536]{1,0:T(8,128)S(1)} fusion(bf16[512,768]{0,1:T(8,128)(2,1)} %bitcast.151, bf16[1,512,1536]{2,1,0:T(8,128)(2,1)S(1)} %copy-done.2), kind=kOutput, calls=%fused_computation.5 | convolution fusion | flops 1209139200 | bytes 7077888 | tf_op jit(solution)/shard_map/dot_general | solution.py:193
  33.1 6.2 %fusion.2 = bf16[1,512,1536]{2,1,0:T(8,128)(2,1)} fusion(bf16[1,512,1536]{2,1,0:T(8,128)(2,1)S(1)} %copy-done.11, bf16[1536,1536]{1,0:T(8,128)(2,1)} %param.8, f32[512]{0:T(512)S(1)} %fusion.112, f32[512,384]{0,1:T(8,128)S(1)} %copy-done.10, f32[512,384]{0,1:T(8,128)S(1)} %copy-done.8, f32[512,384]{0,1:T(8,128)S(1)} %copy-done.6, f32[512,384]{0,1:T(8,128)S(1)} %copy-done.4), kind=kOutput, calls=%fused_computation.14 | convolution fusion | flops 2425356288 | bytes 11012096 | tf_op jit(solution)/shard_map/dot_general | solution.py:233
  39.3 3.3 %add.488 = f32[8,96,1536]{2,1,0:T(8,128)S(1)} add(f32[8,96,1536]{2,1,0:T(8,128)S(1)} %bitcast.142, f32[8,96,1536]{2,1,0:T(8,128)} %collective-permute-done.2) | non-fusion elementwise | flops 1179648 | bytes 14155776 | tf_op jit(solution)/shard_map/add | solution.py:210
  42.7 3.9 %fusion.9 = bf16[512,1536]{0,1:T(8,128)(2,1)S(1)} fusion(bf16[512,1536]{1,0:T(8,128)(2,1)S(1)} %bitcast.143, bf16[1536,1536]{1,0:T(8,128)(2,1)S(1)} %bitcast.167, f32[512]{0:T(512)S(1)} %fusion.112, f32[512,384]{0,1:T(8,128)S(1)} %copy-done.10, f32[512,384]{0,1:T(8,128)S(1)} %copy-done.8, f32[512,384]{0,1:T(8,128)S(1)} %copy-done.6, ...), kind=kOutput, calls=%fused_computation.27 | convolution fusion | flops 2426929152 | bytes 11012096 | tf_op jit(solution)/shard_map/dot_general | solution.py:236
  51.5 2.7 %dynamic-slice_bitcast_fusion.3 = (f32[96,1536]{1,0:T(8,128)}, f32[96,1536]{1,0:T(8,128)}, f32[96,1536]{1,0:T(8,128)S(1)}, f32[96,1536]{1,0:T(8,128)S(1)}, f32[9...) fusion(f32[8,96,1536]{2,1,0:T(8,128)S(1)} %add.488, ...), kind=kLoop, calls=%fused_computation.62 | loop fusion | bytes 18874432 | tf_op jit(solution)/shard_map/jit(dynamic_index_in_dim)/squeeze | solution.py:176
  54.2 2.2 %collective-permute-start.9 = (f32[96,768]{1,0:T(8,128)S(1)}, f32[96,768]{1,0:T(8,128)S(1)}, u32[]{:S(2)}, u32[]{:S(2)}) collective-permute-start(f32[96,768]{1,0:T(8,128)S(1)} %slice.317), channel_id=1, source_target_pairs={{0,2},{4,0},{8,4},{12,8},{14,12},{10,14},{6,10},{2,6},{1,3},{5,1},... | collective-permute-start | bytes 884744 | tf_op jit(solution)/shard_map/ppermute | solution.py:183
  57.7 3.0 %collective-permute-start.3 = (bf16[1,64,1536]{1,2,0:T(8,128)(2,1)S(1)}, bf16[1,64,1536]{1,2,0:T(8,128)(2,1)S(1)}, u32[]{:S(2)}, u32[]{:S(2)}) collective-permute-start(bf16[1,64,1536]{1,2,0:T(8,128)(2,1)S(1)} %get-tuple-element.42), channel_id=1, source_target_pairs={{0,2},{2,4},{4,6},{6,8},{8,10},{10,12},{12,14},{1,3},{3,5},{5,7},{... | collective-permute-start | bytes 589832 | tf_op jit(solution)/shard_map/ppermute | solution.py:21
  63.1 17.1 %collective-permute-done.3 = bf16[1,64,1536]{1,2,0:T(8,128)(2,1)S(1)} collective-permute-done((bf16[1,64,1536]{1,2,0:T(8,128)(2,1)S(1)}, bf16[1,64,1536]{1,2,0:T(8,128)(2,1)S(1)}, u32[]{:S(2)}, u32[]{:S(2)}) %collective-permute-start.3) | collective-permute-done | bytes 196640 | tf_op jit(solution)/shard_map/ppermute | solution.py:21
  86.7 2.5 %collective-permute-start.10 = (f32[96,768]{1,0:T(8,128)S(1)}, f32[96,768]{1,0:T(8,128)S(1)}, u32[]{:S(2)}, u32[]{:S(2)}) collective-permute-start(f32[96,768]{1,0:T(8,128)S(1)} %slice_add_fusion.9), channel_id=1, source_target_pairs={{0,2},{4,0},{8,4},{12,8},{14,12},{10,14},{6,10},{2,6},{1,3},{5,1},... | collective-permute-start | bytes 884744 | tf_op jit(solution)/shard_map/ppermute | solution.py:183
  91.0 6.2 %collective-permute-done.10 = f32[96,768]{1,0:T(8,128)S(1)} collective-permute-done((f32[96,768]{1,0:T(8,128)S(1)}, f32[96,768]{1,0:T(8,128)S(1)}, u32[]{:S(2)}, u32[]{:S(2)}) %collective-permute-start.10) | collective-permute-done | bytes 294944 | tf_op jit(solution)/shard_map/ppermute | solution.py:183
  99.9 5.7 %collective-permute-done.11 = f32[96,768]{1,0:T(8,128)S(1)} collective-permute-done((f32[96,768]{1,0:T(8,128)S(1)}, f32[96,768]{1,0:T(8,128)S(1)}, u32[]{:S(2)}, u32[]{:S(2)}) %collective-permute-start.11) | collective-permute-done | bytes 294944 | tf_op jit(solution)/shard_map/ppermute | solution.py:183
  108.3 4.8 %collective-permute-done.12 = f32[96,768]{1,0:T(8,128)S(1)} collective-permute-done((f32[96,768]{1,0:T(8,128)S(1)}, f32[96,768]{1,0:T(8,128)S(1)}, u32[]{:S(2)}, u32[]{:S(2)}) %collective-permute-start.12) | collective-permute-done | bytes 294944 | tf_op jit(solution)/shard_map/ppermute | solution.py:183
  117.0 5.7 %collective-permute-done.13 = f32[96,768]{1,0:T(8,128)S(1)} collective-permute-done((f32[96,768]{1,0:T(8,128)S(1)}, f32[96,768]{1,0:T(8,128)S(1)}, u32[]{:S(2)}, u32[]{:S(2)}) %collective-permute-start.13) | collective-permute-done | bytes 294944 | tf_op jit(solution)/shard_map/ppermute | solution.py:182
  126.9 9.3 %collective-permute-done.20 = f32[144,384]{1,0:T(8,128)S(1)} collective-permute-done((f32[144,384]{1,0:T(8,128)S(1)}, f32[144,384]{1,0:T(8,128)S(1)}, u32[]{:S(2)}, u32[]{:S(2)}) %collective-permute-start.20) | collective-permute-done | bytes 221216 | tf_op jit(solution)/shard_map/ppermute | solution.py:95
  138.4 2.6 %collective-permute-done.21 = f32[72,384]{1,0:T(8,128)S(1)} collective-permute-done((f32[72,384]{1,0:T(8,128)S(1)}, f32[72,384]{1,0:T(8,128)S(1)}, u32[]{:S(2)}, u32[]{:S(2)}) %collective-permute-start.21) | collective-permute-done | bytes 110624 | tf_op jit(solution)/shard_map/ppermute | solution.py:95
  142.5 2.8 %collective-permute-start.18 = (f32[96,768]{1,0:T(8,128)S(1)}, f32[96,768]{1,0:T(8,128)S(1)}, u32[]{:S(2)}, u32[]{:S(2)}) collective-permute-start(f32[96,768]{1,0:T(8,128)S(1)} %slice_add_fusion.1), channel_id=1, source_target_pairs={{0,2},{4,0},{8,4},{12,8},{14,12},{10,14},{6,10},{2,6},{1,3},{5,1},... | collective-permute-start | bytes 884744 | tf_op jit(solution)/shard_map/ppermute | solution.py:183
  145.3 2.8 %collective-permute-done.22 = f32[36,384]{1,0:T(8,128)S(1)} collective-permute-done((f32[36,384]{1,0:T(8,128)S(1)}, f32[36,384]{1,0:T(8,128)S(1)}, u32[]{:S(2)}, u32[]{:S(2)}) %collective-permute-start.22) | collective-permute-done | bytes 55328 | tf_op jit(solution)/shard_map/ppermute | solution.py:95
  150.7 3.0 %collective-permute-done.23 = f32[36,384]{1,0:T(8,128)S(1)} collective-permute-done((f32[36,384]{1,0:T(8,128)S(1)}, f32[36,384]{1,0:T(8,128)S(1)}, u32[]{:S(2)}, u32[]{:S(2)}) %collective-permute-start.23) | collective-permute-done | bytes 55328 | tf_op jit(solution)/shard_map/ppermute | solution.py:95
  154.1 4.7 %collective-permute-done.24 = f32[72,384]{1,0:T(8,128)S(1)} collective-permute-done((f32[72,384]{1,0:T(8,128)S(1)}, f32[72,384]{1,0:T(8,128)S(1)}, u32[]{:S(2)}, u32[]{:S(2)}) %collective-permute-start.24) | collective-permute-done | bytes 110624 | tf_op jit(solution)/shard_map/ppermute | solution.py:95
  160.4 4.5 %collective-permute-done.25 = f32[144,384]{1,0:T(8,128)S(1)} collective-permute-done((f32[144,384]{1,0:T(8,128)S(1)}, f32[144,384]{1,0:T(8,128)S(1)}, u32[]{:S(2)}, u32[]{:S(2)}) %collective-permute-start.25) | collective-permute-done | bytes 221216 | tf_op jit(solution)/shard_map/ppermute | solution.py:95
  (184 shorter events, 54.7 us)
Async XLA Ops:
  3.8 13.6 %collective-permute-start = (bf16[1,64,1536]{2,1,0:T(8,128)(2,1)}, bf16[1,64,1536]{2,1,0:T(8,128)(2,1)}, u32[]{:S(2)}, u32[]{:S(2)}) collective-permute-start(bf16[1,64,1536]{2,1,0:T(8,128)(2,1)} %get-tuple-element.46), channel_id=1, source_target_pairs={{0,2},{2,4},{4,6},{6,8},{8,10},{10,12},{12,14},{1,3},{3,5},{5,7},{... | collective-permute-start | bytes 589832 | tf_op jit(solution)/shard_map/ppermute | solution.py:21
  9.3 8.3 %collective-permute-start.1 = (bf16[1,64,1536]{2,1,0:T(8,128)(2,1)S(1)}, bf16[1,64,1536]{2,1,0:T(8,128)(2,1)}, u32[]{:S(2)}, u32[]{:S(2)}) collective-permute-start(bf16[1,64,1536]{2,1,0:T(8,128)(2,1)S(1)} %get-tuple-element.47), channel_id=1, source_target_pairs={{2,0},{4,2},{6,4},{8,6},{10,8},{12,10},{14,12},{3,1},{5,3},{7,5},{... | collective-permute-start | bytes 589832 | tf_op jit(solution)/shard_map/ppermute | solution.py:23
  30.2 9.1 %collective-permute-start.2 = (f32[8,96,1536]{2,1,0:T(8,128)}, f32[8,96,1536]{2,1,0:T(8,128)}, u32[]{:S(2)}, u32[]{:S(2)}) collective-permute-start(f32[8,96,1536]{2,1,0:T(8,128)} %bitcast.25), channel_id=1, source_target_pairs={{0,1},{1,0},{2,3},{3,2},{4,5},{5,4},{6,7},{7,6},{8,9},{9,8},{10,11... | collective-permute-start | bytes 14155784 | tf_op jit(solution)/shard_map/ppermute | solution.py:95
  54.2 32.4 %collective-permute-start.9 = (f32[96,768]{1,0:T(8,128)S(1)}, f32[96,768]{1,0:T(8,128)S(1)}, u32[]{:S(2)}, u32[]{:S(2)}) collective-permute-start(f32[96,768]{1,0:T(8,128)S(1)} %slice.317), channel_id=1, source_target_pairs={{0,2},{4,0},{8,4},{12,8},{14,12},{10,14},{6,10},{2,6},{1,3},{5,1},... | collective-permute-start | bytes 884744 | tf_op jit(solution)/shard_map/ppermute | solution.py:183
  56.4 32.8 %collective-permute-start.5 = (f32[96,768]{1,0:T(8,128)S(1)}, f32[96,768]{1,0:T(8,128)S(1)}, u32[]{:S(2)}, u32[]{:S(2)}) collective-permute-start(f32[96,768]{1,0:T(8,128)S(1)} %slice.312), channel_id=1, source_target_pairs={{0,4},{4,8},{8,12},{12,14},{14,10},{10,6},{6,2},{2,0},{1,5},{5,9},... | collective-permute-start | bytes 884744 | tf_op jit(solution)/shard_map/ppermute | solution.py:182
  57.7 22.5 %collective-permute-start.3 = (bf16[1,64,1536]{1,2,0:T(8,128)(2,1)S(1)}, bf16[1,64,1536]{1,2,0:T(8,128)(2,1)S(1)}, u32[]{:S(2)}, u32[]{:S(2)}) collective-permute-start(bf16[1,64,1536]{1,2,0:T(8,128)(2,1)S(1)} %get-tuple-element.42), channel_id=1, source_target_pairs={{0,2},{2,4},{4,6},{6,8},{8,10},{10,12},{12,14},{1,3},{3,5},{5,7},{... | collective-permute-start | bytes 589832 | tf_op jit(solution)/shard_map/ppermute | solution.py:21
  60.6 19.6 %collective-permute-start.4 = (bf16[1,64,1536]{1,2,0:T(8,128)(2,1)S(1)}, bf16[1,64,1536]{1,2,0:T(8,128)(2,1)S(1)}, u32[]{:S(2)}, u32[]{:S(2)}) collective-permute-start(bf16[1,64,1536]{1,2,0:T(8,128)(2,1)S(1)} %get-tuple-element.43), channel_id=1, source_target_pairs={{2,0},{4,2},{6,4},{8,6},{10,8},{12,10},{14,12},{3,1},{5,3},{7,5},{... | collective-permute-start | bytes 589832 | tf_op jit(solution)/shard_map/ppermute | solution.py:23
  86.7 10.5 %collective-permute-start.10 = (f32[96,768]{1,0:T(8,128)S(1)}, f32[96,768]{1,0:T(8,128)S(1)}, u32[]{:S(2)}, u32[]{:S(2)}) collective-permute-start(f32[96,768]{1,0:T(8,128)S(1)} %slice_add_fusion.9), channel_id=1, source_target_pairs={{0,2},{4,0},{8,4},{12,8},{14,12},{10,14},{6,10},{2,6},{1,3},{5,1},... | collective-permute-start | bytes 884744 | tf_op jit(solution)/shard_map/ppermute | solution.py:183
  89.3 8.7 %collective-permute-start.6 = (f32[96,768]{1,0:T(8,128)S(1)}, f32[96,768]{1,0:T(8,128)S(1)}, u32[]{:S(2)}, u32[]{:S(2)}) collective-permute-start(f32[96,768]{1,0:T(8,128)S(1)} %slice_add_fusion.13), channel_id=1, source_target_pairs={{0,4},{4,8},{8,12},{12,14},{14,10},{10,6},{6,2},{2,0},{1,5},{5,9},... | collective-permute-start | bytes 884744 | tf_op jit(solution)/shard_map/ppermute | solution.py:182
  97.3 8.3 %collective-permute-start.11 = (f32[96,768]{1,0:T(8,128)S(1)}, f32[96,768]{1,0:T(8,128)S(1)}, u32[]{:S(2)}, u32[]{:S(2)}) collective-permute-start(f32[96,768]{1,0:T(8,128)S(1)} %slice_add_fusion.8), channel_id=1, source_target_pairs={{0,2},{4,0},{8,4},{12,8},{14,12},{10,14},{6,10},{2,6},{1,3},{5,1},... | collective-permute-start | bytes 884744 | tf_op jit(solution)/shard_map/ppermute | solution.py:183
  98.0 8.0 %collective-permute-start.7 = (f32[96,768]{1,0:T(8,128)S(1)}, f32[96,768]{1,0:T(8,128)S(1)}, u32[]{:S(2)}, u32[]{:S(2)}) collective-permute-start(f32[96,768]{1,0:T(8,128)S(1)} %slice_add_fusion.12), channel_id=1, source_target_pairs={{0,4},{4,8},{8,12},{12,14},{14,10},{10,6},{6,2},{2,0},{1,5},{5,9},... | collective-permute-start | bytes 884744 | tf_op jit(solution)/shard_map/ppermute | solution.py:182
  105.6 7.4 %collective-permute-start.12 = (f32[96,768]{1,0:T(8,128)S(1)}, f32[96,768]{1,0:T(8,128)S(1)}, u32[]{:S(2)}, u32[]{:S(2)}) collective-permute-start(f32[96,768]{1,0:T(8,128)S(1)} %slice_add_fusion.7), channel_id=1, source_target_pairs={{0,2},{4,0},{8,4},{12,8},{14,12},{10,14},{6,10},{2,6},{1,3},{5,1},... | collective-permute-start | bytes 884744 | tf_op jit(solution)/shard_map/ppermute | solution.py:183
  106.0 7.2 %collective-permute-start.8 = (f32[96,768]{1,0:T(8,128)S(1)}, f32[96,768]{1,0:T(8,128)S(1)}, u32[]{:S(2)}, u32[]{:S(2)}) collective-permute-start(f32[96,768]{1,0:T(8,128)S(1)} %slice_add_fusion.11), channel_id=1, source_target_pairs={{0,4},{4,8},{8,12},{12,14},{14,10},{10,6},{6,2},{2,0},{1,5},{5,9},... | collective-permute-start | bytes 884744 | tf_op jit(solution)/shard_map/ppermute | solution.py:182
  113.3 11.3 %collective-permute-start.19 = (f32[144,768]{1,0:T(8,128)S(1)}, f32[144,768]{1,0:T(8,128)S(1)}, u32[]{:S(2)}, u32[]{:S(2)}) collective-permute-start(f32[144,768]{1,0:T(8,128)S(1)} %constant_dynamic-slice_fusion.3), channel_id=1, source_target_pairs={{0,1},{1,0},{2,3},{3,2},{4,5},{5,4},{6,7},{7,6},{8,9},{9,8},{10,11... | collective-permute-start | bytes 1327112 | tf_op jit(solution)/shard_map/ppermute | solution.py:95
  113.3 9.4 %collective-permute-start.13 = (f32[96,768]{1,0:T(8,128)S(1)}, f32[96,768]{1,0:T(8,128)S(1)}, u32[]{:S(2)}, u32[]{:S(2)}) collective-permute-start(f32[96,768]{1,0:T(8,128)S(1)} %slice_add_fusion.10), channel_id=1, source_target_pairs={{0,4},{4,8},{8,12},{12,14},{14,10},{10,6},{6,2},{2,0},{1,5},{5,9},... | collective-permute-start | bytes 884744 | tf_op jit(solution)/shard_map/ppermute | solution.py:182
  116.7 9.1 %collective-permute-start.16 = (f32[96,768]{1,0:T(8,128)S(1)}, f32[96,768]{1,0:T(8,128)S(1)}, u32[]{:S(2)}, u32[]{:S(2)}) collective-permute-start(f32[96,768]{1,0:T(8,128)S(1)} %slice_add_fusion.6), channel_id=1, source_target_pairs={{0,2},{4,0},{8,4},{12,8},{14,12},{10,14},{6,10},{2,6},{1,3},{5,1},... | collective-permute-start | bytes 884744 | tf_op jit(solution)/shard_map/ppermute | solution.py:183
  122.8 13.5 %collective-permute-start.14 = (f32[96,768]{1,0:T(8,128)S(1)}, f32[96,768]{1,0:T(8,128)S(1)}, u32[]{:S(2)}, u32[]{:S(2)}) collective-permute-start(f32[96,768]{1,0:T(8,128)S(1)} %slice_add_fusion.5), channel_id=1, source_target_pairs={{0,4},{4,8},{8,12},{12,14},{14,10},{10,6},{6,2},{2,0},{1,5},{5,9},... | collective-permute-start | bytes 884744 | tf_op jit(solution)/shard_map/ppermute | solution.py:182
  124.7 11.5 %collective-permute-start.20 = (f32[144,384]{1,0:T(8,128)S(1)}, f32[144,384]{1,0:T(8,128)S(1)}, u32[]{:S(2)}, u32[]{:S(2)}) collective-permute-start(f32[144,384]{1,0:T(8,128)S(1)} %constant_dynamic-slice_fusion.2), channel_id=1, source_target_pairs={{0,2},{2,0},{4,6},{6,4},{8,10},{10,8},{12,14},{14,12},{1,3},{3,1},... | collective-permute-start | bytes 663560 | tf_op jit(solution)/shard_map/ppermute | solution.py:95
  125.8 16.6 %collective-permute-start.17 = (f32[96,768]{1,0:T(8,128)S(1)}, f32[96,768]{1,0:T(8,128)S(1)}, u32[]{:S(2)}, u32[]{:S(2)}) collective-permute-start(f32[96,768]{1,0:T(8,128)S(1)} %slice_add_fusion.2), channel_id=1, source_target_pairs={{0,2},{4,0},{8,4},{12,8},{14,12},{10,14},{6,10},{2,6},{1,3},{5,1},... | collective-permute-start | bytes 884744 | tf_op jit(solution)/shard_map/ppermute | solution.py:183
  136.4 13.5 %collective-permute-start.15 = (f32[96,768]{1,0:T(8,128)S(1)}, f32[96,768]{1,0:T(8,128)S(1)}, u32[]{:S(2)}, u32[]{:S(2)}) collective-permute-start(f32[96,768]{1,0:T(8,128)S(1)} %slice_add_fusion.4), channel_id=1, source_target_pairs={{0,4},{4,8},{8,12},{12,14},{14,10},{10,6},{6,2},{2,0},{1,5},{5,9},... | collective-permute-start | bytes 884744 | tf_op jit(solution)/shard_map/ppermute | solution.py:182
  141.1 7.0 %collective-permute-start.22 = (f32[36,384]{1,0:T(8,128)S(1)}, f32[36,384]{1,0:T(8,128)S(1)}, u32[]{:S(2)}, u32[]{:S(2)}) collective-permute-start(f32[36,384]{1,0:T(8,128)S(1)} %constant_dynamic-slice_fusion), channel_id=1, source_target_pairs={{0,8},{2,10},{4,12},{6,14},{8,0},{10,2},{12,4},{14,6},{1,9},{3,11}... | collective-permute-start | bytes 165896 | tf_op jit(solution)/shard_map/ppermute | solution.py:95
  142.5 8.2 %collective-permute-start.18 = (f32[96,768]{1,0:T(8,128)S(1)}, f32[96,768]{1,0:T(8,128)S(1)}, u32[]{:S(2)}, u32[]{:S(2)}) collective-permute-start(f32[96,768]{1,0:T(8,128)S(1)} %slice_add_fusion.1), channel_id=1, source_target_pairs={{0,2},{4,0},{8,4},{12,8},{14,12},{10,14},{6,10},{2,6},{1,3},{5,1},... | collective-permute-start | bytes 884744 | tf_op jit(solution)/shard_map/ppermute | solution.py:183
  148.1 5.5 %collective-permute-start.23 = (f32[36,384]{1,0:T(8,128)S(1)}, f32[36,384]{1,0:T(8,128)S(1)}, u32[]{:S(2)}, u32[]{:S(2)}) collective-permute-start(f32[36,384]{1,0:T(8,128)S(1)} %dynamic-slice_add_fusion.3), channel_id=1, source_target_pairs={{0,8},{2,10},{4,12},{6,14},{8,0},{10,2},{12,4},{14,6},{1,9},{3,11}... | collective-permute-start | bytes 165896 | tf_op jit(solution)/shard_map/ppermute | solution.py:95
  158.8 6.0 %collective-permute-start.25 = (f32[144,384]{1,0:T(8,128)S(1)}, f32[144,384]{1,0:T(8,128)S(1)}, u32[]{:S(2)}, u32[]{:S(2)}) collective-permute-start(f32[144,384]{1,0:T(8,128)S(1)} %constant_dynamic-update-slice_fusion.4), channel_id=1, source_target_pairs={{0,2},{2,0},{4,6},{6,4},{8,10},{10,8},{12,14},{14,12},{1,3},{3,1},... | collective-permute-start | bytes 663560 | tf_op jit(solution)/shard_map/ppermute | solution.py:95
  (28 other events, 224.9 us)

commit v17 on v16

--- a/solution.py
+++ b/solution.py
@@ -181,7 +181,7 @@
     for step in range(count - 1):
         ahead = lax.ppermute(ahead, "seq", forward) + block(-2 - step, True)
         behind = lax.ppermute(behind, "seq", backward) + block(2 + step, False)
-        if step == count // 2 - 1:
+        if step == 0:
             ahead, behind, hold = lax.optimization_barrier((ahead, behind, hold))
     return jnp.concatenate([ahead, behind], axis=1), hold
 
@@ -237,13 +237,13 @@
         cot_rows, point_weight, (((1,), (1,)), ((), ())), preferred_element_type=jnp.float32
     )
     preactivation_gradient = (back.reshape(inputs.shape) * slope * mask3).astype(jnp.bfloat16)
-    padded_gradient = with_halo(preactivation_gradient, (("seq", 1),), DILATION_STEP)
+    if lax.axis_size("rep") == 2:
+        grad_point, held_gradient = ring_reduce_scatter(mine, snake, preactivation_gradient)
+    else:
+        grad_point, held_gradient = mine, preactivation_gradient
+    padded_gradient = with_halo(held_gradient, (("seq", 1),), DILATION_STEP)
     spread = conv_taps(padded_gradient, dense, local_bins, transpose=True)
     conv_local = weight_taps(padded_input, preactivation_gradient, local_bins)
-    if lax.axis_size("rep") == 2:
-        grad_point, conv_local = ring_reduce_scatter(mine, snake, conv_local)
-    else:
-        grad_point = mine
     grad_conv = tree_sum(conv_local) * scale
     grad_inputs = (cotangent.astype(jnp.float32) + mask3 * spread).astype(jnp.bfloat16)
     return (output, grad_inputs, grad_point, grad_conv)

time: 168 us -> 160 us (0.952)
  waiting for transfers between devices: 72.9 us -> 60.6 us
  other arithmetic: 16.7 us -> 19.4 us
  starting transfers between devices: 36.9 us -> 38.8 us
    ppermute x9, waiting for transfers between devices: 27.7 us -> 12.3 us  [swap(): return lax.ppermute(value, axis, [(i, i ^ distance) for i in range(count)])]
    ppermute x7, waiting for transfers between devices: 5.83 us -> 15.6 us  [ring_reduce_scatter(): ahead = lax.ppermute(ahead, 'seq', forward) + block(-2 - step, True)]
    ppermute x9, starting transfers between devices: 4.75 us -> 11.7 us  [swap(): return lax.ppermute(value, axis, [(i, i ^ distance) for i in range(count)])]
    ppermute x7, starting transfers between devices: 9.96 us -> 3.5 us  [ring_reduce_scatter(): behind = lax.ppermute(behind, 'seq', backward) + block(2 + step, False)]
    ppermute x7, waiting for transfers between devices: 18.1 us -> 12.5 us  [ring_reduce_scatter(): behind = lax.ppermute(behind, 'seq', backward) + block(2 + step, False)]
    add x7, other arithmetic: 0.29 us -> 2.01 us  [ring_reduce_scatter(): behind = lax.ppermute(behind, 'seq', backward) + block(2 + step, False)]
  transfers between devices with their start and end apart: 27 -> 27, of which waited for: 17 -> 18; matrix products, arithmetic and copies ran while one was open for 15% -> 17% of each run, Pallas kernels for 0% -> 0%
where the time goes in v17:
time: 160 us
  waiting for transfers between devices  60.6 us (38%)
  starting transfers between devices  38.8 us (24%)
  matrix products  32.7 us (20%)
  other arithmetic  19.4 us (12%)
  local copies, waits for them, and re-layouts  6.31 us (4%)
  between operations  2.29 us (1%)
    ppermute x2, waiting for transfers between devices, with_halo(): lax.ppermute(tail, axis, [(i, (i + 1) % count) for i in range(ends)])  19.9 us
    ppermute x7, waiting for transfers between devices, ring_reduce_scatter(): ahead = lax.ppermute(ahead, 'seq', forward) + block(-2 - step, True)  15.6 us
    ppermute x7, waiting for transfers between devices, ring_reduce_scatter(): behind = lax.ppermute(behind, 'seq', backward) + block(2 + step, False)  12.5 us
    ppermute x9, waiting for transfers between devices, swap(): return lax.ppermute(value, axis, [(i, i ^ distance) for i in range(count)])  12.3 us
    ppermute x9, starting transfers between devices, swap(): return lax.ppermute(value, axis, [(i, i ^ distance) for i in range(count)])  11.7 us
    dot_general x24, matrix products, conv_taps(): lax.dot_general(window, dense[k, :, cols], dims, preferred_element_type=j...  11.6 us
    ppermute x7, starting transfers between devices, ring_reduce_scatter(): ahead = lax.ppermute(ahead, 'seq', forward) + block(-2 - step, True)  11.5 us
    ppermute x2, starting transfers between devices, with_halo(): lax.ppermute(tail, axis, [(i, (i + 1) % count) for i in range(ends)])  9.3 us
  transfers between devices with their start and end apart: 27, of which 18 were waited for; matrix products, arithmetic and copies ran while one was open for 17% of the time, Pallas kernels for 0%

profile of v17, /device:TPU:0, one launch (start us, length us, event | category | flops | bytes accessed | tf_op | source)
XLA Modules:
  0.0 160.2 jit_solution(16429820495818724930)
XLA Ops:
  3.8 5.5 %collective-permute-start = (bf16[1,64,1536]{2,1,0:T(8,128)(2,1)}, bf16[1,64,1536]{2,1,0:T(8,128)(2,1)}, u32[]{:S(2)}, u32[]{:S(2)}) collective-permute-start(bf16[1,64,1536]{2,1,0:T(8,128)(2,1)} %get-tuple-element.46), channel_id=1, source_target_pairs={{0,2},{2,4},{4,6},{6,8},{8,10},{10,12},{12,14},{1,3},{3,5},{5,7},{... | collective-permute-start | bytes 589832 | tf_op jit(solution)/shard_map/ppermute | solution.py:21
  11.4 2.1 %bitcast_multiply_fusion = bf16[3,384,1536]{2,1,0:T(8,128)(2,1)} fusion(bf16[384,1536]{1,0:T(8,128)(2,1)S(1)} %fusion.13, bf16[3,48,1536]{2,1,0:T(8,128)(2,1)S(1)} %copy-done.22), kind=kLoop, calls=%fused_computation.8 | loop fusion | flops 1769472 | bytes 5160960 | tf_op jit(solution)/shard_map/mul | solution.py:49
  13.5 3.9 %collective-permute-done = bf16[1,64,1536]{2,1,0:T(8,128)(2,1)} collective-permute-done((bf16[1,64,1536]{2,1,0:T(8,128)(2,1)}, bf16[1,64,1536]{2,1,0:T(8,128)(2,1)}, u32[]{:S(2)}, u32[]{:S(2)}) %collective-permute-start) | collective-permute-done | bytes 196640 | tf_op jit(solution)/shard_map/ppermute | solution.py:21
  26.7 3.5 %convolution_multiply_fusion = f32[768,1536]{1,0:T(8,128)} fusion(bf16[512,768]{0,1:T(8,128)(2,1)S(1)} %bitcast.152, bf16[1,512,1536]{2,1,0:T(8,128)(2,1)S(1)} %copy-done.2), kind=kOutput, calls=%fused_computation.4 | convolution fusion | flops 1209139200 | bytes 7077888 | tf_op jit(solution)/shard_map/dot_general | solution.py:193
  30.4 2.7 %convolution_multiply_fusion.1 = f32[768,1536]{1,0:T(8,128)S(1)} fusion(bf16[512,768]{0,1:T(8,128)(2,1)} %bitcast.151, bf16[1,512,1536]{2,1,0:T(8,128)(2,1)S(1)} %copy-done.2), kind=kOutput, calls=%fused_computation.5 | convolution fusion | flops 1209139200 | bytes 7077888 | tf_op jit(solution)/shard_map/dot_general | solution.py:193
  33.1 6.2 %fusion.2 = bf16[1,512,1536]{2,1,0:T(8,128)(2,1)} fusion(bf16[1,512,1536]{2,1,0:T(8,128)(2,1)S(1)} %copy-done.11, bf16[1536,1536]{1,0:T(8,128)(2,1)} %param.8, f32[512]{0:T(512)S(1)} %fusion.112, f32[512,384]{0,1:T(8,128)S(1)} %copy-done.10, f32[512,384]{0,1:T(8,128)S(1)} %copy-done.8, f32[512,384]{0,1:T(8,128)S(1)} %copy-done.6, f32[512,384]{0,1:T(8,128)S(1)} %copy-done.4), kind=kOutput, calls=%fused_computation.14 | convolution fusion | flops 2425356288 | bytes 11012096 | tf_op jit(solution)/shard_map/dot_general | solution.py:233
  39.3 3.3 %add.488 = f32[8,96,1536]{2,1,0:T(8,128)S(1)} add(f32[8,96,1536]{2,1,0:T(8,128)S(1)} %bitcast.142, f32[8,96,1536]{2,1,0:T(8,128)} %collective-permute-done.2) | non-fusion elementwise | flops 1179648 | bytes 14155776 | tf_op jit(solution)/shard_map/add | solution.py:210
  42.7 3.9 %fusion.9 = bf16[512,1536]{0,1:T(8,128)(2,1)S(1)} fusion(bf16[512,1536]{1,0:T(8,128)(2,1)S(1)} %bitcast.143, bf16[1536,1536]{1,0:T(8,128)(2,1)S(1)} %bitcast.167, f32[512]{0:T(512)S(1)} %fusion.112, f32[512,384]{0,1:T(8,128)S(1)} %copy-done.10, f32[512,384]{0,1:T(8,128)S(1)} %copy-done.8, f32[512,384]{0,1:T(8,128)S(1)} %copy-done.6, ...), kind=kOutput, calls=%fused_computation.27 | convolution fusion | flops 2426929152 | bytes 11012096 | tf_op jit(solution)/shard_map/dot_general | solution.py:236
  51.5 2.7 %dynamic-slice_bitcast_fusion.6 = (f32[96,1536]{1,0:T(8,128)}, f32[96,1536]{1,0:T(8,128)}, f32[96,1536]{1,0:T(8,128)}, f32[96,1536]{1,0:T(8,128)}, f32[96,1536]{...) fusion(f32[8,96,1536]{2,1,0:T(8,128)S(1)} %add.488, ...), kind=kLoop, calls=%fused_computation.78 | loop fusion | bytes 18874432 | tf_op jit(solution)/shard_map/jit(dynamic_index_in_dim)/squeeze | solution.py:176
  54.2 2.2 %collective-permute-start.4 = (f32[96,768]{1,0:T(8,128)S(1)}, f32[96,768]{1,0:T(8,128)S(1)}, u32[]{:S(2)}, u32[]{:S(2)}) collective-permute-start(f32[96,768]{1,0:T(8,128)S(1)} %slice.300), channel_id=1, source_target_pairs={{0,2},{4,0},{8,4},{12,8},{14,12},{10,14},{6,10},{2,6},{1,3},{5,1},... | collective-permute-start | bytes 884744 | tf_op jit(solution)/shard_map/ppermute | solution.py:183
  58.9 6.1 %collective-permute-done.4 = f32[96,768]{1,0:T(8,128)S(1)} collective-permute-done((f32[96,768]{1,0:T(8,128)S(1)}, f32[96,768]{1,0:T(8,128)S(1)}, u32[]{:S(2)}, u32[]{:S(2)}) %collective-permute-start.4) | collective-permute-done | bytes 294944 | tf_op jit(solution)/shard_map/ppermute | solution.py:183
  67.9 3.8 %collective-permute-start.5 = (bf16[1,64,1536]{1,2,0:T(8,128)(2,1)S(1)}, bf16[1,64,1536]{1,2,0:T(8,128)(2,1)S(1)}, u32[]{:S(2)}, u32[]{:S(2)}) collective-permute-start(bf16[1,64,1536]{1,2,0:T(8,128)(2,1)S(1)} %get-tuple-element.42), channel_id=1, source_target_pairs={{0,2},{2,4},{4,6},{6,8},{8,10},{10,12},{12,14},{1,3},{3,5},{5,7},{... | collective-permute-start | bytes 589832 | tf_op jit(solution)/shard_map/ppermute | solution.py:21
  73.4 2.7 %collective-permute-start.20 = (f32[144,384]{1,0:T(8,128)S(1)}, f32[144,384]{1,0:T(8,128)S(1)}, u32[]{:S(2)}, u32[]{:S(2)}) collective-permute-start(f32[144,384]{1,0:T(8,128)S(1)} %constant_dynamic-slice_fusion.2), channel_id=1, source_target_pairs={{0,2},{2,0},{4,6},{6,4},{8,10},{10,8},{12,14},{14,12},{1,3},{3,1},... | collective-permute-start | bytes 663560 | tf_op jit(solution)/shard_map/ppermute | solution.py:95
  76.1 16.0 %collective-permute-done.5 = bf16[1,64,1536]{1,2,0:T(8,128)(2,1)S(1)} collective-permute-done((bf16[1,64,1536]{1,2,0:T(8,128)(2,1)S(1)}, bf16[1,64,1536]{1,2,0:T(8,128)(2,1)S(1)}, u32[]{:S(2)}, u32[]{:S(2)}) %collective-permute-start.5) | collective-permute-done | bytes 196640 | tf_op jit(solution)/shard_map/ppermute | solution.py:21
  103.7 2.8 %collective-permute-done.21 = f32[72,384]{1,0:T(8,128)S(1)} collective-permute-done((f32[72,384]{1,0:T(8,128)S(1)}, f32[72,384]{1,0:T(8,128)S(1)}, u32[]{:S(2)}, u32[]{:S(2)}) %collective-permute-start.21) | collective-permute-done | bytes 110624 | tf_op jit(solution)/shard_map/ppermute | solution.py:95
  106.6 3.8 %collective-permute-start.22 = (f32[36,384]{1,0:T(8,128)S(1)}, f32[36,384]{1,0:T(8,128)S(1)}, u32[]{:S(2)}, u32[]{:S(2)}) collective-permute-start(f32[36,384]{1,0:T(8,128)S(1)} %constant_dynamic-slice_fusion), channel_id=1, source_target_pairs={{0,8},{2,10},{4,12},{6,14},{8,0},{10,2},{12,4},{14,6},{1,9},{3,11}... | collective-permute-start | bytes 165896 | tf_op jit(solution)/shard_map/ppermute | solution.py:95
  113.1 2.8 %collective-permute-start.23 = (f32[36,384]{1,0:T(8,128)S(1)}, f32[36,384]{1,0:T(8,128)S(1)}, u32[]{:S(2)}, u32[]{:S(2)}) collective-permute-start(f32[36,384]{1,0:T(8,128)S(1)} %dynamic-slice_add_fusion.3), channel_id=1, source_target_pairs={{0,8},{2,10},{4,12},{6,14},{8,0},{10,2},{12,4},{14,6},{1,9},{3,11}... | collective-permute-start | bytes 165896 | tf_op jit(solution)/shard_map/ppermute | solution.py:95
  116.5 5.2 %collective-permute-done.23 = f32[36,384]{1,0:T(8,128)S(1)} collective-permute-done((f32[36,384]{1,0:T(8,128)S(1)}, f32[36,384]{1,0:T(8,128)S(1)}, u32[]{:S(2)}, u32[]{:S(2)}) %collective-permute-start.23) | collective-permute-done | bytes 55328 | tf_op jit(solution)/shard_map/ppermute | solution.py:95
  128.2 4.9 %collective-permute-done.9 = f32[96,768]{1,0:T(8,128)S(1)} collective-permute-done((f32[96,768]{1,0:T(8,128)S(1)}, f32[96,768]{1,0:T(8,128)S(1)}, u32[]{:S(2)}, u32[]{:S(2)}) %collective-permute-start.9) | collective-permute-done | bytes 294944 | tf_op jit(solution)/shard_map/ppermute | solution.py:182
  136.5 3.5 %collective-permute-done.10 = f32[96,768]{1,0:T(8,128)S(1)} collective-permute-done((f32[96,768]{1,0:T(8,128)S(1)}, f32[96,768]{1,0:T(8,128)S(1)}, u32[]{:S(2)}, u32[]{:S(2)}) %collective-permute-start.10) | collective-permute-done | bytes 294944 | tf_op jit(solution)/shard_map/ppermute | solution.py:182
  140.1 2.5 %collective-permute-start.11 = (f32[96,768]{1,0:T(8,128)S(1)}, f32[96,768]{1,0:T(8,128)S(1)}, u32[]{:S(2)}, u32[]{:S(2)}) collective-permute-start(f32[96,768]{1,0:T(8,128)S(1)} %slice_add_fusion.8), channel_id=1, source_target_pairs={{0,4},{4,8},{8,12},{12,14},{14,10},{10,6},{6,2},{2,0},{1,5},{5,9},... | collective-permute-start | bytes 884744 | tf_op jit(solution)/shard_map/ppermute | solution.py:182
  143.6 4.9 %collective-permute-done.11 = f32[96,768]{1,0:T(8,128)S(1)} collective-permute-done((f32[96,768]{1,0:T(8,128)S(1)}, f32[96,768]{1,0:T(8,128)S(1)}, u32[]{:S(2)}, u32[]{:S(2)}) %collective-permute-start.11) | collective-permute-done | bytes 294944 | tf_op jit(solution)/shard_map/ppermute | solution.py:182
  148.5 2.5 %collective-permute-start.12 = (f32[96,768]{1,0:T(8,128)S(1)}, f32[96,768]{1,0:T(8,128)S(1)}, u32[]{:S(2)}, u32[]{:S(2)}) collective-permute-start(f32[96,768]{1,0:T(8,128)S(1)} %slice_add_fusion.7), channel_id=1, source_target_pairs={{0,4},{4,8},{8,12},{12,14},{14,10},{10,6},{6,2},{2,0},{1,5},{5,9},... | collective-permute-start | bytes 884744 | tf_op jit(solution)/shard_map/ppermute | solution.py:182
  155.3 3.9 %collective-permute-done.18 = f32[96,768]{1,0:T(8,128)S(1)} collective-permute-done((f32[96,768]{1,0:T(8,128)S(1)}, f32[96,768]{1,0:T(8,128)S(1)}, u32[]{:S(2)}, u32[]{:S(2)}) %collective-permute-start.18) | collective-permute-done | bytes 294944 | tf_op jit(solution)/shard_map/ppermute | solution.py:183
  (184 shorter events, 56.4 us)
Async XLA Ops:
  3.8 13.6 %collective-permute-start = (bf16[1,64,1536]{2,1,0:T(8,128)(2,1)}, bf16[1,64,1536]{2,1,0:T(8,128)(2,1)}, u32[]{:S(2)}, u32[]{:S(2)}) collective-permute-start(bf16[1,64,1536]{2,1,0:T(8,128)(2,1)} %get-tuple-element.46), channel_id=1, source_target_pairs={{0,2},{2,4},{4,6},{6,8},{8,10},{10,12},{12,14},{1,3},{3,5},{5,7},{... | collective-permute-start | bytes 589832 | tf_op jit(solution)/shard_map/ppermute | solution.py:21
  9.3 8.3 %collective-permute-start.1 = (bf16[1,64,1536]{2,1,0:T(8,128)(2,1)S(1)}, bf16[1,64,1536]{2,1,0:T(8,128)(2,1)}, u32[]{:S(2)}, u32[]{:S(2)}) collective-permute-start(bf16[1,64,1536]{2,1,0:T(8,128)(2,1)S(1)} %get-tuple-element.47), channel_id=1, source_target_pairs={{2,0},{4,2},{6,4},{8,6},{10,8},{12,10},{14,12},{3,1},{5,3},{7,5},{... | collective-permute-start | bytes 589832 | tf_op jit(solution)/shard_map/ppermute | solution.py:23
  30.2 9.1 %collective-permute-start.2 = (f32[8,96,1536]{2,1,0:T(8,128)}, f32[8,96,1536]{2,1,0:T(8,128)}, u32[]{:S(2)}, u32[]{:S(2)}) collective-permute-start(f32[8,96,1536]{2,1,0:T(8,128)} %bitcast.25), channel_id=1, source_target_pairs={{0,1},{1,0},{2,3},{3,2},{4,5},{5,4},{6,7},{7,6},{8,9},{9,8},{10,11... | collective-permute-start | bytes 14155784 | tf_op jit(solution)/shard_map/ppermute | solution.py:95
  54.2 10.8 %collective-permute-start.4 = (f32[96,768]{1,0:T(8,128)S(1)}, f32[96,768]{1,0:T(8,128)S(1)}, u32[]{:S(2)}, u32[]{:S(2)}) collective-permute-start(f32[96,768]{1,0:T(8,128)S(1)} %slice.300), channel_id=1, source_target_pairs={{0,2},{4,0},{8,4},{12,8},{14,12},{10,14},{6,10},{2,6},{1,3},{5,1},... | collective-permute-start | bytes 884744 | tf_op jit(solution)/shard_map/ppermute | solution.py:183
  56.4 9.2 %collective-permute-start.3 = (f32[96,768]{1,0:T(8,128)S(1)}, f32[96,768]{1,0:T(8,128)S(1)}, u32[]{:S(2)}, u32[]{:S(2)}) collective-permute-start(f32[96,768]{1,0:T(8,128)S(1)} %slice.298), channel_id=1, source_target_pairs={{0,4},{4,8},{8,12},{12,14},{14,10},{10,6},{6,2},{2,0},{1,5},{5,9},... | collective-permute-start | bytes 884744 | tf_op jit(solution)/shard_map/ppermute | solution.py:182
  58.7 14.6 %collective-permute-start.19 = (f32[144,768]{1,0:T(8,128)S(1)}, f32[144,768]{1,0:T(8,128)S(1)}, u32[]{:S(2)}, u32[]{:S(2)}) collective-permute-start(f32[144,768]{1,0:T(8,128)S(1)} %constant_dynamic-slice_fusion.3), channel_id=1, source_target_pairs={{0,1},{1,0},{2,3},{3,2},{4,5},{5,4},{6,7},{7,6},{8,9},{9,8},{10,11... | collective-permute-start | bytes 1327112 | tf_op jit(solution)/shard_map/ppermute | solution.py:95
  65.7 37.6 %collective-permute-start.7 = (f32[96,768]{1,0:T(8,128)S(1)}, f32[96,768]{1,0:T(8,128)S(1)}, u32[]{:S(2)}, u32[]{:S(2)}) collective-permute-start(f32[96,768]{1,0:T(8,128)S(1)} %slice_add_fusion.13), channel_id=1, source_target_pairs={{0,4},{4,8},{8,12},{12,14},{14,10},{10,6},{6,2},{2,0},{1,5},{5,9},... | collective-permute-start | bytes 884744 | tf_op jit(solution)/shard_map/ppermute | solution.py:182
  67.0 43.4 %collective-permute-start.13 = (f32[96,768]{1,0:T(8,128)S(1)}, f32[96,768]{1,0:T(8,128)S(1)}, u32[]{:S(2)}, u32[]{:S(2)}) collective-permute-start(f32[96,768]{1,0:T(8,128)S(1)} %slice_add_fusion.12), channel_id=1, source_target_pairs={{0,2},{4,0},{8,4},{12,8},{14,12},{10,14},{6,10},{2,6},{1,3},{5,1},... | collective-permute-start | bytes 884744 | tf_op jit(solution)/shard_map/ppermute | solution.py:183
  67.9 24.1 %collective-permute-start.5 = (bf16[1,64,1536]{1,2,0:T(8,128)(2,1)S(1)}, bf16[1,64,1536]{1,2,0:T(8,128)(2,1)S(1)}, u32[]{:S(2)}, u32[]{:S(2)}) collective-permute-start(bf16[1,64,1536]{1,2,0:T(8,128)(2,1)S(1)} %get-tuple-element.42), channel_id=1, source_target_pairs={{0,2},{2,4},{4,6},{6,8},{8,10},{10,12},{12,14},{1,3},{3,5},{5,7},{... | collective-permute-start | bytes 589832 | tf_op jit(solution)/shard_map/ppermute | solution.py:21
  71.7 20.3 %collective-permute-start.6 = (bf16[1,64,1536]{1,2,0:T(8,128)(2,1)S(1)}, bf16[1,64,1536]{1,2,0:T(8,128)(2,1)S(1)}, u32[]{:S(2)}, u32[]{:S(2)}) collective-permute-start(bf16[1,64,1536]{1,2,0:T(8,128)(2,1)S(1)} %get-tuple-element.43), channel_id=1, source_target_pairs={{2,0},{4,2},{6,4},{8,6},{10,8},{12,10},{14,12},{3,1},{5,3},{7,5},{... | collective-permute-start | bytes 589832 | tf_op jit(solution)/shard_map/ppermute | solution.py:23
  73.4 28.1 %collective-permute-start.20 = (f32[144,384]{1,0:T(8,128)S(1)}, f32[144,384]{1,0:T(8,128)S(1)}, u32[]{:S(2)}, u32[]{:S(2)}) collective-permute-start(f32[144,384]{1,0:T(8,128)S(1)} %constant_dynamic-slice_fusion.2), channel_id=1, source_target_pairs={{0,2},{2,0},{4,6},{6,4},{8,10},{10,8},{12,14},{14,12},{1,3},{3,1},... | collective-permute-start | bytes 663560 | tf_op jit(solution)/shard_map/ppermute | solution.py:95
  103.3 18.9 %collective-permute-start.8 = (f32[96,768]{1,0:T(8,128)S(1)}, f32[96,768]{1,0:T(8,128)}, u32[]{:S(2)}, u32[]{:S(2)}) collective-permute-start(f32[96,768]{1,0:T(8,128)S(1)} %slice_add_fusion.11), channel_id=1, source_target_pairs={{0,4},{4,8},{8,12},{12,14},{14,10},{10,6},{6,2},{2,0},{1,5},{5,9},... | collective-permute-start | bytes 884744 | tf_op jit(solution)/shard_map/ppermute | solution.py:182
  111.1 14.1 %collective-permute-start.14 = (f32[96,768]{1,0:T(8,128)}, f32[96,768]{1,0:T(8,128)}, u32[]{:S(2)}, u32[]{:S(2)}) collective-permute-start(f32[96,768]{1,0:T(8,128)} %slice_add_fusion.5), channel_id=1, source_target_pairs={{0,2},{4,0},{8,4},{12,8},{14,12},{10,14},{6,10},{2,6},{1,3},{5,1},... | collective-permute-start | bytes 884744 | tf_op jit(solution)/shard_map/ppermute | solution.py:183
  113.1 8.5 %collective-permute-start.23 = (f32[36,384]{1,0:T(8,128)S(1)}, f32[36,384]{1,0:T(8,128)S(1)}, u32[]{:S(2)}, u32[]{:S(2)}) collective-permute-start(f32[36,384]{1,0:T(8,128)S(1)} %dynamic-slice_add_fusion.3), channel_id=1, source_target_pairs={{0,8},{2,10},{4,12},{6,14},{8,0},{10,2},{12,4},{14,6},{1,9},{3,11}... | collective-permute-start | bytes 165896 | tf_op jit(solution)/shard_map/ppermute | solution.py:95
  123.3 9.8 %collective-permute-start.9 = (f32[96,768]{1,0:T(8,128)S(1)}, f32[96,768]{1,0:T(8,128)S(1)}, u32[]{:S(2)}, u32[]{:S(2)}) collective-permute-start(f32[96,768]{1,0:T(8,128)S(1)} %slice_add_fusion.10), channel_id=1, source_target_pairs={{0,4},{4,8},{8,12},{12,14},{14,10},{10,6},{6,2},{2,0},{1,5},{5,9},... | collective-permute-start | bytes 884744 | tf_op jit(solution)/shard_map/ppermute | solution.py:182
  126.2 9.0 %collective-permute-start.15 = (f32[96,768]{1,0:T(8,128)S(1)}, f32[96,768]{1,0:T(8,128)S(1)}, u32[]{:S(2)}, u32[]{:S(2)}) collective-permute-start(f32[96,768]{1,0:T(8,128)S(1)} %slice_add_fusion.4), channel_id=1, source_target_pairs={{0,2},{4,0},{8,4},{12,8},{14,12},{10,14},{6,10},{2,6},{1,3},{5,1},... | collective-permute-start | bytes 884744 | tf_op jit(solution)/shard_map/ppermute | solution.py:183
  128.1 8.2 %collective-permute-start.25 = (f32[144,384]{1,0:T(8,128)S(1)}, f32[144,384]{1,0:T(8,128)S(1)}, u32[]{:S(2)}, u32[]{:S(2)}) collective-permute-start(f32[144,384]{1,0:T(8,128)S(1)} %constant_dynamic-update-slice_fusion.4), channel_id=1, source_target_pairs={{0,2},{2,0},{4,6},{6,4},{8,10},{10,8},{12,14},{14,12},{1,3},{3,1},... | collective-permute-start | bytes 663560 | tf_op jit(solution)/shard_map/ppermute | solution.py:95
  133.2 6.8 %collective-permute-start.10 = (f32[96,768]{1,0:T(8,128)S(1)}, f32[96,768]{1,0:T(8,128)S(1)}, u32[]{:S(2)}, u32[]{:S(2)}) collective-permute-start(f32[96,768]{1,0:T(8,128)S(1)} %slice_add_fusion.9), channel_id=1, source_target_pairs={{0,4},{4,8},{8,12},{12,14},{14,10},{10,6},{6,2},{2,0},{1,5},{5,9},... | collective-permute-start | bytes 884744 | tf_op jit(solution)/shard_map/ppermute | solution.py:182
  135.3 8.1 %collective-permute-start.16 = (f32[96,768]{1,0:T(8,128)S(1)}, f32[96,768]{1,0:T(8,128)S(1)}, u32[]{:S(2)}, u32[]{:S(2)}) collective-permute-start(f32[96,768]{1,0:T(8,128)S(1)} %slice_add_fusion.3), channel_id=1, source_target_pairs={{0,2},{4,0},{8,4},{12,8},{14,12},{10,14},{6,10},{2,6},{1,3},{5,1},... | collective-permute-start | bytes 884744 | tf_op jit(solution)/shard_map/ppermute | solution.py:183
  136.3 7.2 %collective-permute-start.26 = (f32[144,768]{1,0:T(8,128)S(1)}, f32[144,768]{1,0:T(8,128)S(1)}, u32[]{:S(2)}, u32[]{:S(2)}) collective-permute-start(f32[144,768]{1,0:T(8,128)S(1)} %constant_dynamic-update-slice_fusion.2), channel_id=1, source_target_pairs={{0,1},{1,0},{2,3},{3,2},{4,5},{5,4},{6,7},{7,6},{8,9},{9,8},{10,11... | collective-permute-start | bytes 1327112 | tf_op jit(solution)/shard_map/ppermute | solution.py:95
  140.1 8.4 %collective-permute-start.11 = (f32[96,768]{1,0:T(8,128)S(1)}, f32[96,768]{1,0:T(8,128)S(1)}, u32[]{:S(2)}, u32[]{:S(2)}) collective-permute-start(f32[96,768]{1,0:T(8,128)S(1)} %slice_add_fusion.8), channel_id=1, source_target_pairs={{0,4},{4,8},{8,12},{12,14},{14,10},{10,6},{6,2},{2,0},{1,5},{5,9},... | collective-permute-start | bytes 884744 | tf_op jit(solution)/shard_map/ppermute | solution.py:182
  143.4 9.0 %collective-permute-start.17 = (f32[96,768]{1,0:T(8,128)S(1)}, f32[96,768]{1,0:T(8,128)S(1)}, u32[]{:S(2)}, u32[]{:S(2)}) collective-permute-start(f32[96,768]{1,0:T(8,128)S(1)} %slice_add_fusion.2), channel_id=1, source_target_pairs={{0,2},{4,0},{8,4},{12,8},{14,12},{10,14},{6,10},{2,6},{1,3},{5,1},... | collective-permute-start | bytes 884744 | tf_op jit(solution)/shard_map/ppermute | solution.py:183
  148.5 6.8 %collective-permute-start.12 = (f32[96,768]{1,0:T(8,128)S(1)}, f32[96,768]{1,0:T(8,128)S(1)}, u32[]{:S(2)}, u32[]{:S(2)}) collective-permute-start(f32[96,768]{1,0:T(8,128)S(1)} %slice_add_fusion.7), channel_id=1, source_target_pairs={{0,4},{4,8},{8,12},{12,14},{14,10},{10,6},{6,2},{2,0},{1,5},{5,9},... | collective-permute-start | bytes 884744 | tf_op jit(solution)/shard_map/ppermute | solution.py:182
  152.5 6.8 %collective-permute-start.18 = (f32[96,768]{1,0:T(8,128)S(1)}, f32[96,768]{1,0:T(8,128)S(1)}, u32[]{:S(2)}, u32[]{:S(2)}) collective-permute-start(f32[96,768]{1,0:T(8,128)S(1)} %slice_add_fusion.1), channel_id=1, source_target_pairs={{0,2},{4,0},{8,4},{12,8},{14,12},{10,14},{6,10},{2,6},{1,3},{5,1},... | collective-permute-start | bytes 884744 | tf_op jit(solution)/shard_map/ppermute | solution.py:183
  (28 other events, 304.4 us)

commit v18 on v11

--- a/solution.py
+++ b/solution.py
@@ -98,12 +98,12 @@
 def halving_plan(rows, cols, steps):
     plan = []
     for _ in range(steps):
-        if cols % 256 == 0:
+        if rows % 16 == 0 or cols % 256:
+            plan.append(0)
+            rows //= 2
+        else:
             plan.append(1)
             cols //= 2
-        else:
-            plan.append(0)
-            rows //= 2
     return plan
 
 

time: 155 us -> 155 us (level)
  no operation moved by 1% of the time
where the time goes in v18:
time: 155 us
  waiting for transfers between devices  51 us (33%)
  starting transfers between devices  43.4 us (28%)
  matrix products  32.7 us (21%)
  other arithmetic  19.3 us (12%)
  local copies, waits for them, and re-layouts  6.29 us (4%)
  between operations  2.37 us (2%)
    ppermute x9, waiting for transfers between devices, swap(): return lax.ppermute(value, axis, [(i, i ^ distance) for i in range(count)])  18.5 us
    ppermute x7, waiting for transfers between devices, ring_reduce_scatter(): ahead = lax.ppermute(ahead, 'seq', forward) + block(-2 - step, True)  17.1 us
    ppermute x2, waiting for transfers between devices, with_halo(): lax.ppermute(tail, axis, [(i, (i + 1) % count) for i in range(ends)])  13.2 us
    ppermute x7, starting transfers between devices, ring_reduce_scatter(): ahead = lax.ppermute(ahead, 'seq', forward) + block(-2 - step, True)  12.4 us
    ppermute x7, starting transfers between devices, ring_reduce_scatter(): behind = lax.ppermute(behind, 'seq', backward) + block(2 + step, False)  11.5 us
    dot_general x24, matrix products, conv_taps(): lax.dot_general(window, dense[k, :, cols], dims, preferred_element_type=j...  11.5 us
    ppermute x2, starting transfers between devices, with_halo(): lax.ppermute(tail, axis, [(i, (i + 1) % count) for i in range(ends)])  9.6 us
    ppermute x9, starting transfers between devices, swap(): return lax.ppermute(value, axis, [(i, i ^ distance) for i in range(count)])  7.29 us
  transfers between devices with their start and end apart: 27, of which 14 were waited for; matrix products, arithmetic and copies ran while one was open for 19% of the time, Pallas kernels for 0%

profile of v18, /device:TPU:0, one launch (start us, length us, event | category | flops | bytes accessed | tf_op | source)
XLA Modules:
  0.0 155.1 jit_solution(13413493439879572077)
XLA Ops:
  3.8 5.5 %collective-permute-start = (bf16[1,64,1536]{2,1,0:T(8,128)(2,1)}, bf16[1,64,1536]{2,1,0:T(8,128)(2,1)}, u32[]{:S(2)}, u32[]{:S(2)}) collective-permute-start(bf16[1,64,1536]{2,1,0:T(8,128)(2,1)} %get-tuple-element.40), channel_id=1, source_target_pairs={{0,2},{2,4},{4,6},{6,8},{8,10},{10,12},{12,14},{1,3},{3,5},{5,7},{... | collective-permute-start | bytes 589832 | tf_op jit(solution)/shard_map/ppermute | solution.py:21
  11.4 2.1 %bitcast_multiply_fusion = bf16[3,384,1536]{2,1,0:T(8,128)(2,1)} fusion(bf16[384,1536]{1,0:T(8,128)(2,1)S(1)} %fusion.13, bf16[3,48,1536]{2,1,0:T(8,128)(2,1)S(1)} %copy-done.22), kind=kLoop, calls=%fused_computation.8 | loop fusion | flops 1769472 | bytes 5160960 | tf_op jit(solution)/shard_map/mul | solution.py:49
  13.5 3.9 %collective-permute-done = bf16[1,64,1536]{2,1,0:T(8,128)(2,1)} collective-permute-done((bf16[1,64,1536]{2,1,0:T(8,128)(2,1)}, bf16[1,64,1536]{2,1,0:T(8,128)(2,1)}, u32[]{:S(2)}, u32[]{:S(2)}) %collective-permute-start) | collective-permute-done | bytes 196640 | tf_op jit(solution)/shard_map/ppermute | solution.py:21
  26.7 3.6 %convolution_multiply_fusion = f32[768,1536]{1,0:T(8,128)} fusion(bf16[512,768]{0,1:T(8,128)(2,1)S(1)} %bitcast.152, bf16[1,512,1536]{2,1,0:T(8,128)(2,1)S(1)} %copy-done.2), kind=kOutput, calls=%fused_computation.4 | convolution fusion | flops 1209139200 | bytes 7077888 | tf_op jit(solution)/shard_map/dot_general | solution.py:191
  30.4 2.7 %convolution_multiply_fusion.1 = f32[768,1536]{1,0:T(8,128)S(1)} fusion(bf16[512,768]{0,1:T(8,128)(2,1)} %bitcast.151, bf16[1,512,1536]{2,1,0:T(8,128)(2,1)S(1)} %copy-done.2), kind=kOutput, calls=%fused_computation.5 | convolution fusion | flops 1209139200 | bytes 7077888 | tf_op jit(solution)/shard_map/dot_general | solution.py:191
  33.1 6.2 %fusion.2 = bf16[1,512,1536]{2,1,0:T(8,128)(2,1)} fusion(bf16[1,512,1536]{2,1,0:T(8,128)(2,1)S(1)} %copy-done.11, bf16[1536,1536]{1,0:T(8,128)(2,1)} %param.8, f32[512]{0:T(512)S(1)} %fusion.112, f32[512,384]{0,1:T(8,128)S(1)} %copy-done.10, f32[512,384]{0,1:T(8,128)S(1)} %copy-done.8, f32[512,384]{0,1:T(8,128)S(1)} %copy-done.6, f32[512,384]{0,1:T(8,128)S(1)} %copy-done.4), kind=kOutput, calls=%fused_computation.14 | convolution fusion | flops 2425356288 | bytes 11012096 | tf_op jit(solution)/shard_map/dot_general | solution.py:231
  39.3 3.3 %add.488 = f32[8,96,1536]{2,1,0:T(8,128)S(1)} add(f32[8,96,1536]{2,1,0:T(8,128)S(1)} %bitcast.142, f32[8,96,1536]{2,1,0:T(8,128)} %collective-permute-done.2) | non-fusion elementwise | flops 1179648 | bytes 14155776 | tf_op jit(solution)/shard_map/add | solution.py:208
  42.7 3.9 %fusion.9 = bf16[512,1536]{0,1:T(8,128)(2,1)S(1)} fusion(bf16[512,1536]{1,0:T(8,128)(2,1)S(1)} %bitcast.143, bf16[1536,1536]{1,0:T(8,128)(2,1)S(1)} %bitcast.167, f32[512]{0:T(512)S(1)} %fusion.112, f32[512,384]{0,1:T(8,128)S(1)} %copy-done.10, f32[512,384]{0,1:T(8,128)S(1)} %copy-done.8, f32[512,384]{0,1:T(8,128)S(1)} %copy-done.6, ...), kind=kOutput, calls=%fused_computation.27 | convolution fusion | flops 2426929152 | bytes 11012096 | tf_op jit(solution)/shard_map/dot_general | solution.py:234
  53.4 4.1 %collective-permute-start.3 = (bf16[1,64,1536]{1,2,0:T(8,128)(2,1)S(1)}, bf16[1,64,1536]{1,2,0:T(8,128)(2,1)S(1)}, u32[]{:S(2)}, u32[]{:S(2)}) collective-permute-start(bf16[1,64,1536]{1,2,0:T(8,128)(2,1)S(1)} %get-tuple-element.36), channel_id=1, source_target_pairs={{0,2},{2,4},{4,6},{6,8},{8,10},{10,12},{12,14},{1,3},{3,5},{5,7},{... | collective-permute-start | bytes 589832 | tf_op jit(solution)/shard_map/ppermute | solution.py:21
  58.8 2.7 %dynamic-slice_bitcast_fusion.8 = (f32[96,1536]{1,0:T(8,128)}, f32[96,1536]{1,0:T(8,128)}, f32[96,1536]{1,0:T(8,128)}, f32[96,1536]{1,0:T(8,128)}, f32[96,1536]{...) fusion(f32[8,96,1536]{2,1,0:T(8,128)S(1)} %add.488, ...), kind=kLoop, calls=%fused_computation.80 | loop fusion | bytes 18874432 | tf_op jit(solution)/shard_map/jit(dynamic_index_in_dim)/squeeze | solution.py:176
  61.5 4.5 %collective-permute-start.5 = (f32[96,768]{1,0:T(8,128)S(1)}, f32[96,768]{1,0:T(8,128)S(1)}, u32[]{:S(2)}, u32[]{:S(2)}) collective-permute-start(f32[96,768]{1,0:T(8,128)S(1)} %slice.312), channel_id=1, source_target_pairs={{0,4},{4,8},{8,12},{12,14},{14,10},{10,6},{6,2},{2,0},{1,5},{5,9},... | collective-permute-start | bytes 884744 | tf_op jit(solution)/shard_map/ppermute | solution.py:182
  66.1 9.3 %collective-permute-done.3 = bf16[1,64,1536]{1,2,0:T(8,128)(2,1)S(1)} collective-permute-done((bf16[1,64,1536]{1,2,0:T(8,128)(2,1)S(1)}, bf16[1,64,1536]{1,2,0:T(8,128)(2,1)S(1)}, u32[]{:S(2)}, u32[]{:S(2)}) %collective-permute-start.3) | collective-permute-done | bytes 196640 | tf_op jit(solution)/shard_map/ppermute | solution.py:21
  84.8 3.4 %collective-permute-start.6 = (f32[96,768]{1,0:T(8,128)S(1)}, f32[96,768]{1,0:T(8,128)S(1)}, u32[]{:S(2)}, u32[]{:S(2)}) collective-permute-start(f32[96,768]{1,0:T(8,128)S(1)} %slice_add_fusion.13), channel_id=1, source_target_pairs={{0,4},{4,8},{8,12},{12,14},{14,10},{10,6},{6,2},{2,0},{1,5},{5,9},... | collective-permute-start | bytes 884744 | tf_op jit(solution)/shard_map/ppermute | solution.py:182
  90.5 6.9 %collective-permute-done.20 = f32[72,768]{1,0:T(8,128)S(1)} collective-permute-done((f32[72,768]{1,0:T(8,128)S(1)}, f32[72,768]{1,0:T(8,128)S(1)}, u32[]{:S(2)}, u32[]{:S(2)}) %collective-permute-start.20) | collective-permute-done | bytes 221216 | tf_op jit(solution)/shard_map/ppermute | solution.py:95
  99.7 2.6 %collective-permute-done.21 = f32[72,384]{1,0:T(8,128)S(1)} collective-permute-done((f32[72,384]{1,0:T(8,128)S(1)}, f32[72,384]{1,0:T(8,128)S(1)}, u32[]{:S(2)}, u32[]{:S(2)}) %collective-permute-start.21) | collective-permute-done | bytes 110624 | tf_op jit(solution)/shard_map/ppermute | solution.py:95
  102.4 3.7 %collective-permute-start.22 = (f32[36,384]{1,0:T(8,128)S(1)}, f32[36,384]{1,0:T(8,128)S(1)}, u32[]{:S(2)}, u32[]{:S(2)}) collective-permute-start(f32[36,384]{1,0:T(8,128)S(1)} %constant_dynamic-slice_fusion), channel_id=1, source_target_pairs={{0,8},{2,10},{4,12},{6,14},{8,0},{10,2},{12,4},{14,6},{1,9},{3,11}... | collective-permute-start | bytes 165896 | tf_op jit(solution)/shard_map/ppermute | solution.py:95
  106.8 2.6 %collective-permute-start.14 = (f32[96,768]{1,0:T(8,128)}, f32[96,768]{1,0:T(8,128)}, u32[]{:S(2)}, u32[]{:S(2)}) collective-permute-start(f32[96,768]{1,0:T(8,128)} %slice_add_fusion.5), channel_id=1, source_target_pairs={{0,2},{4,0},{8,4},{12,8},{14,12},{10,14},{6,10},{2,6},{1,3},{5,1},... | collective-permute-start | bytes 884744 | tf_op jit(solution)/shard_map/ppermute | solution.py:183
  111.9 6.1 %collective-permute-done.23 = f32[36,384]{1,0:T(8,128)S(1)} collective-permute-done((f32[36,384]{1,0:T(8,128)S(1)}, f32[36,384]{1,0:T(8,128)S(1)}, u32[]{:S(2)}, u32[]{:S(2)}) %collective-permute-start.23) | collective-permute-done | bytes 55328 | tf_op jit(solution)/shard_map/ppermute | solution.py:95
  119.4 2.1 %collective-permute-start.8 = (f32[96,768]{1,0:T(8,128)S(1)}, f32[96,768]{1,0:T(8,128)S(1)}, u32[]{:S(2)}, u32[]{:S(2)}) collective-permute-start(f32[96,768]{1,0:T(8,128)S(1)} %slice_add_fusion.11), channel_id=1, source_target_pairs={{0,4},{4,8},{8,12},{12,14},{14,10},{10,6},{6,2},{2,0},{1,5},{5,9},... | collective-permute-start | bytes 884744 | tf_op jit(solution)/shard_map/ppermute | solution.py:182
  125.3 4.4 %collective-permute-done.8 = f32[96,768]{1,0:T(8,128)S(1)} collective-permute-done((f32[96,768]{1,0:T(8,128)S(1)}, f32[96,768]{1,0:T(8,128)S(1)}, u32[]{:S(2)}, u32[]{:S(2)}) %collective-permute-start.8) | collective-permute-done | bytes 294944 | tf_op jit(solution)/shard_map/ppermute | solution.py:182
  135.1 2.5 %collective-permute-done.9 = f32[96,768]{1,0:T(8,128)S(1)} collective-permute-done((f32[96,768]{1,0:T(8,128)S(1)}, f32[96,768]{1,0:T(8,128)S(1)}, u32[]{:S(2)}, u32[]{:S(2)}) %collective-permute-start.9) | collective-permute-done | bytes 294944 | tf_op jit(solution)/shard_map/ppermute | solution.py:182
  138.3 2.4 %collective-permute-start.17 = (f32[96,768]{1,0:T(8,128)S(1)}, f32[96,768]{1,0:T(8,128)S(1)}, u32[]{:S(2)}, u32[]{:S(2)}) collective-permute-start(f32[96,768]{1,0:T(8,128)S(1)} %slice_add_fusion.2), channel_id=1, source_target_pairs={{0,2},{4,0},{8,4},{12,8},{14,12},{10,14},{6,10},{2,6},{1,3},{5,1},... | collective-permute-start | bytes 884744 | tf_op jit(solution)/shard_map/ppermute | solution.py:183
  140.7 4.7 %collective-permute-done.10 = f32[96,768]{1,0:T(8,128)S(1)} collective-permute-done((f32[96,768]{1,0:T(8,128)S(1)}, f32[96,768]{1,0:T(8,128)S(1)}, u32[]{:S(2)}, u32[]{:S(2)}) %collective-permute-start.10) | collective-permute-done | bytes 294944 | tf_op jit(solution)/shard_map/ppermute | solution.py:182
  148.6 5.5 %collective-permute-done.11 = f32[96,768]{1,0:T(8,128)S(1)} collective-permute-done((f32[96,768]{1,0:T(8,128)S(1)}, f32[96,768]{1,0:T(8,128)S(1)}, u32[]{:S(2)}, u32[]{:S(2)}) %collective-permute-start.11) | collective-permute-done | bytes 294944 | tf_op jit(solution)/shard_map/ppermute | solution.py:182
  (184 shorter events, 54.1 us)
Async XLA Ops:
  3.8 13.6 %collective-permute-start = (bf16[1,64,1536]{2,1,0:T(8,128)(2,1)}, bf16[1,64,1536]{2,1,0:T(8,128)(2,1)}, u32[]{:S(2)}, u32[]{:S(2)}) collective-permute-start(bf16[1,64,1536]{2,1,0:T(8,128)(2,1)} %get-tuple-element.40), channel_id=1, source_target_pairs={{0,2},{2,4},{4,6},{6,8},{8,10},{10,12},{12,14},{1,3},{3,5},{5,7},{... | collective-permute-start | bytes 589832 | tf_op jit(solution)/shard_map/ppermute | solution.py:21
  9.3 8.3 %collective-permute-start.1 = (bf16[1,64,1536]{2,1,0:T(8,128)(2,1)S(1)}, bf16[1,64,1536]{2,1,0:T(8,128)(2,1)}, u32[]{:S(2)}, u32[]{:S(2)}) collective-permute-start(bf16[1,64,1536]{2,1,0:T(8,128)(2,1)S(1)} %get-tuple-element.41), channel_id=1, source_target_pairs={{2,0},{4,2},{6,4},{8,6},{10,8},{12,10},{14,12},{3,1},{5,3},{7,5},{... | collective-permute-start | bytes 589832 | tf_op jit(solution)/shard_map/ppermute | solution.py:23
  30.3 9.1 %collective-permute-start.2 = (f32[8,96,1536]{2,1,0:T(8,128)}, f32[8,96,1536]{2,1,0:T(8,128)}, u32[]{:S(2)}, u32[]{:S(2)}) collective-permute-start(f32[8,96,1536]{2,1,0:T(8,128)} %bitcast.25), channel_id=1, source_target_pairs={{0,1},{1,0},{2,3},{3,2},{4,5},{5,4},{6,7},{7,6},{8,9},{9,8},{10,11... | collective-permute-start | bytes 14155784 | tf_op jit(solution)/shard_map/ppermute | solution.py:95
  52.6 35.6 %collective-permute-start.19 = (f32[72,1536]{1,0:T(8,128)S(1)}, f32[72,1536]{1,0:T(8,128)S(1)}, u32[]{:S(2)}, u32[]{:S(2)}) collective-permute-start(f32[72,1536]{1,0:T(8,128)S(1)} %constant_dynamic-slice_fusion.3), channel_id=1, source_target_pairs={{0,1},{1,0},{2,3},{3,2},{4,5},{5,4},{6,7},{7,6},{8,9},{9,8},{10,11... | collective-permute-start | bytes 1327112 | tf_op jit(solution)/shard_map/ppermute | solution.py:95
  53.4 22.0 %collective-permute-start.3 = (bf16[1,64,1536]{1,2,0:T(8,128)(2,1)S(1)}, bf16[1,64,1536]{1,2,0:T(8,128)(2,1)S(1)}, u32[]{:S(2)}, u32[]{:S(2)}) collective-permute-start(bf16[1,64,1536]{1,2,0:T(8,128)(2,1)S(1)} %get-tuple-element.36), channel_id=1, source_target_pairs={{0,2},{2,4},{4,6},{6,8},{8,10},{10,12},{12,14},{1,3},{3,5},{5,7},{... | collective-permute-start | bytes 589832 | tf_op jit(solution)/shard_map/ppermute | solution.py:21
  57.5 17.9 %collective-permute-start.4 = (bf16[1,64,1536]{1,2,0:T(8,128)(2,1)S(1)}, bf16[1,64,1536]{1,2,0:T(8,128)(2,1)S(1)}, u32[]{:S(2)}, u32[]{:S(2)}) collective-permute-start(bf16[1,64,1536]{1,2,0:T(8,128)(2,1)S(1)} %get-tuple-element.37), channel_id=1, source_target_pairs={{2,0},{4,2},{6,4},{8,6},{10,8},{12,10},{14,12},{3,1},{5,3},{7,5},{... | collective-permute-start | bytes 589832 | tf_op jit(solution)/shard_map/ppermute | solution.py:23
  61.5 23.3 %collective-permute-start.5 = (f32[96,768]{1,0:T(8,128)S(1)}, f32[96,768]{1,0:T(8,128)S(1)}, u32[]{:S(2)}, u32[]{:S(2)}) collective-permute-start(f32[96,768]{1,0:T(8,128)S(1)} %slice.312), channel_id=1, source_target_pairs={{0,4},{4,8},{8,12},{12,14},{14,10},{10,6},{6,2},{2,0},{1,5},{5,9},... | collective-permute-start | bytes 884744 | tf_op jit(solution)/shard_map/ppermute | solution.py:182
  66.0 22.4 %collective-permute-start.12 = (f32[96,768]{1,0:T(8,128)S(1)}, f32[96,768]{1,0:T(8,128)S(1)}, u32[]{:S(2)}, u32[]{:S(2)}) collective-permute-start(f32[96,768]{1,0:T(8,128)S(1)} %slice.320), channel_id=1, source_target_pairs={{0,2},{4,0},{8,4},{12,8},{14,12},{10,14},{6,10},{2,6},{1,3},{5,1},... | collective-permute-start | bytes 884744 | tf_op jit(solution)/shard_map/ppermute | solution.py:183
  84.8 12.8 %collective-permute-start.6 = (f32[96,768]{1,0:T(8,128)S(1)}, f32[96,768]{1,0:T(8,128)S(1)}, u32[]{:S(2)}, u32[]{:S(2)}) collective-permute-start(f32[96,768]{1,0:T(8,128)S(1)} %slice_add_fusion.13), channel_id=1, source_target_pairs={{0,4},{4,8},{8,12},{12,14},{14,10},{10,6},{6,2},{2,0},{1,5},{5,9},... | collective-permute-start | bytes 884744 | tf_op jit(solution)/shard_map/ppermute | solution.py:182
  88.4 9.1 %collective-permute-start.20 = (f32[72,768]{1,0:T(8,128)S(1)}, f32[72,768]{1,0:T(8,128)S(1)}, u32[]{:S(2)}, u32[]{:S(2)}) collective-permute-start(f32[72,768]{1,0:T(8,128)S(1)} %constant_dynamic-slice_fusion.2), channel_id=1, source_target_pairs={{0,2},{2,0},{4,6},{6,4},{8,10},{10,8},{12,14},{14,12},{1,3},{3,1},... | collective-permute-start | bytes 663560 | tf_op jit(solution)/shard_map/ppermute | solution.py:95
  88.5 17.6 %collective-permute-start.13 = (f32[96,768]{1,0:T(8,128)S(1)}, f32[96,768]{1,0:T(8,128)S(1)}, u32[]{:S(2)}, u32[]{:S(2)}) collective-permute-start(f32[96,768]{1,0:T(8,128)S(1)} %slice_add_fusion.6), channel_id=1, source_target_pairs={{0,2},{4,0},{8,4},{12,8},{14,12},{10,14},{6,10},{2,6},{1,3},{5,1},... | collective-permute-start | bytes 884744 | tf_op jit(solution)/shard_map/ppermute | solution.py:183
  97.7 20.8 %collective-permute-start.7 = (f32[96,768]{1,0:T(8,128)S(1)}, f32[96,768]{1,0:T(8,128)}, u32[]{:S(2)}, u32[]{:S(2)}) collective-permute-start(f32[96,768]{1,0:T(8,128)S(1)} %slice_add_fusion.12), channel_id=1, source_target_pairs={{0,4},{4,8},{8,12},{12,14},{14,10},{10,6},{6,2},{2,0},{1,5},{5,9},... | collective-permute-start | bytes 884744 | tf_op jit(solution)/shard_map/ppermute | solution.py:182
  102.4 7.1 %collective-permute-start.22 = (f32[36,384]{1,0:T(8,128)S(1)}, f32[36,384]{1,0:T(8,128)S(1)}, u32[]{:S(2)}, u32[]{:S(2)}) collective-permute-start(f32[36,384]{1,0:T(8,128)S(1)} %constant_dynamic-slice_fusion), channel_id=1, source_target_pairs={{0,8},{2,10},{4,12},{6,14},{8,0},{10,2},{12,4},{14,6},{1,9},{3,11}... | collective-permute-start | bytes 165896 | tf_op jit(solution)/shard_map/ppermute | solution.py:95
  106.8 14.7 %collective-permute-start.14 = (f32[96,768]{1,0:T(8,128)}, f32[96,768]{1,0:T(8,128)}, u32[]{:S(2)}, u32[]{:S(2)}) collective-permute-start(f32[96,768]{1,0:T(8,128)} %slice_add_fusion.5), channel_id=1, source_target_pairs={{0,2},{4,0},{8,4},{12,8},{14,12},{10,14},{6,10},{2,6},{1,3},{5,1},... | collective-permute-start | bytes 884744 | tf_op jit(solution)/shard_map/ppermute | solution.py:183
  109.5 8.5 %collective-permute-start.23 = (f32[36,384]{1,0:T(8,128)S(1)}, f32[36,384]{1,0:T(8,128)S(1)}, u32[]{:S(2)}, u32[]{:S(2)}) collective-permute-start(f32[36,384]{1,0:T(8,128)S(1)} %dynamic-slice_add_fusion.3), channel_id=1, source_target_pairs={{0,8},{2,10},{4,12},{6,14},{8,0},{10,2},{12,4},{14,6},{1,9},{3,11}... | collective-permute-start | bytes 165896 | tf_op jit(solution)/shard_map/ppermute | solution.py:95
  119.4 10.2 %collective-permute-start.8 = (f32[96,768]{1,0:T(8,128)S(1)}, f32[96,768]{1,0:T(8,128)S(1)}, u32[]{:S(2)}, u32[]{:S(2)}) collective-permute-start(f32[96,768]{1,0:T(8,128)S(1)} %slice_add_fusion.11), channel_id=1, source_target_pairs={{0,4},{4,8},{8,12},{12,14},{14,10},{10,6},{6,2},{2,0},{1,5},{5,9},... | collective-permute-start | bytes 884744 | tf_op jit(solution)/shard_map/ppermute | solution.py:182
  122.6 8.8 %collective-permute-start.15 = (f32[96,768]{1,0:T(8,128)S(1)}, f32[96,768]{1,0:T(8,128)S(1)}, u32[]{:S(2)}, u32[]{:S(2)}) collective-permute-start(f32[96,768]{1,0:T(8,128)S(1)} %slice_add_fusion.4), channel_id=1, source_target_pairs={{0,2},{4,0},{8,4},{12,8},{14,12},{10,14},{6,10},{2,6},{1,3},{5,1},... | collective-permute-start | bytes 884744 | tf_op jit(solution)/shard_map/ppermute | solution.py:183
  124.4 10.5 %collective-permute-start.25 = (f32[72,768]{1,0:T(8,128)S(1)}, f32[72,768]{1,0:T(8,128)S(1)}, u32[]{:S(2)}, u32[]{:S(2)}) collective-permute-start(f32[72,768]{1,0:T(8,128)S(1)} %constant_dynamic-update-slice_fusion.4), channel_id=1, source_target_pairs={{0,2},{2,0},{4,6},{6,4},{8,10},{10,8},{12,14},{14,12},{1,3},{3,1},... | collective-permute-start | bytes 663560 | tf_op jit(solution)/shard_map/ppermute | solution.py:95
  129.8 7.9 %collective-permute-start.9 = (f32[96,768]{1,0:T(8,128)S(1)}, f32[96,768]{1,0:T(8,128)S(1)}, u32[]{:S(2)}, u32[]{:S(2)}) collective-permute-start(f32[96,768]{1,0:T(8,128)S(1)} %slice_add_fusion.10), channel_id=1, source_target_pairs={{0,4},{4,8},{8,12},{12,14},{14,10},{10,6},{6,2},{2,0},{1,5},{5,9},... | collective-permute-start | bytes 884744 | tf_op jit(solution)/shard_map/ppermute | solution.py:182
  131.4 6.8 %collective-permute-start.16 = (f32[96,768]{1,0:T(8,128)S(1)}, f32[96,768]{1,0:T(8,128)S(1)}, u32[]{:S(2)}, u32[]{:S(2)}) collective-permute-start(f32[96,768]{1,0:T(8,128)S(1)} %slice_add_fusion.3), channel_id=1, source_target_pairs={{0,2},{4,0},{8,4},{12,8},{14,12},{10,14},{6,10},{2,6},{1,3},{5,1},... | collective-permute-start | bytes 884744 | tf_op jit(solution)/shard_map/ppermute | solution.py:183
  137.7 7.7 %collective-permute-start.10 = (f32[96,768]{1,0:T(8,128)S(1)}, f32[96,768]{1,0:T(8,128)S(1)}, u32[]{:S(2)}, u32[]{:S(2)}) collective-permute-start(f32[96,768]{1,0:T(8,128)S(1)} %slice_add_fusion.9), channel_id=1, source_target_pairs={{0,4},{4,8},{8,12},{12,14},{14,10},{10,6},{6,2},{2,0},{1,5},{5,9},... | collective-permute-start | bytes 884744 | tf_op jit(solution)/shard_map/ppermute | solution.py:182
  138.3 7.3 %collective-permute-start.17 = (f32[96,768]{1,0:T(8,128)S(1)}, f32[96,768]{1,0:T(8,128)S(1)}, u32[]{:S(2)}, u32[]{:S(2)}) collective-permute-start(f32[96,768]{1,0:T(8,128)S(1)} %slice_add_fusion.2), channel_id=1, source_target_pairs={{0,2},{4,0},{8,4},{12,8},{14,12},{10,14},{6,10},{2,6},{1,3},{5,1},... | collective-permute-start | bytes 884744 | tf_op jit(solution)/shard_map/ppermute | solution.py:183
  145.5 8.7 %collective-permute-start.11 = (f32[96,768]{1,0:T(8,128)S(1)}, f32[96,768]{1,0:T(8,128)S(1)}, u32[]{:S(2)}, u32[]{:S(2)}) collective-permute-start(f32[96,768]{1,0:T(8,128)S(1)} %slice_add_fusion.8), channel_id=1, source_target_pairs={{0,4},{4,8},{8,12},{12,14},{14,10},{10,6},{6,2},{2,0},{1,5},{5,9},... | collective-permute-start | bytes 884744 | tf_op jit(solution)/shard_map/ppermute | solution.py:182
  145.6 8.6 %collective-permute-start.18 = (f32[96,768]{1,0:T(8,128)S(1)}, f32[96,768]{1,0:T(8,128)S(1)}, u32[]{:S(2)}, u32[]{:S(2)}) collective-permute-start(f32[96,768]{1,0:T(8,128)S(1)} %slice_add_fusion.1), channel_id=1, source_target_pairs={{0,2},{4,0},{8,4},{12,8},{14,12},{10,14},{6,10},{2,6},{1,3},{5,1},... | collective-permute-start | bytes 884744 | tf_op jit(solution)/shard_map/ppermute | solution.py:183
  (28 other events, 312.7 us)

commit v19 on v18

--- a/solution.py
+++ b/solution.py
@@ -184,7 +184,7 @@
     return jnp.concatenate([ahead, behind], axis=1)
 
 
-def point_gradient(act_rows, cot_rows, scale, snake):
+def point_gradient(act_rows, cot_rows, scale, snake, slope):
     chans = act_rows.shape[1]
     seq_count = lax.axis_size("seq")
     rep_count = lax.axis_size("rep")
@@ -193,9 +193,9 @@
     ) * scale
     if rep_count != 2:
         partial = product(act_rows, cot_rows)
-        partial, cot_rows = lax.optimization_barrier((partial, cot_rows))
+        partial, slope = lax.optimization_barrier((partial, slope))
         total = lax.psum_scatter(partial, ("seq", "rep"), scatter_dimension=0, tiled=True)
-        return total, cot_rows
+        return total, slope
     block = chans // (seq_count * rep_count)
     blocks = act_rows.reshape(act_rows.shape[0], seq_count, rep_count, block)
     rep_index = lax.axis_index("rep")
@@ -206,8 +206,8 @@
         return product(cols, cot_rows).reshape(seq_count, block, chans)
 
     mine = rows_of(rep_index) + swap(rows_of(1 - rep_index), "rep", 1)
-    mine, cot_rows = lax.optimization_barrier((mine, cot_rows))
-    return ring_reduce_scatter(mine, snake), cot_rows
+    mine, slope = lax.optimization_barrier((mine, slope))
+    return ring_reduce_scatter(mine, snake), slope
 
 
 def on_device(snake, inputs, lengths, conv_weight, point_weight, cotangent):
@@ -230,7 +230,7 @@
     cot_rows = cotangent.reshape(local_bins, chans)
     proj = jnp.dot(act_rows, point_weight, preferred_element_type=jnp.float32).reshape(inputs.shape)
     output = (inputs.astype(jnp.float32) + proj).astype(jnp.bfloat16)
-    grad_point, cot_rows = point_gradient(act_rows, cot_rows, scale, snake)
+    grad_point, slope = point_gradient(act_rows, cot_rows, scale, snake, slope)
     back = lax.dot_general(
         cot_rows, point_weight, (((1,), (1,)), ((), ())), preferred_element_type=jnp.float32
     )

time: 155 us -> 181 us (1.17)
  local copies, waits for them, and re-layouts: 6.29 us -> 19.5 us
  other arithmetic: 19.3 us -> 25.4 us
  waiting for transfers between devices: 51 us -> 56.8 us
  starting transfers between devices: 43.4 us -> 40.7 us
  matrix products: 32.7 us -> 35.3 us
    unnamed x50 -> x70, local copies, waits for them, and re-layouts: 0.66 us -> 10.9 us
    ppermute x2, waiting for transfers between devices: 13.2 us -> 19.5 us  [with_halo(): lax.ppermute(tail, axis, [(i, (i + 1) % count) for i in range(ends)])]
    dot_general x1, matrix products: 3.86 us -> 6.8 us  [on_device(): lax.dot_general(cot_rows, point_weight, (((1,), (1,)), ((), ())), preferr...]
    add x0 -> x1, other arithmetic: none -> 2.38 us  [gelu_pair(): return (pre * cdf, cdf + pre * dens)]
  transfers between devices with their start and end apart: 27 -> 27, of which waited for: 14 -> 13; matrix products, arithmetic and copies ran while one was open for 19% -> 26% of each run, Pallas kernels for 0% -> 0%
where the time goes in v19:
time: 181 us; the launch traced here: 180 us
  waiting for transfers between devices  56.8 us (31%)
  starting transfers between devices  40.7 us (22%)
  matrix products  35.3 us (20%)
  other arithmetic  25.4 us (14%)
  local copies, waits for them, and re-layouts  19.5 us (11%)
  between operations  2.31 us (1%)
    ppermute x2, waiting for transfers between devices, with_halo(): lax.ppermute(tail, axis, [(i, (i + 1) % count) for i in range(ends)])  19.5 us
    ppermute x9, waiting for transfers between devices, swap(): return lax.ppermute(value, axis, [(i, i ^ distance) for i in range(count)])  18.2 us
    ppermute x7, waiting for transfers between devices, ring_reduce_scatter(): ahead = lax.ppermute(ahead, 'seq', forward) + block(-2 - step, True)  17.3 us
    ppermute x7, starting transfers between devices, ring_reduce_scatter(): behind = lax.ppermute(behind, 'seq', backward) + block(2 + step, False)  11.4 us
    ppermute x7, starting transfers between devices, ring_reduce_scatter(): ahead = lax.ppermute(ahead, 'seq', forward) + block(-2 - step, True)  11 us
    unnamed x70, local copies, waits for them, and re-layouts  10.9 us
    dot_general x24, matrix products, conv_taps(): lax.dot_general(window, dense[k, :, cols], dims, preferred_element_type=j...  10.1 us
    ppermute x2, starting transfers between devices, with_halo(): lax.ppermute(tail, axis, [(i, (i + 1) % count) for i in range(ends)])  9.18 us
  transfers between devices with their start and end apart: 27, of which 13 were waited for; matrix products, arithmetic and copies ran while one was open for 26% of the time, Pallas kernels for 0%

profile of v19, /device:TPU:0, one launch (start us, length us, event | category | flops | bytes accessed | tf_op | source)
XLA Modules:
  0.0 180.0 jit_solution(12648084927483578125)
XLA Ops:
  4.3 4.9 %collective-permute-start = (bf16[1,64,1536]{1,2,0:T(8,128)(2,1)}, bf16[1,64,1536]{1,2,0:T(8,128)(2,1)S(1)}, u32[]{:S(2)}, u32[]{:S(2)}) collective-permute-start(bf16[1,64,1536]{1,2,0:T(8,128)(2,1)} %get-tuple-element.46), channel_id=1, source_target_pairs={{0,2},{2,4},{4,6},{6,8},{8,10},{10,12},{12,14},{1,3},{3,5},{5,7},{... | collective-permute-start | bytes 589832 | tf_op jit(solution)/shard_map/ppermute | solution.py:21
  11.7 3.1 %bitcast_multiply_fusion = bf16[3,384,1536]{2,1,0:T(8,128)(2,1)} fusion(bf16[384,1536]{1,0:T(8,128)(2,1)S(1)} %fusion.11, bf16[3,48,1536]{2,1,0:T(8,128)(2,1)} %param.7), kind=kLoop, calls=%fused_computation.8 | loop fusion | flops 1769472 | bytes 5160960 | tf_op jit(solution)/shard_map/mul | solution.py:49
  14.8 11.4 %collective-permute-done = bf16[1,64,1536]{1,2,0:T(8,128)(2,1)S(1)} collective-permute-done((bf16[1,64,1536]{1,2,0:T(8,128)(2,1)}, bf16[1,64,1536]{1,2,0:T(8,128)(2,1)S(1)}, u32[]{:S(2)}, u32[]{:S(2)}) %collective-permute-start) | collective-permute-done | bytes 196640 | tf_op jit(solution)/shard_map/ppermute | solution.py:21
  34.8 2.4 %fusion.5 = (f32[1,512,1536]{1,2,0:T(8,128)}, f32[1,512,1536]{1,2,0:T(8,128)S(1)}) fusion(f32[1,512,384]{1,2,0:T(8,128)S(1)} %bitcast.162, f32[1,512,384]{1,2,0:T(8,128)S(1)} %bitcast.161, f32[1,512,384]{1,2,0:T(8,128)S(1)} %bitcast.160, f32[1,512,384]{1,2,0:T(8,128)S(1)} %bitcast.159), kind=kLoop, calls=%fused_computation.17 | loop fusion | flops 8650752 | bytes 9437184 | tf_op jit(solution)/shard_map/add | solution.py:33
  39.7 3.5 %convolution_multiply_fusion = f32[768,1536]{1,0:T(8,128)} fusion(bf16[512,768]{0,1:T(8,128)(2,1)S(1)} %bitcast.164, bf16[1,512,1536]{2,1,0:T(8,128)(2,1)S(1)} %copy-done.2), kind=kOutput, calls=%fused_computation.4 | convolution fusion | flops 1209139200 | bytes 7077888 | tf_op jit(solution)/shard_map/dot_general | solution.py:191
  46.0 6.8 %convolution_bitcast_fusion = f32[1,512,1536]{1,2,0:T(8,128)} fusion(bf16[1536,1536]{1,0:T(8,128)(2,1)} %param.8, bf16[1,512,1536]{2,1,0:T(8,128)(2,1)S(1)} %copy-done.2), kind=kOutput, calls=%fused_computation.10 | convolution fusion | flops 2415919104 | bytes 9437184 | tf_op jit(solution)/shard_map/dot_general | solution.py:234
  52.8 7.6 %fusion.1 = bf16[1,512,1536]{1,2,0:T(8,128)(2,1)} fusion(bf16[1,512,1536]{1,2,0:T(8,128)(2,1)S(1)} %copy-done.5, bf16[1536,1536]{1,0:T(8,128)(2,1)} %param.8, f32[512,384]{0,1:T(8,128)S(1)} %copy-done.15, f32[512,384]{0,1:T(8,128)S(1)} %copy-done.13, f32[512,384]{0,1:T(8,128)S(1)} %copy-done.11, f32[512,384]{0,1:T(8,128)S(1)} %copy-done.9, f32[512]{0:T(512)S(1)} %fusion.116), kind=kOutput, calls=%fused_computation.13 | convolution fusion | flops 2425356288 | bytes 11012096 | tf_op jit(solution)/shard_map/dot_general | solution.py:231
  60.4 2.6 %copy.13 = bf16[1,512,1536]{2,1,0:T(8,128)(2,1)} copy(bf16[1,512,1536]{1,2,0:T(8,128)(2,1)} %fusion.1) | data formatting | bytes 3145728
  63.0 2.5 %convolution_multiply_fusion.1 = f32[768,1536]{1,0:T(8,128)S(1)} fusion(bf16[512,768]{0,1:T(8,128)(2,1)} %bitcast.163, bf16[1,512,1536]{2,1,0:T(8,128)(2,1)S(1)} %copy-done.2), kind=kOutput, calls=%fused_computation.5 | convolution fusion | flops 1209139200 | bytes 7077888 | tf_op jit(solution)/shard_map/dot_general | solution.py:191
  65.5 3.5 %add.506 = f32[8,96,1536]{2,1,0:T(8,128)S(1)} add(f32[8,96,1536]{2,1,0:T(8,128)S(1)} %bitcast.155, f32[8,96,1536]{2,1,0:T(8,128)} %collective-permute-done.2) | non-fusion elementwise | flops 1179648 | bytes 14155776 | tf_op jit(solution)/shard_map/add | solution.py:208
  78.2 4.3 %collective-permute-start.3 = (bf16[1,64,1536]{1,2,0:T(8,128)(2,1)S(1)}, bf16[1,64,1536]{1,2,0:T(8,128)(2,1)S(1)}, u32[]{:S(2)}, u32[]{:S(2)}) collective-permute-start(bf16[1,64,1536]{1,2,0:T(8,128)(2,1)S(1)} %get-tuple-element.42), channel_id=1, source_target_pairs={{0,2},{2,4},{4,6},{6,8},{8,10},{10,12},{12,14},{1,3},{3,5},{5,7},{... | collective-permute-start | bytes 589832 | tf_op jit(solution)/shard_map/ppermute | solution.py:21
  83.8 3.2 %dynamic-slice_bitcast_fusion.8 = (f32[96,1536]{1,0:T(8,128)}, f32[96,1536]{1,0:T(8,128)S(1)}, f32[96,1536]{1,0:T(8,128)}, f32[96,1536]{1,0:T(8,128)}, f32[96,15...) fusion(f32[8,96,1536]{2,1,0:T(8,128)S(1)} %add.506, ...), kind=kLoop, calls=%fused_computation.84 | loop fusion | bytes 18874432 | tf_op jit(solution)/shard_map/jit(dynamic_index_in_dim)/squeeze | solution.py:176
  87.7 3.8 %collective-permute-start.5 = (f32[96,768]{1,0:T(8,128)}, f32[96,768]{1,0:T(8,128)}, u32[]{:S(2)}, u32[]{:S(2)}) collective-permute-start(f32[96,768]{1,0:T(8,128)} %slice.312), channel_id=1, source_target_pairs={{0,4},{4,8},{8,12},{12,14},{14,10},{10,6},{6,2},{2,0},{1,5},{5,9},... | collective-permute-start | bytes 884744 | tf_op jit(solution)/shard_map/ppermute | solution.py:182
  92.3 8.1 %collective-permute-done.3 = bf16[1,64,1536]{1,2,0:T(8,128)(2,1)S(1)} collective-permute-done((bf16[1,64,1536]{1,2,0:T(8,128)(2,1)S(1)}, bf16[1,64,1536]{1,2,0:T(8,128)(2,1)S(1)}, u32[]{:S(2)}, u32[]{:S(2)}) %collective-permute-start.3) | collective-permute-done | bytes 196640 | tf_op jit(solution)/shard_map/ppermute | solution.py:21
  110.5 2.8 %collective-permute-start.6 = (f32[96,768]{1,0:T(8,128)S(1)}, f32[96,768]{1,0:T(8,128)S(1)}, u32[]{:S(2)}, u32[]{:S(2)}) collective-permute-start(f32[96,768]{1,0:T(8,128)S(1)} %slice_add_fusion.13), channel_id=1, source_target_pairs={{0,4},{4,8},{8,12},{12,14},{14,10},{10,6},{6,2},{2,0},{1,5},{5,9},... | collective-permute-start | bytes 884744 | tf_op jit(solution)/shard_map/ppermute | solution.py:182
  116.6 6.5 %collective-permute-done.20 = f32[72,768]{1,0:T(8,128)S(1)} collective-permute-done((f32[72,768]{1,0:T(8,128)S(1)}, f32[72,768]{1,0:T(8,128)S(1)}, u32[]{:S(2)}, u32[]{:S(2)}) %collective-permute-start.20) | collective-permute-done | bytes 221216 | tf_op jit(solution)/shard_map/ppermute | solution.py:95
  125.4 2.6 %collective-permute-done.21 = f32[72,384]{1,0:T(8,128)S(1)} collective-permute-done((f32[72,384]{1,0:T(8,128)S(1)}, f32[72,384]{1,0:T(8,128)S(1)}, u32[]{:S(2)}, u32[]{:S(2)}) %collective-permute-start.21) | collective-permute-done | bytes 110624 | tf_op jit(solution)/shard_map/ppermute | solution.py:95
  128.0 3.1 %collective-permute-start.22 = (f32[36,384]{1,0:T(8,128)S(1)}, f32[36,384]{1,0:T(8,128)S(1)}, u32[]{:S(2)}, u32[]{:S(2)}) collective-permute-start(f32[36,384]{1,0:T(8,128)S(1)} %constant_dynamic-slice_fusion), channel_id=1, source_target_pairs={{0,8},{2,10},{4,12},{6,14},{8,0},{10,2},{12,4},{14,6},{1,9},{3,11}... | collective-permute-start | bytes 165896 | tf_op jit(solution)/shard_map/ppermute | solution.py:95
  131.8 2.6 %collective-permute-start.14 = (f32[96,768]{1,0:T(8,128)}, f32[96,768]{1,0:T(8,128)}, u32[]{:S(2)}, u32[]{:S(2)}) collective-permute-start(f32[96,768]{1,0:T(8,128)} %slice_add_fusion.5), channel_id=1, source_target_pairs={{0,2},{4,0},{8,4},{12,8},{14,12},{10,14},{6,10},{2,6},{1,3},{5,1},... | collective-permute-start | bytes 884744 | tf_op jit(solution)/shard_map/ppermute | solution.py:183
  136.9 6.1 %collective-permute-done.23 = f32[36,384]{1,0:T(8,128)S(1)} collective-permute-done((f32[36,384]{1,0:T(8,128)S(1)}, f32[36,384]{1,0:T(8,128)S(1)}, u32[]{:S(2)}, u32[]{:S(2)}) %collective-permute-start.23) | collective-permute-done | bytes 55328 | tf_op jit(solution)/shard_map/ppermute | solution.py:95
  150.3 4.5 %collective-permute-done.8 = f32[96,768]{1,0:T(8,128)S(1)} collective-permute-done((f32[96,768]{1,0:T(8,128)S(1)}, f32[96,768]{1,0:T(8,128)S(1)}, u32[]{:S(2)}, u32[]{:S(2)}) %collective-permute-start.8) | collective-permute-done | bytes 294944 | tf_op jit(solution)/shard_map/ppermute | solution.py:182
  160.1 2.6 %collective-permute-done.9 = f32[96,768]{1,0:T(8,128)S(1)} collective-permute-done((f32[96,768]{1,0:T(8,128)S(1)}, f32[96,768]{1,0:T(8,128)S(1)}, u32[]{:S(2)}, u32[]{:S(2)}) %collective-permute-start.9) | collective-permute-done | bytes 294944 | tf_op jit(solution)/shard_map/ppermute | solution.py:182
  165.6 4.7 %collective-permute-done.10 = f32[96,768]{1,0:T(8,128)S(1)} collective-permute-done((f32[96,768]{1,0:T(8,128)S(1)}, f32[96,768]{1,0:T(8,128)S(1)}, u32[]{:S(2)}, u32[]{:S(2)}) %collective-permute-start.10) | collective-permute-done | bytes 294944 | tf_op jit(solution)/shard_map/ppermute | solution.py:182
  173.6 5.5 %collective-permute-done.11 = f32[96,768]{1,0:T(8,128)S(1)} collective-permute-done((f32[96,768]{1,0:T(8,128)S(1)}, f32[96,768]{1,0:T(8,128)S(1)}, u32[]{:S(2)}, u32[]{:S(2)}) %collective-permute-start.11) | collective-permute-done | bytes 294944 | tf_op jit(solution)/shard_map/ppermute | solution.py:182
  (204 shorter events, 69.1 us)
Async XLA Ops:
  4.3 22.0 %collective-permute-start = (bf16[1,64,1536]{1,2,0:T(8,128)(2,1)}, bf16[1,64,1536]{1,2,0:T(8,128)(2,1)S(1)}, u32[]{:S(2)}, u32[]{:S(2)}) collective-permute-start(bf16[1,64,1536]{1,2,0:T(8,128)(2,1)} %get-tuple-element.46), channel_id=1, source_target_pairs={{0,2},{2,4},{4,6},{6,8},{8,10},{10,12},{12,14},{1,3},{3,5},{5,7},{... | collective-permute-start | bytes 589832 | tf_op jit(solution)/shard_map/ppermute | solution.py:21
  9.2 17.8 %collective-permute-start.1 = (bf16[1,64,1536]{1,2,0:T(8,128)(2,1)S(1)}, bf16[1,64,1536]{1,2,0:T(8,128)(2,1)}, u32[]{:S(2)}, u32[]{:S(2)}) collective-permute-start(bf16[1,64,1536]{1,2,0:T(8,128)(2,1)S(1)} %get-tuple-element.47), channel_id=1, source_target_pairs={{2,0},{4,2},{6,4},{8,6},{10,8},{12,10},{14,12},{3,1},{5,3},{7,5},{... | collective-permute-start | bytes 589832 | tf_op jit(solution)/shard_map/ppermute | solution.py:23
  43.2 22.3 %collective-permute-start.2 = (f32[8,96,1536]{2,1,0:T(8,128)}, f32[8,96,1536]{2,1,0:T(8,128)}, u32[]{:S(2)}, u32[]{:S(2)}) collective-permute-start(f32[8,96,1536]{2,1,0:T(8,128)} %bitcast.26), channel_id=1, source_target_pairs={{0,1},{1,0},{2,3},{3,2},{4,5},{5,4},{6,7},{7,6},{8,9},{9,8},{10,11... | collective-permute-start | bytes 14155784 | tf_op jit(solution)/shard_map/ppermute | solution.py:95
  77.7 35.6 %collective-permute-start.19 = (f32[72,1536]{1,0:T(8,128)}, f32[72,1536]{1,0:T(8,128)S(1)}, u32[]{:S(2)}, u32[]{:S(2)}) collective-permute-start(f32[72,1536]{1,0:T(8,128)} %constant_dynamic-slice_fusion.3), channel_id=1, source_target_pairs={{0,1},{1,0},{2,3},{3,2},{4,5},{5,4},{6,7},{7,6},{8,9},{9,8},{10,11... | collective-permute-start | bytes 1327112 | tf_op jit(solution)/shard_map/ppermute | solution.py:95
  78.2 22.2 %collective-permute-start.3 = (bf16[1,64,1536]{1,2,0:T(8,128)(2,1)S(1)}, bf16[1,64,1536]{1,2,0:T(8,128)(2,1)S(1)}, u32[]{:S(2)}, u32[]{:S(2)}) collective-permute-start(bf16[1,64,1536]{1,2,0:T(8,128)(2,1)S(1)} %get-tuple-element.42), channel_id=1, source_target_pairs={{0,2},{2,4},{4,6},{6,8},{8,10},{10,12},{12,14},{1,3},{3,5},{5,7},{... | collective-permute-start | bytes 589832 | tf_op jit(solution)/shard_map/ppermute | solution.py:21
  82.5 17.9 %collective-permute-start.4 = (bf16[1,64,1536]{1,2,0:T(8,128)(2,1)S(1)}, bf16[1,64,1536]{1,2,0:T(8,128)(2,1)S(1)}, u32[]{:S(2)}, u32[]{:S(2)}) collective-permute-start(bf16[1,64,1536]{1,2,0:T(8,128)(2,1)S(1)} %get-tuple-element.43), channel_id=1, source_target_pairs={{2,0},{4,2},{6,4},{8,6},{10,8},{12,10},{14,12},{3,1},{5,3},{7,5},{... | collective-permute-start | bytes 589832 | tf_op jit(solution)/shard_map/ppermute | solution.py:23
  87.7 21.5 %collective-permute-start.5 = (f32[96,768]{1,0:T(8,128)}, f32[96,768]{1,0:T(8,128)}, u32[]{:S(2)}, u32[]{:S(2)}) collective-permute-start(f32[96,768]{1,0:T(8,128)} %slice.312), channel_id=1, source_target_pairs={{0,4},{4,8},{8,12},{12,14},{14,10},{10,6},{6,2},{2,0},{1,5},{5,9},... | collective-permute-start | bytes 884744 | tf_op jit(solution)/shard_map/ppermute | solution.py:182
  92.3 21.1 %collective-permute-start.12 = (f32[96,768]{1,0:T(8,128)}, f32[96,768]{1,0:T(8,128)}, u32[]{:S(2)}, u32[]{:S(2)}) collective-permute-start(f32[96,768]{1,0:T(8,128)} %slice.320), channel_id=1, source_target_pairs={{0,2},{4,0},{8,4},{12,8},{14,12},{10,14},{6,10},{2,6},{1,3},{5,1},... | collective-permute-start | bytes 884744 | tf_op jit(solution)/shard_map/ppermute | solution.py:183
  110.5 12.8 %collective-permute-start.6 = (f32[96,768]{1,0:T(8,128)S(1)}, f32[96,768]{1,0:T(8,128)S(1)}, u32[]{:S(2)}, u32[]{:S(2)}) collective-permute-start(f32[96,768]{1,0:T(8,128)S(1)} %slice_add_fusion.13), channel_id=1, source_target_pairs={{0,4},{4,8},{8,12},{12,14},{14,10},{10,6},{6,2},{2,0},{1,5},{5,9},... | collective-permute-start | bytes 884744 | tf_op jit(solution)/shard_map/ppermute | solution.py:182
  113.3 9.8 %collective-permute-start.20 = (f32[72,768]{1,0:T(8,128)S(1)}, f32[72,768]{1,0:T(8,128)S(1)}, u32[]{:S(2)}, u32[]{:S(2)}) collective-permute-start(f32[72,768]{1,0:T(8,128)S(1)} %constant_dynamic-slice_fusion.2), channel_id=1, source_target_pairs={{0,2},{2,0},{4,6},{6,4},{8,10},{10,8},{12,14},{14,12},{1,3},{3,1},... | collective-permute-start | bytes 663560 | tf_op jit(solution)/shard_map/ppermute | solution.py:95
  114.5 16.6 %collective-permute-start.13 = (f32[96,768]{1,0:T(8,128)S(1)}, f32[96,768]{1,0:T(8,128)S(1)}, u32[]{:S(2)}, u32[]{:S(2)}) collective-permute-start(f32[96,768]{1,0:T(8,128)S(1)} %slice_add_fusion.6), channel_id=1, source_target_pairs={{0,2},{4,0},{8,4},{12,8},{14,12},{10,14},{6,10},{2,6},{1,3},{5,1},... | collective-permute-start | bytes 884744 | tf_op jit(solution)/shard_map/ppermute | solution.py:183
  123.3 20.1 %collective-permute-start.7 = (f32[96,768]{1,0:T(8,128)S(1)}, f32[96,768]{1,0:T(8,128)}, u32[]{:S(2)}, u32[]{:S(2)}) collective-permute-start(f32[96,768]{1,0:T(8,128)S(1)} %slice_add_fusion.12), channel_id=1, source_target_pairs={{0,4},{4,8},{8,12},{12,14},{14,10},{10,6},{6,2},{2,0},{1,5},{5,9},... | collective-permute-start | bytes 884744 | tf_op jit(solution)/shard_map/ppermute | solution.py:182
  128.0 6.4 %collective-permute-start.22 = (f32[36,384]{1,0:T(8,128)S(1)}, f32[36,384]{1,0:T(8,128)S(1)}, u32[]{:S(2)}, u32[]{:S(2)}) collective-permute-start(f32[36,384]{1,0:T(8,128)S(1)} %constant_dynamic-slice_fusion), channel_id=1, source_target_pairs={{0,8},{2,10},{4,12},{6,14},{8,0},{10,2},{12,4},{14,6},{1,9},{3,11}... | collective-permute-start | bytes 165896 | tf_op jit(solution)/shard_map/ppermute | solution.py:95
  131.8 14.7 %collective-permute-start.14 = (f32[96,768]{1,0:T(8,128)}, f32[96,768]{1,0:T(8,128)}, u32[]{:S(2)}, u32[]{:S(2)}) collective-permute-start(f32[96,768]{1,0:T(8,128)} %slice_add_fusion.5), channel_id=1, source_target_pairs={{0,2},{4,0},{8,4},{12,8},{14,12},{10,14},{6,10},{2,6},{1,3},{5,1},... | collective-permute-start | bytes 884744 | tf_op jit(solution)/shard_map/ppermute | solution.py:183
  134.5 8.5 %collective-permute-start.23 = (f32[36,384]{1,0:T(8,128)S(1)}, f32[36,384]{1,0:T(8,128)S(1)}, u32[]{:S(2)}, u32[]{:S(2)}) collective-permute-start(f32[36,384]{1,0:T(8,128)S(1)} %dynamic-slice_add_fusion.3), channel_id=1, source_target_pairs={{0,8},{2,10},{4,12},{6,14},{8,0},{10,2},{12,4},{14,6},{1,9},{3,11}... | collective-permute-start | bytes 165896 | tf_op jit(solution)/shard_map/ppermute | solution.py:95
  144.5 10.3 %collective-permute-start.8 = (f32[96,768]{1,0:T(8,128)S(1)}, f32[96,768]{1,0:T(8,128)S(1)}, u32[]{:S(2)}, u32[]{:S(2)}) collective-permute-start(f32[96,768]{1,0:T(8,128)S(1)} %slice_add_fusion.11), channel_id=1, source_target_pairs={{0,4},{4,8},{8,12},{12,14},{14,10},{10,6},{6,2},{2,0},{1,5},{5,9},... | collective-permute-start | bytes 884744 | tf_op jit(solution)/shard_map/ppermute | solution.py:182
  147.5 8.9 %collective-permute-start.15 = (f32[96,768]{1,0:T(8,128)S(1)}, f32[96,768]{1,0:T(8,128)S(1)}, u32[]{:S(2)}, u32[]{:S(2)}) collective-permute-start(f32[96,768]{1,0:T(8,128)S(1)} %slice_add_fusion.4), channel_id=1, source_target_pairs={{0,2},{4,0},{8,4},{12,8},{14,12},{10,14},{6,10},{2,6},{1,3},{5,1},... | collective-permute-start | bytes 884744 | tf_op jit(solution)/shard_map/ppermute | solution.py:183
  149.4 10.5 %collective-permute-start.25 = (f32[72,768]{1,0:T(8,128)S(1)}, f32[72,768]{1,0:T(8,128)S(1)}, u32[]{:S(2)}, u32[]{:S(2)}) collective-permute-start(f32[72,768]{1,0:T(8,128)S(1)} %constant_dynamic-update-slice_fusion.4), channel_id=1, source_target_pairs={{0,2},{2,0},{4,6},{6,4},{8,10},{10,8},{12,14},{14,12},{1,3},{3,1},... | collective-permute-start | bytes 663560 | tf_op jit(solution)/shard_map/ppermute | solution.py:95
  154.8 7.9 %collective-permute-start.9 = (f32[96,768]{1,0:T(8,128)S(1)}, f32[96,768]{1,0:T(8,128)S(1)}, u32[]{:S(2)}, u32[]{:S(2)}) collective-permute-start(f32[96,768]{1,0:T(8,128)S(1)} %slice_add_fusion.10), channel_id=1, source_target_pairs={{0,4},{4,8},{8,12},{12,14},{14,10},{10,6},{6,2},{2,0},{1,5},{5,9},... | collective-permute-start | bytes 884744 | tf_op jit(solution)/shard_map/ppermute | solution.py:182
  156.4 6.8 %collective-permute-start.16 = (f32[96,768]{1,0:T(8,128)S(1)}, f32[96,768]{1,0:T(8,128)S(1)}, u32[]{:S(2)}, u32[]{:S(2)}) collective-permute-start(f32[96,768]{1,0:T(8,128)S(1)} %slice_add_fusion.3), channel_id=1, source_target_pairs={{0,2},{4,0},{8,4},{12,8},{14,12},{10,14},{6,10},{2,6},{1,3},{5,1},... | collective-permute-start | bytes 884744 | tf_op jit(solution)/shard_map/ppermute | solution.py:183
  162.7 7.7 %collective-permute-start.10 = (f32[96,768]{1,0:T(8,128)S(1)}, f32[96,768]{1,0:T(8,128)S(1)}, u32[]{:S(2)}, u32[]{:S(2)}) collective-permute-start(f32[96,768]{1,0:T(8,128)S(1)} %slice_add_fusion.9), channel_id=1, source_target_pairs={{0,4},{4,8},{8,12},{12,14},{14,10},{10,6},{6,2},{2,0},{1,5},{5,9},... | collective-permute-start | bytes 884744 | tf_op jit(solution)/shard_map/ppermute | solution.py:182
  163.2 7.2 %collective-permute-start.17 = (f32[96,768]{1,0:T(8,128)S(1)}, f32[96,768]{1,0:T(8,128)S(1)}, u32[]{:S(2)}, u32[]{:S(2)}) collective-permute-start(f32[96,768]{1,0:T(8,128)S(1)} %slice_add_fusion.2), channel_id=1, source_target_pairs={{0,2},{4,0},{8,4},{12,8},{14,12},{10,14},{6,10},{2,6},{1,3},{5,1},... | collective-permute-start | bytes 884744 | tf_op jit(solution)/shard_map/ppermute | solution.py:183
  170.4 8.7 %collective-permute-start.11 = (f32[96,768]{1,0:T(8,128)S(1)}, f32[96,768]{1,0:T(8,128)S(1)}, u32[]{:S(2)}, u32[]{:S(2)}) collective-permute-start(f32[96,768]{1,0:T(8,128)S(1)} %slice_add_fusion.8), channel_id=1, source_target_pairs={{0,4},{4,8},{8,12},{12,14},{14,10},{10,6},{6,2},{2,0},{1,5},{5,9},... | collective-permute-start | bytes 884744 | tf_op jit(solution)/shard_map/ppermute | solution.py:182
  170.5 8.6 %collective-permute-start.18 = (f32[96,768]{1,0:T(8,128)S(1)}, f32[96,768]{1,0:T(8,128)S(1)}, u32[]{:S(2)}, u32[]{:S(2)}) collective-permute-start(f32[96,768]{1,0:T(8,128)S(1)} %slice_add_fusion.1), channel_id=1, source_target_pairs={{0,2},{4,0},{8,4},{12,8},{14,12},{10,14},{6,10},{2,6},{1,3},{5,1},... | collective-permute-start | bytes 884744 | tf_op jit(solution)/shard_map/ppermute | solution.py:183
  (36 other events, 292.2 us)

commit v20 on v18

--- a/solution.py
+++ b/solution.py
@@ -219,9 +219,13 @@
     positions = seq_index * local_bins + jnp.arange(local_bins, dtype=jnp.int32)
     mask = (positions[None, :] < lengths[:, None]).astype(jnp.float32)
     mask3 = mask[:, :, None]
-    masked_input = (inputs.astype(jnp.float32) * mask3).astype(jnp.bfloat16)
     scale = 1.0 / math.sqrt(rep_count * seq_count * local_bins)
-    padded_input = with_halo(masked_input, (("seq", 1),), DILATION_STEP)
+    spots = seq_index * local_bins - DILATION_STEP + jnp.arange(
+        local_bins + 2 * DILATION_STEP, dtype=jnp.int32
+    )
+    pad_mask = (spots[None, :] < lengths[:, None]).astype(jnp.float32)[:, :, None]
+    padded_input = with_halo(inputs, (("seq", 1),), DILATION_STEP)
+    padded_input = (padded_input.astype(jnp.float32) * pad_mask).astype(jnp.bfloat16)
     dense = dense_weight(conv_weight)
     pre = conv_taps(padded_input, dense, local_bins)
     act_val, slope = gelu_pair(pre)

time: 155 us -> 157 us (1.013)
  waiting for transfers between devices: 51 us -> 41.1 us
  local copies, waits for them, and re-layouts: 6.29 us -> 14.2 us
  other arithmetic: 19.3 us -> 24.7 us
  matrix products: 32.7 us -> 31 us
    ppermute x2, waiting for transfers between devices: 13.2 us -> 7.4 us  [with_halo(): lax.ppermute(tail, axis, [(i, (i + 1) % count) for i in range(ends)])]
    ppermute x7, starting transfers between devices: 11.5 us -> 6.42 us  [ring_reduce_scatter(): behind = lax.ppermute(behind, 'seq', backward) + block(2 + step, False)]
    unnamed x50 -> x66, local copies, waits for them, and re-layouts: 0.66 us -> 5.4 us
    ppermute x9, waiting for transfers between devices: 18.5 us -> 14.7 us  [swap(): return lax.ppermute(value, axis, [(i, i ^ distance) for i in range(count)])]
    ppermute x9, starting transfers between devices: 7.29 us -> 10.1 us  [swap(): return lax.ppermute(value, axis, [(i, i ^ distance) for i in range(count)])]
    ppermute x7, starting transfers between devices: 12.4 us -> 15.2 us  [ring_reduce_scatter(): ahead = lax.ppermute(ahead, 'seq', forward) + block(-2 - step, True)]
    ppermute x7, waiting for transfers between devices: 1.83 us -> 3.81 us  [ring_reduce_scatter(): behind = lax.ppermute(behind, 'seq', backward) + block(2 + step, False)]
    ppermute x7, waiting for transfers between devices: 17.1 us -> 15.2 us  [ring_reduce_scatter(): ahead = lax.ppermute(ahead, 'seq', forward) + block(-2 - step, True)]
  transfers between devices with their start and end apart: 27 -> 27, of which waited for: 14 -> 13; matrix products, arithmetic and copies ran while one was open for 19% -> 25% of each run, Pallas kernels for 0% -> 0%
where the time goes in v20:
time: 157 us
  starting transfers between devices  43.7 us (28%)
  waiting for transfers between devices  41.1 us (26%)
  matrix products  31 us (20%)
  other arithmetic  24.7 us (16%)
  local copies, waits for them, and re-layouts  14.2 us (9%)
  between operations  2.27 us (1%)
    ppermute x7, waiting for transfers between devices, ring_reduce_scatter(): ahead = lax.ppermute(ahead, 'seq', forward) + block(-2 - step, True)  15.2 us
    ppermute x7, starting transfers between devices, ring_reduce_scatter(): ahead = lax.ppermute(ahead, 'seq', forward) + block(-2 - step, True)  15.2 us
    ppermute x9, waiting for transfers between devices, swap(): return lax.ppermute(value, axis, [(i, i ^ distance) for i in range(count)])  14.7 us
    ppermute x9, starting transfers between devices, swap(): return lax.ppermute(value, axis, [(i, i ^ distance) for i in range(count)])  10.1 us
    dot_general x24, matrix products, conv_taps(): lax.dot_general(window, dense[k, :, cols], dims, preferred_element_type=j...  9.78 us
    ppermute x2, starting transfers between devices, with_halo(): lax.ppermute(tail, axis, [(i, (i + 1) % count) for i in range(ends)])  9.46 us
    ppermute x2, waiting for transfers between devices, with_halo(): lax.ppermute(tail, axis, [(i, (i + 1) % count) for i in range(ends)])  7.4 us
    ppermute x7, starting transfers between devices, ring_reduce_scatter(): behind = lax.ppermute(behind, 'seq', backward) + block(2 + step, False)  6.42 us
  transfers between devices with their start and end apart: 27, of which 13 were waited for; matrix products, arithmetic and copies ran while one was open for 25% of the time, Pallas kernels for 0%

profile of v20, /device:TPU:0, one launch (start us, length us, event | category | flops | bytes accessed | tf_op | source)
XLA Modules:
  0.0 157.0 jit_solution(13724078509512743907)
XLA Ops:
  1.7 4.9 %collective-permute-start = (bf16[1,64,1536]{2,1,0:T(8,128)(2,1)S(1)}, bf16[1,64,1536]{2,1,0:T(8,128)(2,1)S(1)}, u32[]{:S(2)}, u32[]{:S(2)}) collective-permute-start(bf16[1,64,1536]{2,1,0:T(8,128)(2,1)S(1)} %get-tuple-element.44), channel_id=1, source_target_pairs={{0,2},{2,4},{4,6},{6,8},{8,10},{10,12},{12,14},{1,3},{3,5},{5,7},{... | collective-permute-start | bytes 589832 | tf_op jit(solution)/shard_map/ppermute | solution.py:21
  11.7 3.1 %bitcast_multiply_fusion = bf16[3,384,1536]{2,1,0:T(8,128)(2,1)} fusion(bf16[384,1536]{1,0:T(8,128)(2,1)S(1)} %fusion.13, bf16[3,48,1536]{2,1,0:T(8,128)(2,1)} %param.7), kind=kLoop, calls=%fused_computation.7 | loop fusion | flops 1769472 | bytes 5160960 | tf_op jit(solution)/shard_map/mul | solution.py:49
  15.6 1.8 %multiply_convert_fusion = bf16[640,1536]{1,0:T(8,128)(2,1)S(1)} fusion(bf16[64,1536]{1,0:T(8,128)(2,1)} %bitcast.172, bf16[512,1536]{1,0:T(8,128)(2,1)S(1)} %bitcast.157, bf16[64,1536]{1,0:T(8,128)(2,1)} %bitcast.171, f32[640]{0:T(1024)S(1)} %fusion.110), kind=kLoop, calls=%fused_computation.6 | loop fusion | flops 7864320 | bytes 3934720 | tf_op jit(solution)/shard_map/convert_element_type | solution.py:228
  25.3 3.5 %convolution_multiply_fusion = f32[768,1536]{1,0:T(8,128)} fusion(bf16[512,768]{0,1:T(8,128)(2,1)S(1)} %bitcast.156, bf16[1,512,1536]{2,1,0:T(8,128)(2,1)S(1)} %copy-done.2), kind=kOutput, calls=%fused_computation.4 | convolution fusion | flops 1209139200 | bytes 7077888 | tf_op jit(solution)/shard_map/dot_general | solution.py:191
  30.5 2.7 %convolution_multiply_fusion.1 = f32[768,1536]{1,0:T(8,128)S(1)} fusion(bf16[512,768]{0,1:T(8,128)(2,1)} %bitcast.155, bf16[1,512,1536]{2,1,0:T(8,128)(2,1)S(1)} %copy-done.2), kind=kOutput, calls=%fused_computation.5 | convolution fusion | flops 1209139200 | bytes 7077888 | tf_op jit(solution)/shard_map/dot_general | solution.py:191
  33.2 6.2 %fusion.8 = bf16[1,512,1536]{2,1,0:T(8,128)(2,1)} fusion(bf16[1536,1536]{1,0:T(8,128)(2,1)} %param.8, bf16[1,512,1536]{2,1,0:T(8,128)(2,1)S(1)} %copy-done.13, f32[512]{0:T(512)S(1)} %fusion.113, f32[512,384]{0,1:T(8,128)S(1)} %copy-done.11, f32[512,384]{0,1:T(8,128)S(1)} %copy-done.9, f32[512,384]{0,1:T(8,128)S(1)} %copy-done.7, f32[512,384]{0,1:T(8,128)S(1)} %copy-done.5), kind=kOutput, calls=%fused_computation.25 | convolution fusion | flops 2425356288 | bytes 11012096 | tf_op jit(solution)/shard_map/dot_general | solution.py:235
  39.5 3.3 %add.502 = f32[8,96,1536]{2,1,0:T(8,128)S(1)} add(f32[8,96,1536]{2,1,0:T(8,128)S(1)} %bitcast.146, f32[8,96,1536]{2,1,0:T(8,128)} %collective-permute-done.2) | non-fusion elementwise | flops 1179648 | bytes 14155776 | tf_op jit(solution)/shard_map/add | solution.py:208
  42.8 3.9 %fusion.9 = bf16[512,1536]{0,1:T(8,128)(2,1)S(1)} fusion(bf16[512,1536]{1,0:T(8,128)(2,1)S(1)} %bitcast.147, bf16[1536,1536]{1,0:T(8,128)(2,1)S(1)} %bitcast.174, f32[512]{0:T(512)S(1)} %fusion.113, f32[512,384]{0,1:T(8,128)S(1)} %copy-done.11, f32[512,384]{0,1:T(8,128)S(1)} %copy-done.9, f32[512,384]{0,1:T(8,128)S(1)} %copy-done.7, ...), kind=kOutput, calls=%fused_computation.26 | convolution fusion | flops 2426929152 | bytes 11012096 | tf_op jit(solution)/shard_map/dot_general | solution.py:238
  54.3 4.6 %collective-permute-start.3 = (bf16[1,64,1536]{1,2,0:T(8,128)(2,1)S(1)}, bf16[1,64,1536]{1,2,0:T(8,128)(2,1)S(1)}, u32[]{:S(2)}, u32[]{:S(2)}) collective-permute-start(bf16[1,64,1536]{1,2,0:T(8,128)(2,1)S(1)} %get-tuple-element.40), channel_id=1, source_target_pairs={{0,2},{2,4},{4,6},{6,8},{8,10},{10,12},{12,14},{1,3},{3,5},{5,7},{... | collective-permute-start | bytes 589832 | tf_op jit(solution)/shard_map/ppermute | solution.py:21
  60.2 3.2 %dynamic-slice_bitcast_fusion.8 = (f32[96,1536]{1,0:T(8,128)}, f32[96,1536]{1,0:T(8,128)S(1)}, f32[96,1536]{1,0:T(8,128)}, f32[96,1536]{1,0:T(8,128)}, f32[96,15...) fusion(f32[8,96,1536]{2,1,0:T(8,128)S(1)} %add.502, ...), kind=kLoop, calls=%fused_computation.78 | loop fusion | bytes 18874432 | tf_op jit(solution)/shard_map/jit(dynamic_index_in_dim)/squeeze | solution.py:176
  64.1 4.5 %collective-permute-start.5 = (f32[96,768]{1,0:T(8,128)}, f32[96,768]{1,0:T(8,128)}, u32[]{:S(2)}, u32[]{:S(2)}) collective-permute-start(f32[96,768]{1,0:T(8,128)} %slice.310), channel_id=1, source_target_pairs={{0,4},{4,8},{8,12},{12,14},{14,10},{10,6},{6,2},{2,0},{1,5},{5,9},... | collective-permute-start | bytes 884744 | tf_op jit(solution)/shard_map/ppermute | solution.py:182
  69.4 7.4 %collective-permute-done.3 = bf16[1,64,1536]{1,2,0:T(8,128)(2,1)S(1)} collective-permute-done((bf16[1,64,1536]{1,2,0:T(8,128)(2,1)S(1)}, bf16[1,64,1536]{1,2,0:T(8,128)(2,1)S(1)}, u32[]{:S(2)}, u32[]{:S(2)}) %collective-permute-start.3) | collective-permute-done | bytes 196640 | tf_op jit(solution)/shard_map/ppermute | solution.py:21
  87.1 3.4 %collective-permute-start.6 = (f32[96,768]{1,0:T(8,128)S(1)}, f32[96,768]{1,0:T(8,128)S(1)}, u32[]{:S(2)}, u32[]{:S(2)}) collective-permute-start(f32[96,768]{1,0:T(8,128)S(1)} %slice_add_fusion.13), channel_id=1, source_target_pairs={{0,4},{4,8},{8,12},{12,14},{14,10},{10,6},{6,2},{2,0},{1,5},{5,9},... | collective-permute-start | bytes 884744 | tf_op jit(solution)/shard_map/ppermute | solution.py:182
  92.8 2.0 %collective-permute-start.13 = (f32[96,768]{1,0:T(8,128)S(1)}, f32[96,768]{1,0:T(8,128)S(1)}, u32[]{:S(2)}, u32[]{:S(2)}) collective-permute-start(f32[96,768]{1,0:T(8,128)S(1)} %slice_add_fusion.6), channel_id=1, source_target_pairs={{0,2},{4,0},{8,4},{12,8},{14,12},{10,14},{6,10},{2,6},{1,3},{5,1},... | collective-permute-start | bytes 884744 | tf_op jit(solution)/shard_map/ppermute | solution.py:183
  94.8 4.9 %collective-permute-done.20 = f32[72,768]{1,0:T(8,128)S(1)} collective-permute-done((f32[72,768]{1,0:T(8,128)S(1)}, f32[72,768]{1,0:T(8,128)S(1)}, u32[]{:S(2)}, u32[]{:S(2)}) %collective-permute-start.20) | collective-permute-done | bytes 221216 | tf_op jit(solution)/shard_map/ppermute | solution.py:95
  102.7 1.9 %collective-permute-done.21 = f32[72,384]{1,0:T(8,128)S(1)} collective-permute-done((f32[72,384]{1,0:T(8,128)S(1)}, f32[72,384]{1,0:T(8,128)S(1)}, u32[]{:S(2)}, u32[]{:S(2)}) %collective-permute-start.21) | collective-permute-done | bytes 110624 | tf_op jit(solution)/shard_map/ppermute | solution.py:95
  104.6 3.7 %collective-permute-start.22 = (f32[36,384]{1,0:T(8,128)S(1)}, f32[36,384]{1,0:T(8,128)S(1)}, u32[]{:S(2)}, u32[]{:S(2)}) collective-permute-start(f32[36,384]{1,0:T(8,128)S(1)} %constant_dynamic-slice_fusion), channel_id=1, source_target_pairs={{0,8},{2,10},{4,12},{6,14},{8,0},{10,2},{12,4},{14,6},{1,9},{3,11}... | collective-permute-start | bytes 165896 | tf_op jit(solution)/shard_map/ppermute | solution.py:95
  110.8 3.2 %collective-permute-start.23 = (f32[36,384]{1,0:T(8,128)S(1)}, f32[36,384]{1,0:T(8,128)S(1)}, u32[]{:S(2)}, u32[]{:S(2)}) collective-permute-start(f32[36,384]{1,0:T(8,128)S(1)} %dynamic-slice_add_fusion.3), channel_id=1, source_target_pairs={{0,8},{2,10},{4,12},{6,14},{8,0},{10,2},{12,4},{14,6},{1,9},{3,11}... | collective-permute-start | bytes 165896 | tf_op jit(solution)/shard_map/ppermute | solution.py:95
  114.6 6.0 %collective-permute-done.23 = f32[36,384]{1,0:T(8,128)S(1)} collective-permute-done((f32[36,384]{1,0:T(8,128)S(1)}, f32[36,384]{1,0:T(8,128)S(1)}, u32[]{:S(2)}, u32[]{:S(2)}) %collective-permute-start.23) | collective-permute-done | bytes 55328 | tf_op jit(solution)/shard_map/ppermute | solution.py:95
  128.3 4.2 %collective-permute-done.8 = f32[96,768]{1,0:T(8,128)S(1)} collective-permute-done((f32[96,768]{1,0:T(8,128)S(1)}, f32[96,768]{1,0:T(8,128)S(1)}, u32[]{:S(2)}, u32[]{:S(2)}) %collective-permute-start.8) | collective-permute-done | bytes 294944 | tf_op jit(solution)/shard_map/ppermute | solution.py:182
  136.5 2.8 %collective-permute-done.9 = f32[96,768]{1,0:T(8,128)S(1)} collective-permute-done((f32[96,768]{1,0:T(8,128)S(1)}, f32[96,768]{1,0:T(8,128)S(1)}, u32[]{:S(2)}, u32[]{:S(2)}) %collective-permute-start.9) | collective-permute-done | bytes 294944 | tf_op jit(solution)/shard_map/ppermute | solution.py:182
  142.4 4.4 %collective-permute-done.10 = f32[96,768]{1,0:T(8,128)S(1)} collective-permute-done((f32[96,768]{1,0:T(8,128)S(1)}, f32[96,768]{1,0:T(8,128)S(1)}, u32[]{:S(2)}, u32[]{:S(2)}) %collective-permute-start.10) | collective-permute-done | bytes 294944 | tf_op jit(solution)/shard_map/ppermute | solution.py:182
  150.2 3.9 %collective-permute-done.11 = f32[96,768]{1,0:T(8,128)S(1)} collective-permute-done((f32[96,768]{1,0:T(8,128)S(1)}, f32[96,768]{1,0:T(8,128)S(1)}, u32[]{:S(2)}, u32[]{:S(2)}) %collective-permute-start.11) | collective-permute-done | bytes 294944 | tf_op jit(solution)/shard_map/ppermute | solution.py:182
  154.1 1.9 %collective-permute-done.18 = f32[96,768]{1,0:T(8,128)S(1)} collective-permute-done((f32[96,768]{1,0:T(8,128)S(1)}, f32[96,768]{1,0:T(8,128)S(1)}, u32[]{:S(2)}, u32[]{:S(2)}) %collective-permute-start.18) | collective-permute-done | bytes 294944 | tf_op jit(solution)/shard_map/ppermute | solution.py:183
  (200 shorter events, 63.3 us)
Async XLA Ops:
  1.7 13.2 %collective-permute-start = (bf16[1,64,1536]{2,1,0:T(8,128)(2,1)S(1)}, bf16[1,64,1536]{2,1,0:T(8,128)(2,1)S(1)}, u32[]{:S(2)}, u32[]{:S(2)}) collective-permute-start(bf16[1,64,1536]{2,1,0:T(8,128)(2,1)S(1)} %get-tuple-element.44), channel_id=1, source_target_pairs={{0,2},{2,4},{4,6},{6,8},{8,10},{10,12},{12,14},{1,3},{3,5},{5,7},{... | collective-permute-start | bytes 589832 | tf_op jit(solution)/shard_map/ppermute | solution.py:21
  6.6 8.3 %collective-permute-start.1 = (bf16[1,64,1536]{2,1,0:T(8,128)(2,1)S(1)}, bf16[1,64,1536]{2,1,0:T(8,128)(2,1)S(1)}, u32[]{:S(2)}, u32[]{:S(2)}) collective-permute-start(bf16[1,64,1536]{2,1,0:T(8,128)(2,1)S(1)} %get-tuple-element.45), channel_id=1, source_target_pairs={{2,0},{4,2},{6,4},{8,6},{10,8},{12,10},{14,12},{3,1},{5,3},{7,5},{... | collective-permute-start | bytes 589832 | tf_op jit(solution)/shard_map/ppermute | solution.py:23
  28.8 10.7 %collective-permute-start.2 = (f32[8,96,1536]{2,1,0:T(8,128)}, f32[8,96,1536]{2,1,0:T(8,128)}, u32[]{:S(2)}, u32[]{:S(2)}) collective-permute-start(f32[8,96,1536]{2,1,0:T(8,128)} %bitcast.27), channel_id=1, source_target_pairs={{0,1},{1,0},{2,3},{3,2},{4,5},{5,4},{6,7},{7,6},{8,9},{9,8},{10,11... | collective-permute-start | bytes 14155784 | tf_op jit(solution)/shard_map/ppermute | solution.py:95
  53.6 36.9 %collective-permute-start.19 = (f32[72,1536]{1,0:T(8,128)}, f32[72,1536]{1,0:T(8,128)}, u32[]{:S(2)}, u32[]{:S(2)}) collective-permute-start(f32[72,1536]{1,0:T(8,128)} %constant_dynamic-slice_fusion.3), channel_id=1, source_target_pairs={{0,1},{1,0},{2,3},{3,2},{4,5},{5,4},{6,7},{7,6},{8,9},{9,8},{10,11... | collective-permute-start | bytes 1327112 | tf_op jit(solution)/shard_map/ppermute | solution.py:95
  54.3 22.5 %collective-permute-start.3 = (bf16[1,64,1536]{1,2,0:T(8,128)(2,1)S(1)}, bf16[1,64,1536]{1,2,0:T(8,128)(2,1)S(1)}, u32[]{:S(2)}, u32[]{:S(2)}) collective-permute-start(bf16[1,64,1536]{1,2,0:T(8,128)(2,1)S(1)} %get-tuple-element.40), channel_id=1, source_target_pairs={{0,2},{2,4},{4,6},{6,8},{8,10},{10,12},{12,14},{1,3},{3,5},{5,7},{... | collective-permute-start | bytes 589832 | tf_op jit(solution)/shard_map/ppermute | solution.py:21
  58.9 17.9 %collective-permute-start.4 = (bf16[1,64,1536]{1,2,0:T(8,128)(2,1)S(1)}, bf16[1,64,1536]{1,2,0:T(8,128)(2,1)S(1)}, u32[]{:S(2)}, u32[]{:S(2)}) collective-permute-start(bf16[1,64,1536]{1,2,0:T(8,128)(2,1)S(1)} %get-tuple-element.41), channel_id=1, source_target_pairs={{2,0},{4,2},{6,4},{8,6},{10,8},{12,10},{14,12},{3,1},{5,3},{7,5},{... | collective-permute-start | bytes 589832 | tf_op jit(solution)/shard_map/ppermute | solution.py:23
  64.1 21.8 %collective-permute-start.5 = (f32[96,768]{1,0:T(8,128)}, f32[96,768]{1,0:T(8,128)}, u32[]{:S(2)}, u32[]{:S(2)}) collective-permute-start(f32[96,768]{1,0:T(8,128)} %slice.310), channel_id=1, source_target_pairs={{0,4},{4,8},{8,12},{12,14},{14,10},{10,6},{6,2},{2,0},{1,5},{5,9},... | collective-permute-start | bytes 884744 | tf_op jit(solution)/shard_map/ppermute | solution.py:182
  69.4 22.3 %collective-permute-start.12 = (f32[96,768]{1,0:T(8,128)}, f32[96,768]{1,0:T(8,128)}, u32[]{:S(2)}, u32[]{:S(2)}) collective-permute-start(f32[96,768]{1,0:T(8,128)} %slice.318), channel_id=1, source_target_pairs={{0,2},{4,0},{8,4},{12,8},{14,12},{10,14},{6,10},{2,6},{1,3},{5,1},... | collective-permute-start | bytes 884744 | tf_op jit(solution)/shard_map/ppermute | solution.py:183
  87.1 13.5 %collective-permute-start.6 = (f32[96,768]{1,0:T(8,128)S(1)}, f32[96,768]{1,0:T(8,128)S(1)}, u32[]{:S(2)}, u32[]{:S(2)}) collective-permute-start(f32[96,768]{1,0:T(8,128)S(1)} %slice_add_fusion.13), channel_id=1, source_target_pairs={{0,4},{4,8},{8,12},{12,14},{14,10},{10,6},{6,2},{2,0},{1,5},{5,9},... | collective-permute-start | bytes 884744 | tf_op jit(solution)/shard_map/ppermute | solution.py:182
  91.6 8.1 %collective-permute-start.20 = (f32[72,768]{1,0:T(8,128)S(1)}, f32[72,768]{1,0:T(8,128)S(1)}, u32[]{:S(2)}, u32[]{:S(2)}) collective-permute-start(f32[72,768]{1,0:T(8,128)S(1)} %constant_dynamic-slice_fusion.2), channel_id=1, source_target_pairs={{0,2},{2,0},{4,6},{6,4},{8,10},{10,8},{12,14},{14,12},{1,3},{3,1},... | collective-permute-start | bytes 663560 | tf_op jit(solution)/shard_map/ppermute | solution.py:95
  92.8 15.5 %collective-permute-start.13 = (f32[96,768]{1,0:T(8,128)S(1)}, f32[96,768]{1,0:T(8,128)S(1)}, u32[]{:S(2)}, u32[]{:S(2)}) collective-permute-start(f32[96,768]{1,0:T(8,128)S(1)} %slice_add_fusion.6), channel_id=1, source_target_pairs={{0,2},{4,0},{8,4},{12,8},{14,12},{10,14},{6,10},{2,6},{1,3},{5,1},... | collective-permute-start | bytes 884744 | tf_op jit(solution)/shard_map/ppermute | solution.py:183
  101.3 19.9 %collective-permute-start.7 = (f32[96,768]{1,0:T(8,128)}, f32[96,768]{1,0:T(8,128)}, u32[]{:S(2)}, u32[]{:S(2)}) collective-permute-start(f32[96,768]{1,0:T(8,128)} %slice_add_fusion.12), channel_id=1, source_target_pairs={{0,4},{4,8},{8,12},{12,14},{14,10},{10,6},{6,2},{2,0},{1,5},{5,9},... | collective-permute-start | bytes 884744 | tf_op jit(solution)/shard_map/ppermute | solution.py:182
  104.6 6.1 %collective-permute-start.22 = (f32[36,384]{1,0:T(8,128)S(1)}, f32[36,384]{1,0:T(8,128)S(1)}, u32[]{:S(2)}, u32[]{:S(2)}) collective-permute-start(f32[36,384]{1,0:T(8,128)S(1)} %constant_dynamic-slice_fusion), channel_id=1, source_target_pairs={{0,8},{2,10},{4,12},{6,14},{8,0},{10,2},{12,4},{14,6},{1,9},{3,11}... | collective-permute-start | bytes 165896 | tf_op jit(solution)/shard_map/ppermute | solution.py:95
  109.1 15.0 %collective-permute-start.14 = (f32[96,768]{1,0:T(8,128)}, f32[96,768]{1,0:T(8,128)}, u32[]{:S(2)}, u32[]{:S(2)}) collective-permute-start(f32[96,768]{1,0:T(8,128)} %slice_add_fusion.5), channel_id=1, source_target_pairs={{0,2},{4,0},{8,4},{12,8},{14,12},{10,14},{6,10},{2,6},{1,3},{5,1},... | collective-permute-start | bytes 884744 | tf_op jit(solution)/shard_map/ppermute | solution.py:183
  110.8 9.7 %collective-permute-start.23 = (f32[36,384]{1,0:T(8,128)S(1)}, f32[36,384]{1,0:T(8,128)S(1)}, u32[]{:S(2)}, u32[]{:S(2)}) collective-permute-start(f32[36,384]{1,0:T(8,128)S(1)} %dynamic-slice_add_fusion.3), channel_id=1, source_target_pairs={{0,8},{2,10},{4,12},{6,14},{8,0},{10,2},{12,4},{14,6},{1,9},{3,11}... | collective-permute-start | bytes 165896 | tf_op jit(solution)/shard_map/ppermute | solution.py:95
  122.3 10.2 %collective-permute-start.8 = (f32[96,768]{1,0:T(8,128)S(1)}, f32[96,768]{1,0:T(8,128)S(1)}, u32[]{:S(2)}, u32[]{:S(2)}) collective-permute-start(f32[96,768]{1,0:T(8,128)S(1)} %slice_add_fusion.11), channel_id=1, source_target_pairs={{0,4},{4,8},{8,12},{12,14},{14,10},{10,6},{6,2},{2,0},{1,5},{5,9},... | collective-permute-start | bytes 884744 | tf_op jit(solution)/shard_map/ppermute | solution.py:182
  125.1 8.6 %collective-permute-start.15 = (f32[96,768]{1,0:T(8,128)S(1)}, f32[96,768]{1,0:T(8,128)S(1)}, u32[]{:S(2)}, u32[]{:S(2)}) collective-permute-start(f32[96,768]{1,0:T(8,128)S(1)} %slice_add_fusion.4), channel_id=1, source_target_pairs={{0,2},{4,0},{8,4},{12,8},{14,12},{10,14},{6,10},{2,6},{1,3},{5,1},... | collective-permute-start | bytes 884744 | tf_op jit(solution)/shard_map/ppermute | solution.py:183
  126.9 9.4 %collective-permute-start.25 = (f32[72,768]{1,0:T(8,128)S(1)}, f32[72,768]{1,0:T(8,128)S(1)}, u32[]{:S(2)}, u32[]{:S(2)}) collective-permute-start(f32[72,768]{1,0:T(8,128)S(1)} %constant_dynamic-update-slice_fusion.4), channel_id=1, source_target_pairs={{0,2},{2,0},{4,6},{6,4},{8,10},{10,8},{12,14},{14,12},{1,3},{3,1},... | collective-permute-start | bytes 663560 | tf_op jit(solution)/shard_map/ppermute | solution.py:95
  132.5 6.8 %collective-permute-start.9 = (f32[96,768]{1,0:T(8,128)S(1)}, f32[96,768]{1,0:T(8,128)S(1)}, u32[]{:S(2)}, u32[]{:S(2)}) collective-permute-start(f32[96,768]{1,0:T(8,128)S(1)} %slice_add_fusion.10), channel_id=1, source_target_pairs={{0,4},{4,8},{8,12},{12,14},{14,10},{10,6},{6,2},{2,0},{1,5},{5,9},... | collective-permute-start | bytes 884744 | tf_op jit(solution)/shard_map/ppermute | solution.py:182
  133.8 8.3 %collective-permute-start.16 = (f32[96,768]{1,0:T(8,128)S(1)}, f32[96,768]{1,0:T(8,128)S(1)}, u32[]{:S(2)}, u32[]{:S(2)}) collective-permute-start(f32[96,768]{1,0:T(8,128)S(1)} %slice_add_fusion.3), channel_id=1, source_target_pairs={{0,2},{4,0},{8,4},{12,8},{14,12},{10,14},{6,10},{2,6},{1,3},{5,1},... | collective-permute-start | bytes 884744 | tf_op jit(solution)/shard_map/ppermute | solution.py:183
  139.3 7.4 %collective-permute-start.10 = (f32[96,768]{1,0:T(8,128)S(1)}, f32[96,768]{1,0:T(8,128)S(1)}, u32[]{:S(2)}, u32[]{:S(2)}) collective-permute-start(f32[96,768]{1,0:T(8,128)S(1)} %slice_add_fusion.9), channel_id=1, source_target_pairs={{0,4},{4,8},{8,12},{12,14},{14,10},{10,6},{6,2},{2,0},{1,5},{5,9},... | collective-permute-start | bytes 884744 | tf_op jit(solution)/shard_map/ppermute | solution.py:182
  142.2 6.8 %collective-permute-start.17 = (f32[96,768]{1,0:T(8,128)S(1)}, f32[96,768]{1,0:T(8,128)S(1)}, u32[]{:S(2)}, u32[]{:S(2)}) collective-permute-start(f32[96,768]{1,0:T(8,128)S(1)} %slice_add_fusion.2), channel_id=1, source_target_pairs={{0,2},{4,0},{8,4},{12,8},{14,12},{10,14},{6,10},{2,6},{1,3},{5,1},... | collective-permute-start | bytes 884744 | tf_op jit(solution)/shard_map/ppermute | solution.py:183
  146.8 7.3 %collective-permute-start.11 = (f32[96,768]{1,0:T(8,128)S(1)}, f32[96,768]{1,0:T(8,128)S(1)}, u32[]{:S(2)}, u32[]{:S(2)}) collective-permute-start(f32[96,768]{1,0:T(8,128)S(1)} %slice_add_fusion.8), channel_id=1, source_target_pairs={{0,4},{4,8},{8,12},{12,14},{14,10},{10,6},{6,2},{2,0},{1,5},{5,9},... | collective-permute-start | bytes 884744 | tf_op jit(solution)/shard_map/ppermute | solution.py:182
  149.0 7.1 %collective-permute-start.18 = (f32[96,768]{1,0:T(8,128)S(1)}, f32[96,768]{1,0:T(8,128)S(1)}, u32[]{:S(2)}, u32[]{:S(2)}) collective-permute-start(f32[96,768]{1,0:T(8,128)S(1)} %slice_add_fusion.1), channel_id=1, source_target_pairs={{0,2},{4,0},{8,4},{12,8},{14,12},{10,14},{6,10},{2,6},{1,3},{5,1},... | collective-permute-start | bytes 884744 | tf_op jit(solution)/shard_map/ppermute | solution.py:183
  (35 other events, 332.6 us)
